TPU v7x, 512 devices: a whole 4x4x16 slice. The times are simulated.
512 devices in a mesh: fibre: 128 (over x, y_hi, z), seg: 4 (over y_lo, core).
Axes of the slice: x: 4, y: 4 (y_hi: 2, y_lo: 2; y = y_hi * 2 + y_lo), z: 16, core: 2. Of those that a mesh axis runs over, the one named last changes fastest.
Arguments:
- data: bfloat16 [4, 1024, 2048], P('seg', 'fibre')
- sources: int32 [2, 4], replicated, may hold values from 0 to 7
- owners: int32 [2], replicated, may hold values from 0 to 127
Outputs:
- correlations: float32 [2, 4, 1024, 1024], P(None, None, ('fibre', 'seg'))
All inputs are finite; a program needn't handle non-finite values.
Results may differ from a plain program's by a relative error of at most 0.0066.
Values may be sent and summed in bfloat16 or wider, within the bound.
No kernel may reach another device: no remote copies, remote signals or barrier semaphores. Data moves between devices by JAX's collectives and lax.ppermute only.
A program may use at most 64 MiB of HBM per device.

v0:
```python
import math

import jax
import jax.numpy as jnp
from jax import lax
from jax.sharding import PartitionSpec as P

BAND = 128
LAGS = 1024


def spread(block, axis, holder):
    block = jnp.where(lax.axis_index(axis) == holder, block, jnp.zeros_like(block))
    return lax.psum(block, axis)


def extended(cells, sides, width):
    for axis, dim in sides:
        count = lax.axis_size(axis)
        ends = count - 1
        head = lax.slice_in_dim(cells, 0, width, axis=dim)
        tail = lax.slice_in_dim(cells, cells.shape[dim] - width, cells.shape[dim], axis=dim)
        cells = jnp.concatenate(
            [
                lax.ppermute(tail, axis, [(i, (i + 1) % count) for i in range(ends)]),
                cells,
                lax.ppermute(head, axis, [((i + 1) % count, i) for i in range(ends)]),
            ],
            axis=dim,
        )
    return cells


def make_tables(length, lags):
    half = length // 2
    times = jnp.arange(length, dtype=jnp.int32)
    freqs = jnp.arange(half, dtype=jnp.int32)
    phase = times[:, None] * freqs[None, :] % length
    angle = phase.astype(jnp.float32) * (2.0 * math.pi / length)
    forward = jnp.concatenate([jnp.cos(angle), -jnp.sin(angle)], axis=1).astype(jnp.bfloat16)
    shifts = jnp.arange(lags, dtype=jnp.int32) - lags // 2 + length
    phase_back = freqs[:, None] * shifts[None, :] % length
    angle_back = phase_back.astype(jnp.float32) * (2.0 * math.pi / length)
    inverse = jnp.concatenate([jnp.cos(angle_back), -jnp.sin(angle_back)], axis=0) * (
        1.0 / math.sqrt(half)
    )
    return (forward, inverse)


def whiten(spectra, band):
    lead = spectra.shape[:-1]
    width = spectra.shape[-1] // 2
    parts = spectra.reshape(lead + (2, width // band, band))
    power = jnp.sum(parts * parts, axis=(-3, -1)) / (2.0 * band)
    scale = lax.rsqrt(power + 1e-06)
    return (parts * scale[..., None, :, None]).reshape(spectra.shape)


def cross_sum(receivers, emitters):
    half = receivers.shape[2] // 2
    rec_re, rec_im = (receivers[..., :half], receivers[..., half:])
    emi_re, emi_im = (emitters[..., :half], emitters[..., half:])
    real_part = jnp.einsum("sck,snk->nck", rec_re, emi_re, preferred_element_type=jnp.float32)
    real_part = real_part + jnp.einsum(
        "sck,snk->nck", rec_im, emi_im, preferred_element_type=jnp.float32
    )
    imag_part = jnp.einsum("sck,snk->nck", rec_im, emi_re, preferred_element_type=jnp.float32)
    imag_part = imag_part - jnp.einsum(
        "sck,snk->nck", rec_re, emi_im, preferred_element_type=jnp.float32
    )
    return jnp.concatenate([real_part, imag_part], axis=-1)


def correlate(cross, inverse):
    count, chans, width = cross.shape
    flat = jnp.dot(cross.reshape(count * chans, width), inverse, precision=lax.Precision.HIGHEST)
    return flat.reshape(count, chans, inverse.shape[1])


def shards(data, sources, owners):
    seg_dev, ch_dev, length = data.shape
    steps = sources.shape[0]
    forward, inverse = make_tables(length, LAGS)
    spectra = jnp.dot(
        data.reshape(seg_dev * ch_dev, length), forward, preferred_element_type=jnp.float32
    )
    white = whiten(spectra.reshape(seg_dev, ch_dev, length), BAND).astype(jnp.bfloat16)
    selector = (sources[:, :, None] == jnp.arange(ch_dev, dtype=jnp.int32)[None, None, :]).astype(
        jnp.bfloat16
    )
    picked = jnp.einsum("pnc,scf->psnf", selector, white, preferred_element_type=jnp.float32)
    received = []
    for step in range(steps):
        received.append(spread(picked[step].astype(jnp.bfloat16), "fibre", owners[step]))
    chosen = jnp.stack(received)
    padded = extended(white, (("fibre", 1),), 4)
    total = padded[:, 0:ch_dev].astype(jnp.float32)
    for offset in range(1, 8):
        total = total + padded[:, offset : offset + ch_dev].astype(jnp.float32)
    stacked = (total * 0.125).astype(jnp.bfloat16)
    partial_list = [correlate(cross_sum(stacked, chosen[step]), inverse) for step in range(steps)]
    return lax.psum_scatter(jnp.stack(partial_list), "seg", scatter_dimension=2, tiled=True)


def solution(mesh):
    return jax.shard_map(
        shards,
        mesh=mesh,
        in_specs=(P("seg", "fibre", None), P(), P()),
        out_specs=P(None, None, ("fibre", "seg"), None),
        check_vma=False,
    )
```

profile of v0, /device:TPU:1, one launch (start us, length us, event | category | flops | bytes accessed | tf_op | source)
XLA Modules:
  0.0 840.4 jit_solution(10892744764179894782)
XLA Ops:
  6.5 0.0 copy-start
  6.5 0.0 all-reduce.4.cloned.1.call-start
  6.5 33.8 %negate_convert_fusion = (bf16[2048,1024]{1,0:T(8,128)(2,1)S(1)}, bf16[2048,1024]{1,0:T(8,128)(2,1)S(1)}) fusion(), kind=kLoop, calls=%fused_computation.12 | loop fusion | flops 35651584 | bytes 8388608 | tf_op jit(solution)/shard_map/convert.44
  40.4 0.0 copy-done
  40.4 0.0 copy-start.2
  40.4 0.0 copy-start.1
  40.4 1.2 fusion.57
  41.6 0.1 reduce_sum.9
  41.7 0.1 mul.100
  41.8 4.4 collective-permute-start
  46.2 1.3 collective-permute-start.1
  47.5 0.0 copy-done.2
  47.5 0.2 fusion.26
  47.8 0.0 copy-done.1
  47.8 0.6 fusion.56
  49.7 604.6 %all-reduce.1 = (bf16[1,4,2048]{2,1,0:T(4,128)(2,1)S(1)}, bf16[1,4,2048]{2,1,0:T(4,128)(2,1)S(1)}) all-reduce(bf16[1,4,2048]{2,1,0:T(4,128)(2,1)S(1)} %get-tuple-element.18, bf16[1,4,2048]{2,1,0:T(4,128)(2,1)S(1)} %get-tuple-element.17), channel_id=1, replica_groups=mesh['fibre'=128,'seg'=4] {'fibre'}, use_global_device_ids=true, to_apply=%region_2.3 | all-reduce | flops 16384 | bytes 65536 | tf_op jit(solution)/shard_map/psum | solution.py:14
  654.3 16.7 %fusion.27 = (f32[1024,1024]{1,0:T(8,128)S(1)}, f32[1024,1024]{1,0:T(8,128)S(1)}) fusion(s32[1024]{0:T(1024)S(1)} %iota_add_fusion), kind=kLoop, calls=%fused_computation.34 | loop fusion | flops 15728640 | bytes 8392704 | tf_op jit(solution)/shard_map/cos | solution.py:44
  671.0 0.0 collective-permute-done
  671.0 0.0 collective-permute-done.1
  671.0 0.1 multiply_convert_fusion
  671.1 0.1 add_bitcast_fusion.1
  671.2 5.0 fusion.28
  676.2 5.0 fusion.31
  681.3 0.9 copy.4
  682.2 0.0 all-reduce.4.cloned.1.call-update
  682.2 1.3 dynamic-slice
  684.1 148.0 %all-reduce.4.cloned.1.call-done = f32[2,4,8,1024]{3,1,0,2:T(4,128)} async-done(((f32[2,4,8,1024]{3,1,0,2:T(4,128)}), f32[2,4,8,1024]{3,1,0,2:T(4,128)}) %all-reduce.4.cloned.1.call-update) | async-done | bytes 262160
  832.1 0.8 constant_dynamic-slice_fusion
  832.9 0.7 copy.5
  (9 shorter events, 0.1 us)
Async XLA Ops:
  6.5 33.9 %copy-start = (bf16[1,8,2048]{2,1,0:T(8,128)(2,1)S(1)}, bf16[1,8,2048]{2,1,0:T(8,128)(2,1)}, u32[]{:S(2)}) copy-start(bf16[1,8,2048]{2,1,0:T(8,128)(2,1)} %param.3) | copy-start | bytes 98308
  6.5 825.5 %all-reduce.4.cloned.1.call-start = ((), (), s32[]{:S(2)}) async-start(), calls=%async_computation | async-start | bytes 524288
  40.4 7.1 copy-start.2
  40.4 7.3 copy-start.1
  41.8 629.2 %collective-permute-start = (bf16[1,4,2048]{2,1,0:T(4,128)(2,1)S(1)}, bf16[1,4,2048]{2,1,0:T(4,128)(2,1)S(1)}, u32[]{:S(2)}, u32[]{:S(2)}) collective-permute-start(bf16[1,4,2048]{2,1,0:T(4,128)(2,1)S(1)} %get-tuple-element.15), channel_id=1, source_target_pairs={{0,4},{4,8},{8,12},{12,16},{16,20},{20,24},{24,28},{28,32},{32,36}... | collective-permute-start | bytes 49160 | tf_op jit(solution)/shard_map/ppermute | solution.py:25
  46.2 624.8 %collective-permute-start.1 = (bf16[1,4,2048]{2,1,0:T(4,128)(2,1)S(1)}, bf16[1,4,2048]{2,1,0:T(4,128)(2,1)S(1)}, u32[]{:S(2)}, u32[]{:S(2)}) collective-permute-start(bf16[1,4,2048]{2,1,0:T(4,128)(2,1)S(1)} %get-tuple-element.16), channel_id=1, source_target_pairs={{4,0},{8,4},{12,8},{16,12},{20,16},{24,20},{28,24},{32,28},{36,32}... | collective-permute-start | bytes 49160 | tf_op jit(solution)/shard_map/ppermute | solution.py:27
Sparse Core Ops, SparseCore 0:
  682.3 149.7 all-reduce.3
where the time goes:
time: 841 us; the launch traced here: 840 us
  blocking collectives  605 us (72%)
  waiting for transfers between devices  148 us (18%)
  other arithmetic  50.9 us (6%)
  between operations  15.5 us (2%)
  matrix products  11.4 us (1%)
    psum x1, blocking collectives, spread(): return lax.psum(block, axis)  605 us
    unnamed x2, waiting for transfers between devices  148 us
    another operation x4, other arithmetic  33.9 us
  transfers between devices with their start and end apart: 3, of which 1 were waited for; matrix products, arithmetic and copies ran while one was open for 2% of the time, Pallas kernels for 0%

commit v1 on v0

v1 whole, which is shorter than its diff:
```python
import math

import jax
import jax.numpy as jnp
from jax import lax
from jax.sharding import PartitionSpec as P

BAND = 128
LAGS = 1024
LOW = 4
HIGH = 3


def radices(count):
    if count == 128:
        return [4, 4, 2, 4]
    out = []
    while count % 4 == 0:
        out.append(4)
        count //= 4
    while count % 2 == 0:
        out.append(2)
        count //= 2
    if count > 1:
        out.append(count)
    return out


def broadcast(block, axis):
    count = lax.axis_size(axis)
    stride = 1
    for radix in radices(count):
        total = block
        for shift in range(1, radix):
            perm = []
            for i in range(count):
                digit = (i // stride) % radix
                perm.append((i, i + ((digit + shift) % radix - digit) * stride))
            total = total + lax.ppermute(block, axis, perm)
        block = total
        stride *= radix
    return block


def gather(block, axis):
    count = lax.axis_size(axis)
    pieces = [block]
    for shift in range(1, count):
        pieces.append(lax.ppermute(block, axis, [(i, (i + shift) % count) for i in range(count)]))
    return jnp.concatenate(pieces, axis=0)


def halo(cells, axis, dim):
    count = lax.axis_size(axis)
    ends = count - 1
    tail = lax.slice_in_dim(cells, cells.shape[dim] - LOW, cells.shape[dim], axis=dim)
    head = lax.slice_in_dim(cells, 0, HIGH, axis=dim)
    return jnp.concatenate(
        [
            lax.ppermute(tail, axis, [(i, i + 1) for i in range(ends)]),
            cells,
            lax.ppermute(head, axis, [(i + 1, i) for i in range(ends)]),
        ],
        axis=dim,
    )


def cos_sin(phase, period):
    angle = phase.astype(jnp.float32) * (2.0 * math.pi / period)
    return jnp.cos(angle), jnp.sin(angle)


def make_forward(length):
    half = length // 2
    lo_count = 64
    hi_count = length // lo_count
    freqs = jnp.arange(half, dtype=jnp.int32)
    hi = jnp.arange(hi_count, dtype=jnp.int32)
    lo = jnp.arange(lo_count, dtype=jnp.int32)
    hi_c, hi_s = cos_sin(hi[:, None] * freqs[None, :] % hi_count, hi_count)
    lo_c, lo_s = cos_sin(lo[:, None] * freqs[None, :] % length, length)
    cos = hi_c[:, None, :] * lo_c[None, :, :] - hi_s[:, None, :] * lo_s[None, :, :]
    sin = hi_s[:, None, :] * lo_c[None, :, :] + hi_c[:, None, :] * lo_s[None, :, :]
    table = jnp.concatenate([cos, -sin], axis=-1)
    return table.reshape(length, length).astype(jnp.bfloat16)


def make_inverse(length, lags):
    half = length // 2
    lo_count = 32
    hi_count = half // lo_count
    period = length // lo_count
    shifts = jnp.arange(lags, dtype=jnp.int32) - lags // 2 + length
    hi = jnp.arange(hi_count, dtype=jnp.int32)
    lo = jnp.arange(lo_count, dtype=jnp.int32)
    hi_c, hi_s = cos_sin(hi[:, None] * shifts[None, :] % period, period)
    lo_c, lo_s = cos_sin(lo[:, None] * shifts[None, :] % length, length)
    cos = hi_c[:, None, :] * lo_c[None, :, :] - hi_s[:, None, :] * lo_s[None, :, :]
    sin = hi_s[:, None, :] * lo_c[None, :, :] + hi_c[:, None, :] * lo_s[None, :, :]
    table = jnp.concatenate([cos.reshape(half, lags), -sin.reshape(half, lags)], axis=0)
    return table * (1.0 / math.sqrt(half))


def whiten(spectra, band):
    lead = spectra.shape[:-1]
    width = spectra.shape[-1] // 2
    parts = spectra.reshape(lead + (2, width // band, band))
    power = jnp.sum(parts * parts, axis=(-3, -1)) / (2.0 * band)
    scale = lax.rsqrt(power + 1e-06)
    return (parts * scale[..., None, :, None]).reshape(spectra.shape)


def cross_sum(receivers, emitters):
    half = receivers.shape[2] // 2
    rec_re, rec_im = (receivers[..., :half], receivers[..., half:])
    emi_re, emi_im = (emitters[..., :half], emitters[..., half:])
    real_part = jnp.einsum("sck,snk->nck", rec_re, emi_re, preferred_element_type=jnp.float32)
    real_part = real_part + jnp.einsum(
        "sck,snk->nck", rec_im, emi_im, preferred_element_type=jnp.float32
    )
    imag_part = jnp.einsum("sck,snk->nck", rec_im, emi_re, preferred_element_type=jnp.float32)
    imag_part = imag_part - jnp.einsum(
        "sck,snk->nck", rec_re, emi_im, preferred_element_type=jnp.float32
    )
    return jnp.concatenate([real_part, imag_part], axis=-1)


def shards(data, sources, owners):
    seg_dev, ch_dev, length = data.shape
    steps, nsrc = sources.shape
    seg_count = lax.axis_size("seg")
    per = ch_dev // seg_count
    selector = (sources[:, :, None] == jnp.arange(ch_dev, dtype=jnp.int32)[None, None, :]).astype(
        jnp.bfloat16
    )
    picked = jnp.einsum("pnc,scf->spnf", selector, data, preferred_element_type=jnp.float32)
    picked = picked.astype(jnp.bfloat16)
    here = lax.axis_index("fibre")
    masked = [
        jnp.where(here == owners[step], picked[:, step], jnp.zeros_like(picked[:, step]))
        for step in range(steps)
    ]
    received = broadcast(jnp.concatenate(masked, axis=1), "fibre")
    window = halo(data, "fibre", 1)
    rows = window.shape[1]
    block = jnp.concatenate([window, received], axis=1)
    block = gather(block, "seg")
    segs = block.shape[0]
    forward = make_forward(length)
    inverse = make_inverse(length, LAGS)
    spectra = jnp.dot(
        block.reshape(segs * block.shape[1], length), forward, preferred_element_type=jnp.float32
    )
    white = whiten(spectra.reshape(block.shape), BAND).astype(jnp.bfloat16)
    chosen = white[:, rows:].reshape(segs, steps, nsrc, length)
    start = lax.axis_index("seg") * per
    part = lax.dynamic_slice_in_dim(white[:, :rows], start, per + LOW + HIGH, axis=1)
    total = part[:, 0:per].astype(jnp.float32)
    for offset in range(1, LOW + HIGH + 1):
        total = total + part[:, offset : offset + per].astype(jnp.float32)
    stacked = (total * 0.125).astype(jnp.bfloat16)
    cross = jnp.stack([cross_sum(stacked, chosen[:, step]) for step in range(steps)])
    flat = jnp.dot(
        cross.reshape(-1, length), inverse, precision=lax.Precision.HIGHEST
    )
    return flat.reshape(steps, nsrc, per, LAGS)


def solution(mesh):
    return jax.shard_map(
        shards,
        mesh=mesh,
        in_specs=(P("seg", "fibre", None), P(), P()),
        out_specs=P(None, None, ("fibre", "seg"), None),
        check_vma=False,
    )
```

time: 841 us -> 160 us (0.19)
  blocking collectives: 605 us -> 0 us
  waiting for transfers between devices: 148 us -> 3.66 us
  starting transfers between devices: 5.67 us -> 69.1 us
  other arithmetic: 50.9 us -> 20.7 us
  matrix products: 11.4 us -> 36.2 us
  local copies, waits for them, and re-layouts: 4.38 us -> 27.1 us
  between operations: 15.5 us -> 1.79 us
    psum x1 -> x0, blocking collectives: 605 us -> none  [spread(): return lax.psum(block, axis)]
    unnamed x2 -> x0, waiting for transfers between devices: 148 us -> none
    ppermute x2 -> x15, starting transfers between devices: 5.66 us -> 69.1 us  [the longest x10 52.1 us: broadcast(): total = total + lax.ppermute(block, axis, perm)]
    another operation x5 -> x3, other arithmetic: 33.9 us -> 5 us
    dot_general x4 -> x11, matrix products: 11.4 us -> 36.2 us  [the longest x1 8.01 us: shards(): jnp.dot(cross.reshape(-1, length), inverse, precision=lax.Precision.HIGHEST)]
    cos x1, other arithmetic: 16.7 us -> 1.02 us  [cos_sin(): return (jnp.cos(angle), jnp.sin(angle))]
    dot_general x0 -> x2, local copies, waits for them, and re-layouts: none -> 13 us  [the longest x1 12.3 us: shards(): jnp.dot(block.reshape(segs * block.shape[1], length), forward, preferred_...]
  transfers between devices with their start and end apart: 3 -> 15, of which waited for: 1 -> 2; matrix products, arithmetic and copies ran while one was open for 2% -> 22% of each run, Pallas kernels for 0% -> 0%
where the time goes in v1:
time: 160 us; the launch traced here: 159 us
  starting transfers between devices  69.1 us (43%)
  matrix products  36.2 us (23%)
  local copies, waits for them, and re-layouts  27.1 us (17%)
  other arithmetic  20.7 us (13%)
  waiting for transfers between devices  3.66 us (2%)
  between operations  1.79 us (1%)
    ppermute x10, starting transfers between devices, broadcast(): total = total + lax.ppermute(block, axis, perm)  52.1 us
    ppermute x3, starting transfers between devices, gather(): lax.ppermute(block, axis, [(i, (i + shift) % count) for i in range(count)])  13.1 us
    dot_general x1, local copies, waits for them, and re-layouts, shards(): jnp.dot(block.reshape(segs * block.shape[1], length), forward, preferred_...  12.3 us
    dot_general x1, other arithmetic, shards(): jnp.dot(block.reshape(segs * block.shape[1], length), forward, preferred_...  8.21 us
    dot_general x1, matrix products, shards(): jnp.dot(cross.reshape(-1, length), inverse, precision=lax.Precision.HIGHEST)  8.01 us
    dot_general x1, matrix products, shards(): jnp.dot(block.reshape(segs * block.shape[1], length), forward, preferred_...  6.14 us
    dot_general x2, matrix products, cross_sum(): jnp.einsum('sck,snk->nck', rec_re, emi_im, preferred_element_type=jnp.flo...  5.85 us
    dot_general x2, matrix products, cross_sum(): jnp.einsum('sck,snk->nck', rec_im, emi_im, preferred_element_type=jnp.flo...  5.65 us
  transfers between devices with their start and end apart: 15, of which 2 were waited for; matrix products, arithmetic and copies ran while one was open for 22% of the time, Pallas kernels for 0%

profile of v1, /device:TPU:1, one launch (start us, length us, event | category | flops | bytes accessed | tf_op | source)
XLA Modules:
  0.0 158.6 jit_solution(15989559513726365374)
XLA Ops:
  0.0 1.4 fusion.103
  2.7 1.0 fusion.6
  3.7 4.4 %collective-permute-start.2 = (bf16[1,8,2048]{2,1,0:T(8,128)(2,1)S(1)}, bf16[1,8,2048]{2,1,0:T(8,128)(2,1)S(1)}, u32[]{:S(2)}, u32[]{:S(2)}) collective-permute-start(bf16[1,8,2048]{2,1,0:T(8,128)(2,1)S(1)} %pad_maximum_fusion.1), channel_id=1, source_target_pairs={{0,4},{4,8},{8,12},{12,0},{16,20},{20,24},{24,28},{28,16},{32,36},... | collective-permute-start | bytes 98312 | tf_op jit(solution)/shard_map/ppermute | solution.py:39
  8.1 4.9 %collective-permute-start.3 = (bf16[1,8,2048]{2,1,0:T(8,128)(2,1)S(1)}, bf16[1,8,2048]{2,1,0:T(8,128)(2,1)S(1)}, u32[]{:S(2)}, u32[]{:S(2)}) collective-permute-start(bf16[1,8,2048]{2,1,0:T(8,128)(2,1)S(1)} %pad_maximum_fusion.1), channel_id=1, source_target_pairs={{0,8},{4,12},{8,0},{12,4},{16,24},{20,28},{24,16},{28,20},{32,40},... | collective-permute-start | bytes 98312 | tf_op jit(solution)/shard_map/ppermute | solution.py:39
  13.0 2.6 %collective-permute-start.4 = (bf16[1,8,2048]{2,1,0:T(8,128)(2,1)S(1)}, bf16[1,8,2048]{2,1,0:T(8,128)(2,1)S(1)}, u32[]{:S(2)}, u32[]{:S(2)}) collective-permute-start(bf16[1,8,2048]{2,1,0:T(8,128)(2,1)S(1)} %pad_maximum_fusion.1), channel_id=1, source_target_pairs={{0,12},{4,0},{8,4},{12,8},{16,28},{20,16},{24,20},{28,24},{32,44},... | collective-permute-start | bytes 98312 | tf_op jit(solution)/shard_map/ppermute | solution.py:39
  15.7 0.8 slice.74
  16.5 2.6 %collective-permute-start = (bf16[1,4,2048]{2,1,0:T(4,128)(2,1)S(1)}, bf16[1,4,2048]{2,1,0:T(4,128)(2,1)S(1)}, u32[]{:S(2)}, u32[]{:S(2)}) collective-permute-start(bf16[1,4,2048]{2,1,0:T(4,128)(2,1)S(1)} %slice.74), channel_id=1, source_target_pairs={{0,4},{4,8},{8,12},{12,16},{16,20},{20,24},{24,28},{28,32},{32,36}... | collective-permute-start | bytes 49160 | tf_op jit(solution)/shard_map/ppermute | solution.py:60
  19.1 0.8 slice.75
  19.9 1.3 collective-permute-start.1
  21.2 1.0 fusion.81
  22.2 0.5 fusion.88
  22.7 5.0 %subtract_convert_fusion = (bf16[32,64,1024]{2,1,0:T(8,128)(2,1)}, bf16[32,64,1024]{2,1,0:T(8,128)(2,1)}) fusion(f32[64,1024]{1,0:T(8,128)S(1)} %get-tuple-element.31, f32[32,1024]{1,0:T(8,128)S(1)} %get-tuple-element.33, f32[64,1024]{1,0:T(8,128)S(1)} %get-tuple-element.32, f32[32,1024]{1,0:T(8,128)S(1)} %get-tuple-element.34), kind=kLoop, calls=%fused_computation.7 | loop fusion | flops 18874368 | bytes 9175040 | tf_op jit(solution)/shard_map/convert.3
  27.7 11.4 %collective-permute-start.5 = (bf16[1,8,2048]{2,1,0:T(8,128)(2,1)S(1)}, bf16[1,8,2048]{2,1,0:T(8,128)(2,1)S(1)}, u32[]{:S(2)}, u32[]{:S(2)}) collective-permute-start(bf16[1,8,2048]{2,1,0:T(8,128)(2,1)S(1)} %add_add_fusion.2), channel_id=1, source_target_pairs={{0,16},{4,20},{8,24},{12,28},{16,32},{20,36},{24,40},{28,44},{32,4... | collective-permute-start | bytes 98312 | tf_op jit(solution)/shard_map/ppermute | solution.py:39
  39.1 8.8 %collective-permute-start.6 = (bf16[1,8,2048]{2,1,0:T(8,128)(2,1)S(1)}, bf16[1,8,2048]{2,1,0:T(8,128)(2,1)S(1)}, u32[]{:S(2)}, u32[]{:S(2)}) collective-permute-start(bf16[1,8,2048]{2,1,0:T(8,128)(2,1)S(1)} %add_add_fusion.2), channel_id=1, source_target_pairs={{0,32},{4,36},{8,40},{12,44},{16,48},{20,52},{24,56},{28,60},{32,0... | collective-permute-start | bytes 98312 | tf_op jit(solution)/shard_map/ppermute | solution.py:39
  48.0 5.2 %collective-permute-start.7 = (bf16[1,8,2048]{2,1,0:T(8,128)(2,1)S(1)}, bf16[1,8,2048]{2,1,0:T(8,128)(2,1)S(1)}, u32[]{:S(2)}, u32[]{:S(2)}) collective-permute-start(bf16[1,8,2048]{2,1,0:T(8,128)(2,1)S(1)} %add_add_fusion.2), channel_id=1, source_target_pairs={{0,48},{4,52},{8,56},{12,60},{16,0},{20,4},{24,8},{28,12},{32,16},... | collective-permute-start | bytes 98312 | tf_op jit(solution)/shard_map/ppermute | solution.py:39
  53.2 8.2 %maximum_bitcast_fusion = bf16[2048,2048]{0,1:T(8,128)(2,1)} fusion(bf16[2048,1024]{1,0:T(8,128)(2,1)} %bitcast.98, bf16[2048,1024]{1,0:T(8,128)(2,1)} %bitcast.97), kind=kLoop, calls=%fused_computation | loop fusion | flops 16777216 | bytes 16777216 | tf_op jit(solution)/shard_map/dot_general | solution.py:151
  61.4 4.8 %collective-permute-start.8 = (bf16[1,8,2048]{2,1,0:T(8,128)(2,1)S(1)}, bf16[1,8,2048]{2,1,0:T(8,128)(2,1)S(1)}, u32[]{:S(2)}, u32[]{:S(2)}) collective-permute-start(bf16[1,8,2048]{2,1,0:T(8,128)(2,1)S(1)} %add_add_fusion.1), channel_id=1, source_target_pairs={{0,64},{4,68},{8,72},{12,76},{16,80},{20,84},{24,88},{28,92},{32,9... | collective-permute-start | bytes 98312 | tf_op jit(solution)/shard_map/ppermute | solution.py:39
  66.3 1.3 collective-permute-done.8
  67.6 4.7 %collective-permute-start.10 = (bf16[1,8,2048]{2,1,0:T(8,128)(2,1)S(1)}, bf16[1,8,2048]{2,1,0:T(8,128)(2,1)S(1)}, u32[]{:S(2)}, u32[]{:S(2)}) collective-permute-start(bf16[1,8,2048]{2,1,0:T(8,128)(2,1)S(1)} %add.164), channel_id=1, source_target_pairs={{0,256},{4,260},{8,264},{12,268},{16,272},{20,276},{24,280},{28,28... | collective-permute-start | bytes 98312 | tf_op jit(solution)/shard_map/ppermute | solution.py:39
  72.3 2.8 %collective-permute-start.11 = (bf16[1,8,2048]{2,1,0:T(8,128)(2,1)S(1)}, bf16[1,8,2048]{2,1,0:T(8,128)(2,1)S(1)}, u32[]{:S(2)}, u32[]{:S(2)}) collective-permute-start(bf16[1,8,2048]{2,1,0:T(8,128)(2,1)S(1)} %add.164), channel_id=1, source_target_pairs={{0,384},{4,388},{8,392},{12,396},{16,400},{20,404},{24,408},{28,41... | collective-permute-start | bytes 98312 | tf_op jit(solution)/shard_map/ppermute | solution.py:39
  75.0 2.5 %collective-permute-start.9 = (bf16[1,8,2048]{2,1,0:T(8,128)(2,1)S(1)}, bf16[1,8,2048]{2,1,0:T(8,128)(2,1)S(1)}, u32[]{:S(2)}, u32[]{:S(2)}) collective-permute-start(bf16[1,8,2048]{2,1,0:T(8,128)(2,1)S(1)} %add.164), channel_id=1, source_target_pairs={{0,128},{4,132},{8,136},{12,140},{16,144},{20,148},{24,152},{28,15... | collective-permute-start | bytes 98312 | tf_op jit(solution)/shard_map/ppermute | solution.py:39
  77.6 1.0 fusion.93
  78.6 2.3 %collective-permute-done.9 = bf16[1,8,2048]{2,1,0:T(8,128)(2,1)S(1)} collective-permute-done((bf16[1,8,2048]{2,1,0:T(8,128)(2,1)S(1)}, bf16[1,8,2048]{2,1,0:T(8,128)(2,1)S(1)}, u32[]{:S(2)}, u32[]{:S(2)}) %collective-permute-start.9) | collective-permute-done | bytes 32800 | tf_op jit(solution)/shard_map/ppermute | solution.py:39
  81.0 8.9 %collective-permute-start.12 = (bf16[1,23,2048]{2,1,0:T(8,128)(2,1)S(1)}, bf16[1,23,2048]{2,1,0:T(8,128)(2,1)S(1)}, u32[]{:S(2)}, u32[]{:S(2)}) collective-permute-start(bf16[1,23,2048]{2,1,0:T(8,128)(2,1)S(1)} %pad_maximum_fusion), channel_id=1, source_target_pairs={{0,1},{1,2},{2,3},{3,0},{4,5},{5,6},{6,7},{7,4},{8,9},{9,10},{10,1... | collective-permute-start | bytes 282632 | tf_op jit(solution)/shard_map/ppermute | solution.py:49
  89.9 2.1 %collective-permute-start.13 = (bf16[1,23,2048]{2,1,0:T(8,128)(2,1)S(1)}, bf16[1,23,2048]{2,1,0:T(8,128)(2,1)S(1)}, u32[]{:S(2)}, u32[]{:S(2)}) collective-permute-start(bf16[1,23,2048]{2,1,0:T(8,128)(2,1)S(1)} %pad_maximum_fusion), channel_id=1, source_target_pairs={{0,2},{1,3},{2,0},{3,1},{4,6},{5,7},{6,4},{7,5},{8,10},{9,11},{10,... | collective-permute-start | bytes 282632 | tf_op jit(solution)/shard_map/ppermute | solution.py:49
  92.0 2.1 %collective-permute-start.14 = (bf16[1,23,2048]{2,1,0:T(8,128)(2,1)S(1)}, bf16[1,23,2048]{2,1,0:T(8,128)(2,1)S(1)}, u32[]{:S(2)}, u32[]{:S(2)}) collective-permute-start(bf16[1,23,2048]{2,1,0:T(8,128)(2,1)S(1)} %pad_maximum_fusion), channel_id=1, source_target_pairs={{0,3},{1,0},{2,1},{3,2},{4,7},{5,4},{6,5},{7,6},{8,11},{9,8},{10,9... | collective-permute-start | bytes 282632 | tf_op jit(solution)/shard_map/ppermute | solution.py:49
  94.1 4.5 %multiply_subtract_fusion = (f32[32,32,1024]{2,1,0:T(8,128)}, f32[32,32,1024]{2,1,0:T(8,128)}) fusion(f32[32,1024]{1,0:T(8,128)S(1)} %get-tuple-element.25, f32[32,1024]{1,0:T(8,128)S(1)} %get-tuple-element.24, f32[32,1024]{1,0:T(8,128)S(1)} %get-tuple-element.26, f32[32,1024]{1,0:T(8,128)S(1)} %get-tuple-element.23), kind=kLoop, calls=%fused_computation.10 | loop fusion | flops 7340032 | bytes 8912896 | tf_op jit(solution)/shard_map/sub | solution.py:98
  98.6 12.3 %copy.34 = bf16[2048,2048]{1,0:T(8,128)(2,1)} copy(bf16[2048,2048]{0,1:T(8,128)(2,1)} %maximum_bitcast_fusion) | data formatting | bytes 16777216 | tf_op jit(solution)/shard_map/dot_general | solution.py:151
  110.9 6.1 %multiply_reduce_fusion = (f32[4,23,8]{1,2,0:T(8,128)S(1)}, f32[4,23,2,8,128]{4,1,3,2,0:T(8,128)S(1)}) fusion(bf16[2,8,128,2048,1]{3,2,1,0,4:T(8,128)(2,1)} %bitcast.99, bf16[1,23,2048]{2,1,0:T(8,128)(2,1)S(1)} %collective-permute-done.14, bf16[1,23,2048]{2,1,0:T(8,128)(2,1)S(1)} %collective-permute-done.13, ...), kind=kOutput, calls=%fused_computation.38 | convolution fusion | flops 774765824 | bytes 9522048 | tf_op jit(solution)/shard_map/dot_general | solution.py:151
  117.8 0.7 fusion.101
  118.5 1.5 copy.55
  120.5 0.5 copy.40
  121.0 1.2 copy.39
  122.2 2.3 %fusion.15 = f32[1024,4,2]{1,2,0:T(2,128)} fusion(bf16[4,2,1024]{0,1,2:T(2,128)(2,1)S(1)} %copy.40, bf16[4,1,4,2048]{2,0,3,1:T(4,128)(2,1)S(1)} %copy.55), kind=kOutput, calls=%fused_computation.21 | convolution fusion | flops 65536 | bytes 114688 | tf_op jit(solution)/shard_map/sck,snk->nck/dot_general | solution.py:118
  124.5 2.2 %fusion.19 = f32[1024,4,2]{1,2,0:T(2,128)} fusion(bf16[4,2,1024]{0,1,2:T(2,128)(2,1)S(1)} %copy-done.5, bf16[4,1,4,2048]{2,0,3,1:T(4,128)(2,1)S(1)} %copy.55), kind=kOutput, calls=%fused_computation.25 | convolution fusion | flops 65536 | bytes 114688 | tf_op jit(solution)/shard_map/sck,snk->nck/dot_general | solution.py:122
  126.7 1.5 copy.66
  128.2 1.3 copy-done.2
  129.5 3.3 %fusion.7 = f32[1024,4,2]{1,2,0:T(2,128)} fusion(bf16[4,2,1024]{0,1,2:T(2,128)(2,1)} %copy-done.4, bf16[4,1,4,2048]{2,0,3,1:T(4,128)(2,1)S(1)} %copy.66), kind=kOutput, calls=%fused_computation.13 | convolution fusion | flops 65536 | bytes 114688 | tf_op jit(solution)/shard_map/sck,snk->nck/dot_general | solution.py:118
  132.9 3.6 %fusion.11 = f32[1024,4,2]{1,2,0:T(2,128)} fusion(bf16[4,2,1024]{0,1,2:T(2,128)(2,1)S(1)} %copy-done.6, bf16[4,1,4,2048]{2,0,3,1:T(4,128)(2,1)} %copy-done.2), kind=kOutput, calls=%fused_computation.17 | convolution fusion | flops 65536 | bytes 114688 | tf_op jit(solution)/shard_map/sck,snk->nck/dot_general | solution.py:122
  136.5 1.2 fusion.32
  137.7 1.1 copy.43
  138.8 2.6 %fusion.26 = f32[4,2,1024]{0,1,2:T(2,128)S(1)} fusion(f32[1024,4,2]{1,2,0:T(2,128)} %fusion.19, bf16[4,2,1024]{0,1,2:T(2,128)(2,1)} %copy-done.4, bf16[4,1,4,2048]{2,0,3,1:T(4,128)(2,1)S(1)} %copy-done.1), kind=kOutput, calls=%fused_computation.30 | convolution fusion | flops 73728 | bytes 147456 | tf_op jit(solution)/shard_map/sck,snk->nck/dot_general | solution.py:121
  141.4 1.1 copy.44
  142.5 3.1 %fusion.44 = f32[4,2,1024]{0,1,2:T(2,128)S(1)} fusion(f32[1024,4,2]{1,2,0:T(2,128)} %fusion.7, bf16[4,2,1024]{0,1,2:T(2,128)(2,1)} %copy.39, bf16[4,1,4,2048]{2,0,3,1:T(4,128)(2,1)} %copy-done.2), kind=kOutput, calls=%fused_computation.36 | convolution fusion | flops 73728 | bytes 147456 | tf_op jit(solution)/shard_map/sck,snk->nck/dot_general | solution.py:117
  145.6 1.1 copy.50
  146.7 2.6 %fusion.38 = f32[4,2,1024]{0,1,2:T(2,128)S(1)} fusion(f32[1024,4,2]{1,2,0:T(2,128)} %fusion.11, bf16[4,2,1024]{0,1,2:T(2,128)(2,1)} %copy-done.4, bf16[4,1,4,2048]{2,0,3,1:T(4,128)(2,1)S(1)} %copy-done.3), kind=kOutput, calls=%fused_computation.34 | convolution fusion | flops 73728 | bytes 147456 | tf_op jit(solution)/shard_map/sck,snk->nck/dot_general | solution.py:121
  149.9 8.0 %fusion.1 = f32[2,4,2,1024]{3,1,2,0:T(4,128)S(1)} fusion(f32[1024,1024]{1,0:T(8,128)} %bitcast.96, f32[1024,1024]{1,0:T(8,128)} %bitcast.95, f32[1,4,2,2048]{3,1,2,0:T(4,128)S(1)} %maximum_bitcast_fusion.4, f32[1,4,2,2048]{3,1,2,0:T(4,128)S(1)} %maximum_bitcast_fusion.3), kind=kOutput, calls=%fused_computation.3 | convolution fusion | flops 406880256 | bytes 8585216 | tf_op jit(solution)/shard_map/dot_general | solution.py:163
  157.9 0.7 copy.52
  (59 shorter events, 2.0 us)
Async XLA Ops:
  3.7 24.0 %collective-permute-start.2 = (bf16[1,8,2048]{2,1,0:T(8,128)(2,1)S(1)}, bf16[1,8,2048]{2,1,0:T(8,128)(2,1)S(1)}, u32[]{:S(2)}, u32[]{:S(2)}) collective-permute-start(bf16[1,8,2048]{2,1,0:T(8,128)(2,1)S(1)} %pad_maximum_fusion.1), channel_id=1, source_target_pairs={{0,4},{4,8},{8,12},{12,0},{16,20},{20,24},{24,28},{28,16},{32,36},... | collective-permute-start | bytes 98312 | tf_op jit(solution)/shard_map/ppermute | solution.py:39
  8.1 19.6 %collective-permute-start.3 = (bf16[1,8,2048]{2,1,0:T(8,128)(2,1)S(1)}, bf16[1,8,2048]{2,1,0:T(8,128)(2,1)S(1)}, u32[]{:S(2)}, u32[]{:S(2)}) collective-permute-start(bf16[1,8,2048]{2,1,0:T(8,128)(2,1)S(1)} %pad_maximum_fusion.1), channel_id=1, source_target_pairs={{0,8},{4,12},{8,0},{12,4},{16,24},{20,28},{24,16},{28,20},{32,40},... | collective-permute-start | bytes 98312 | tf_op jit(solution)/shard_map/ppermute | solution.py:39
  13.0 14.7 %collective-permute-start.4 = (bf16[1,8,2048]{2,1,0:T(8,128)(2,1)S(1)}, bf16[1,8,2048]{2,1,0:T(8,128)(2,1)S(1)}, u32[]{:S(2)}, u32[]{:S(2)}) collective-permute-start(bf16[1,8,2048]{2,1,0:T(8,128)(2,1)S(1)} %pad_maximum_fusion.1), channel_id=1, source_target_pairs={{0,12},{4,0},{8,4},{12,8},{16,28},{20,16},{24,20},{28,24},{32,44},... | collective-permute-start | bytes 98312 | tf_op jit(solution)/shard_map/ppermute | solution.py:39
  16.5 64.5 %collective-permute-start = (bf16[1,4,2048]{2,1,0:T(4,128)(2,1)S(1)}, bf16[1,4,2048]{2,1,0:T(4,128)(2,1)S(1)}, u32[]{:S(2)}, u32[]{:S(2)}) collective-permute-start(bf16[1,4,2048]{2,1,0:T(4,128)(2,1)S(1)} %slice.74), channel_id=1, source_target_pairs={{0,4},{4,8},{8,12},{12,16},{16,20},{20,24},{24,28},{28,32},{32,36}... | collective-permute-start | bytes 49160 | tf_op jit(solution)/shard_map/ppermute | solution.py:60
  19.9 61.0 %collective-permute-start.1 = (bf16[1,3,2048]{2,1,0:T(4,128)(2,1)S(1)}, bf16[1,3,2048]{2,1,0:T(4,128)(2,1)S(1)}, u32[]{:S(2)}, u32[]{:S(2)}) collective-permute-start(bf16[1,3,2048]{2,1,0:T(4,128)(2,1)S(1)} %slice.75), channel_id=1, source_target_pairs={{4,0},{8,4},{12,8},{16,12},{20,16},{24,20},{28,24},{32,28},{36,32}... | collective-permute-start | bytes 36872 | tf_op jit(solution)/shard_map/ppermute | solution.py:62
  27.7 33.6 %collective-permute-start.5 = (bf16[1,8,2048]{2,1,0:T(8,128)(2,1)S(1)}, bf16[1,8,2048]{2,1,0:T(8,128)(2,1)S(1)}, u32[]{:S(2)}, u32[]{:S(2)}) collective-permute-start(bf16[1,8,2048]{2,1,0:T(8,128)(2,1)S(1)} %add_add_fusion.2), channel_id=1, source_target_pairs={{0,16},{4,20},{8,24},{12,28},{16,32},{20,36},{24,40},{28,44},{32,4... | collective-permute-start | bytes 98312 | tf_op jit(solution)/shard_map/ppermute | solution.py:39
  39.1 22.3 %collective-permute-start.6 = (bf16[1,8,2048]{2,1,0:T(8,128)(2,1)S(1)}, bf16[1,8,2048]{2,1,0:T(8,128)(2,1)S(1)}, u32[]{:S(2)}, u32[]{:S(2)}) collective-permute-start(bf16[1,8,2048]{2,1,0:T(8,128)(2,1)S(1)} %add_add_fusion.2), channel_id=1, source_target_pairs={{0,32},{4,36},{8,40},{12,44},{16,48},{20,52},{24,56},{28,60},{32,0... | collective-permute-start | bytes 98312 | tf_op jit(solution)/shard_map/ppermute | solution.py:39
  48.0 13.4 %collective-permute-start.7 = (bf16[1,8,2048]{2,1,0:T(8,128)(2,1)S(1)}, bf16[1,8,2048]{2,1,0:T(8,128)(2,1)S(1)}, u32[]{:S(2)}, u32[]{:S(2)}) collective-permute-start(bf16[1,8,2048]{2,1,0:T(8,128)(2,1)S(1)} %add_add_fusion.2), channel_id=1, source_target_pairs={{0,48},{4,52},{8,56},{12,60},{16,0},{20,4},{24,8},{28,12},{32,16},... | collective-permute-start | bytes 98312 | tf_op jit(solution)/shard_map/ppermute | solution.py:39
  53.2 27.8 %copy-start.7 = (bf16[1,8,2048]{2,1,0:T(8,128)(2,1)S(1)}, bf16[1,8,2048]{2,1,0:T(8,128)(2,1)}, u32[]{:S(2)}) copy-start(bf16[1,8,2048]{2,1,0:T(8,128)(2,1)} %param.3) | copy-start | bytes 98308
  61.4 6.2 %collective-permute-start.8 = (bf16[1,8,2048]{2,1,0:T(8,128)(2,1)S(1)}, bf16[1,8,2048]{2,1,0:T(8,128)(2,1)S(1)}, u32[]{:S(2)}, u32[]{:S(2)}) collective-permute-start(bf16[1,8,2048]{2,1,0:T(8,128)(2,1)S(1)} %add_add_fusion.1), channel_id=1, source_target_pairs={{0,64},{4,68},{8,72},{12,76},{16,80},{20,84},{24,88},{28,92},{32,9... | collective-permute-start | bytes 98312 | tf_op jit(solution)/shard_map/ppermute | solution.py:39
  67.6 11.0 %collective-permute-start.10 = (bf16[1,8,2048]{2,1,0:T(8,128)(2,1)S(1)}, bf16[1,8,2048]{2,1,0:T(8,128)(2,1)S(1)}, u32[]{:S(2)}, u32[]{:S(2)}) collective-permute-start(bf16[1,8,2048]{2,1,0:T(8,128)(2,1)S(1)} %add.164), channel_id=1, source_target_pairs={{0,256},{4,260},{8,264},{12,268},{16,272},{20,276},{24,280},{28,28... | collective-permute-start | bytes 98312 | tf_op jit(solution)/shard_map/ppermute | solution.py:39
  72.3 6.3 %collective-permute-start.11 = (bf16[1,8,2048]{2,1,0:T(8,128)(2,1)S(1)}, bf16[1,8,2048]{2,1,0:T(8,128)(2,1)S(1)}, u32[]{:S(2)}, u32[]{:S(2)}) collective-permute-start(bf16[1,8,2048]{2,1,0:T(8,128)(2,1)S(1)} %add.164), channel_id=1, source_target_pairs={{0,384},{4,388},{8,392},{12,396},{16,400},{20,404},{24,408},{28,41... | collective-permute-start | bytes 98312 | tf_op jit(solution)/shard_map/ppermute | solution.py:39
  75.0 5.9 %collective-permute-start.9 = (bf16[1,8,2048]{2,1,0:T(8,128)(2,1)S(1)}, bf16[1,8,2048]{2,1,0:T(8,128)(2,1)S(1)}, u32[]{:S(2)}, u32[]{:S(2)}) collective-permute-start(bf16[1,8,2048]{2,1,0:T(8,128)(2,1)S(1)} %add.164), channel_id=1, source_target_pairs={{0,128},{4,132},{8,136},{12,140},{16,144},{20,148},{24,152},{28,15... | collective-permute-start | bytes 98312 | tf_op jit(solution)/shard_map/ppermute | solution.py:39
  81.0 29.9 %collective-permute-start.12 = (bf16[1,23,2048]{2,1,0:T(8,128)(2,1)S(1)}, bf16[1,23,2048]{2,1,0:T(8,128)(2,1)S(1)}, u32[]{:S(2)}, u32[]{:S(2)}) collective-permute-start(bf16[1,23,2048]{2,1,0:T(8,128)(2,1)S(1)} %pad_maximum_fusion), channel_id=1, source_target_pairs={{0,1},{1,2},{2,3},{3,0},{4,5},{5,6},{6,7},{7,4},{8,9},{9,10},{10,1... | collective-permute-start | bytes 282632 | tf_op jit(solution)/shard_map/ppermute | solution.py:49
  89.9 21.0 %collective-permute-start.13 = (bf16[1,23,2048]{2,1,0:T(8,128)(2,1)S(1)}, bf16[1,23,2048]{2,1,0:T(8,128)(2,1)S(1)}, u32[]{:S(2)}, u32[]{:S(2)}) collective-permute-start(bf16[1,23,2048]{2,1,0:T(8,128)(2,1)S(1)} %pad_maximum_fusion), channel_id=1, source_target_pairs={{0,2},{1,3},{2,0},{3,1},{4,6},{5,7},{6,4},{7,5},{8,10},{9,11},{10,... | collective-permute-start | bytes 282632 | tf_op jit(solution)/shard_map/ppermute | solution.py:49
  92.0 19.0 %collective-permute-start.14 = (bf16[1,23,2048]{2,1,0:T(8,128)(2,1)S(1)}, bf16[1,23,2048]{2,1,0:T(8,128)(2,1)S(1)}, u32[]{:S(2)}, u32[]{:S(2)}) collective-permute-start(bf16[1,23,2048]{2,1,0:T(8,128)(2,1)S(1)} %pad_maximum_fusion), channel_id=1, source_target_pairs={{0,3},{1,0},{2,1},{3,2},{4,7},{5,4},{6,5},{7,6},{8,11},{9,8},{10,9... | collective-permute-start | bytes 282632 | tf_op jit(solution)/shard_map/ppermute | solution.py:49
  119.9 4.6 %copy-start = (bf16[4,1,4,2048]{2,0,3,1:T(4,128)(2,1)}, bf16[4,1,4,2048]{2,0,3,1:T(4,128)(2,1)S(1)}, u32[]{:S(2)}) copy-start(bf16[4,1,4,2048]{2,0,3,1:T(4,128)(2,1)S(1)} %copy.55) | copy-start | bytes 196612
  121.0 3.5 %copy-start.4 = (bf16[4,2,1024]{0,1,2:T(2,128)(2,1)}, bf16[4,2,1024]{0,1,2:T(2,128)(2,1)S(1)}, u32[]{:S(2)}) copy-start(bf16[4,2,1024]{0,1,2:T(2,128)(2,1)S(1)} %copy.40) | copy-start | bytes 49156
  122.2 2.3 %copy-start.5 = (bf16[4,2,1024]{0,1,2:T(2,128)(2,1)S(1)}, bf16[4,2,1024]{0,1,2:T(2,128)(2,1)}, u32[]{:S(2)}) copy-start(bf16[4,2,1024]{0,1,2:T(2,128)(2,1)} %copy.39) | copy-start | bytes 49156
  124.5 2.2 %copy-start.8 = (bf16[4,1,4,2048]{3,0,2,1:T(4,128)(2,1)S(1)}, bf16[4,1,4,2048]{3,0,2,1:T(4,128)(2,1)}, u32[]{:S(2)}) copy-start(bf16[4,1,4,2048]{3,0,2,1:T(4,128)(2,1)} %get-tuple-element.18) | copy-start | bytes 196612
  128.2 1.3 copy-start.2
  129.5 3.3 %copy-start.6 = (bf16[4,2,1024]{0,1,2:T(2,128)(2,1)S(1)}, bf16[4,2,1024]{0,1,2:T(2,128)(2,1)}, u32[]{:S(2)}) copy-start(bf16[4,2,1024]{0,1,2:T(2,128)(2,1)} %copy.39) | copy-start | bytes 49156
  132.9 3.6 %copy-start.1 = (bf16[4,1,4,2048]{2,0,3,1:T(4,128)(2,1)S(1)}, bf16[4,1,4,2048]{2,0,3,1:T(4,128)(2,1)}, u32[]{:S(2)}) copy-start(bf16[4,1,4,2048]{2,0,3,1:T(4,128)(2,1)} %copy-done) | copy-start | bytes 196612
  132.9 3.6 %copy-start.12 = (f32[1024,4,2]{1,2,0:T(2,128)S(1)}, f32[1024,4,2]{1,2,0:T(2,128)}, u32[]{:S(2)}) copy-start(f32[1024,4,2]{1,2,0:T(2,128)} %fusion.15) | copy-start | bytes 98308
  142.5 4.2 %copy-start.3 = (bf16[4,1,4,2048]{2,0,3,1:T(4,128)(2,1)S(1)}, bf16[4,1,4,2048]{2,0,3,1:T(4,128)(2,1)}, u32[]{:S(2)}) copy-start(bf16[4,1,4,2048]{2,0,3,1:T(4,128)(2,1)} %copy-done.2) | copy-start | bytes 196612
  146.7 3.1 %copy-start.9 = (f32[4,2,1024]{2,0,1:T(4,128)S(1)}, f32[4,2,1024]{2,0,1:T(4,128)}, u32[]{:S(2)}) copy-start(f32[4,2,1024]{2,0,1:T(4,128)} %copy.43) | copy-start | bytes 98308
  146.7 3.1 %copy-start.10 = (f32[4,2,1024]{2,0,1:T(4,128)S(1)}, f32[4,2,1024]{2,0,1:T(4,128)}, u32[]{:S(2)}) copy-start(f32[4,2,1024]{2,0,1:T(4,128)} %copy.44) | copy-start | bytes 98308
  146.7 3.2 %copy-start.11 = (f32[4,2,1024]{2,0,1:T(4,128)S(1)}, f32[4,2,1024]{2,0,1:T(4,128)}, u32[]{:S(2)}) copy-start(f32[4,2,1024]{2,0,1:T(4,128)} %copy.50) | copy-start | bytes 98308

commit v2 on v1

--- a/solution.py
+++ b/solution.py
@@ -81,8 +81,9 @@
     lo_c, lo_s = cos_sin(lo[:, None] * freqs[None, :] % length, length)
     cos = hi_c[:, None, :] * lo_c[None, :, :] - hi_s[:, None, :] * lo_s[None, :, :]
     sin = hi_s[:, None, :] * lo_c[None, :, :] + hi_c[:, None, :] * lo_s[None, :, :]
-    table = jnp.concatenate([cos, -sin], axis=-1)
-    return table.reshape(length, length).astype(jnp.bfloat16)
+    cos = cos.reshape(length, half).astype(jnp.bfloat16)
+    sin = sin.reshape(length, half).astype(jnp.bfloat16)
+    return cos, sin
 
 
 def make_inverse(length, lags):
@@ -111,17 +112,13 @@
 
 
 def cross_sum(receivers, emitters):
-    half = receivers.shape[2] // 2
-    rec_re, rec_im = (receivers[..., :half], receivers[..., half:])
-    emi_re, emi_im = (emitters[..., :half], emitters[..., half:])
-    real_part = jnp.einsum("sck,snk->nck", rec_re, emi_re, preferred_element_type=jnp.float32)
-    real_part = real_part + jnp.einsum(
-        "sck,snk->nck", rec_im, emi_im, preferred_element_type=jnp.float32
-    )
-    imag_part = jnp.einsum("sck,snk->nck", rec_im, emi_re, preferred_element_type=jnp.float32)
-    imag_part = imag_part - jnp.einsum(
-        "sck,snk->nck", rec_re, emi_im, preferred_element_type=jnp.float32
-    )
+    half = receivers.shape[-1] // 2
+    rec = receivers.astype(jnp.float32)[:, None, None]
+    emi = emitters.astype(jnp.float32)[:, :, :, None]
+    rec_re, rec_im = (rec[..., :half], rec[..., half:])
+    emi_re, emi_im = (emi[..., :half], emi[..., half:])
+    real_part = jnp.sum(rec_re * emi_re, axis=0) + jnp.sum(rec_im * emi_im, axis=0)
+    imag_part = jnp.sum(rec_im * emi_re, axis=0) - jnp.sum(rec_re * emi_im, axis=0)
     return jnp.concatenate([real_part, imag_part], axis=-1)
 
 
@@ -146,10 +143,15 @@
     block = jnp.concatenate([window, received], axis=1)
     block = gather(block, "seg")
     segs = block.shape[0]
-    forward = make_forward(length)
+    cos, sin = make_forward(length)
     inverse = make_inverse(length, LAGS)
-    spectra = jnp.dot(
-        block.reshape(segs * block.shape[1], length), forward, preferred_element_type=jnp.float32
+    flat_rows = block.reshape(segs * block.shape[1], length)
+    spectra = jnp.concatenate(
+        [
+            jnp.dot(flat_rows, cos, preferred_element_type=jnp.float32),
+            -jnp.dot(flat_rows, sin, preferred_element_type=jnp.float32),
+        ],
+        axis=-1,
     )
     white = whiten(spectra.reshape(block.shape), BAND).astype(jnp.bfloat16)
     chosen = white[:, rows:].reshape(segs, steps, nsrc, length)
@@ -159,10 +161,8 @@
     for offset in range(1, LOW + HIGH + 1):
         total = total + part[:, offset : offset + per].astype(jnp.float32)
     stacked = (total * 0.125).astype(jnp.bfloat16)
-    cross = jnp.stack([cross_sum(stacked, chosen[:, step]) for step in range(steps)])
-    flat = jnp.dot(
-        cross.reshape(-1, length), inverse, precision=lax.Precision.HIGHEST
-    )
+    cross = cross_sum(stacked, chosen)
+    flat = jnp.dot(cross.reshape(-1, length), inverse, precision=lax.Precision.HIGHEST)
     return flat.reshape(steps, nsrc, per, LAGS)
 
 

time: 160 us -> 106 us (0.66)
  matrix products: 36.2 us -> 12.9 us
  local copies, waits for them, and re-layouts: 27.1 us -> 4.63 us
  other arithmetic: 20.7 us -> 13.3 us
    dot_general x9 -> x2, matrix products: 27.2 us -> 3.93 us  [the longest x1 3.13 us: shards(): jnp.dot(flat_rows, cos, preferred_element_type=jnp.float32)]
    dot_general x1 -> x0, local copies, waits for them, and re-layouts: 12.3 us -> none  [shards(): jnp.dot(block.reshape(segs * block.shape[1], length), forward, preferred_...]
    dot_general x1 -> x0, other arithmetic: 8.21 us -> none  [shards(): jnp.dot(block.reshape(segs * block.shape[1], length), forward, preferred_...]
    another operation x3 -> x0, other arithmetic: 5 us -> none
    convert_element_type x1 -> x2, other arithmetic: 0.09 us -> 4.87 us  [the longest x1 4.84 us: make_forward(): cos = cos.reshape(length, half).astype(jnp.bfloat16)]
    unnamed x28 -> x6, local copies, waits for them, and re-layouts: 4.29 us -> 0.5 us
    slice x7 -> x0, local copies, waits for them, and re-layouts: 2.93 us -> none  [the longest x3 1.66 us: cross_sum(): rec_re, rec_im = (receivers[..., :half], receivers[..., half:])]
    add x2 -> x0, local copies, waits for them, and re-layouts: 2.15 us -> none  [cross_sum(): real_part + jnp.einsum('sck,snk->nck', rec_im, emi_im, preferred_element_...]
  transfers between devices with their start and end apart: 15 -> 15, of which waited for: 2 -> 2; matrix products, arithmetic and copies ran while one was open for 22% -> 13% of each run, Pallas kernels for 0% -> 0%
where the time goes in v2:
time: 106 us; the launch traced here: 105 us
  starting transfers between devices  69.3 us (65%)
  other arithmetic  13.3 us (13%)
  matrix products  12.9 us (12%)
  local copies, waits for them, and re-layouts  4.63 us (4%)
  waiting for transfers between devices  3.66 us (3%)
  between operations  1.65 us (2%)
    ppermute x10, starting transfers between devices, broadcast(): total = total + lax.ppermute(block, axis, perm)  52.1 us
    ppermute x3, starting transfers between devices, gather(): lax.ppermute(block, axis, [(i, (i + shift) % count) for i in range(count)])  13.3 us
    dot_general x1, matrix products, shards(): jnp.dot(cross.reshape(-1, length), inverse, precision=lax.Precision.HIGHEST)  8.01 us
    convert_element_type x1, other arithmetic, make_forward(): cos = cos.reshape(length, half).astype(jnp.bfloat16)  4.84 us
    sub x1, other arithmetic, make_inverse(): hi_c[:, None, :] * lo_c[None, :, :] - hi_s[:, None, :] * lo_s[None, :, :]  4.43 us
    ppermute x10, waiting for transfers between devices, broadcast(): total = total + lax.ppermute(block, axis, perm)  3.65 us
    dot_general x1, matrix products, shards(): jnp.dot(flat_rows, cos, preferred_element_type=jnp.float32)  3.13 us
    ppermute x1, starting transfers between devices, halo(): lax.ppermute(tail, axis, [(i, i + 1) for i in range(ends)])  2.64 us
  transfers between devices with their start and end apart: 15, of which 2 were waited for; matrix products, arithmetic and copies ran while one was open for 13% of the time, Pallas kernels for 0%

profile of v2, /device:TPU:1, one launch (start us, length us, event | category | flops | bytes accessed | tf_op | source)
XLA Modules:
  0.0 105.4 jit_solution(3948859944926702049)
XLA Ops:
  0.0 1.3 %fusion.48 = (s32[1]{0:T(128)}, s32[1]{0:T(128)}) fusion(s32[2]{0:T(128)} %param.5), kind=kLoop, calls=%fused_computation.90 | loop fusion | bytes 16 | tf_op jit(solution)/shard_map/slice | solution.py:137
  2.5 1.0 fusion.6
  3.6 4.4 %collective-permute-start.2 = (bf16[1,8,2048]{2,1,0:T(8,128)(2,1)S(1)}, bf16[1,8,2048]{2,1,0:T(8,128)(2,1)S(1)}, u32[]{:S(2)}, u32[]{:S(2)}) collective-permute-start(bf16[1,8,2048]{2,1,0:T(8,128)(2,1)S(1)} %pad_maximum_fusion.3), channel_id=1, source_target_pairs={{0,4},{4,8},{8,12},{12,0},{16,20},{20,24},{24,28},{28,16},{32,36},... | collective-permute-start | bytes 98312 | tf_op jit(solution)/shard_map/ppermute | solution.py:39
  8.0 4.9 %collective-permute-start.3 = (bf16[1,8,2048]{2,1,0:T(8,128)(2,1)S(1)}, bf16[1,8,2048]{2,1,0:T(8,128)(2,1)S(1)}, u32[]{:S(2)}, u32[]{:S(2)}) collective-permute-start(bf16[1,8,2048]{2,1,0:T(8,128)(2,1)S(1)} %pad_maximum_fusion.3), channel_id=1, source_target_pairs={{0,8},{4,12},{8,0},{12,4},{16,24},{20,28},{24,16},{28,20},{32,40},... | collective-permute-start | bytes 98312 | tf_op jit(solution)/shard_map/ppermute | solution.py:39
  12.9 2.6 %collective-permute-start.4 = (bf16[1,8,2048]{2,1,0:T(8,128)(2,1)S(1)}, bf16[1,8,2048]{2,1,0:T(8,128)(2,1)S(1)}, u32[]{:S(2)}, u32[]{:S(2)}) collective-permute-start(bf16[1,8,2048]{2,1,0:T(8,128)(2,1)S(1)} %pad_maximum_fusion.3), channel_id=1, source_target_pairs={{0,12},{4,0},{8,4},{12,8},{16,28},{20,16},{24,20},{28,24},{32,44},... | collective-permute-start | bytes 98312 | tf_op jit(solution)/shard_map/ppermute | solution.py:39
  15.5 0.8 slice.60
  16.3 2.6 %collective-permute-start = (bf16[1,4,2048]{2,1,0:T(4,128)(2,1)S(1)}, bf16[1,4,2048]{2,1,0:T(4,128)(2,1)S(1)}, u32[]{:S(2)}, u32[]{:S(2)}) collective-permute-start(bf16[1,4,2048]{2,1,0:T(4,128)(2,1)S(1)} %slice.60), channel_id=1, source_target_pairs={{0,4},{4,8},{8,12},{12,16},{16,20},{20,24},{24,28},{28,32},{32,36}... | collective-permute-start | bytes 49160 | tf_op jit(solution)/shard_map/ppermute | solution.py:60
  18.9 0.8 slice.61
  19.7 1.3 %collective-permute-start.1 = (bf16[1,3,2048]{2,1,0:T(4,128)(2,1)S(1)}, bf16[1,3,2048]{2,1,0:T(4,128)(2,1)S(1)}, u32[]{:S(2)}, u32[]{:S(2)}) collective-permute-start(bf16[1,3,2048]{2,1,0:T(4,128)(2,1)S(1)} %slice.61), channel_id=1, source_target_pairs={{4,0},{8,4},{12,8},{16,12},{20,16},{24,20},{28,24},{32,28},{36,32}... | collective-permute-start | bytes 36872 | tf_op jit(solution)/shard_map/ppermute | solution.py:62
  21.0 1.0 fusion.28
  22.0 0.5 fusion.35
  22.6 0.0 collective-permute-done.2
  22.6 0.0 collective-permute-done.3
  22.6 11.4 %collective-permute-start.5 = (bf16[1,8,2048]{2,1,0:T(8,128)(2,1)S(1)}, bf16[1,8,2048]{2,1,0:T(8,128)(2,1)S(1)}, u32[]{:S(2)}, u32[]{:S(2)}) collective-permute-start(bf16[1,8,2048]{2,1,0:T(8,128)(2,1)S(1)} %add_add_fusion.2), channel_id=1, source_target_pairs={{0,16},{4,20},{8,24},{12,28},{16,32},{20,36},{24,40},{28,44},{32,4... | collective-permute-start | bytes 98312 | tf_op jit(solution)/shard_map/ppermute | solution.py:39
  34.0 8.8 %collective-permute-start.6 = (bf16[1,8,2048]{2,1,0:T(8,128)(2,1)S(1)}, bf16[1,8,2048]{2,1,0:T(8,128)(2,1)S(1)}, u32[]{:S(2)}, u32[]{:S(2)}) collective-permute-start(bf16[1,8,2048]{2,1,0:T(8,128)(2,1)S(1)} %add_add_fusion.2), channel_id=1, source_target_pairs={{0,32},{4,36},{8,40},{12,44},{16,48},{20,52},{24,56},{28,60},{32,0... | collective-permute-start | bytes 98312 | tf_op jit(solution)/shard_map/ppermute | solution.py:39
  42.9 5.2 %collective-permute-start.7 = (bf16[1,8,2048]{2,1,0:T(8,128)(2,1)S(1)}, bf16[1,8,2048]{2,1,0:T(8,128)(2,1)S(1)}, u32[]{:S(2)}, u32[]{:S(2)}) collective-permute-start(bf16[1,8,2048]{2,1,0:T(8,128)(2,1)S(1)} %add_add_fusion.2), channel_id=1, source_target_pairs={{0,48},{4,52},{8,56},{12,60},{16,0},{20,4},{24,8},{28,12},{32,16},... | collective-permute-start | bytes 98312 | tf_op jit(solution)/shard_map/ppermute | solution.py:39
  48.0 0.0 copy-start.1
  48.1 4.8 %subtract_convert_fusion = (bf16[32,64,1024]{2,1,0:T(8,128)(2,1)}, bf16[32,64,1024]{2,1,0:T(8,128)(2,1)}) fusion(f32[64,1024]{1,0:T(8,128)S(1)} %get-tuple-element.29, f32[32,1024]{1,0:T(8,128)S(1)} %get-tuple-element.31, f32[64,1024]{1,0:T(8,128)S(1)} %get-tuple-element.30, f32[32,1024]{1,0:T(8,128)S(1)} %get-tuple-element.32), kind=kLoop, calls=%fused_computation.6 | loop fusion | flops 16777216 | bytes 9175040 | tf_op jit(solution)/shard_map/convert_element_type | solution.py:84
  52.9 4.8 %collective-permute-start.8 = (bf16[1,8,2048]{2,1,0:T(8,128)(2,1)S(1)}, bf16[1,8,2048]{2,1,0:T(8,128)(2,1)S(1)}, u32[]{:S(2)}, u32[]{:S(2)}) collective-permute-start(bf16[1,8,2048]{2,1,0:T(8,128)(2,1)S(1)} %add_add_fusion.1), channel_id=1, source_target_pairs={{0,64},{4,68},{8,72},{12,76},{16,80},{20,84},{24,88},{28,92},{32,9... | collective-permute-start | bytes 98312 | tf_op jit(solution)/shard_map/ppermute | solution.py:39
  57.8 1.3 %collective-permute-done.8 = bf16[1,8,2048]{2,1,0:T(8,128)(2,1)S(1)} collective-permute-done((bf16[1,8,2048]{2,1,0:T(8,128)(2,1)S(1)}, bf16[1,8,2048]{2,1,0:T(8,128)(2,1)S(1)}, u32[]{:S(2)}, u32[]{:S(2)}) %collective-permute-start.8) | collective-permute-done | bytes 32800 | tf_op jit(solution)/shard_map/ppermute | solution.py:39
  59.1 4.7 %collective-permute-start.10 = (bf16[1,8,2048]{2,1,0:T(8,128)(2,1)S(1)}, bf16[1,8,2048]{2,1,0:T(8,128)(2,1)S(1)}, u32[]{:S(2)}, u32[]{:S(2)}) collective-permute-start(bf16[1,8,2048]{2,1,0:T(8,128)(2,1)S(1)} %add.163), channel_id=1, source_target_pairs={{0,256},{4,260},{8,264},{12,268},{16,272},{20,276},{24,280},{28,28... | collective-permute-start | bytes 98312 | tf_op jit(solution)/shard_map/ppermute | solution.py:39
  63.8 2.8 %collective-permute-start.11 = (bf16[1,8,2048]{2,1,0:T(8,128)(2,1)S(1)}, bf16[1,8,2048]{2,1,0:T(8,128)(2,1)S(1)}, u32[]{:S(2)}, u32[]{:S(2)}) collective-permute-start(bf16[1,8,2048]{2,1,0:T(8,128)(2,1)S(1)} %add.163), channel_id=1, source_target_pairs={{0,384},{4,388},{8,392},{12,396},{16,400},{20,404},{24,408},{28,41... | collective-permute-start | bytes 98312 | tf_op jit(solution)/shard_map/ppermute | solution.py:39
  66.5 2.5 %collective-permute-start.9 = (bf16[1,8,2048]{2,1,0:T(8,128)(2,1)S(1)}, bf16[1,8,2048]{2,1,0:T(8,128)(2,1)S(1)}, u32[]{:S(2)}, u32[]{:S(2)}) collective-permute-start(bf16[1,8,2048]{2,1,0:T(8,128)(2,1)S(1)} %add.163), channel_id=1, source_target_pairs={{0,128},{4,132},{8,136},{12,140},{16,144},{20,148},{24,152},{28,15... | collective-permute-start | bytes 98312 | tf_op jit(solution)/shard_map/ppermute | solution.py:39
  69.1 1.0 fusion.40
  70.1 2.3 %collective-permute-done.9 = bf16[1,8,2048]{2,1,0:T(8,128)(2,1)S(1)} collective-permute-done((bf16[1,8,2048]{2,1,0:T(8,128)(2,1)S(1)}, bf16[1,8,2048]{2,1,0:T(8,128)(2,1)S(1)}, u32[]{:S(2)}, u32[]{:S(2)}) %collective-permute-start.9) | collective-permute-done | bytes 32800 | tf_op jit(solution)/shard_map/ppermute | solution.py:39
  72.5 0.1 pad_maximum_fusion.2
  72.5 8.9 %collective-permute-start.12 = (bf16[1,23,2048]{2,1,0:T(8,128)(2,1)S(1)}, bf16[1,23,2048]{2,1,0:T(8,128)(2,1)S(1)}, u32[]{:S(2)}, u32[]{:S(2)}) collective-permute-start(bf16[1,23,2048]{2,1,0:T(8,128)(2,1)S(1)} %pad_maximum_fusion.2), channel_id=1, source_target_pairs={{0,1},{1,2},{2,3},{3,0},{4,5},{5,6},{6,7},{7,4},{8,9},{9,10},{10,1... | collective-permute-start | bytes 282632 | tf_op jit(solution)/shard_map/ppermute | solution.py:49
  81.4 2.1 %collective-permute-start.13 = (bf16[1,23,2048]{2,1,0:T(8,128)(2,1)S(1)}, bf16[1,23,2048]{2,1,0:T(8,128)(2,1)S(1)}, u32[]{:S(2)}, u32[]{:S(2)}) collective-permute-start(bf16[1,23,2048]{2,1,0:T(8,128)(2,1)S(1)} %pad_maximum_fusion.2), channel_id=1, source_target_pairs={{0,2},{1,3},{2,0},{3,1},{4,6},{5,7},{6,4},{7,5},{8,10},{9,11},{10,... | collective-permute-start | bytes 282632 | tf_op jit(solution)/shard_map/ppermute | solution.py:49
  83.5 2.3 %collective-permute-start.14 = (bf16[1,23,2048]{2,1,0:T(8,128)(2,1)S(1)}, bf16[1,23,2048]{2,1,0:T(8,128)(2,1)S(1)}, u32[]{:S(2)}, u32[]{:S(2)}) collective-permute-start(bf16[1,23,2048]{2,1,0:T(8,128)(2,1)S(1)} %pad_maximum_fusion.2), channel_id=1, source_target_pairs={{0,3},{1,0},{2,1},{3,2},{4,7},{5,4},{6,5},{7,6},{8,11},{9,8},{10,9... | collective-permute-start | bytes 282632 | tf_op jit(solution)/shard_map/ppermute | solution.py:49
  85.8 4.4 %multiply_subtract_fusion = (f32[32,32,1024]{2,1,0:T(8,128)}, f32[32,32,1024]{2,1,0:T(8,128)}) fusion(f32[32,1024]{1,0:T(8,128)S(1)} %get-tuple-element.25, f32[32,1024]{1,0:T(8,128)S(1)} %get-tuple-element.24, f32[32,1024]{1,0:T(8,128)S(1)} %get-tuple-element.26, f32[32,1024]{1,0:T(8,128)S(1)} %get-tuple-element.23), kind=kLoop, calls=%fused_computation.9 | loop fusion | flops 7340032 | bytes 8912896 | tf_op jit(solution)/shard_map/sub | solution.py:99
  90.3 0.1 pad_maximum_fusion.1
  90.3 0.1 reshape.306
  90.5 3.1 %fusion.49 = f32[92,1024]{1,0:T(8,128)S(1)} fusion(bf16[92,2048]{1,0:T(8,128)(2,1)S(1)} %reshape.306, bf16[2048,1024]{1,0:T(8,128)(2,1)} %bitcast.47), kind=kOutput, calls=%fused_computation.91 | convolution fusion | flops 385875968 | bytes 4947968 | tf_op jit(solution)/shard_map/dot_general | solution.py:151
  93.6 0.3 copy-done
  93.9 0.8 convolution_negate_fusion
  94.7 0.2 fusion.47
  94.9 0.1 copy.8
  95.0 0.1 slice.88
  95.1 0.2 reduce_sum.45
  95.3 0.2 mul.400
  95.4 0.1 mul.401
  95.6 0.1 reshape_reshape.3
  95.7 0.1 multiply_convert_fusion
  95.8 0.1 reshape.308
  95.9 0.4 bitcast_convert_fusion
  96.4 0.3 multiply_reduce_fusion.3
  96.7 8.0 %fusion.1 = f32[2,4,2,1024]{3,1,2,0:T(4,128)S(1)} fusion(f32[1024,1024]{1,0:T(8,128)} %bitcast.49, f32[1024,1024]{1,0:T(8,128)} %bitcast.48, f32[2,4,2,1024]{3,1,2,0:T(4,128)S(1)} %sub.26, f32[2,4,2,1024]{3,1,2,0:T(4,128)S(1)} %add.180), kind=kOutput, calls=%fused_computation.2 | convolution fusion | flops 406880256 | bytes 8585216 | tf_op jit(solution)/shard_map/dot_general | solution.py:165
  104.7 0.7 copy.6
  (27 shorter events, 0.3 us)
Async XLA Ops:
  3.6 19.0 %collective-permute-start.2 = (bf16[1,8,2048]{2,1,0:T(8,128)(2,1)S(1)}, bf16[1,8,2048]{2,1,0:T(8,128)(2,1)S(1)}, u32[]{:S(2)}, u32[]{:S(2)}) collective-permute-start(bf16[1,8,2048]{2,1,0:T(8,128)(2,1)S(1)} %pad_maximum_fusion.3), channel_id=1, source_target_pairs={{0,4},{4,8},{8,12},{12,0},{16,20},{20,24},{24,28},{28,16},{32,36},... | collective-permute-start | bytes 98312 | tf_op jit(solution)/shard_map/ppermute | solution.py:39
  8.0 14.6 %collective-permute-start.3 = (bf16[1,8,2048]{2,1,0:T(8,128)(2,1)S(1)}, bf16[1,8,2048]{2,1,0:T(8,128)(2,1)S(1)}, u32[]{:S(2)}, u32[]{:S(2)}) collective-permute-start(bf16[1,8,2048]{2,1,0:T(8,128)(2,1)S(1)} %pad_maximum_fusion.3), channel_id=1, source_target_pairs={{0,8},{4,12},{8,0},{12,4},{16,24},{20,28},{24,16},{28,20},{32,40},... | collective-permute-start | bytes 98312 | tf_op jit(solution)/shard_map/ppermute | solution.py:39
  12.9 9.7 %collective-permute-start.4 = (bf16[1,8,2048]{2,1,0:T(8,128)(2,1)S(1)}, bf16[1,8,2048]{2,1,0:T(8,128)(2,1)S(1)}, u32[]{:S(2)}, u32[]{:S(2)}) collective-permute-start(bf16[1,8,2048]{2,1,0:T(8,128)(2,1)S(1)} %pad_maximum_fusion.3), channel_id=1, source_target_pairs={{0,12},{4,0},{8,4},{12,8},{16,28},{20,16},{24,20},{28,24},{32,44},... | collective-permute-start | bytes 98312 | tf_op jit(solution)/shard_map/ppermute | solution.py:39
  16.3 56.2 %collective-permute-start = (bf16[1,4,2048]{2,1,0:T(4,128)(2,1)S(1)}, bf16[1,4,2048]{2,1,0:T(4,128)(2,1)S(1)}, u32[]{:S(2)}, u32[]{:S(2)}) collective-permute-start(bf16[1,4,2048]{2,1,0:T(4,128)(2,1)S(1)} %slice.60), channel_id=1, source_target_pairs={{0,4},{4,8},{8,12},{12,16},{16,20},{20,24},{24,28},{28,32},{32,36}... | collective-permute-start | bytes 49160 | tf_op jit(solution)/shard_map/ppermute | solution.py:60
  19.7 52.7 %collective-permute-start.1 = (bf16[1,3,2048]{2,1,0:T(4,128)(2,1)S(1)}, bf16[1,3,2048]{2,1,0:T(4,128)(2,1)S(1)}, u32[]{:S(2)}, u32[]{:S(2)}) collective-permute-start(bf16[1,3,2048]{2,1,0:T(4,128)(2,1)S(1)} %slice.61), channel_id=1, source_target_pairs={{4,0},{8,4},{12,8},{16,12},{20,16},{24,20},{28,24},{32,28},{36,32}... | collective-permute-start | bytes 36872 | tf_op jit(solution)/shard_map/ppermute | solution.py:62
  22.6 30.3 %collective-permute-start.5 = (bf16[1,8,2048]{2,1,0:T(8,128)(2,1)S(1)}, bf16[1,8,2048]{2,1,0:T(8,128)(2,1)S(1)}, u32[]{:S(2)}, u32[]{:S(2)}) collective-permute-start(bf16[1,8,2048]{2,1,0:T(8,128)(2,1)S(1)} %add_add_fusion.2), channel_id=1, source_target_pairs={{0,16},{4,20},{8,24},{12,28},{16,32},{20,36},{24,40},{28,44},{32,4... | collective-permute-start | bytes 98312 | tf_op jit(solution)/shard_map/ppermute | solution.py:39
  34.0 18.9 %collective-permute-start.6 = (bf16[1,8,2048]{2,1,0:T(8,128)(2,1)S(1)}, bf16[1,8,2048]{2,1,0:T(8,128)(2,1)S(1)}, u32[]{:S(2)}, u32[]{:S(2)}) collective-permute-start(bf16[1,8,2048]{2,1,0:T(8,128)(2,1)S(1)} %add_add_fusion.2), channel_id=1, source_target_pairs={{0,32},{4,36},{8,40},{12,44},{16,48},{20,52},{24,56},{28,60},{32,0... | collective-permute-start | bytes 98312 | tf_op jit(solution)/shard_map/ppermute | solution.py:39
  42.9 10.0 %collective-permute-start.7 = (bf16[1,8,2048]{2,1,0:T(8,128)(2,1)S(1)}, bf16[1,8,2048]{2,1,0:T(8,128)(2,1)S(1)}, u32[]{:S(2)}, u32[]{:S(2)}) collective-permute-start(bf16[1,8,2048]{2,1,0:T(8,128)(2,1)S(1)} %add_add_fusion.2), channel_id=1, source_target_pairs={{0,48},{4,52},{8,56},{12,60},{16,0},{20,4},{24,8},{28,12},{32,16},... | collective-permute-start | bytes 98312 | tf_op jit(solution)/shard_map/ppermute | solution.py:39
  48.0 24.4 %copy-start.1 = (bf16[1,8,2048]{2,1,0:T(8,128)(2,1)S(1)}, bf16[1,8,2048]{2,1,0:T(8,128)(2,1)}, u32[]{:S(2)}) copy-start(bf16[1,8,2048]{2,1,0:T(8,128)(2,1)} %param.3) | copy-start | bytes 98308
  52.9 6.2 %collective-permute-start.8 = (bf16[1,8,2048]{2,1,0:T(8,128)(2,1)S(1)}, bf16[1,8,2048]{2,1,0:T(8,128)(2,1)S(1)}, u32[]{:S(2)}, u32[]{:S(2)}) collective-permute-start(bf16[1,8,2048]{2,1,0:T(8,128)(2,1)S(1)} %add_add_fusion.1), channel_id=1, source_target_pairs={{0,64},{4,68},{8,72},{12,76},{16,80},{20,84},{24,88},{28,92},{32,9... | collective-permute-start | bytes 98312 | tf_op jit(solution)/shard_map/ppermute | solution.py:39
  59.1 11.0 %collective-permute-start.10 = (bf16[1,8,2048]{2,1,0:T(8,128)(2,1)S(1)}, bf16[1,8,2048]{2,1,0:T(8,128)(2,1)S(1)}, u32[]{:S(2)}, u32[]{:S(2)}) collective-permute-start(bf16[1,8,2048]{2,1,0:T(8,128)(2,1)S(1)} %add.163), channel_id=1, source_target_pairs={{0,256},{4,260},{8,264},{12,268},{16,272},{20,276},{24,280},{28,28... | collective-permute-start | bytes 98312 | tf_op jit(solution)/shard_map/ppermute | solution.py:39
  63.8 6.3 %collective-permute-start.11 = (bf16[1,8,2048]{2,1,0:T(8,128)(2,1)S(1)}, bf16[1,8,2048]{2,1,0:T(8,128)(2,1)S(1)}, u32[]{:S(2)}, u32[]{:S(2)}) collective-permute-start(bf16[1,8,2048]{2,1,0:T(8,128)(2,1)S(1)} %add.163), channel_id=1, source_target_pairs={{0,384},{4,388},{8,392},{12,396},{16,400},{20,404},{24,408},{28,41... | collective-permute-start | bytes 98312 | tf_op jit(solution)/shard_map/ppermute | solution.py:39
  66.5 5.9 %collective-permute-start.9 = (bf16[1,8,2048]{2,1,0:T(8,128)(2,1)S(1)}, bf16[1,8,2048]{2,1,0:T(8,128)(2,1)S(1)}, u32[]{:S(2)}, u32[]{:S(2)}) collective-permute-start(bf16[1,8,2048]{2,1,0:T(8,128)(2,1)S(1)} %add.163), channel_id=1, source_target_pairs={{0,128},{4,132},{8,136},{12,140},{16,144},{20,148},{24,152},{28,15... | collective-permute-start | bytes 98312 | tf_op jit(solution)/shard_map/ppermute | solution.py:39
  72.5 17.7 %collective-permute-start.12 = (bf16[1,23,2048]{2,1,0:T(8,128)(2,1)S(1)}, bf16[1,23,2048]{2,1,0:T(8,128)(2,1)S(1)}, u32[]{:S(2)}, u32[]{:S(2)}) collective-permute-start(bf16[1,23,2048]{2,1,0:T(8,128)(2,1)S(1)} %pad_maximum_fusion.2), channel_id=1, source_target_pairs={{0,1},{1,2},{2,3},{3,0},{4,5},{5,6},{6,7},{7,4},{8,9},{9,10},{10,1... | collective-permute-start | bytes 282632 | tf_op jit(solution)/shard_map/ppermute | solution.py:49
  81.4 8.9 %collective-permute-start.13 = (bf16[1,23,2048]{2,1,0:T(8,128)(2,1)S(1)}, bf16[1,23,2048]{2,1,0:T(8,128)(2,1)S(1)}, u32[]{:S(2)}, u32[]{:S(2)}) collective-permute-start(bf16[1,23,2048]{2,1,0:T(8,128)(2,1)S(1)} %pad_maximum_fusion.2), channel_id=1, source_target_pairs={{0,2},{1,3},{2,0},{3,1},{4,6},{5,7},{6,4},{7,5},{8,10},{9,11},{10,... | collective-permute-start | bytes 282632 | tf_op jit(solution)/shard_map/ppermute | solution.py:49
  83.5 6.8 %collective-permute-start.14 = (bf16[1,23,2048]{2,1,0:T(8,128)(2,1)S(1)}, bf16[1,23,2048]{2,1,0:T(8,128)(2,1)S(1)}, u32[]{:S(2)}, u32[]{:S(2)}) collective-permute-start(bf16[1,23,2048]{2,1,0:T(8,128)(2,1)S(1)} %pad_maximum_fusion.2), channel_id=1, source_target_pairs={{0,3},{1,0},{2,1},{3,2},{4,7},{5,4},{6,5},{7,6},{8,11},{9,8},{10,9... | collective-permute-start | bytes 282632 | tf_op jit(solution)/shard_map/ppermute | solution.py:49
  90.5 3.5 %copy-start = (bf16[32,64,1024]{2,1,0:T(8,128)(2,1)S(1)}, bf16[32,64,1024]{2,1,0:T(8,128)(2,1)}, u32[]{:S(2)}) copy-start(bf16[32,64,1024]{2,1,0:T(8,128)(2,1)} %get-tuple-element.14) | copy-start | bytes 12582916

commit v3 on v2

--- a/solution.py
+++ b/solution.py
@@ -13,7 +13,7 @@
 
 def radices(count):
     if count == 128:
-        return [4, 4, 2, 4]
+        return [2] * 7
     out = []
     while count % 4 == 0:
         out.append(4)
@@ -162,7 +162,7 @@
         total = total + part[:, offset : offset + per].astype(jnp.float32)
     stacked = (total * 0.125).astype(jnp.bfloat16)
     cross = cross_sum(stacked, chosen)
-    flat = jnp.dot(cross.reshape(-1, length), inverse, precision=lax.Precision.HIGHEST)
+    flat = jnp.dot(cross.reshape(-1, length), inverse, precision=lax.Precision.HIGH)
     return flat.reshape(steps, nsrc, per, LAGS)
 
 

time: 106 us -> 102 us (0.962)
  starting transfers between devices: 69.3 us -> 66.2 us
  matrix products: 12.9 us -> 10.7 us
  waiting for transfers between devices: 3.66 us -> 5.06 us
    ppermute x10 -> x7, starting transfers between devices: 52.1 us -> 47.3 us  [broadcast(): total = total + lax.ppermute(block, axis, perm)]
    dot_general x1, matrix products: 8.01 us -> 5.75 us  [shards(): jnp.dot(cross.reshape(-1, length), inverse, precision=lax.Precision.HIGH)]
    ppermute x10 -> x7, waiting for transfers between devices: 3.65 us -> 5.05 us  [broadcast(): total = total + lax.ppermute(block, axis, perm)]
  transfers between devices with their start and end apart: 15 -> 12, of which waited for: 2 -> 5; matrix products, arithmetic and copies ran while one was open for 13% -> 13% of each run, Pallas kernels for 0% -> 0%
where the time goes in v3:
time: 102 us
  starting transfers between devices  66.2 us (65%)
  other arithmetic  13.3 us (13%)
  matrix products  10.7 us (10%)
  waiting for transfers between devices  5.06 us (5%)
  local copies, waits for them, and re-layouts  4.65 us (5%)
  between operations  1.67 us (2%)
    ppermute x7, starting transfers between devices, broadcast(): total = total + lax.ppermute(block, axis, perm)  47.3 us
    ppermute x3, starting transfers between devices, gather(): lax.ppermute(block, axis, [(i, (i + shift) % count) for i in range(count)])  14.3 us
    dot_general x1, matrix products, shards(): jnp.dot(cross.reshape(-1, length), inverse, precision=lax.Precision.HIGH)  5.75 us
    ppermute x7, waiting for transfers between devices, broadcast(): total = total + lax.ppermute(block, axis, perm)  5.05 us
    convert_element_type x1, other arithmetic, make_forward(): cos = cos.reshape(length, half).astype(jnp.bfloat16)  4.84 us
    sub x1, other arithmetic, make_inverse(): hi_c[:, None, :] * lo_c[None, :, :] - hi_s[:, None, :] * lo_s[None, :, :]  4.43 us
    ppermute x1, starting transfers between devices, halo(): lax.ppermute(tail, axis, [(i, i + 1) for i in range(ends)])  3.36 us
    dot_general x1, matrix products, shards(): jnp.dot(flat_rows, cos, preferred_element_type=jnp.float32)  3.13 us
  transfers between devices with their start and end apart: 12, of which 5 were waited for; matrix products, arithmetic and copies ran while one was open for 13% of the time, Pallas kernels for 0%

profile of v3, /device:TPU:1, one launch (start us, length us, event | category | flops | bytes accessed | tf_op | source)
XLA Modules:
  0.0 101.6 jit_solution(4057517661097859204)
XLA Ops:
  0.0 1.3 %fusion.49 = (s32[1]{0:T(128)}, s32[1]{0:T(128)}) fusion(s32[2]{0:T(128)} %param.5), kind=kLoop, calls=%fused_computation.88 | loop fusion | bytes 16 | tf_op jit(solution)/shard_map/slice | solution.py:137
  2.6 1.0 fusion.6
  3.7 4.4 %collective-permute-start.2 = (bf16[1,8,2048]{2,1,0:T(8,128)(2,1)S(1)}, bf16[1,8,2048]{2,1,0:T(8,128)(2,1)S(1)}, u32[]{:S(2)}, u32[]{:S(2)}) collective-permute-start(bf16[1,8,2048]{2,1,0:T(8,128)(2,1)S(1)} %pad_maximum_fusion.3), channel_id=1, source_target_pairs={{0,4},{4,0},{8,12},{12,8},{16,20},{20,16},{24,28},{28,24},{32,36},... | collective-permute-start | bytes 98312 | tf_op jit(solution)/shard_map/ppermute | solution.py:39
  8.0 1.3 %collective-permute-done.2 = bf16[1,8,2048]{2,1,0:T(8,128)(2,1)S(1)} collective-permute-done((bf16[1,8,2048]{2,1,0:T(8,128)(2,1)S(1)}, bf16[1,8,2048]{2,1,0:T(8,128)(2,1)S(1)}, u32[]{:S(2)}, u32[]{:S(2)}) %collective-permute-start.2) | collective-permute-done | bytes 32800 | tf_op jit(solution)/shard_map/ppermute | solution.py:39
  9.4 4.9 %collective-permute-start.3 = (bf16[1,8,2048]{2,1,0:T(8,128)(2,1)S(1)}, bf16[1,8,2048]{2,1,0:T(8,128)(2,1)S(1)}, u32[]{:S(2)}, u32[]{:S(2)}) collective-permute-start(bf16[1,8,2048]{2,1,0:T(8,128)(2,1)S(1)} %fusion.47), channel_id=1, source_target_pairs={{0,8},{4,12},{8,0},{12,4},{16,24},{20,28},{24,16},{28,20},{32,40},... | collective-permute-start | bytes 98312 | tf_op jit(solution)/shard_map/ppermute | solution.py:39
  14.3 0.8 slice.60
  15.0 3.4 %collective-permute-start = (bf16[1,4,2048]{2,1,0:T(4,128)(2,1)S(1)}, bf16[1,4,2048]{2,1,0:T(4,128)(2,1)S(1)}, u32[]{:S(2)}, u32[]{:S(2)}) collective-permute-start(bf16[1,4,2048]{2,1,0:T(4,128)(2,1)S(1)} %slice.60), channel_id=1, source_target_pairs={{0,4},{4,8},{8,12},{12,16},{16,20},{20,24},{24,28},{28,32},{32,36}... | collective-permute-start | bytes 49160 | tf_op jit(solution)/shard_map/ppermute | solution.py:60
  18.4 0.8 slice.61
  19.2 1.3 %collective-permute-start.1 = (bf16[1,3,2048]{2,1,0:T(4,128)(2,1)S(1)}, bf16[1,3,2048]{2,1,0:T(4,128)(2,1)S(1)}, u32[]{:S(2)}, u32[]{:S(2)}) collective-permute-start(bf16[1,3,2048]{2,1,0:T(4,128)(2,1)S(1)} %slice.61), channel_id=1, source_target_pairs={{4,0},{8,4},{12,8},{16,12},{20,16},{24,20},{28,24},{32,28},{36,32}... | collective-permute-start | bytes 36872 | tf_op jit(solution)/shard_map/ppermute | solution.py:62
  20.5 0.0 collective-permute-done.3
  20.5 10.7 %collective-permute-start.4 = (bf16[1,8,2048]{2,1,0:T(8,128)(2,1)S(1)}, bf16[1,8,2048]{2,1,0:T(8,128)(2,1)S(1)}, u32[]{:S(2)}, u32[]{:S(2)}) collective-permute-start(bf16[1,8,2048]{2,1,0:T(8,128)(2,1)S(1)} %add.149), channel_id=1, source_target_pairs={{0,16},{4,20},{8,24},{12,28},{16,0},{20,4},{24,8},{28,12},{32,48},... | collective-permute-start | bytes 98312 | tf_op jit(solution)/shard_map/ppermute | solution.py:39
  31.2 1.0 %fusion.28 = (f32[64,1024]{1,0:T(8,128)S(1)}, f32[64,1024]{1,0:T(8,128)S(1)}) fusion(), kind=kLoop, calls=%fused_computation.56 | loop fusion | flops 917504 | bytes 524288 | tf_op jit(solution)/shard_map/sin | solution.py:70
  32.2 0.7 collective-permute-done.4
  32.9 11.9 %collective-permute-start.5 = (bf16[1,8,2048]{2,1,0:T(8,128)(2,1)S(1)}, bf16[1,8,2048]{2,1,0:T(8,128)(2,1)S(1)}, u32[]{:S(2)}, u32[]{:S(2)}) collective-permute-start(bf16[1,8,2048]{2,1,0:T(8,128)(2,1)S(1)} %add.150), channel_id=1, source_target_pairs={{0,32},{4,36},{8,40},{12,44},{16,48},{20,52},{24,56},{28,60},{32,0... | collective-permute-start | bytes 98312 | tf_op jit(solution)/shard_map/ppermute | solution.py:39
  44.8 0.5 fusion.35
  45.3 1.1 %collective-permute-done.5 = bf16[1,8,2048]{2,1,0:T(8,128)(2,1)S(1)} collective-permute-done((bf16[1,8,2048]{2,1,0:T(8,128)(2,1)S(1)}, bf16[1,8,2048]{2,1,0:T(8,128)(2,1)S(1)}, u32[]{:S(2)}, u32[]{:S(2)}) %collective-permute-start.5) | collective-permute-done | bytes 32800 | tf_op jit(solution)/shard_map/ppermute | solution.py:39
  46.4 7.7 %collective-permute-start.6 = (bf16[1,8,2048]{2,1,0:T(8,128)(2,1)S(1)}, bf16[1,8,2048]{2,1,0:T(8,128)(2,1)S(1)}, u32[]{:S(2)}, u32[]{:S(2)}) collective-permute-start(bf16[1,8,2048]{2,1,0:T(8,128)(2,1)S(1)} %add.151), channel_id=1, source_target_pairs={{0,64},{4,68},{8,72},{12,76},{16,80},{20,84},{24,88},{28,92},{32,9... | collective-permute-start | bytes 98312 | tf_op jit(solution)/shard_map/ppermute | solution.py:39
  54.1 0.0 copy-start.1
  54.1 4.8 %subtract_convert_fusion = (bf16[32,64,1024]{2,1,0:T(8,128)(2,1)}, bf16[32,64,1024]{2,1,0:T(8,128)(2,1)}) fusion(f32[64,1024]{1,0:T(8,128)S(1)} %get-tuple-element.29, f32[32,1024]{1,0:T(8,128)S(1)} %get-tuple-element.31, f32[64,1024]{1,0:T(8,128)S(1)} %get-tuple-element.30, f32[32,1024]{1,0:T(8,128)S(1)} %get-tuple-element.32), kind=kLoop, calls=%fused_computation.6 | loop fusion | flops 16777216 | bytes 9175040 | tf_op jit(solution)/shard_map/convert_element_type | solution.py:84
  59.0 3.1 %collective-permute-start.7 = (bf16[1,8,2048]{2,1,0:T(8,128)(2,1)S(1)}, bf16[1,8,2048]{2,1,0:T(8,128)(2,1)S(1)}, u32[]{:S(2)}, u32[]{:S(2)}) collective-permute-start(bf16[1,8,2048]{2,1,0:T(8,128)(2,1)S(1)} %add.152), channel_id=1, source_target_pairs={{0,128},{4,132},{8,136},{12,140},{16,144},{20,148},{24,152},{28,15... | collective-permute-start | bytes 98312 | tf_op jit(solution)/shard_map/ppermute | solution.py:39
  62.1 1.5 %collective-permute-done.7 = bf16[1,8,2048]{2,1,0:T(8,128)(2,1)S(1)} collective-permute-done((bf16[1,8,2048]{2,1,0:T(8,128)(2,1)S(1)}, bf16[1,8,2048]{2,1,0:T(8,128)(2,1)S(1)}, u32[]{:S(2)}, u32[]{:S(2)}) %collective-permute-start.7) | collective-permute-done | bytes 32800 | tf_op jit(solution)/shard_map/ppermute | solution.py:39
  63.6 4.7 %collective-permute-start.8 = (bf16[1,8,2048]{2,1,0:T(8,128)(2,1)S(1)}, bf16[1,8,2048]{2,1,0:T(8,128)(2,1)S(1)}, u32[]{:S(2)}, u32[]{:S(2)}) collective-permute-start(bf16[1,8,2048]{2,1,0:T(8,128)(2,1)S(1)} %add.153), channel_id=1, source_target_pairs={{0,256},{4,260},{8,264},{12,268},{16,272},{20,276},{24,280},{28,28... | collective-permute-start | bytes 98312 | tf_op jit(solution)/shard_map/ppermute | solution.py:39
  68.3 1.0 %fusion.40 = (f32[32,1024]{1,0:T(8,128)S(1)}, f32[32,1024]{1,0:T(8,128)S(1)}, f32[32,1024]{1,0:T(8,128)S(1)}, f32[32,1024]{1,0:T(8,128)S(1)}) fusion(s32[1024]{0:T(1024)S(1)} %iota_add_fusion), kind=kLoop, calls=%fused_computation.70 | loop fusion | flops 786432 | bytes 528384 | tf_op jit(solution)/shard_map/cos | solution.py:70
  69.3 0.5 collective-permute-done.8
  69.8 0.0 collective-permute-done
  69.8 0.1 pad_maximum_fusion.2
  69.9 2.6 %collective-permute-start.10 = (bf16[1,23,2048]{2,1,0:T(8,128)(2,1)S(1)}, bf16[1,23,2048]{2,1,0:T(8,128)(2,1)S(1)}, u32[]{:S(2)}, u32[]{:S(2)}) collective-permute-start(bf16[1,23,2048]{2,1,0:T(8,128)(2,1)S(1)} %pad_maximum_fusion.2), channel_id=1, source_target_pairs={{0,2},{1,3},{2,0},{3,1},{4,6},{5,7},{6,4},{7,5},{8,10},{9,11},{10,... | collective-permute-start | bytes 282632 | tf_op jit(solution)/shard_map/ppermute | solution.py:49
  72.5 9.7 %collective-permute-start.11 = (bf16[1,23,2048]{2,1,0:T(8,128)(2,1)S(1)}, bf16[1,23,2048]{2,1,0:T(8,128)(2,1)S(1)}, u32[]{:S(2)}, u32[]{:S(2)}) collective-permute-start(bf16[1,23,2048]{2,1,0:T(8,128)(2,1)S(1)} %pad_maximum_fusion.2), channel_id=1, source_target_pairs={{0,3},{1,0},{2,1},{3,2},{4,7},{5,4},{6,5},{7,6},{8,11},{9,8},{10,9... | collective-permute-start | bytes 282632 | tf_op jit(solution)/shard_map/ppermute | solution.py:49
  82.2 2.0 %collective-permute-start.9 = (bf16[1,23,2048]{2,1,0:T(8,128)(2,1)S(1)}, bf16[1,23,2048]{2,1,0:T(8,128)(2,1)S(1)}, u32[]{:S(2)}, u32[]{:S(2)}) collective-permute-start(bf16[1,23,2048]{2,1,0:T(8,128)(2,1)S(1)} %pad_maximum_fusion.2), channel_id=1, source_target_pairs={{0,1},{1,2},{2,3},{3,0},{4,5},{5,6},{6,7},{7,4},{8,9},{9,10},{10,1... | collective-permute-start | bytes 282632 | tf_op jit(solution)/shard_map/ppermute | solution.py:49
  84.3 4.4 %multiply_subtract_fusion = (f32[32,32,1024]{2,1,0:T(8,128)}, f32[32,32,1024]{2,1,0:T(8,128)}) fusion(f32[32,1024]{1,0:T(8,128)S(1)} %get-tuple-element.25, f32[32,1024]{1,0:T(8,128)S(1)} %get-tuple-element.24, f32[32,1024]{1,0:T(8,128)S(1)} %get-tuple-element.26, f32[32,1024]{1,0:T(8,128)S(1)} %get-tuple-element.23), kind=kLoop, calls=%fused_computation.9 | loop fusion | flops 7340032 | bytes 8912896 | tf_op jit(solution)/shard_map/sub | solution.py:99
  88.7 0.1 pad_maximum_fusion.1
  88.8 0.1 reshape.306
  88.9 3.1 %fusion.50 = f32[92,1024]{1,0:T(8,128)S(1)} fusion(bf16[92,2048]{1,0:T(8,128)(2,1)S(1)} %reshape.306, bf16[2048,1024]{1,0:T(8,128)(2,1)} %bitcast.49), kind=kOutput, calls=%fused_computation.89 | convolution fusion | flops 385875968 | bytes 4947968 | tf_op jit(solution)/shard_map/dot_general | solution.py:151
  92.0 0.3 copy-done
  92.3 0.8 convolution_negate_fusion
  93.1 0.2 fusion.48
  93.3 0.1 copy.8
  93.5 0.1 slice.88
  93.5 0.2 reduce_sum.45
  93.7 0.2 mul.400
  93.9 0.1 mul.401
  94.0 0.1 reshape_reshape.3
  94.1 0.1 multiply_convert_fusion
  94.3 0.1 reshape.308
  94.4 0.4 bitcast_convert_fusion
  94.8 0.3 multiply_reduce_fusion.3
  95.1 5.8 %fusion.1 = f32[2,4,2,1024]{3,1,2,0:T(4,128)S(1)} fusion(f32[1024,1024]{1,0:T(8,128)} %bitcast.47, f32[1024,1024]{1,0:T(8,128)} %bitcast.46, f32[2,4,2,1024]{3,1,2,0:T(4,128)S(1)} %sub.26, f32[2,4,2,1024]{3,1,2,0:T(4,128)S(1)} %add.168), kind=kOutput, calls=%fused_computation.2 | convolution fusion | flops 205553664 | bytes 8585216 | tf_op jit(solution)/shard_map/dot_general | solution.py:165
  100.9 0.7 copy.6
  (24 shorter events, 0.3 us)
Async XLA Ops:
  3.7 5.7 %collective-permute-start.2 = (bf16[1,8,2048]{2,1,0:T(8,128)(2,1)S(1)}, bf16[1,8,2048]{2,1,0:T(8,128)(2,1)S(1)}, u32[]{:S(2)}, u32[]{:S(2)}) collective-permute-start(bf16[1,8,2048]{2,1,0:T(8,128)(2,1)S(1)} %pad_maximum_fusion.3), channel_id=1, source_target_pairs={{0,4},{4,0},{8,12},{12,8},{16,20},{20,16},{24,28},{28,24},{32,36},... | collective-permute-start | bytes 98312 | tf_op jit(solution)/shard_map/ppermute | solution.py:39
  9.4 11.1 %collective-permute-start.3 = (bf16[1,8,2048]{2,1,0:T(8,128)(2,1)S(1)}, bf16[1,8,2048]{2,1,0:T(8,128)(2,1)S(1)}, u32[]{:S(2)}, u32[]{:S(2)}) collective-permute-start(bf16[1,8,2048]{2,1,0:T(8,128)(2,1)S(1)} %fusion.47), channel_id=1, source_target_pairs={{0,8},{4,12},{8,0},{12,4},{16,24},{20,28},{24,16},{28,20},{32,40},... | collective-permute-start | bytes 98312 | tf_op jit(solution)/shard_map/ppermute | solution.py:39
  15.0 54.8 %collective-permute-start = (bf16[1,4,2048]{2,1,0:T(4,128)(2,1)S(1)}, bf16[1,4,2048]{2,1,0:T(4,128)(2,1)S(1)}, u32[]{:S(2)}, u32[]{:S(2)}) collective-permute-start(bf16[1,4,2048]{2,1,0:T(4,128)(2,1)S(1)} %slice.60), channel_id=1, source_target_pairs={{0,4},{4,8},{8,12},{12,16},{16,20},{20,24},{24,28},{28,32},{32,36}... | collective-permute-start | bytes 49160 | tf_op jit(solution)/shard_map/ppermute | solution.py:60
  19.2 50.6 %collective-permute-start.1 = (bf16[1,3,2048]{2,1,0:T(4,128)(2,1)S(1)}, bf16[1,3,2048]{2,1,0:T(4,128)(2,1)S(1)}, u32[]{:S(2)}, u32[]{:S(2)}) collective-permute-start(bf16[1,3,2048]{2,1,0:T(4,128)(2,1)S(1)} %slice.61), channel_id=1, source_target_pairs={{4,0},{8,4},{12,8},{16,12},{20,16},{24,20},{28,24},{32,28},{36,32}... | collective-permute-start | bytes 36872 | tf_op jit(solution)/shard_map/ppermute | solution.py:62
  20.5 12.4 %collective-permute-start.4 = (bf16[1,8,2048]{2,1,0:T(8,128)(2,1)S(1)}, bf16[1,8,2048]{2,1,0:T(8,128)(2,1)S(1)}, u32[]{:S(2)}, u32[]{:S(2)}) collective-permute-start(bf16[1,8,2048]{2,1,0:T(8,128)(2,1)S(1)} %add.149), channel_id=1, source_target_pairs={{0,16},{4,20},{8,24},{12,28},{16,0},{20,4},{24,8},{28,12},{32,48},... | collective-permute-start | bytes 98312 | tf_op jit(solution)/shard_map/ppermute | solution.py:39
  32.9 13.5 %collective-permute-start.5 = (bf16[1,8,2048]{2,1,0:T(8,128)(2,1)S(1)}, bf16[1,8,2048]{2,1,0:T(8,128)(2,1)S(1)}, u32[]{:S(2)}, u32[]{:S(2)}) collective-permute-start(bf16[1,8,2048]{2,1,0:T(8,128)(2,1)S(1)} %add.150), channel_id=1, source_target_pairs={{0,32},{4,36},{8,40},{12,44},{16,48},{20,52},{24,56},{28,60},{32,0... | collective-permute-start | bytes 98312 | tf_op jit(solution)/shard_map/ppermute | solution.py:39
  46.4 12.6 %collective-permute-start.6 = (bf16[1,8,2048]{2,1,0:T(8,128)(2,1)S(1)}, bf16[1,8,2048]{2,1,0:T(8,128)(2,1)S(1)}, u32[]{:S(2)}, u32[]{:S(2)}) collective-permute-start(bf16[1,8,2048]{2,1,0:T(8,128)(2,1)S(1)} %add.151), channel_id=1, source_target_pairs={{0,64},{4,68},{8,72},{12,76},{16,80},{20,84},{24,88},{28,92},{32,9... | collective-permute-start | bytes 98312 | tf_op jit(solution)/shard_map/ppermute | solution.py:39
  54.1 15.7 %copy-start.1 = (bf16[1,8,2048]{2,1,0:T(8,128)(2,1)S(1)}, bf16[1,8,2048]{2,1,0:T(8,128)(2,1)}, u32[]{:S(2)}) copy-start(bf16[1,8,2048]{2,1,0:T(8,128)(2,1)} %param.3) | copy-start | bytes 98308
  59.0 4.7 %collective-permute-start.7 = (bf16[1,8,2048]{2,1,0:T(8,128)(2,1)S(1)}, bf16[1,8,2048]{2,1,0:T(8,128)(2,1)S(1)}, u32[]{:S(2)}, u32[]{:S(2)}) collective-permute-start(bf16[1,8,2048]{2,1,0:T(8,128)(2,1)S(1)} %add.152), channel_id=1, source_target_pairs={{0,128},{4,132},{8,136},{12,140},{16,144},{20,148},{24,152},{28,15... | collective-permute-start | bytes 98312 | tf_op jit(solution)/shard_map/ppermute | solution.py:39
  63.6 6.2 %collective-permute-start.8 = (bf16[1,8,2048]{2,1,0:T(8,128)(2,1)S(1)}, bf16[1,8,2048]{2,1,0:T(8,128)(2,1)S(1)}, u32[]{:S(2)}, u32[]{:S(2)}) collective-permute-start(bf16[1,8,2048]{2,1,0:T(8,128)(2,1)S(1)} %add.153), channel_id=1, source_target_pairs={{0,256},{4,260},{8,264},{12,268},{16,272},{20,276},{24,280},{28,28... | collective-permute-start | bytes 98312 | tf_op jit(solution)/shard_map/ppermute | solution.py:39
  69.9 18.8 %collective-permute-start.10 = (bf16[1,23,2048]{2,1,0:T(8,128)(2,1)S(1)}, bf16[1,23,2048]{2,1,0:T(8,128)(2,1)S(1)}, u32[]{:S(2)}, u32[]{:S(2)}) collective-permute-start(bf16[1,23,2048]{2,1,0:T(8,128)(2,1)S(1)} %pad_maximum_fusion.2), channel_id=1, source_target_pairs={{0,2},{1,3},{2,0},{3,1},{4,6},{5,7},{6,4},{7,5},{8,10},{9,11},{10,... | collective-permute-start | bytes 282632 | tf_op jit(solution)/shard_map/ppermute | solution.py:49
  72.5 16.2 %collective-permute-start.11 = (bf16[1,23,2048]{2,1,0:T(8,128)(2,1)S(1)}, bf16[1,23,2048]{2,1,0:T(8,128)(2,1)S(1)}, u32[]{:S(2)}, u32[]{:S(2)}) collective-permute-start(bf16[1,23,2048]{2,1,0:T(8,128)(2,1)S(1)} %pad_maximum_fusion.2), channel_id=1, source_target_pairs={{0,3},{1,0},{2,1},{3,2},{4,7},{5,4},{6,5},{7,6},{8,11},{9,8},{10,9... | collective-permute-start | bytes 282632 | tf_op jit(solution)/shard_map/ppermute | solution.py:49
  82.2 6.5 %collective-permute-start.9 = (bf16[1,23,2048]{2,1,0:T(8,128)(2,1)S(1)}, bf16[1,23,2048]{2,1,0:T(8,128)(2,1)S(1)}, u32[]{:S(2)}, u32[]{:S(2)}) collective-permute-start(bf16[1,23,2048]{2,1,0:T(8,128)(2,1)S(1)} %pad_maximum_fusion.2), channel_id=1, source_target_pairs={{0,1},{1,2},{2,3},{3,0},{4,5},{5,6},{6,7},{7,4},{8,9},{9,10},{10,1... | collective-permute-start | bytes 282632 | tf_op jit(solution)/shard_map/ppermute | solution.py:49
  88.9 3.5 %copy-start = (bf16[32,64,1024]{2,1,0:T(8,128)(2,1)S(1)}, bf16[32,64,1024]{2,1,0:T(8,128)(2,1)}, u32[]{:S(2)}) copy-start(bf16[32,64,1024]{2,1,0:T(8,128)(2,1)} %get-tuple-element.14) | copy-start | bytes 12582916

commit v4 on v3

--- a/solution.py
+++ b/solution.py
@@ -138,31 +138,38 @@
         for step in range(steps)
     ]
     received = broadcast(jnp.concatenate(masked, axis=1), "fibre")
-    window = halo(data, "fibre", 1)
-    rows = window.shape[1]
-    block = jnp.concatenate([window, received], axis=1)
-    block = gather(block, "seg")
-    segs = block.shape[0]
+    window = gather(halo(data, "fibre", 1), "seg")
+    chosen = gather(received, "seg")
+    segs, rows, _ = window.shape
     cos, sin = make_forward(length)
     inverse = make_inverse(length, LAGS)
-    flat_rows = block.reshape(segs * block.shape[1], length)
-    spectra = jnp.concatenate(
-        [
-            jnp.dot(flat_rows, cos, preferred_element_type=jnp.float32),
-            -jnp.dot(flat_rows, sin, preferred_element_type=jnp.float32),
-        ],
-        axis=-1,
-    )
-    white = whiten(spectra.reshape(block.shape), BAND).astype(jnp.bfloat16)
-    chosen = white[:, rows:].reshape(segs, steps, nsrc, length)
+
+    def transform(block):
+        flat_rows = block.reshape(-1, length)
+        spectra = jnp.concatenate(
+            [
+                jnp.dot(flat_rows, cos, preferred_element_type=jnp.float32),
+                -jnp.dot(flat_rows, sin, preferred_element_type=jnp.float32),
+            ],
+            axis=-1,
+        )
+        return whiten(spectra.reshape(block.shape), BAND).astype(jnp.bfloat16)
+
+    white = transform(window)
     start = lax.axis_index("seg") * per
-    part = lax.dynamic_slice_in_dim(white[:, :rows], start, per + LOW + HIGH, axis=1)
+    part = lax.dynamic_slice_in_dim(white, start, per + LOW + HIGH, axis=1)
     total = part[:, 0:per].astype(jnp.float32)
     for offset in range(1, LOW + HIGH + 1):
         total = total + part[:, offset : offset + per].astype(jnp.float32)
     stacked = (total * 0.125).astype(jnp.bfloat16)
-    cross = cross_sum(stacked, chosen)
-    flat = jnp.dot(cross.reshape(-1, length), inverse, precision=lax.Precision.HIGH)
+    emitters = transform(chosen).reshape(segs, steps, nsrc, length)
+    cross = cross_sum(stacked, emitters)
+    flat = lax.dot_general(
+        inverse,
+        cross.reshape(-1, length),
+        (((0,), (1,)), ((), ())),
+        precision=lax.Precision.HIGH,
+    ).T
     return flat.reshape(steps, nsrc, per, LAGS)
 
 

time: 102 us -> 115 us (1.13)
  waiting for transfers between devices: 5.06 us -> 12 us
  matrix products: 10.7 us -> 14.6 us
  starting transfers between devices: 66.2 us -> 67.6 us
    ppermute x3 -> x6, starting transfers between devices: 14.3 us -> 27.8 us  [gather(): lax.ppermute(block, axis, [(i, (i + shift) % count) for i in range(count)])]
    ppermute x7, starting transfers between devices: 47.3 us -> 36.6 us  [broadcast(): total = total + lax.ppermute(block, axis, perm)]
    dot_general x3 -> x5, matrix products: 9.68 us -> 13.6 us  [the longest x1 5.75 us: shards(): lax.dot_general(inverse, cross.reshape(-1, length), (((0,), (1,)), ((), (...]
    ppermute x7, waiting for transfers between devices: 5.05 us -> 8.75 us  [broadcast(): total = total + lax.ppermute(block, axis, perm)]
    ppermute x3 -> x6, waiting for transfers between devices: 0.01 us -> 3.29 us  [gather(): lax.ppermute(block, axis, [(i, (i + shift) % count) for i in range(count)])]
    ppermute x1, starting transfers between devices: 3.36 us -> 1.92 us  [halo(): lax.ppermute(tail, axis, [(i, i + 1) for i in range(ends)])]
  transfers between devices with their start and end apart: 12 -> 15, of which waited for: 5 -> 6; matrix products, arithmetic and copies ran while one was open for 13% -> 17% of each run, Pallas kernels for 0% -> 0%
where the time goes in v4:
time: 115 us; the launch traced here: 114 us
  starting transfers between devices  67.6 us (59%)
  matrix products  14.6 us (13%)
  other arithmetic  13.2 us (11%)
  waiting for transfers between devices  12 us (10%)
  local copies, waits for them, and re-layouts  4.97 us (4%)
  between operations  1.79 us (2%)
    ppermute x7, starting transfers between devices, broadcast(): total = total + lax.ppermute(block, axis, perm)  36.6 us
    ppermute x6, starting transfers between devices, gather(): lax.ppermute(block, axis, [(i, (i + shift) % count) for i in range(count)])  27.8 us
    ppermute x7, waiting for transfers between devices, broadcast(): total = total + lax.ppermute(block, axis, perm)  8.75 us
    dot_general x1, matrix products, shards(): lax.dot_general(inverse, cross.reshape(-1, length), (((0,), (1,)), ((), (...  5.75 us
    convert_element_type x1, other arithmetic, make_forward(): cos = cos.reshape(length, half).astype(jnp.bfloat16)  4.84 us
    sub x1, other arithmetic, make_inverse(): hi_c[:, None, :] * lo_c[None, :, :] - hi_s[:, None, :] * lo_s[None, :, :]  4.42 us
    dot_general x2, matrix products, transform(): jnp.dot(flat_rows, sin, preferred_element_type=jnp.float32)  4.01 us
    dot_general x2, matrix products, transform(): jnp.dot(flat_rows, cos, preferred_element_type=jnp.float32)  3.84 us
  transfers between devices with their start and end apart: 15, of which 6 were waited for; matrix products, arithmetic and copies ran while one was open for 17% of the time, Pallas kernels for 0%

profile of v4, /device:TPU:1, one launch (start us, length us, event | category | flops | bytes accessed | tf_op | source)
XLA Modules:
  0.0 114.2 jit_solution(8789545916613743343)
XLA Ops:
  0.0 1.3 %fusion.55 = (s32[1]{0:T(128)}, s32[1]{0:T(128)}) fusion(s32[2]{0:T(128)} %param.5), kind=kLoop, calls=%fused_computation.99 | loop fusion | bytes 16 | tf_op jit(solution)/shard_map/slice | solution.py:137
  2.6 1.0 fusion.6
  3.7 4.4 %collective-permute-start.5 = (bf16[1,8,2048]{2,1,0:T(8,128)(2,1)S(1)}, bf16[1,8,2048]{2,1,0:T(8,128)(2,1)S(1)}, u32[]{:S(2)}, u32[]{:S(2)}) collective-permute-start(bf16[1,8,2048]{2,1,0:T(8,128)(2,1)S(1)} %pad_maximum_fusion.4), channel_id=1, source_target_pairs={{0,4},{4,0},{8,12},{12,8},{16,20},{20,16},{24,28},{28,24},{32,36},... | collective-permute-start | bytes 98312 | tf_op jit(solution)/shard_map/ppermute | solution.py:39
  8.0 0.8 slice.54
  8.8 1.9 %collective-permute-start = (bf16[1,4,2048]{2,1,0:T(4,128)(2,1)S(1)}, bf16[1,4,2048]{2,1,0:T(4,128)(2,1)S(1)}, u32[]{:S(2)}, u32[]{:S(2)}) collective-permute-start(bf16[1,4,2048]{2,1,0:T(4,128)(2,1)S(1)} %slice.54), channel_id=1, source_target_pairs={{0,4},{4,8},{8,12},{12,16},{16,20},{20,24},{24,28},{28,32},{32,36}... | collective-permute-start | bytes 49160 | tf_op jit(solution)/shard_map/ppermute | solution.py:60
  10.7 0.8 slice.55
  11.5 1.3 %collective-permute-start.1 = (bf16[1,3,2048]{2,1,0:T(4,128)(2,1)S(1)}, bf16[1,3,2048]{2,1,0:T(4,128)(2,1)S(1)}, u32[]{:S(2)}, u32[]{:S(2)}) collective-permute-start(bf16[1,3,2048]{2,1,0:T(4,128)(2,1)S(1)} %slice.55), channel_id=1, source_target_pairs={{4,0},{8,4},{12,8},{16,12},{20,16},{24,20},{28,24},{32,28},{36,32}... | collective-permute-start | bytes 36872 | tf_op jit(solution)/shard_map/ppermute | solution.py:62
  12.8 1.0 fusion.30
  13.8 0.5 fusion.37
  14.4 4.8 %subtract_convert_fusion = (bf16[32,64,1024]{2,1,0:T(8,128)(2,1)}, bf16[32,64,1024]{2,1,0:T(8,128)(2,1)}) fusion(f32[64,1024]{1,0:T(8,128)S(1)} %get-tuple-element.31, f32[32,1024]{1,0:T(8,128)S(1)} %get-tuple-element.33, f32[64,1024]{1,0:T(8,128)S(1)} %get-tuple-element.32, f32[32,1024]{1,0:T(8,128)S(1)} %get-tuple-element.34), kind=kLoop, calls=%fused_computation.6 | loop fusion | flops 16777216 | bytes 9175040 | tf_op jit(solution)/shard_map/convert_element_type | solution.py:84
  19.2 1.0 fusion.42
  20.3 4.1 %collective-permute-start.2 = (bf16[1,15,2048]{2,1,0:T(8,128)(2,1)S(1)}, bf16[1,15,2048]{2,1,0:T(8,128)(2,1)S(1)}, u32[]{:S(2)}, u32[]{:S(2)}) collective-permute-start(bf16[1,15,2048]{2,1,0:T(8,128)(2,1)S(1)} %pad_maximum_fusion.3), channel_id=1, source_target_pairs={{0,1},{1,2},{2,3},{3,0},{4,5},{5,6},{6,7},{7,4},{8,9},{9,10},{10,1... | collective-permute-start | bytes 184328 | tf_op jit(solution)/shard_map/ppermute | solution.py:49
  24.5 7.5 %collective-permute-start.3 = (bf16[1,15,2048]{2,1,0:T(8,128)(2,1)S(1)}, bf16[1,15,2048]{2,1,0:T(8,128)(2,1)S(1)}, u32[]{:S(2)}, u32[]{:S(2)}) collective-permute-start(bf16[1,15,2048]{2,1,0:T(8,128)(2,1)S(1)} %pad_maximum_fusion.3), channel_id=1, source_target_pairs={{0,2},{1,3},{2,0},{3,1},{4,6},{5,7},{6,4},{7,5},{8,10},{9,11},{10,... | collective-permute-start | bytes 184328 | tf_op jit(solution)/shard_map/ppermute | solution.py:49
  31.9 1.9 %collective-permute-start.4 = (bf16[1,15,2048]{2,1,0:T(8,128)(2,1)S(1)}, bf16[1,15,2048]{2,1,0:T(8,128)(2,1)S(1)}, u32[]{:S(2)}, u32[]{:S(2)}) collective-permute-start(bf16[1,15,2048]{2,1,0:T(8,128)(2,1)S(1)} %pad_maximum_fusion.3), channel_id=1, source_target_pairs={{0,3},{1,0},{2,1},{3,2},{4,7},{5,4},{6,5},{7,6},{8,11},{9,8},{10,9... | collective-permute-start | bytes 184328 | tf_op jit(solution)/shard_map/ppermute | solution.py:49
  33.9 3.7 %collective-permute-start.6 = (bf16[1,8,2048]{2,1,0:T(8,128)(2,1)S(1)}, bf16[1,8,2048]{2,1,0:T(8,128)(2,1)S(1)}, u32[]{:S(2)}, u32[]{:S(2)}) collective-permute-start(bf16[1,8,2048]{2,1,0:T(8,128)(2,1)S(1)} %fusion.52), channel_id=1, source_target_pairs={{0,8},{4,12},{8,0},{12,4},{16,24},{20,28},{24,16},{28,20},{32,40},... | collective-permute-start | bytes 98312 | tf_op jit(solution)/shard_map/ppermute | solution.py:39
  37.6 4.4 %multiply_subtract_fusion = (f32[32,32,1024]{2,1,0:T(8,128)}, f32[32,32,1024]{2,1,0:T(8,128)}) fusion(f32[32,1024]{1,0:T(8,128)S(1)} %get-tuple-element.27, f32[32,1024]{1,0:T(8,128)S(1)} %get-tuple-element.26, f32[32,1024]{1,0:T(8,128)S(1)} %get-tuple-element.28, f32[32,1024]{1,0:T(8,128)S(1)} %get-tuple-element.25), kind=kLoop, calls=%fused_computation.9 | loop fusion | flops 7340032 | bytes 8912896 | tf_op jit(solution)/shard_map/sub | solution.py:99
  42.1 7.4 %collective-permute-start.7 = (bf16[1,8,2048]{2,1,0:T(8,128)(2,1)S(1)}, bf16[1,8,2048]{2,1,0:T(8,128)(2,1)S(1)}, u32[]{:S(2)}, u32[]{:S(2)}) collective-permute-start(bf16[1,8,2048]{2,1,0:T(8,128)(2,1)S(1)} %add.186), channel_id=1, source_target_pairs={{0,16},{4,20},{8,24},{12,28},{16,0},{20,4},{24,8},{28,12},{32,48},... | collective-permute-start | bytes 98312 | tf_op jit(solution)/shard_map/ppermute | solution.py:39
  49.7 3.2 %convolution_negate_fusion = f32[60,1024]{1,0:T(8,128)S(1)} fusion(bf16[60,2048]{1,0:T(8,128)(2,1)S(1)} %reshape.338, bf16[2048,1024]{1,0:T(8,128)(2,1)} %bitcast.57), kind=kOutput, calls=%fused_computation.12 | convolution fusion | flops 251719680 | bytes 4685824 | tf_op jit(solution)/shard_map/dot_general | solution.py:152
  52.8 0.3 copy-done.1
  53.1 0.8 fusion.56
  54.0 0.1 copy.22
  54.2 0.1 reduce_sum.54
  54.3 0.1 copy.15
  54.4 8.0 %collective-permute-start.8 = (bf16[1,8,2048]{2,1,0:T(8,128)(2,1)S(1)}, bf16[1,8,2048]{2,1,0:T(8,128)(2,1)S(1)}, u32[]{:S(2)}, u32[]{:S(2)}) collective-permute-start(bf16[1,8,2048]{2,1,0:T(8,128)(2,1)S(1)} %add.187), channel_id=1, source_target_pairs={{0,32},{4,36},{8,40},{12,44},{16,48},{20,52},{24,56},{28,60},{32,0... | collective-permute-start | bytes 98312 | tf_op jit(solution)/shard_map/ppermute | solution.py:39
  62.4 0.1 copy.16
  62.5 0.1 mul.497
  62.7 0.2 mul.498
  62.9 5.1 %collective-permute-done.8 = bf16[1,8,2048]{2,1,0:T(8,128)(2,1)S(1)} collective-permute-done((bf16[1,8,2048]{2,1,0:T(8,128)(2,1)S(1)}, bf16[1,8,2048]{2,1,0:T(8,128)(2,1)S(1)}, u32[]{:S(2)}, u32[]{:S(2)}) %collective-permute-start.8) | collective-permute-done | bytes 32800 | tf_op jit(solution)/shard_map/ppermute | solution.py:39
  67.9 4.5 %collective-permute-start.9 = (bf16[1,8,2048]{2,1,0:T(8,128)(2,1)S(1)}, bf16[1,8,2048]{2,1,0:T(8,128)(2,1)S(1)}, u32[]{:S(2)}, u32[]{:S(2)}) collective-permute-start(bf16[1,8,2048]{2,1,0:T(8,128)(2,1)S(1)} %add.188), channel_id=1, source_target_pairs={{0,64},{4,68},{8,72},{12,76},{16,80},{20,84},{24,88},{28,92},{32,9... | collective-permute-start | bytes 98312 | tf_op jit(solution)/shard_map/ppermute | solution.py:39
  72.6 1.5 %collective-permute-done.9 = bf16[1,8,2048]{2,1,0:T(8,128)(2,1)S(1)} collective-permute-done((bf16[1,8,2048]{2,1,0:T(8,128)(2,1)S(1)}, bf16[1,8,2048]{2,1,0:T(8,128)(2,1)S(1)}, u32[]{:S(2)}, u32[]{:S(2)}) %collective-permute-start.9) | collective-permute-done | bytes 32800 | tf_op jit(solution)/shard_map/ppermute | solution.py:39
  74.1 3.8 %collective-permute-start.10 = (bf16[1,8,2048]{2,1,0:T(8,128)(2,1)S(1)}, bf16[1,8,2048]{2,1,0:T(8,128)(2,1)S(1)}, u32[]{:S(2)}, u32[]{:S(2)}) collective-permute-start(bf16[1,8,2048]{2,1,0:T(8,128)(2,1)S(1)} %add.189), channel_id=1, source_target_pairs={{0,128},{4,132},{8,136},{12,140},{16,144},{20,148},{24,152},{28,15... | collective-permute-start | bytes 98312 | tf_op jit(solution)/shard_map/ppermute | solution.py:39
  77.9 0.2 fusion.7
  78.1 1.1 collective-permute-done.10
  79.2 4.9 %collective-permute-start.11 = (bf16[1,8,2048]{2,1,0:T(8,128)(2,1)S(1)}, bf16[1,8,2048]{2,1,0:T(8,128)(2,1)S(1)}, u32[]{:S(2)}, u32[]{:S(2)}) collective-permute-start(bf16[1,8,2048]{2,1,0:T(8,128)(2,1)S(1)} %add.190), channel_id=1, source_target_pairs={{0,256},{4,260},{8,264},{12,268},{16,272},{20,276},{24,280},{28,28... | collective-permute-start | bytes 98312 | tf_op jit(solution)/shard_map/ppermute | solution.py:39
  84.1 0.2 bitcast_convert_fusion
  84.3 1.1 collective-permute-done.11
  85.4 9.9 %collective-permute-start.12 = (bf16[1,8,2048]{2,1,0:T(8,128)(2,1)S(1)}, bf16[1,8,2048]{2,1,0:T(8,128)(2,1)S(1)}, u32[]{:S(2)}, u32[]{:S(2)}) collective-permute-start(bf16[1,8,2048]{2,1,0:T(8,128)(2,1)S(1)} %add.191), channel_id=1, source_target_pairs={{0,1},{1,2},{2,3},{3,0},{4,5},{5,6},{6,7},{7,4},{8,9},{9,10},{10,1... | collective-permute-start | bytes 98312 | tf_op jit(solution)/shard_map/ppermute | solution.py:49
  95.3 2.4 %collective-permute-start.13 = (bf16[1,8,2048]{2,1,0:T(8,128)(2,1)S(1)}, bf16[1,8,2048]{2,1,0:T(8,128)(2,1)S(1)}, u32[]{:S(2)}, u32[]{:S(2)}) collective-permute-start(bf16[1,8,2048]{2,1,0:T(8,128)(2,1)S(1)} %add.191), channel_id=1, source_target_pairs={{0,2},{1,3},{2,0},{3,1},{4,6},{5,7},{6,4},{7,5},{8,10},{9,11},{10,... | collective-permute-start | bytes 98312 | tf_op jit(solution)/shard_map/ppermute | solution.py:49
  97.7 1.9 %collective-permute-start.14 = (bf16[1,8,2048]{2,1,0:T(8,128)(2,1)S(1)}, bf16[1,8,2048]{2,1,0:T(8,128)(2,1)S(1)}, u32[]{:S(2)}, u32[]{:S(2)}) collective-permute-start(bf16[1,8,2048]{2,1,0:T(8,128)(2,1)S(1)} %add.191), channel_id=1, source_target_pairs={{0,3},{1,0},{2,1},{3,2},{4,7},{5,4},{6,5},{7,6},{8,11},{9,8},{10,9... | collective-permute-start | bytes 98312 | tf_op jit(solution)/shard_map/ppermute | solution.py:49
  99.7 0.3 collective-permute-done.13
  100.0 3.0 %collective-permute-done.14 = bf16[1,8,2048]{2,1,0:T(8,128)(2,1)S(1)} collective-permute-done((bf16[1,8,2048]{2,1,0:T(8,128)(2,1)S(1)}, bf16[1,8,2048]{2,1,0:T(8,128)(2,1)S(1)}, u32[]{:S(2)}, u32[]{:S(2)}) %collective-permute-start.14) | collective-permute-done | bytes 32800 | tf_op jit(solution)/shard_map/ppermute | solution.py:49
  103.0 3.0 %fusion.44 = f32[32,1024]{1,0:T(8,128)S(1)} fusion(bf16[2048,1024]{1,0:T(8,128)(2,1)} %bitcast.59, bf16[1,8,2048]{2,1,0:T(8,128)(2,1)S(1)} %collective-permute-done.14, bf16[1,8,2048]{2,1,0:T(8,128)(2,1)S(1)} %collective-permute-done.13, bf16[1,8,2048]{2,1,0:T(8,128)(2,1)S(1)} %collective-permute-done.12, bf16[1,8,2048]{2,1,0:T(8,128)(2,1)S(1)} %add.191), kind=kOutput, calls=%fused_computation.81 | convolution fusion | flops 134414336 | bytes 4456448 | tf_op jit(solution)/shard_map/dot_general | solution.py:151
  106.0 0.8 convolution_negate_fusion.1
  106.9 0.1 reduce_sum.55
  107.1 0.1 mul.507
  107.5 0.3 multiply_reduce_fusion.3
  107.8 5.8 %fusion.1 = f32[2,4,2,1024]{3,1,2,0:T(4,128)S(1)} fusion(f32[1024,1024]{1,0:T(8,128)} %bitcast.62, f32[1024,1024]{1,0:T(8,128)} %bitcast.61, f32[2,4,2,1024]{3,1,2,0:T(4,128)S(1)} %sub.32, f32[2,4,2,1024]{3,1,2,0:T(4,128)S(1)} %add.194), kind=kOutput, calls=%fused_computation.2 | convolution fusion | flops 205553664 | bytes 8585216 | tf_op jit(solution)/shard_map/dot_general | solution.py:167
  113.5 0.7 copy.19
  (42 shorter events, 1.0 us)
Async XLA Ops:
  3.7 30.2 %collective-permute-start.5 = (bf16[1,8,2048]{2,1,0:T(8,128)(2,1)S(1)}, bf16[1,8,2048]{2,1,0:T(8,128)(2,1)S(1)}, u32[]{:S(2)}, u32[]{:S(2)}) collective-permute-start(bf16[1,8,2048]{2,1,0:T(8,128)(2,1)S(1)} %pad_maximum_fusion.4), channel_id=1, source_target_pairs={{0,4},{4,0},{8,12},{12,8},{16,20},{20,16},{24,28},{28,24},{32,36},... | collective-permute-start | bytes 98312 | tf_op jit(solution)/shard_map/ppermute | solution.py:39
  8.8 11.4 %collective-permute-start = (bf16[1,4,2048]{2,1,0:T(4,128)(2,1)S(1)}, bf16[1,4,2048]{2,1,0:T(4,128)(2,1)S(1)}, u32[]{:S(2)}, u32[]{:S(2)}) collective-permute-start(bf16[1,4,2048]{2,1,0:T(4,128)(2,1)S(1)} %slice.54), channel_id=1, source_target_pairs={{0,4},{4,8},{8,12},{12,16},{16,20},{20,24},{24,28},{28,32},{32,36}... | collective-permute-start | bytes 49160 | tf_op jit(solution)/shard_map/ppermute | solution.py:60
  11.5 8.7 %collective-permute-start.1 = (bf16[1,3,2048]{2,1,0:T(4,128)(2,1)S(1)}, bf16[1,3,2048]{2,1,0:T(4,128)(2,1)S(1)}, u32[]{:S(2)}, u32[]{:S(2)}) collective-permute-start(bf16[1,3,2048]{2,1,0:T(4,128)(2,1)S(1)} %slice.55), channel_id=1, source_target_pairs={{4,0},{8,4},{12,8},{16,12},{20,16},{24,20},{28,24},{32,28},{36,32}... | collective-permute-start | bytes 36872 | tf_op jit(solution)/shard_map/ppermute | solution.py:62
  14.4 5.9 %copy-start.2 = (bf16[1,8,2048]{2,1,0:T(8,128)(2,1)S(1)}, bf16[1,8,2048]{2,1,0:T(8,128)(2,1)}, u32[]{:S(2)}) copy-start(bf16[1,8,2048]{2,1,0:T(8,128)(2,1)} %param.3) | copy-start | bytes 98308
  20.3 29.1 %collective-permute-start.2 = (bf16[1,15,2048]{2,1,0:T(8,128)(2,1)S(1)}, bf16[1,15,2048]{2,1,0:T(8,128)(2,1)S(1)}, u32[]{:S(2)}, u32[]{:S(2)}) collective-permute-start(bf16[1,15,2048]{2,1,0:T(8,128)(2,1)S(1)} %pad_maximum_fusion.3), channel_id=1, source_target_pairs={{0,1},{1,2},{2,3},{3,0},{4,5},{5,6},{6,7},{7,4},{8,9},{9,10},{10,1... | collective-permute-start | bytes 184328 | tf_op jit(solution)/shard_map/ppermute | solution.py:49
  24.5 25.0 %collective-permute-start.3 = (bf16[1,15,2048]{2,1,0:T(8,128)(2,1)S(1)}, bf16[1,15,2048]{2,1,0:T(8,128)(2,1)S(1)}, u32[]{:S(2)}, u32[]{:S(2)}) collective-permute-start(bf16[1,15,2048]{2,1,0:T(8,128)(2,1)S(1)} %pad_maximum_fusion.3), channel_id=1, source_target_pairs={{0,2},{1,3},{2,0},{3,1},{4,6},{5,7},{6,4},{7,5},{8,10},{9,11},{10,... | collective-permute-start | bytes 184328 | tf_op jit(solution)/shard_map/ppermute | solution.py:49
  31.9 17.6 %collective-permute-start.4 = (bf16[1,15,2048]{2,1,0:T(8,128)(2,1)S(1)}, bf16[1,15,2048]{2,1,0:T(8,128)(2,1)S(1)}, u32[]{:S(2)}, u32[]{:S(2)}) collective-permute-start(bf16[1,15,2048]{2,1,0:T(8,128)(2,1)S(1)} %pad_maximum_fusion.3), channel_id=1, source_target_pairs={{0,3},{1,0},{2,1},{3,2},{4,7},{5,4},{6,5},{7,6},{8,11},{9,8},{10,9... | collective-permute-start | bytes 184328 | tf_op jit(solution)/shard_map/ppermute | solution.py:49
  33.9 8.2 %collective-permute-start.6 = (bf16[1,8,2048]{2,1,0:T(8,128)(2,1)S(1)}, bf16[1,8,2048]{2,1,0:T(8,128)(2,1)S(1)}, u32[]{:S(2)}, u32[]{:S(2)}) collective-permute-start(bf16[1,8,2048]{2,1,0:T(8,128)(2,1)S(1)} %fusion.52), channel_id=1, source_target_pairs={{0,8},{4,12},{8,0},{12,4},{16,24},{20,28},{24,16},{28,20},{32,40},... | collective-permute-start | bytes 98312 | tf_op jit(solution)/shard_map/ppermute | solution.py:39
  42.1 12.4 %collective-permute-start.7 = (bf16[1,8,2048]{2,1,0:T(8,128)(2,1)S(1)}, bf16[1,8,2048]{2,1,0:T(8,128)(2,1)S(1)}, u32[]{:S(2)}, u32[]{:S(2)}) collective-permute-start(bf16[1,8,2048]{2,1,0:T(8,128)(2,1)S(1)} %add.186), channel_id=1, source_target_pairs={{0,16},{4,20},{8,24},{12,28},{16,0},{20,4},{24,8},{28,12},{32,48},... | collective-permute-start | bytes 98312 | tf_op jit(solution)/shard_map/ppermute | solution.py:39
  49.6 3.5 %copy-start.1 = (bf16[32,64,1024]{2,1,0:T(8,128)(2,1)S(1)}, bf16[32,64,1024]{2,1,0:T(8,128)(2,1)}, u32[]{:S(2)}) copy-start(bf16[32,64,1024]{2,1,0:T(8,128)(2,1)} %get-tuple-element.11) | copy-start | bytes 12582916
  54.4 13.5 %collective-permute-start.8 = (bf16[1,8,2048]{2,1,0:T(8,128)(2,1)S(1)}, bf16[1,8,2048]{2,1,0:T(8,128)(2,1)S(1)}, u32[]{:S(2)}, u32[]{:S(2)}) collective-permute-start(bf16[1,8,2048]{2,1,0:T(8,128)(2,1)S(1)} %add.187), channel_id=1, source_target_pairs={{0,32},{4,36},{8,40},{12,44},{16,48},{20,52},{24,56},{28,60},{32,0... | collective-permute-start | bytes 98312 | tf_op jit(solution)/shard_map/ppermute | solution.py:39
  67.9 6.2 %collective-permute-start.9 = (bf16[1,8,2048]{2,1,0:T(8,128)(2,1)S(1)}, bf16[1,8,2048]{2,1,0:T(8,128)(2,1)S(1)}, u32[]{:S(2)}, u32[]{:S(2)}) collective-permute-start(bf16[1,8,2048]{2,1,0:T(8,128)(2,1)S(1)} %add.188), channel_id=1, source_target_pairs={{0,64},{4,68},{8,72},{12,76},{16,80},{20,84},{24,88},{28,92},{32,9... | collective-permute-start | bytes 98312 | tf_op jit(solution)/shard_map/ppermute | solution.py:39
  72.6 33.4 %copy-start = (bf16[32,64,1024]{2,1,0:T(8,128)(2,1)S(1)}, bf16[32,64,1024]{2,1,0:T(8,128)(2,1)}, u32[]{:S(2)}) copy-start(bf16[32,64,1024]{2,1,0:T(8,128)(2,1)} %get-tuple-element.12) | copy-start | bytes 12582916
  74.1 5.1 %collective-permute-start.10 = (bf16[1,8,2048]{2,1,0:T(8,128)(2,1)S(1)}, bf16[1,8,2048]{2,1,0:T(8,128)(2,1)S(1)}, u32[]{:S(2)}, u32[]{:S(2)}) collective-permute-start(bf16[1,8,2048]{2,1,0:T(8,128)(2,1)S(1)} %add.189), channel_id=1, source_target_pairs={{0,128},{4,132},{8,136},{12,140},{16,144},{20,148},{24,152},{28,15... | collective-permute-start | bytes 98312 | tf_op jit(solution)/shard_map/ppermute | solution.py:39
  79.2 6.2 %collective-permute-start.11 = (bf16[1,8,2048]{2,1,0:T(8,128)(2,1)S(1)}, bf16[1,8,2048]{2,1,0:T(8,128)(2,1)S(1)}, u32[]{:S(2)}, u32[]{:S(2)}) collective-permute-start(bf16[1,8,2048]{2,1,0:T(8,128)(2,1)S(1)} %add.190), channel_id=1, source_target_pairs={{0,256},{4,260},{8,264},{12,268},{16,272},{20,276},{24,280},{28,28... | collective-permute-start | bytes 98312 | tf_op jit(solution)/shard_map/ppermute | solution.py:39
  85.4 14.3 %collective-permute-start.12 = (bf16[1,8,2048]{2,1,0:T(8,128)(2,1)S(1)}, bf16[1,8,2048]{2,1,0:T(8,128)(2,1)S(1)}, u32[]{:S(2)}, u32[]{:S(2)}) collective-permute-start(bf16[1,8,2048]{2,1,0:T(8,128)(2,1)S(1)} %add.191), channel_id=1, source_target_pairs={{0,1},{1,2},{2,3},{3,0},{4,5},{5,6},{6,7},{7,4},{8,9},{9,10},{10,1... | collective-permute-start | bytes 98312 | tf_op jit(solution)/shard_map/ppermute | solution.py:49
  95.3 4.7 %collective-permute-start.13 = (bf16[1,8,2048]{2,1,0:T(8,128)(2,1)S(1)}, bf16[1,8,2048]{2,1,0:T(8,128)(2,1)S(1)}, u32[]{:S(2)}, u32[]{:S(2)}) collective-permute-start(bf16[1,8,2048]{2,1,0:T(8,128)(2,1)S(1)} %add.191), channel_id=1, source_target_pairs={{0,2},{1,3},{2,0},{3,1},{4,6},{5,7},{6,4},{7,5},{8,10},{9,11},{10,... | collective-permute-start | bytes 98312 | tf_op jit(solution)/shard_map/ppermute | solution.py:49
  97.7 5.2 %collective-permute-start.14 = (bf16[1,8,2048]{2,1,0:T(8,128)(2,1)S(1)}, bf16[1,8,2048]{2,1,0:T(8,128)(2,1)S(1)}, u32[]{:S(2)}, u32[]{:S(2)}) collective-permute-start(bf16[1,8,2048]{2,1,0:T(8,128)(2,1)S(1)} %add.191), channel_id=1, source_target_pairs={{0,3},{1,0},{2,1},{3,2},{4,7},{5,4},{6,5},{7,6},{8,11},{9,8},{10,9... | collective-permute-start | bytes 98312 | tf_op jit(solution)/shard_map/ppermute | solution.py:49

commit v5 on v3

--- a/solution.py
+++ b/solution.py
@@ -44,10 +44,12 @@
 
 def gather(block, axis):
     count = lax.axis_size(axis)
-    pieces = [block]
-    for shift in range(1, count):
-        pieces.append(lax.ppermute(block, axis, [(i, (i + shift) % count) for i in range(count)]))
-    return jnp.concatenate(pieces, axis=0)
+    stride = 1
+    while stride < count:
+        partner = lax.ppermute(block, axis, [(i, i ^ stride) for i in range(count)])
+        block = jnp.concatenate([block, partner], axis=0)
+        stride *= 2
+    return block
 
 
 def halo(cells, axis, dim):
@@ -127,17 +129,14 @@
     steps, nsrc = sources.shape
     seg_count = lax.axis_size("seg")
     per = ch_dev // seg_count
-    selector = (sources[:, :, None] == jnp.arange(ch_dev, dtype=jnp.int32)[None, None, :]).astype(
-        jnp.bfloat16
+    here = lax.axis_index("fibre")
+    channels = jnp.arange(ch_dev, dtype=jnp.int32)
+    keep = (sources[:, :, None] == channels[None, None, :]) & (here == owners)[:, None, None]
+    picked = jnp.sum(
+        jnp.where(keep.reshape(1, steps * nsrc, ch_dev, 1), data[:, None], jnp.zeros_like(data[:, None])),
+        axis=2,
     )
-    picked = jnp.einsum("pnc,scf->spnf", selector, data, preferred_element_type=jnp.float32)
-    picked = picked.astype(jnp.bfloat16)
-    here = lax.axis_index("fibre")
-    masked = [
-        jnp.where(here == owners[step], picked[:, step], jnp.zeros_like(picked[:, step]))
-        for step in range(steps)
-    ]
-    received = broadcast(jnp.concatenate(masked, axis=1), "fibre")
+    received = broadcast(picked, "fibre")
     window = halo(data, "fibre", 1)
     rows = window.shape[1]
     block = jnp.concatenate([window, received], axis=1)

time: 102 us -> 102 us (level)
  other arithmetic: 13.3 us -> 15 us
  waiting for transfers between devices: 5.06 us -> 6.62 us
  between operations: 1.67 us -> 0.37 us
    ppermute x3 -> x2, starting transfers between devices: 14.3 us -> 11.8 us  [gather(): partner = lax.ppermute(block, axis, [(i, i ^ stride) for i in range(count)])]
    ppermute x7, starting transfers between devices: 47.3 us -> 48.9 us  [broadcast(): total = total + lax.ppermute(block, axis, perm)]
    slice x1 -> x0, local copies, waits for them, and re-layouts: 1.34 us -> none  [shards(): owners[step]]
    ppermute x3 -> x2, waiting for transfers between devices: 0.01 us -> 1.06 us  [gather(): partner = lax.ppermute(block, axis, [(i, i ^ stride) for i in range(count)])]
  transfers between devices with their start and end apart: 12 -> 11, of which waited for: 5 -> 6; matrix products, arithmetic and copies ran while one was open for 13% -> 13% of each run, Pallas kernels for 0% -> 0%
where the time goes in v5:
time: 102 us; the launch traced here: 101 us
  starting transfers between devices  65.3 us (64%)
  other arithmetic  15 us (15%)
  matrix products  9.68 us (9%)
  waiting for transfers between devices  6.62 us (6%)
  local copies, waits for them, and re-layouts  4.24 us (4%)
    ppermute x7, starting transfers between devices, broadcast(): total = total + lax.ppermute(block, axis, perm)  48.9 us
    ppermute x2, starting transfers between devices, gather(): partner = lax.ppermute(block, axis, [(i, i ^ stride) for i in range(count)])  11.8 us
    dot_general x1, matrix products, shards(): jnp.dot(cross.reshape(-1, length), inverse, precision=lax.Precision.HIGH)  5.75 us
    ppermute x7, waiting for transfers between devices, broadcast(): total = total + lax.ppermute(block, axis, perm)  5.55 us
    convert_element_type x1, other arithmetic, make_forward(): cos = cos.reshape(length, half).astype(jnp.bfloat16)  4.83 us
    sub x1, other arithmetic, make_inverse(): hi_c[:, None, :] * lo_c[None, :, :] - hi_s[:, None, :] * lo_s[None, :, :]  4.42 us
    ppermute x1, starting transfers between devices, halo(): lax.ppermute(tail, axis, [(i, i + 1) for i in range(ends)])  3.36 us
    dot_general x1, matrix products, shards(): jnp.dot(flat_rows, cos, preferred_element_type=jnp.float32)  3.13 us
  transfers between devices with their start and end apart: 11, of which 6 were waited for; matrix products, arithmetic and copies ran while one was open for 13% of the time, Pallas kernels for 0%

profile of v5, /device:TPU:1, one launch (start us, length us, event | category | flops | bytes accessed | tf_op | source)
XLA Modules:
  0.0 101.2 jit_solution(11172945726132144675)
XLA Ops:
  0.0 0.7 broadcast_compare_fusion
  0.7 0.1 and.92
  0.7 0.1 and.93
  0.8 0.8 eq.31
  1.6 0.1 fusion.40
  1.7 0.9 select_reduce_fusion
  2.6 4.4 %collective-permute-start.2 = (bf16[1,8,2048]{2,1,0:T(8,128)(2,1)S(1)}, bf16[1,8,2048]{2,1,0:T(8,128)(2,1)S(1)}, u32[]{:S(2)}, u32[]{:S(2)}) collective-permute-start(bf16[1,8,2048]{2,1,0:T(8,128)(2,1)S(1)} %bitcast.41), channel_id=1, source_target_pairs={{0,4},{4,0},{8,12},{12,8},{16,20},{20,16},{24,28},{28,24},{32,36},... | collective-permute-start | bytes 98312 | tf_op jit(solution)/shard_map/ppermute | solution.py:39
  7.0 1.3 %collective-permute-done.2 = bf16[1,8,2048]{2,1,0:T(8,128)(2,1)S(1)} collective-permute-done((bf16[1,8,2048]{2,1,0:T(8,128)(2,1)S(1)}, bf16[1,8,2048]{2,1,0:T(8,128)(2,1)S(1)}, u32[]{:S(2)}, u32[]{:S(2)}) %collective-permute-start.2) | collective-permute-done | bytes 32800 | tf_op jit(solution)/shard_map/ppermute | solution.py:39
  8.3 4.9 %collective-permute-start.3 = (bf16[1,8,2048]{2,1,0:T(8,128)(2,1)S(1)}, bf16[1,8,2048]{2,1,0:T(8,128)(2,1)S(1)}, u32[]{:S(2)}, u32[]{:S(2)}) collective-permute-start(bf16[1,8,2048]{2,1,0:T(8,128)(2,1)S(1)} %bitcast_add_fusion), channel_id=1, source_target_pairs={{0,8},{4,12},{8,0},{12,4},{16,24},{20,28},{24,16},{28,20},{32,40},... | collective-permute-start | bytes 98312 | tf_op jit(solution)/shard_map/ppermute | solution.py:39
  13.2 1.3 %collective-permute-done.3 = bf16[1,8,2048]{2,1,0:T(8,128)(2,1)S(1)} collective-permute-done((bf16[1,8,2048]{2,1,0:T(8,128)(2,1)S(1)}, bf16[1,8,2048]{2,1,0:T(8,128)(2,1)S(1)}, u32[]{:S(2)}, u32[]{:S(2)}) %collective-permute-start.3) | collective-permute-done | bytes 32800 | tf_op jit(solution)/shard_map/ppermute | solution.py:39
  14.5 8.8 %collective-permute-start.4 = (bf16[1,8,2048]{2,1,0:T(8,128)(2,1)S(1)}, bf16[1,8,2048]{2,1,0:T(8,128)(2,1)S(1)}, u32[]{:S(2)}, u32[]{:S(2)}) collective-permute-start(bf16[1,8,2048]{2,1,0:T(8,128)(2,1)S(1)} %add.149), channel_id=1, source_target_pairs={{0,16},{4,20},{8,24},{12,28},{16,0},{20,4},{24,8},{28,12},{32,48},... | collective-permute-start | bytes 98312 | tf_op jit(solution)/shard_map/ppermute | solution.py:39
  23.3 0.8 slice.48
  24.1 3.4 %collective-permute-start = (bf16[1,4,2048]{2,1,0:T(4,128)(2,1)S(1)}, bf16[1,4,2048]{2,1,0:T(4,128)(2,1)S(1)}, u32[]{:S(2)}, u32[]{:S(2)}) collective-permute-start(bf16[1,4,2048]{2,1,0:T(4,128)(2,1)S(1)} %slice.48), channel_id=1, source_target_pairs={{0,4},{4,8},{8,12},{12,16},{16,20},{20,24},{24,28},{28,32},{32,36}... | collective-permute-start | bytes 49160 | tf_op jit(solution)/shard_map/ppermute | solution.py:62
  27.4 0.8 slice.49
  28.2 1.3 %collective-permute-start.1 = (bf16[1,3,2048]{2,1,0:T(4,128)(2,1)S(1)}, bf16[1,3,2048]{2,1,0:T(4,128)(2,1)S(1)}, u32[]{:S(2)}, u32[]{:S(2)}) collective-permute-start(bf16[1,3,2048]{2,1,0:T(4,128)(2,1)S(1)} %slice.49), channel_id=1, source_target_pairs={{4,0},{8,4},{12,8},{16,12},{20,16},{24,20},{28,24},{32,28},{36,32}... | collective-permute-start | bytes 36872 | tf_op jit(solution)/shard_map/ppermute | solution.py:64
  29.5 11.7 %collective-permute-start.5 = (bf16[1,8,2048]{2,1,0:T(8,128)(2,1)S(1)}, bf16[1,8,2048]{2,1,0:T(8,128)(2,1)S(1)}, u32[]{:S(2)}, u32[]{:S(2)}) collective-permute-start(bf16[1,8,2048]{2,1,0:T(8,128)(2,1)S(1)} %add.150), channel_id=1, source_target_pairs={{0,32},{4,36},{8,40},{12,44},{16,48},{20,52},{24,56},{28,60},{32,0... | collective-permute-start | bytes 98312 | tf_op jit(solution)/shard_map/ppermute | solution.py:39
  41.2 1.0 %fusion.27 = (f32[64,1024]{1,0:T(8,128)S(1)}, f32[64,1024]{1,0:T(8,128)S(1)}) fusion(), kind=kLoop, calls=%fused_computation.56 | loop fusion | flops 917504 | bytes 524288 | tf_op jit(solution)/shard_map/sin | solution.py:72
  42.2 0.7 collective-permute-done.5
  42.9 9.1 %collective-permute-start.6 = (bf16[1,8,2048]{2,1,0:T(8,128)(2,1)S(1)}, bf16[1,8,2048]{2,1,0:T(8,128)(2,1)S(1)}, u32[]{:S(2)}, u32[]{:S(2)}) collective-permute-start(bf16[1,8,2048]{2,1,0:T(8,128)(2,1)S(1)} %add.151), channel_id=1, source_target_pairs={{0,64},{4,68},{8,72},{12,76},{16,80},{20,84},{24,88},{28,92},{32,9... | collective-permute-start | bytes 98312 | tf_op jit(solution)/shard_map/ppermute | solution.py:39
  52.1 0.5 fusion.34
  52.6 0.8 collective-permute-done.6
  53.4 5.3 %collective-permute-start.7 = (bf16[1,8,2048]{2,1,0:T(8,128)(2,1)S(1)}, bf16[1,8,2048]{2,1,0:T(8,128)(2,1)S(1)}, u32[]{:S(2)}, u32[]{:S(2)}) collective-permute-start(bf16[1,8,2048]{2,1,0:T(8,128)(2,1)S(1)} %add.152), channel_id=1, source_target_pairs={{0,128},{4,132},{8,136},{12,140},{16,144},{20,148},{24,152},{28,15... | collective-permute-start | bytes 98312 | tf_op jit(solution)/shard_map/ppermute | solution.py:39
  58.8 4.8 %subtract_convert_fusion = (bf16[32,64,1024]{2,1,0:T(8,128)(2,1)}, bf16[32,64,1024]{2,1,0:T(8,128)(2,1)}) fusion(f32[64,1024]{1,0:T(8,128)S(1)} %get-tuple-element.25, f32[32,1024]{1,0:T(8,128)S(1)} %get-tuple-element.27, f32[64,1024]{1,0:T(8,128)S(1)} %get-tuple-element.26, f32[32,1024]{1,0:T(8,128)S(1)} %get-tuple-element.28), kind=kLoop, calls=%fused_computation.6 | loop fusion | flops 16777216 | bytes 9175040 | tf_op jit(solution)/shard_map/convert_element_type | solution.py:86
  63.6 4.7 %collective-permute-start.8 = (bf16[1,8,2048]{2,1,0:T(8,128)(2,1)S(1)}, bf16[1,8,2048]{2,1,0:T(8,128)(2,1)S(1)}, u32[]{:S(2)}, u32[]{:S(2)}) collective-permute-start(bf16[1,8,2048]{2,1,0:T(8,128)(2,1)S(1)} %add.153), channel_id=1, source_target_pairs={{0,256},{4,260},{8,264},{12,268},{16,272},{20,276},{24,280},{28,28... | collective-permute-start | bytes 98312 | tf_op jit(solution)/shard_map/ppermute | solution.py:39
  68.3 1.5 %collective-permute-done.8 = bf16[1,8,2048]{2,1,0:T(8,128)(2,1)S(1)} collective-permute-done((bf16[1,8,2048]{2,1,0:T(8,128)(2,1)S(1)}, bf16[1,8,2048]{2,1,0:T(8,128)(2,1)S(1)}, u32[]{:S(2)}, u32[]{:S(2)}) %collective-permute-start.8) | collective-permute-done | bytes 32800 | tf_op jit(solution)/shard_map/ppermute | solution.py:39
  69.9 9.2 %collective-permute-start.9 = (bf16[1,23,2048]{2,1,0:T(8,128)(2,1)S(1)}, bf16[1,23,2048]{2,1,0:T(8,128)(2,1)S(1)}, u32[]{:S(2)}, u32[]{:S(2)}) collective-permute-start(bf16[1,23,2048]{2,1,0:T(8,128)(2,1)S(1)} %pad_maximum_fusion.3), channel_id=1, source_target_pairs={{0,1},{1,0},{2,3},{3,2},{4,5},{5,4},{6,7},{7,6},{8,9},{9,8},{10,11... | collective-permute-start | bytes 282632 | tf_op jit(solution)/shard_map/ppermute | solution.py:49
  79.1 1.0 %fusion.39 = (f32[32,1024]{1,0:T(8,128)S(1)}, f32[32,1024]{1,0:T(8,128)S(1)}, f32[32,1024]{1,0:T(8,128)S(1)}, f32[32,1024]{1,0:T(8,128)S(1)}) fusion(s32[1024]{0:T(1024)S(1)} %iota_add_fusion), kind=kLoop, calls=%fused_computation.70 | loop fusion | flops 786432 | bytes 528384 | tf_op jit(solution)/shard_map/cos | solution.py:72
  80.1 0.1 pad_maximum_fusion.2
  80.2 2.7 %collective-permute-start.10 = (bf16[2,23,2048]{2,1,0:T(8,128)(2,1)S(1)}, bf16[2,23,2048]{2,1,0:T(8,128)(2,1)S(1)}, u32[]{:S(2)}, u32[]{:S(2)}) collective-permute-start(bf16[2,23,2048]{2,1,0:T(8,128)(2,1)S(1)} %pad_maximum_fusion.2), channel_id=1, source_target_pairs={{0,2},{1,3},{2,0},{3,1},{4,6},{5,7},{6,4},{7,5},{8,10},{9,11},{10,... | collective-permute-start | bytes 565256 | tf_op jit(solution)/shard_map/ppermute | solution.py:49
  82.8 4.4 %multiply_subtract_fusion = (f32[32,32,1024]{2,1,0:T(8,128)}, f32[32,32,1024]{2,1,0:T(8,128)}) fusion(f32[32,1024]{1,0:T(8,128)S(1)} %get-tuple-element.23, f32[32,1024]{1,0:T(8,128)S(1)} %get-tuple-element.22, f32[32,1024]{1,0:T(8,128)S(1)} %get-tuple-element.24, f32[32,1024]{1,0:T(8,128)S(1)} %get-tuple-element.21), kind=kLoop, calls=%fused_computation.9 | loop fusion | flops 7340032 | bytes 8912896 | tf_op jit(solution)/shard_map/sub | solution.py:101
  87.3 1.1 %collective-permute-done.10 = bf16[2,23,2048]{2,1,0:T(8,128)(2,1)S(1)} collective-permute-done((bf16[2,23,2048]{2,1,0:T(8,128)(2,1)S(1)}, bf16[2,23,2048]{2,1,0:T(8,128)(2,1)S(1)}, u32[]{:S(2)}, u32[]{:S(2)}) %collective-permute-start.10) | collective-permute-done | bytes 188448 | tf_op jit(solution)/shard_map/ppermute | solution.py:49
  88.3 0.1 pad_maximum_fusion.1
  88.4 0.1 reshape.306
  88.5 3.1 %fusion.44 = f32[92,1024]{1,0:T(8,128)S(1)} fusion(bf16[92,2048]{1,0:T(8,128)(2,1)S(1)} %reshape.306, bf16[2048,1024]{1,0:T(8,128)(2,1)} %bitcast.36), kind=kOutput, calls=%fused_computation.83 | convolution fusion | flops 385875968 | bytes 4947968 | tf_op jit(solution)/shard_map/dot_general | solution.py:150
  91.7 0.3 copy-done
  92.0 0.8 convolution_negate_fusion
  92.8 0.2 fusion.43
  92.9 0.1 copy.9
  93.1 0.2 reduce_sum.61
  93.3 0.2 mul.400
  93.5 0.1 mul.401
  93.6 0.1 reshape_reshape.3
  93.7 0.1 multiply_convert_fusion
  93.9 0.1 reshape.308
  94.0 0.4 bitcast_convert_fusion
  94.4 0.3 multiply_reduce_fusion.3
  94.8 5.8 %fusion.1 = f32[2,4,2,1024]{3,1,2,0:T(4,128)S(1)} fusion(f32[1024,1024]{1,0:T(8,128)} %bitcast.34, f32[1024,1024]{1,0:T(8,128)} %bitcast.33, f32[2,4,2,1024]{3,1,2,0:T(4,128)S(1)} %sub.26, f32[2,4,2,1024]{3,1,2,0:T(4,128)S(1)} %add.168), kind=kOutput, calls=%fused_computation.2 | convolution fusion | flops 205553664 | bytes 8585216 | tf_op jit(solution)/shard_map/dot_general | solution.py:164
  100.5 0.7 copy.7
  (25 shorter events, 0.3 us)
Async XLA Ops:
  2.6 5.7 %collective-permute-start.2 = (bf16[1,8,2048]{2,1,0:T(8,128)(2,1)S(1)}, bf16[1,8,2048]{2,1,0:T(8,128)(2,1)S(1)}, u32[]{:S(2)}, u32[]{:S(2)}) collective-permute-start(bf16[1,8,2048]{2,1,0:T(8,128)(2,1)S(1)} %bitcast.41), channel_id=1, source_target_pairs={{0,4},{4,0},{8,12},{12,8},{16,20},{20,16},{24,28},{28,24},{32,36},... | collective-permute-start | bytes 98312 | tf_op jit(solution)/shard_map/ppermute | solution.py:39
  8.3 6.2 %collective-permute-start.3 = (bf16[1,8,2048]{2,1,0:T(8,128)(2,1)S(1)}, bf16[1,8,2048]{2,1,0:T(8,128)(2,1)S(1)}, u32[]{:S(2)}, u32[]{:S(2)}) collective-permute-start(bf16[1,8,2048]{2,1,0:T(8,128)(2,1)S(1)} %bitcast_add_fusion), channel_id=1, source_target_pairs={{0,8},{4,12},{8,0},{12,4},{16,24},{20,28},{24,16},{28,20},{32,40},... | collective-permute-start | bytes 98312 | tf_op jit(solution)/shard_map/ppermute | solution.py:39
  14.5 15.0 %collective-permute-start.4 = (bf16[1,8,2048]{2,1,0:T(8,128)(2,1)S(1)}, bf16[1,8,2048]{2,1,0:T(8,128)(2,1)S(1)}, u32[]{:S(2)}, u32[]{:S(2)}) collective-permute-start(bf16[1,8,2048]{2,1,0:T(8,128)(2,1)S(1)} %add.149), channel_id=1, source_target_pairs={{0,16},{4,20},{8,24},{12,28},{16,0},{20,4},{24,8},{28,12},{32,48},... | collective-permute-start | bytes 98312 | tf_op jit(solution)/shard_map/ppermute | solution.py:39
  24.1 45.7 %collective-permute-start = (bf16[1,4,2048]{2,1,0:T(4,128)(2,1)S(1)}, bf16[1,4,2048]{2,1,0:T(4,128)(2,1)S(1)}, u32[]{:S(2)}, u32[]{:S(2)}) collective-permute-start(bf16[1,4,2048]{2,1,0:T(4,128)(2,1)S(1)} %slice.48), channel_id=1, source_target_pairs={{0,4},{4,8},{8,12},{12,16},{16,20},{20,24},{24,28},{28,32},{32,36}... | collective-permute-start | bytes 49160 | tf_op jit(solution)/shard_map/ppermute | solution.py:62
  28.2 41.6 %collective-permute-start.1 = (bf16[1,3,2048]{2,1,0:T(4,128)(2,1)S(1)}, bf16[1,3,2048]{2,1,0:T(4,128)(2,1)S(1)}, u32[]{:S(2)}, u32[]{:S(2)}) collective-permute-start(bf16[1,3,2048]{2,1,0:T(4,128)(2,1)S(1)} %slice.49), channel_id=1, source_target_pairs={{4,0},{8,4},{12,8},{16,12},{20,16},{24,20},{28,24},{32,28},{36,32}... | collective-permute-start | bytes 36872 | tf_op jit(solution)/shard_map/ppermute | solution.py:64
  29.5 13.4 %collective-permute-start.5 = (bf16[1,8,2048]{2,1,0:T(8,128)(2,1)S(1)}, bf16[1,8,2048]{2,1,0:T(8,128)(2,1)S(1)}, u32[]{:S(2)}, u32[]{:S(2)}) collective-permute-start(bf16[1,8,2048]{2,1,0:T(8,128)(2,1)S(1)} %add.150), channel_id=1, source_target_pairs={{0,32},{4,36},{8,40},{12,44},{16,48},{20,52},{24,56},{28,60},{32,0... | collective-permute-start | bytes 98312 | tf_op jit(solution)/shard_map/ppermute | solution.py:39
  42.9 10.4 %collective-permute-start.6 = (bf16[1,8,2048]{2,1,0:T(8,128)(2,1)S(1)}, bf16[1,8,2048]{2,1,0:T(8,128)(2,1)S(1)}, u32[]{:S(2)}, u32[]{:S(2)}) collective-permute-start(bf16[1,8,2048]{2,1,0:T(8,128)(2,1)S(1)} %add.151), channel_id=1, source_target_pairs={{0,64},{4,68},{8,72},{12,76},{16,80},{20,84},{24,88},{28,92},{32,9... | collective-permute-start | bytes 98312 | tf_op jit(solution)/shard_map/ppermute | solution.py:39
  53.4 10.2 %collective-permute-start.7 = (bf16[1,8,2048]{2,1,0:T(8,128)(2,1)S(1)}, bf16[1,8,2048]{2,1,0:T(8,128)(2,1)S(1)}, u32[]{:S(2)}, u32[]{:S(2)}) collective-permute-start(bf16[1,8,2048]{2,1,0:T(8,128)(2,1)S(1)} %add.152), channel_id=1, source_target_pairs={{0,128},{4,132},{8,136},{12,140},{16,144},{20,148},{24,152},{28,15... | collective-permute-start | bytes 98312 | tf_op jit(solution)/shard_map/ppermute | solution.py:39
  58.8 11.1 %copy-start.1 = (bf16[1,8,2048]{2,1,0:T(8,128)(2,1)S(1)}, bf16[1,8,2048]{2,1,0:T(8,128)(2,1)}, u32[]{:S(2)}) copy-start(bf16[1,8,2048]{2,1,0:T(8,128)(2,1)} %param.3) | copy-start | bytes 98308
  63.6 6.2 %collective-permute-start.8 = (bf16[1,8,2048]{2,1,0:T(8,128)(2,1)S(1)}, bf16[1,8,2048]{2,1,0:T(8,128)(2,1)S(1)}, u32[]{:S(2)}, u32[]{:S(2)}) collective-permute-start(bf16[1,8,2048]{2,1,0:T(8,128)(2,1)S(1)} %add.153), channel_id=1, source_target_pairs={{0,256},{4,260},{8,264},{12,268},{16,272},{20,276},{24,280},{28,28... | collective-permute-start | bytes 98312 | tf_op jit(solution)/shard_map/ppermute | solution.py:39
  69.9 10.2 %collective-permute-start.9 = (bf16[1,23,2048]{2,1,0:T(8,128)(2,1)S(1)}, bf16[1,23,2048]{2,1,0:T(8,128)(2,1)S(1)}, u32[]{:S(2)}, u32[]{:S(2)}) collective-permute-start(bf16[1,23,2048]{2,1,0:T(8,128)(2,1)S(1)} %pad_maximum_fusion.3), channel_id=1, source_target_pairs={{0,1},{1,0},{2,3},{3,2},{4,5},{5,4},{6,7},{7,6},{8,9},{9,8},{10,11... | collective-permute-start | bytes 282632 | tf_op jit(solution)/shard_map/ppermute | solution.py:49
  80.2 8.2 %collective-permute-start.10 = (bf16[2,23,2048]{2,1,0:T(8,128)(2,1)S(1)}, bf16[2,23,2048]{2,1,0:T(8,128)(2,1)S(1)}, u32[]{:S(2)}, u32[]{:S(2)}) collective-permute-start(bf16[2,23,2048]{2,1,0:T(8,128)(2,1)S(1)} %pad_maximum_fusion.2), channel_id=1, source_target_pairs={{0,2},{1,3},{2,0},{3,1},{4,6},{5,7},{6,4},{7,5},{8,10},{9,11},{10,... | collective-permute-start | bytes 565256 | tf_op jit(solution)/shard_map/ppermute | solution.py:49
  88.5 3.5 %copy-start = (bf16[32,64,1024]{2,1,0:T(8,128)(2,1)S(1)}, bf16[32,64,1024]{2,1,0:T(8,128)(2,1)}, u32[]{:S(2)}) copy-start(bf16[32,64,1024]{2,1,0:T(8,128)(2,1)} %get-tuple-element.14) | copy-start | bytes 12582916

commit v6 on v5

--- a/solution.py
+++ b/solution.py
@@ -88,20 +88,34 @@
     return cos, sin
 
 
-def make_inverse(length, lags):
+def inverse_transform(cross, lags):
+    count, length = cross.shape
     half = length // 2
-    lo_count = 32
-    hi_count = half // lo_count
-    period = length // lo_count
-    shifts = jnp.arange(lags, dtype=jnp.int32) - lags // 2 + length
-    hi = jnp.arange(hi_count, dtype=jnp.int32)
-    lo = jnp.arange(lo_count, dtype=jnp.int32)
-    hi_c, hi_s = cos_sin(hi[:, None] * shifts[None, :] % period, period)
-    lo_c, lo_s = cos_sin(lo[:, None] * shifts[None, :] % length, length)
-    cos = hi_c[:, None, :] * lo_c[None, :, :] - hi_s[:, None, :] * lo_s[None, :, :]
-    sin = hi_s[:, None, :] * lo_c[None, :, :] + hi_c[:, None, :] * lo_s[None, :, :]
-    table = jnp.concatenate([cos.reshape(half, lags), -sin.reshape(half, lags)], axis=0)
-    return table * (1.0 / math.sqrt(half))
+    inner = 32
+    outer = half // inner
+    period = length // inner
+    turns = lags // period
+    shift = length - lags // 2
+    hi = jnp.arange(outer, dtype=jnp.int32)
+    lo = jnp.arange(inner, dtype=jnp.int32)
+    cols = jnp.arange(period, dtype=jnp.int32)
+    laps = jnp.arange(turns, dtype=jnp.int32)
+    e_c, e_s = cos_sin(hi[:, None] * cols[None, :] % period, period)
+    first = jnp.concatenate(
+        [jnp.concatenate([e_c, e_s], axis=1), jnp.concatenate([-e_s, e_c], axis=1)], axis=0
+    )
+    parts = jnp.concatenate(
+        [cross[:, :half].reshape(count, outer, inner), cross[:, half:].reshape(count, outer, inner)],
+        axis=1,
+    )
+    spun = jnp.einsum("rab,am->rbm", parts, first, precision=lax.Precision.HIGHEST)
+    u_re, u_im = spun[..., :period], spun[..., period:]
+    t_c, t_s = cos_sin(lo[:, None] * (cols[None, :] + shift) % length, length)
+    twisted = jnp.concatenate([u_re * t_c - u_im * t_s, u_re * t_s + u_im * t_c], axis=1)
+    f_c, f_s = cos_sin(lo[:, None] * laps[None, :] % inner, inner)
+    second = jnp.concatenate([f_c, -f_s], axis=0)
+    out = jnp.einsum("rbm,bq->rqm", twisted, second, precision=lax.Precision.HIGHEST)
+    return out.reshape(count, lags) * (1.0 / math.sqrt(half))
 
 
 def whiten(spectra, band):
@@ -143,7 +157,6 @@
     block = gather(block, "seg")
     segs = block.shape[0]
     cos, sin = make_forward(length)
-    inverse = make_inverse(length, LAGS)
     flat_rows = block.reshape(segs * block.shape[1], length)
     spectra = jnp.concatenate(
         [
@@ -161,7 +174,7 @@
         total = total + part[:, offset : offset + per].astype(jnp.float32)
     stacked = (total * 0.125).astype(jnp.bfloat16)
     cross = cross_sum(stacked, chosen)
-    flat = jnp.dot(cross.reshape(-1, length), inverse, precision=lax.Precision.HIGH)
+    flat = inverse_transform(cross.reshape(-1, length), LAGS)
     return flat.reshape(steps, nsrc, per, LAGS)
 
 

time: 102 us -> 96.5 us (0.946)
  other arithmetic: 15 us -> 10 us
  matrix products: 9.68 us -> 4.75 us
  waiting for transfers between devices: 6.62 us -> 10.9 us
    ppermute x2, waiting for transfers between devices: 1.06 us -> 6.18 us  [gather(): partner = lax.ppermute(block, axis, [(i, i ^ stride) for i in range(count)])]
    dot_general x1 -> x2, matrix products: 5.75 us -> 0.82 us  [the longest x1 0.42 us: inverse_transform(): jnp.einsum('rab,am->rbm', parts, first, precision=lax.Precision.HIGHEST)]
    sub x1, other arithmetic: 4.42 us -> 0.15 us  [inverse_transform(): u_re * t_c - u_im * t_s]
    ppermute x1, starting transfers between devices: 3.36 us -> 1.92 us  [halo(): lax.ppermute(tail, axis, [(i, i + 1) for i in range(ends)])]
  transfers between devices with their start and end apart: 11 -> 11, of which waited for: 6 -> 7; matrix products, arithmetic and copies ran while one was open for 13% -> 9% of each run, Pallas kernels for 0% -> 0%
where the time goes in v6:
time: 96.5 us; the launch traced here: 95.4 us
  starting transfers between devices  64.3 us (67%)
  waiting for transfers between devices  10.9 us (11%)
  other arithmetic  10 us (10%)
  local copies, waits for them, and re-layouts  4.97 us (5%)
  matrix products  4.75 us (5%)
    ppermute x7, starting transfers between devices, broadcast(): total = total + lax.ppermute(block, axis, perm)  49.1 us
    ppermute x2, starting transfers between devices, gather(): partner = lax.ppermute(block, axis, [(i, i ^ stride) for i in range(count)])  12 us
    ppermute x2, waiting for transfers between devices, gather(): partner = lax.ppermute(block, axis, [(i, i ^ stride) for i in range(count)])  6.18 us
    convert_element_type x1, other arithmetic, make_forward(): cos = cos.reshape(length, half).astype(jnp.bfloat16)  4.89 us
    ppermute x7, waiting for transfers between devices, broadcast(): total = total + lax.ppermute(block, axis, perm)  4.68 us
    dot_general x1, matrix products, shards(): jnp.dot(flat_rows, cos, preferred_element_type=jnp.float32)  3.13 us
  transfers between devices with their start and end apart: 11, of which 7 were waited for; matrix products, arithmetic and copies ran while one was open for 9% of the time, Pallas kernels for 0%

profile of v6, /device:TPU:1, one launch (start us, length us, event | category | flops | bytes accessed | tf_op | source)
XLA Modules:
  0.0 95.4 jit_solution(9935306877182391)
XLA Ops:
  0.0 0.7 broadcast_compare_fusion
  0.7 0.1 and.98
  0.8 0.8 eq.34
  1.7 0.9 select_reduce_fusion
  2.6 4.4 %collective-permute-start.2 = (bf16[1,8,2048]{2,1,0:T(8,128)(2,1)S(1)}, bf16[1,8,2048]{2,1,0:T(8,128)(2,1)S(1)}, u32[]{:S(2)}, u32[]{:S(2)}) collective-permute-start(bf16[1,8,2048]{2,1,0:T(8,128)(2,1)S(1)} %bitcast.40), channel_id=1, source_target_pairs={{0,4},{4,0},{8,12},{12,8},{16,20},{20,16},{24,28},{28,24},{32,36},... | collective-permute-start | bytes 98312 | tf_op jit(solution)/shard_map/ppermute | solution.py:39
  7.0 0.8 slice.56
  7.8 1.9 %collective-permute-start = (bf16[1,4,2048]{2,1,0:T(4,128)(2,1)S(1)}, bf16[1,4,2048]{2,1,0:T(4,128)(2,1)S(1)}, u32[]{:S(2)}, u32[]{:S(2)}) collective-permute-start(bf16[1,4,2048]{2,1,0:T(4,128)(2,1)S(1)} %slice.56), channel_id=1, source_target_pairs={{0,4},{4,8},{8,12},{12,16},{16,20},{20,24},{24,28},{28,32},{32,36}... | collective-permute-start | bytes 49160 | tf_op jit(solution)/shard_map/ppermute | solution.py:62
  9.7 0.8 slice.57
  10.5 1.3 %collective-permute-start.1 = (bf16[1,3,2048]{2,1,0:T(4,128)(2,1)S(1)}, bf16[1,3,2048]{2,1,0:T(4,128)(2,1)S(1)}, u32[]{:S(2)}, u32[]{:S(2)}) collective-permute-start(bf16[1,3,2048]{2,1,0:T(4,128)(2,1)S(1)} %slice.57), channel_id=1, source_target_pairs={{4,0},{8,4},{12,8},{16,12},{20,16},{24,20},{28,24},{32,28},{36,32}... | collective-permute-start | bytes 36872 | tf_op jit(solution)/shard_map/ppermute | solution.py:64
  11.8 7.0 %collective-permute-start.3 = (bf16[1,8,2048]{2,1,0:T(8,128)(2,1)S(1)}, bf16[1,8,2048]{2,1,0:T(8,128)(2,1)S(1)}, u32[]{:S(2)}, u32[]{:S(2)}) collective-permute-start(bf16[1,8,2048]{2,1,0:T(8,128)(2,1)S(1)} %bitcast_add_fusion), channel_id=1, source_target_pairs={{0,8},{4,12},{8,0},{12,4},{16,24},{20,28},{24,16},{28,20},{32,40},... | collective-permute-start | bytes 98312 | tf_op jit(solution)/shard_map/ppermute | solution.py:39
  18.7 1.0 %fusion.17 = (f32[64,1024]{1,0:T(8,128)S(1)}, f32[64,1024]{1,0:T(8,128)S(1)}) fusion(), kind=kLoop, calls=%fused_computation.41 | loop fusion | flops 917504 | bytes 524288 | tf_op jit(solution)/shard_map/sin | solution.py:72
  19.8 0.3 collective-permute-done.3
  20.1 9.4 %collective-permute-start.4 = (bf16[1,8,2048]{2,1,0:T(8,128)(2,1)S(1)}, bf16[1,8,2048]{2,1,0:T(8,128)(2,1)S(1)}, u32[]{:S(2)}, u32[]{:S(2)}) collective-permute-start(bf16[1,8,2048]{2,1,0:T(8,128)(2,1)S(1)} %add.163), channel_id=1, source_target_pairs={{0,16},{4,20},{8,24},{12,28},{16,0},{20,4},{24,8},{28,12},{32,48},... | collective-permute-start | bytes 98312 | tf_op jit(solution)/shard_map/ppermute | solution.py:39
  29.4 0.5 fusion.22
  30.0 0.8 collective-permute-done.4
  30.8 13.4 %collective-permute-start.5 = (bf16[1,8,2048]{2,1,0:T(8,128)(2,1)S(1)}, bf16[1,8,2048]{2,1,0:T(8,128)(2,1)S(1)}, u32[]{:S(2)}, u32[]{:S(2)}) collective-permute-start(bf16[1,8,2048]{2,1,0:T(8,128)(2,1)S(1)} %add.164), channel_id=1, source_target_pairs={{0,32},{4,36},{8,40},{12,44},{16,48},{20,52},{24,56},{28,60},{32,0... | collective-permute-start | bytes 98312 | tf_op jit(solution)/shard_map/ppermute | solution.py:39
  44.2 4.9 %subtract_convert_fusion = (bf16[32,64,1024]{2,1,0:T(8,128)(2,1)}, bf16[32,64,1024]{2,1,0:T(8,128)(2,1)}) fusion(f32[64,1024]{1,0:T(8,128)S(1)} %get-tuple-element.23, f32[32,1024]{1,0:T(8,128)S(1)} %get-tuple-element.25, f32[64,1024]{1,0:T(8,128)S(1)} %get-tuple-element.24, f32[32,1024]{1,0:T(8,128)S(1)} %get-tuple-element.26), kind=kLoop, calls=%fused_computation.1 | loop fusion | flops 16777216 | bytes 9175040 | tf_op jit(solution)/shard_map/convert_element_type | solution.py:86
  49.1 4.8 %collective-permute-start.6 = (bf16[1,8,2048]{2,1,0:T(8,128)(2,1)S(1)}, bf16[1,8,2048]{2,1,0:T(8,128)(2,1)S(1)}, u32[]{:S(2)}, u32[]{:S(2)}) collective-permute-start(bf16[1,8,2048]{2,1,0:T(8,128)(2,1)S(1)} %add.165), channel_id=1, source_target_pairs={{0,64},{4,68},{8,72},{12,76},{16,80},{20,84},{24,88},{28,92},{32,9... | collective-permute-start | bytes 98312 | tf_op jit(solution)/shard_map/ppermute | solution.py:39
  54.0 1.2 %collective-permute-done.6 = bf16[1,8,2048]{2,1,0:T(8,128)(2,1)S(1)} collective-permute-done((bf16[1,8,2048]{2,1,0:T(8,128)(2,1)S(1)}, bf16[1,8,2048]{2,1,0:T(8,128)(2,1)S(1)}, u32[]{:S(2)}, u32[]{:S(2)}) %collective-permute-start.6) | collective-permute-done | bytes 32800 | tf_op jit(solution)/shard_map/ppermute | solution.py:39
  55.3 4.9 %collective-permute-start.7 = (bf16[1,8,2048]{2,1,0:T(8,128)(2,1)S(1)}, bf16[1,8,2048]{2,1,0:T(8,128)(2,1)S(1)}, u32[]{:S(2)}, u32[]{:S(2)}) collective-permute-start(bf16[1,8,2048]{2,1,0:T(8,128)(2,1)S(1)} %add.166), channel_id=1, source_target_pairs={{0,128},{4,132},{8,136},{12,140},{16,144},{20,148},{24,152},{28,15... | collective-permute-start | bytes 98312 | tf_op jit(solution)/shard_map/ppermute | solution.py:39
  60.3 1.2 %collective-permute-done.7 = bf16[1,8,2048]{2,1,0:T(8,128)(2,1)S(1)} collective-permute-done((bf16[1,8,2048]{2,1,0:T(8,128)(2,1)S(1)}, bf16[1,8,2048]{2,1,0:T(8,128)(2,1)S(1)}, u32[]{:S(2)}, u32[]{:S(2)}) %collective-permute-start.7) | collective-permute-done | bytes 32800 | tf_op jit(solution)/shard_map/ppermute | solution.py:39
  61.5 5.2 %collective-permute-start.8 = (bf16[1,8,2048]{2,1,0:T(8,128)(2,1)S(1)}, bf16[1,8,2048]{2,1,0:T(8,128)(2,1)S(1)}, u32[]{:S(2)}, u32[]{:S(2)}) collective-permute-start(bf16[1,8,2048]{2,1,0:T(8,128)(2,1)S(1)} %add.167), channel_id=1, source_target_pairs={{0,256},{4,260},{8,264},{12,268},{16,272},{20,276},{24,280},{28,28... | collective-permute-start | bytes 98312 | tf_op jit(solution)/shard_map/ppermute | solution.py:39
  66.8 1.2 %collective-permute-done.8 = bf16[1,8,2048]{2,1,0:T(8,128)(2,1)S(1)} collective-permute-done((bf16[1,8,2048]{2,1,0:T(8,128)(2,1)S(1)}, bf16[1,8,2048]{2,1,0:T(8,128)(2,1)S(1)}, u32[]{:S(2)}, u32[]{:S(2)}) %collective-permute-start.8) | collective-permute-done | bytes 32800 | tf_op jit(solution)/shard_map/ppermute | solution.py:39
  68.1 9.4 %collective-permute-start.9 = (bf16[1,23,2048]{2,1,0:T(8,128)(2,1)S(1)}, bf16[1,23,2048]{2,1,0:T(8,128)(2,1)S(1)}, u32[]{:S(2)}, u32[]{:S(2)}) collective-permute-start(bf16[1,23,2048]{2,1,0:T(8,128)(2,1)S(1)} %pad_maximum_fusion.3), channel_id=1, source_target_pairs={{0,1},{1,0},{2,3},{3,2},{4,5},{5,4},{6,7},{7,6},{8,9},{9,8},{10,11... | collective-permute-start | bytes 282632 | tf_op jit(solution)/shard_map/ppermute | solution.py:49
  77.5 0.9 collective-permute-done.9
  78.5 2.7 %collective-permute-start.10 = (bf16[2,23,2048]{2,1,0:T(8,128)(2,1)S(1)}, bf16[2,23,2048]{2,1,0:T(8,128)(2,1)S(1)}, u32[]{:S(2)}, u32[]{:S(2)}) collective-permute-start(bf16[2,23,2048]{2,1,0:T(8,128)(2,1)S(1)} %pad_maximum_fusion.2), channel_id=1, source_target_pairs={{0,2},{1,3},{2,0},{3,1},{4,6},{5,7},{6,4},{7,5},{8,10},{9,11},{10,... | collective-permute-start | bytes 565256 | tf_op jit(solution)/shard_map/ppermute | solution.py:49
  81.2 0.1 fusion.50
  81.2 5.3 %collective-permute-done.10 = bf16[2,23,2048]{2,1,0:T(8,128)(2,1)S(1)} collective-permute-done((bf16[2,23,2048]{2,1,0:T(8,128)(2,1)S(1)}, bf16[2,23,2048]{2,1,0:T(8,128)(2,1)S(1)}, u32[]{:S(2)}, u32[]{:S(2)}) %collective-permute-start.10) | collective-permute-done | bytes 188448 | tf_op jit(solution)/shard_map/ppermute | solution.py:49
  86.6 0.1 reshape.252
  86.7 3.1 %fusion.60 = f32[92,1024]{1,0:T(8,128)S(1)} fusion(bf16[92,2048]{1,0:T(8,128)(2,1)S(1)} %reshape.252, bf16[2048,1024]{1,0:T(8,128)(2,1)} %bitcast.35), kind=kOutput, calls=%fused_computation.106 | convolution fusion | flops 385875968 | bytes 4947968 | tf_op jit(solution)/shard_map/dot_general | solution.py:163
  89.9 0.3 copy-done
  90.2 0.8 convolution_negate_fusion
  91.0 0.2 fusion.59
  91.1 0.1 copy.14
  91.3 0.2 reduce_sum.61
  91.5 0.2 mul.441
  91.7 0.1 mul.442
  91.8 0.1 reshape_reshape.3
  92.2 0.4 bitcast_convert_fusion
  92.6 0.3 multiply_reduce_fusion.3
  93.0 0.2 add.183
  93.1 0.1 copy.12
  93.4 0.2 sub.24
  93.5 0.1 copy.13
  93.7 0.4 fusion.7
  94.1 0.1 multiply_subtract_fusion
  94.3 0.4 fusion
  94.7 0.7 mul.478
  (35 shorter events, 1.1 us)
Async XLA Ops:
  2.6 9.1 %collective-permute-start.2 = (bf16[1,8,2048]{2,1,0:T(8,128)(2,1)S(1)}, bf16[1,8,2048]{2,1,0:T(8,128)(2,1)S(1)}, u32[]{:S(2)}, u32[]{:S(2)}) collective-permute-start(bf16[1,8,2048]{2,1,0:T(8,128)(2,1)S(1)} %bitcast.40), channel_id=1, source_target_pairs={{0,4},{4,0},{8,12},{12,8},{16,20},{20,16},{24,28},{28,24},{32,36},... | collective-permute-start | bytes 98312 | tf_op jit(solution)/shard_map/ppermute | solution.py:39
  7.8 60.3 %collective-permute-start = (bf16[1,4,2048]{2,1,0:T(4,128)(2,1)S(1)}, bf16[1,4,2048]{2,1,0:T(4,128)(2,1)S(1)}, u32[]{:S(2)}, u32[]{:S(2)}) collective-permute-start(bf16[1,4,2048]{2,1,0:T(4,128)(2,1)S(1)} %slice.56), channel_id=1, source_target_pairs={{0,4},{4,8},{8,12},{12,16},{16,20},{20,24},{24,28},{28,32},{32,36}... | collective-permute-start | bytes 49160 | tf_op jit(solution)/shard_map/ppermute | solution.py:62
  10.5 57.6 %collective-permute-start.1 = (bf16[1,3,2048]{2,1,0:T(4,128)(2,1)S(1)}, bf16[1,3,2048]{2,1,0:T(4,128)(2,1)S(1)}, u32[]{:S(2)}, u32[]{:S(2)}) collective-permute-start(bf16[1,3,2048]{2,1,0:T(4,128)(2,1)S(1)} %slice.57), channel_id=1, source_target_pairs={{4,0},{8,4},{12,8},{16,12},{20,16},{24,20},{28,24},{32,28},{36,32}... | collective-permute-start | bytes 36872 | tf_op jit(solution)/shard_map/ppermute | solution.py:64
  11.8 8.3 %collective-permute-start.3 = (bf16[1,8,2048]{2,1,0:T(8,128)(2,1)S(1)}, bf16[1,8,2048]{2,1,0:T(8,128)(2,1)S(1)}, u32[]{:S(2)}, u32[]{:S(2)}) collective-permute-start(bf16[1,8,2048]{2,1,0:T(8,128)(2,1)S(1)} %bitcast_add_fusion), channel_id=1, source_target_pairs={{0,8},{4,12},{8,0},{12,4},{16,24},{20,28},{24,16},{28,20},{32,40},... | collective-permute-start | bytes 98312 | tf_op jit(solution)/shard_map/ppermute | solution.py:39
  20.1 10.7 %collective-permute-start.4 = (bf16[1,8,2048]{2,1,0:T(8,128)(2,1)S(1)}, bf16[1,8,2048]{2,1,0:T(8,128)(2,1)S(1)}, u32[]{:S(2)}, u32[]{:S(2)}) collective-permute-start(bf16[1,8,2048]{2,1,0:T(8,128)(2,1)S(1)} %add.163), channel_id=1, source_target_pairs={{0,16},{4,20},{8,24},{12,28},{16,0},{20,4},{24,8},{28,12},{32,48},... | collective-permute-start | bytes 98312 | tf_op jit(solution)/shard_map/ppermute | solution.py:39
  30.8 18.3 %collective-permute-start.5 = (bf16[1,8,2048]{2,1,0:T(8,128)(2,1)S(1)}, bf16[1,8,2048]{2,1,0:T(8,128)(2,1)S(1)}, u32[]{:S(2)}, u32[]{:S(2)}) collective-permute-start(bf16[1,8,2048]{2,1,0:T(8,128)(2,1)S(1)} %add.164), channel_id=1, source_target_pairs={{0,32},{4,36},{8,40},{12,44},{16,48},{20,52},{24,56},{28,60},{32,0... | collective-permute-start | bytes 98312 | tf_op jit(solution)/shard_map/ppermute | solution.py:39
  44.2 23.9 %copy-start.1 = (bf16[1,8,2048]{2,1,0:T(8,128)(2,1)S(1)}, bf16[1,8,2048]{2,1,0:T(8,128)(2,1)}, u32[]{:S(2)}) copy-start(bf16[1,8,2048]{2,1,0:T(8,128)(2,1)} %param.3) | copy-start | bytes 98308
  49.1 6.2 %collective-permute-start.6 = (bf16[1,8,2048]{2,1,0:T(8,128)(2,1)S(1)}, bf16[1,8,2048]{2,1,0:T(8,128)(2,1)S(1)}, u32[]{:S(2)}, u32[]{:S(2)}) collective-permute-start(bf16[1,8,2048]{2,1,0:T(8,128)(2,1)S(1)} %add.165), channel_id=1, source_target_pairs={{0,64},{4,68},{8,72},{12,76},{16,80},{20,84},{24,88},{28,92},{32,9... | collective-permute-start | bytes 98312 | tf_op jit(solution)/shard_map/ppermute | solution.py:39
  55.3 6.2 %collective-permute-start.7 = (bf16[1,8,2048]{2,1,0:T(8,128)(2,1)S(1)}, bf16[1,8,2048]{2,1,0:T(8,128)(2,1)S(1)}, u32[]{:S(2)}, u32[]{:S(2)}) collective-permute-start(bf16[1,8,2048]{2,1,0:T(8,128)(2,1)S(1)} %add.166), channel_id=1, source_target_pairs={{0,128},{4,132},{8,136},{12,140},{16,144},{20,148},{24,152},{28,15... | collective-permute-start | bytes 98312 | tf_op jit(solution)/shard_map/ppermute | solution.py:39
  61.5 6.5 %collective-permute-start.8 = (bf16[1,8,2048]{2,1,0:T(8,128)(2,1)S(1)}, bf16[1,8,2048]{2,1,0:T(8,128)(2,1)S(1)}, u32[]{:S(2)}, u32[]{:S(2)}) collective-permute-start(bf16[1,8,2048]{2,1,0:T(8,128)(2,1)S(1)} %add.167), channel_id=1, source_target_pairs={{0,256},{4,260},{8,264},{12,268},{16,272},{20,276},{24,280},{28,28... | collective-permute-start | bytes 98312 | tf_op jit(solution)/shard_map/ppermute | solution.py:39
  68.1 10.3 %collective-permute-start.9 = (bf16[1,23,2048]{2,1,0:T(8,128)(2,1)S(1)}, bf16[1,23,2048]{2,1,0:T(8,128)(2,1)S(1)}, u32[]{:S(2)}, u32[]{:S(2)}) collective-permute-start(bf16[1,23,2048]{2,1,0:T(8,128)(2,1)S(1)} %pad_maximum_fusion.3), channel_id=1, source_target_pairs={{0,1},{1,0},{2,3},{3,2},{4,5},{5,4},{6,7},{7,6},{8,9},{9,8},{10,11... | collective-permute-start | bytes 282632 | tf_op jit(solution)/shard_map/ppermute | solution.py:49
  78.5 8.0 %collective-permute-start.10 = (bf16[2,23,2048]{2,1,0:T(8,128)(2,1)S(1)}, bf16[2,23,2048]{2,1,0:T(8,128)(2,1)S(1)}, u32[]{:S(2)}, u32[]{:S(2)}) collective-permute-start(bf16[2,23,2048]{2,1,0:T(8,128)(2,1)S(1)} %pad_maximum_fusion.2), channel_id=1, source_target_pairs={{0,2},{1,3},{2,0},{3,1},{4,6},{5,7},{6,4},{7,5},{8,10},{9,11},{10,... | collective-permute-start | bytes 565256 | tf_op jit(solution)/shard_map/ppermute | solution.py:49
  86.7 3.5 %copy-start = (bf16[32,64,1024]{2,1,0:T(8,128)(2,1)S(1)}, bf16[32,64,1024]{2,1,0:T(8,128)(2,1)}, u32[]{:S(2)}) copy-start(bf16[32,64,1024]{2,1,0:T(8,128)(2,1)} %get-tuple-element.14) | copy-start | bytes 12582916

commit v7 on v6

--- a/solution.py
+++ b/solution.py
@@ -12,8 +12,8 @@
 
 
 def radices(count):
-    if count == 128:
-        return [2] * 7
+    if count == 64:
+        return [2] * 6
     out = []
     while count % 4 == 0:
         out.append(4)
@@ -26,10 +26,14 @@
     return out
 
 
-def broadcast(block, axis):
+def broadcast(block, axis, rider):
     count = lax.axis_size(axis)
-    stride = 1
-    for radix in radices(count):
+    width = block.shape[1]
+    both = lax.ppermute(jnp.concatenate([block, rider], axis=1), axis, [(i, i ^ 1) for i in range(count)])
+    block = block + both[:, :width]
+    carried = both[:, width:]
+    stride = 2
+    for radix in radices(count // 2):
         total = block
         for shift in range(1, radix):
             perm = []
@@ -39,7 +43,7 @@
             total = total + lax.ppermute(block, axis, perm)
         block = total
         stride *= radix
-    return block
+    return block, carried
 
 
 def gather(block, axis):
@@ -52,19 +56,23 @@
     return block
 
 
-def halo(cells, axis, dim):
+def edges(cells, axis):
     count = lax.axis_size(axis)
-    ends = count - 1
-    tail = lax.slice_in_dim(cells, cells.shape[dim] - LOW, cells.shape[dim], axis=dim)
-    head = lax.slice_in_dim(cells, 0, HIGH, axis=dim)
-    return jnp.concatenate(
-        [
-            lax.ppermute(tail, axis, [(i, i + 1) for i in range(ends)]),
-            cells,
-            lax.ppermute(head, axis, [(i + 1, i) for i in range(ends)]),
-        ],
-        axis=dim,
-    )
+    odd = lax.axis_index(axis) % 2 == 1
+    rows = cells.shape[1]
+    tail = lax.slice_in_dim(cells, rows - LOW, rows, axis=1)
+    head = jnp.pad(lax.slice_in_dim(cells, 0, HIGH, axis=1), ((0, 0), (0, LOW - HIGH), (0, 0)))
+    rider = jnp.where(odd, head, tail)
+    other = jnp.where(odd, tail, head)
+    perm = [(i, i + 1) if i % 2 else (i, i - 1) for i in range(count)]
+    perm = [(i, j) for i, j in perm if 0 <= j < count]
+    return rider, lax.ppermute(other, axis, perm), odd
+
+
+def halo(cells, near, far, odd):
+    lower = jnp.where(odd, near, far)
+    upper = jnp.where(odd, far, near)[:, :HIGH]
+    return jnp.concatenate([lower, cells, upper], axis=1)
 
 
 def cos_sin(phase, period):
@@ -150,8 +158,9 @@
         jnp.where(keep.reshape(1, steps * nsrc, ch_dev, 1), data[:, None], jnp.zeros_like(data[:, None])),
         axis=2,
     )
-    received = broadcast(picked, "fibre")
-    window = halo(data, "fibre", 1)
+    rider, far, odd = edges(data, "fibre")
+    received, near = broadcast(picked, "fibre", rider)
+    window = halo(data, near, far, odd)
     rows = window.shape[1]
     block = jnp.concatenate([window, received], axis=1)
     block = gather(block, "seg")

time: 96.5 us -> 95.7 us (level)
  starting transfers between devices: 64.3 us -> 62.5 us
  waiting for transfers between devices: 10.9 us -> 12.6 us
  local copies, waits for them, and re-layouts: 4.97 us -> 3.44 us
  other arithmetic: 10 us -> 11 us
    ppermute x7 -> x6, starting transfers between devices: 49.1 us -> 46.3 us  [broadcast(): total = total + lax.ppermute(block, axis, perm)]
    ppermute x2, starting transfers between devices: 3.2 us -> 5.04 us  [the longest x1 4.38 us: broadcast(): lax.ppermute(jnp.concatenate([block, rider], axis=1), axis, [(i, i ^ 1) f...]
    ppermute x7 -> x6, waiting for transfers between devices: 4.68 us -> 6.33 us  [broadcast(): total = total + lax.ppermute(block, axis, perm)]
    slice x2 -> x0, local copies, waits for them, and re-layouts: 1.54 us -> none  [the longest x1 0.77 us: halo(): lax.slice_in_dim(cells, cells.shape[dim] - LOW, cells.shape[dim], axis=dim)]
  transfers between devices with their start and end apart: 11 -> 10, of which waited for: 7 -> 7; matrix products, arithmetic and copies ran while one was open for 9% -> 7% of each run, Pallas kernels for 0% -> 0%
where the time goes in v7:
time: 95.7 us; the launch traced here: 94.8 us
  starting transfers between devices  62.5 us (65%)
  waiting for transfers between devices  12.6 us (13%)
  other arithmetic  11 us (11%)
  matrix products  4.75 us (5%)
  local copies, waits for them, and re-layouts  3.44 us (4%)
    ppermute x6, starting transfers between devices, broadcast(): total = total + lax.ppermute(block, axis, perm)  46.3 us
    ppermute x2, starting transfers between devices, gather(): partner = lax.ppermute(block, axis, [(i, i ^ stride) for i in range(count)])  11.2 us
    ppermute x6, waiting for transfers between devices, broadcast(): total = total + lax.ppermute(block, axis, perm)  6.33 us
    ppermute x2, waiting for transfers between devices, gather(): partner = lax.ppermute(block, axis, [(i, i ^ stride) for i in range(count)])  6.31 us
    convert_element_type x1, other arithmetic, make_forward(): cos = cos.reshape(length, half).astype(jnp.bfloat16)  4.88 us
    ppermute x1, starting transfers between devices, broadcast(): lax.ppermute(jnp.concatenate([block, rider], axis=1), axis, [(i, i ^ 1) f...  4.38 us
    dot_general x1, matrix products, shards(): jnp.dot(flat_rows, cos, preferred_element_type=jnp.float32)  3.13 us
  transfers between devices with their start and end apart: 10, of which 7 were waited for; matrix products, arithmetic and copies ran while one was open for 7% of the time, Pallas kernels for 0%

profile of v7, /device:TPU:1, one launch (start us, length us, event | category | flops | bytes accessed | tf_op | source)
XLA Modules:
  0.0 94.8 jit_solution(5553637965609650625)
XLA Ops:
  0.0 0.7 broadcast_compare_fusion
  0.7 0.1 and.104
  0.8 0.8 eq.40
  1.7 0.9 broadcast_select_fusion.1
  2.6 0.9 select_reduce_fusion
  3.5 4.4 %collective-permute-start = (bf16[1,12,2048]{2,1,0:T(8,128)(2,1)S(1)}, bf16[1,12,2048]{2,1,0:T(8,128)(2,1)S(1)}, u32[]{:S(2)}, u32[]{:S(2)}) collective-permute-start(bf16[1,12,2048]{2,1,0:T(8,128)(2,1)S(1)} %pad_maximum_fusion.4), channel_id=1, source_target_pairs={{0,4},{4,0},{8,12},{12,8},{16,20},{20,16},{24,28},{28,24},{32,36},... | collective-permute-start | bytes 147464 | tf_op jit(solution)/shard_map/ppermute | solution.py:32
  7.9 0.7 collective-permute-start.1
  8.6 1.0 %fusion.17 = (f32[64,1024]{1,0:T(8,128)S(1)}, f32[64,1024]{1,0:T(8,128)S(1)}) fusion(), kind=kLoop, calls=%fused_computation.41 | loop fusion | flops 917504 | bytes 524288 | tf_op jit(solution)/shard_map/sin | solution.py:80
  9.6 0.5 fusion.22
  10.2 6.2 %collective-permute-start.2 = (bf16[1,8,2048]{2,1,0:T(8,128)(2,1)S(1)}, bf16[1,8,2048]{2,1,0:T(8,128)(2,1)S(1)}, u32[]{:S(2)}, u32[]{:S(2)}) collective-permute-start(bf16[1,8,2048]{2,1,0:T(8,128)(2,1)S(1)} %slice_add_fusion), channel_id=1, source_target_pairs={{0,8},{4,12},{8,0},{12,4},{16,24},{20,28},{24,16},{28,20},{32,40},... | collective-permute-start | bytes 98312 | tf_op jit(solution)/shard_map/ppermute | solution.py:43
  16.4 4.9 %subtract_convert_fusion = (bf16[32,64,1024]{2,1,0:T(8,128)(2,1)}, bf16[32,64,1024]{2,1,0:T(8,128)(2,1)}) fusion(f32[64,1024]{1,0:T(8,128)S(1)} %get-tuple-element.27, f32[32,1024]{1,0:T(8,128)S(1)} %get-tuple-element.29, f32[64,1024]{1,0:T(8,128)S(1)} %get-tuple-element.28, f32[32,1024]{1,0:T(8,128)S(1)} %get-tuple-element.30), kind=kLoop, calls=%fused_computation.1 | loop fusion | flops 16777216 | bytes 9175040 | tf_op jit(solution)/shard_map/convert_element_type | solution.py:94
  21.3 8.8 %collective-permute-start.3 = (bf16[1,8,2048]{2,1,0:T(8,128)(2,1)S(1)}, bf16[1,8,2048]{2,1,0:T(8,128)(2,1)S(1)}, u32[]{:S(2)}, u32[]{:S(2)}) collective-permute-start(bf16[1,8,2048]{2,1,0:T(8,128)(2,1)S(1)} %add.168), channel_id=1, source_target_pairs={{0,16},{4,20},{8,24},{12,28},{16,0},{20,4},{24,8},{28,12},{32,48},... | collective-permute-start | bytes 98312 | tf_op jit(solution)/shard_map/ppermute | solution.py:43
  30.1 0.1 fusion.47
  30.2 1.3 %collective-permute-done.3 = bf16[1,8,2048]{2,1,0:T(8,128)(2,1)S(1)} collective-permute-done((bf16[1,8,2048]{2,1,0:T(8,128)(2,1)S(1)}, bf16[1,8,2048]{2,1,0:T(8,128)(2,1)S(1)}, u32[]{:S(2)}, u32[]{:S(2)}) %collective-permute-start.3) | collective-permute-done | bytes 32800 | tf_op jit(solution)/shard_map/ppermute | solution.py:43
  31.5 12.5 %collective-permute-start.4 = (bf16[1,8,2048]{2,1,0:T(8,128)(2,1)S(1)}, bf16[1,8,2048]{2,1,0:T(8,128)(2,1)S(1)}, u32[]{:S(2)}, u32[]{:S(2)}) collective-permute-start(bf16[1,8,2048]{2,1,0:T(8,128)(2,1)S(1)} %add.169), channel_id=1, source_target_pairs={{0,32},{4,36},{8,40},{12,44},{16,48},{20,52},{24,56},{28,60},{32,0... | collective-permute-start | bytes 98312 | tf_op jit(solution)/shard_map/ppermute | solution.py:43
  44.0 0.1 fusion.54
  44.1 1.3 %collective-permute-done.4 = bf16[1,8,2048]{2,1,0:T(8,128)(2,1)S(1)} collective-permute-done((bf16[1,8,2048]{2,1,0:T(8,128)(2,1)S(1)}, bf16[1,8,2048]{2,1,0:T(8,128)(2,1)S(1)}, u32[]{:S(2)}, u32[]{:S(2)}) %collective-permute-start.4) | collective-permute-done | bytes 32800 | tf_op jit(solution)/shard_map/ppermute | solution.py:43
  45.4 7.9 %collective-permute-start.5 = (bf16[1,8,2048]{2,1,0:T(8,128)(2,1)S(1)}, bf16[1,8,2048]{2,1,0:T(8,128)(2,1)S(1)}, u32[]{:S(2)}, u32[]{:S(2)}) collective-permute-start(bf16[1,8,2048]{2,1,0:T(8,128)(2,1)S(1)} %add.170), channel_id=1, source_target_pairs={{0,64},{4,68},{8,72},{12,76},{16,80},{20,84},{24,88},{28,92},{32,9... | collective-permute-start | bytes 98312 | tf_op jit(solution)/shard_map/ppermute | solution.py:43
  53.4 1.2 %collective-permute-done.5 = bf16[1,8,2048]{2,1,0:T(8,128)(2,1)S(1)} collective-permute-done((bf16[1,8,2048]{2,1,0:T(8,128)(2,1)S(1)}, bf16[1,8,2048]{2,1,0:T(8,128)(2,1)S(1)}, u32[]{:S(2)}, u32[]{:S(2)}) %collective-permute-start.5) | collective-permute-done | bytes 32800 | tf_op jit(solution)/shard_map/ppermute | solution.py:43
  54.7 5.8 %collective-permute-start.6 = (bf16[1,8,2048]{2,1,0:T(8,128)(2,1)S(1)}, bf16[1,8,2048]{2,1,0:T(8,128)(2,1)S(1)}, u32[]{:S(2)}, u32[]{:S(2)}) collective-permute-start(bf16[1,8,2048]{2,1,0:T(8,128)(2,1)S(1)} %add.171), channel_id=1, source_target_pairs={{0,128},{4,132},{8,136},{12,140},{16,144},{20,148},{24,152},{28,15... | collective-permute-start | bytes 98312 | tf_op jit(solution)/shard_map/ppermute | solution.py:43
  60.5 1.3 %collective-permute-done.6 = bf16[1,8,2048]{2,1,0:T(8,128)(2,1)S(1)} collective-permute-done((bf16[1,8,2048]{2,1,0:T(8,128)(2,1)S(1)}, bf16[1,8,2048]{2,1,0:T(8,128)(2,1)S(1)}, u32[]{:S(2)}, u32[]{:S(2)}) %collective-permute-start.6) | collective-permute-done | bytes 32800 | tf_op jit(solution)/shard_map/ppermute | solution.py:43
  61.8 5.0 %collective-permute-start.7 = (bf16[1,8,2048]{2,1,0:T(8,128)(2,1)S(1)}, bf16[1,8,2048]{2,1,0:T(8,128)(2,1)S(1)}, u32[]{:S(2)}, u32[]{:S(2)}) collective-permute-start(bf16[1,8,2048]{2,1,0:T(8,128)(2,1)S(1)} %add.172), channel_id=1, source_target_pairs={{0,256},{4,260},{8,264},{12,268},{16,272},{20,276},{24,280},{28,28... | collective-permute-start | bytes 98312 | tf_op jit(solution)/shard_map/ppermute | solution.py:43
  66.8 1.3 %collective-permute-done.7 = bf16[1,8,2048]{2,1,0:T(8,128)(2,1)S(1)} collective-permute-done((bf16[1,8,2048]{2,1,0:T(8,128)(2,1)S(1)}, bf16[1,8,2048]{2,1,0:T(8,128)(2,1)S(1)}, u32[]{:S(2)}, u32[]{:S(2)}) %collective-permute-start.7) | collective-permute-done | bytes 32800 | tf_op jit(solution)/shard_map/ppermute | solution.py:43
  68.2 8.7 %collective-permute-start.8 = (bf16[1,23,2048]{2,1,0:T(8,128)(2,1)S(1)}, bf16[1,23,2048]{2,1,0:T(8,128)(2,1)S(1)}, u32[]{:S(2)}, u32[]{:S(2)}) collective-permute-start(bf16[1,23,2048]{2,1,0:T(8,128)(2,1)S(1)} %pad_maximum_fusion.3), channel_id=1, source_target_pairs={{0,1},{1,0},{2,3},{3,2},{4,5},{5,4},{6,7},{7,6},{8,9},{9,8},{10,11... | collective-permute-start | bytes 282632 | tf_op jit(solution)/shard_map/ppermute | solution.py:53
  76.9 0.9 collective-permute-done.8
  77.9 2.5 %collective-permute-start.9 = (bf16[2,23,2048]{2,1,0:T(8,128)(2,1)S(1)}, bf16[2,23,2048]{2,1,0:T(8,128)(2,1)S(1)}, u32[]{:S(2)}, u32[]{:S(2)}) collective-permute-start(bf16[2,23,2048]{2,1,0:T(8,128)(2,1)S(1)} %pad_maximum_fusion.2), channel_id=1, source_target_pairs={{0,2},{1,3},{2,0},{3,1},{4,6},{5,7},{6,4},{7,5},{8,10},{9,11},{10,... | collective-permute-start | bytes 565256 | tf_op jit(solution)/shard_map/ppermute | solution.py:53
  80.4 0.1 fusion.50
  80.5 5.4 %collective-permute-done.9 = bf16[2,23,2048]{2,1,0:T(8,128)(2,1)S(1)} collective-permute-done((bf16[2,23,2048]{2,1,0:T(8,128)(2,1)S(1)}, bf16[2,23,2048]{2,1,0:T(8,128)(2,1)S(1)}, u32[]{:S(2)}, u32[]{:S(2)}) %collective-permute-start.9) | collective-permute-done | bytes 188448 | tf_op jit(solution)/shard_map/ppermute | solution.py:53
  86.0 0.1 reshape.252
  86.1 3.1 %fusion.60 = f32[92,1024]{1,0:T(8,128)S(1)} fusion(bf16[92,2048]{1,0:T(8,128)(2,1)S(1)} %reshape.252, bf16[2048,1024]{1,0:T(8,128)(2,1)} %bitcast.35), kind=kOutput, calls=%fused_computation.112 | convolution fusion | flops 385875968 | bytes 4947968 | tf_op jit(solution)/shard_map/dot_general | solution.py:172
  89.2 0.3 copy-done
  89.5 0.8 convolution_negate_fusion
  90.3 0.2 fusion.59
  90.5 0.1 copy.14
  90.7 0.2 reduce_sum.61
  90.9 0.2 mul.441
  91.1 0.1 mul.442
  91.2 0.1 reshape_reshape.3
  91.6 0.4 bitcast_convert_fusion
  92.0 0.3 multiply_reduce_fusion.3
  92.4 0.2 add.188
  92.5 0.1 copy.12
  92.8 0.2 sub.24
  92.9 0.1 copy.13
  93.1 0.4 fusion.7
  93.5 0.1 multiply_subtract_fusion
  93.7 0.4 fusion
  94.1 0.7 mul.478
  (35 shorter events, 1.0 us)
Async XLA Ops:
  3.5 6.6 %collective-permute-start = (bf16[1,12,2048]{2,1,0:T(8,128)(2,1)S(1)}, bf16[1,12,2048]{2,1,0:T(8,128)(2,1)S(1)}, u32[]{:S(2)}, u32[]{:S(2)}) collective-permute-start(bf16[1,12,2048]{2,1,0:T(8,128)(2,1)S(1)} %pad_maximum_fusion.4), channel_id=1, source_target_pairs={{0,4},{4,0},{8,12},{12,8},{16,20},{20,16},{24,28},{28,24},{32,36},... | collective-permute-start | bytes 147464 | tf_op jit(solution)/shard_map/ppermute | solution.py:32
  7.9 52.5 %collective-permute-start.1 = (bf16[1,4,2048]{2,1,0:T(4,128)(2,1)S(1)}, bf16[1,4,2048]{2,1,0:T(4,128)(2,1)S(1)}, u32[]{:S(2)}, u32[]{:S(2)}) collective-permute-start(bf16[1,4,2048]{2,1,0:T(4,128)(2,1)S(1)} %get-tuple-element.23), channel_id=1, source_target_pairs={{4,8},{8,4},{12,16},{16,12},{20,24},{24,20},{28,32},{32,28},{36,40... | collective-permute-start | bytes 49160 | tf_op jit(solution)/shard_map/ppermute | solution.py:69
  10.2 11.1 %collective-permute-start.2 = (bf16[1,8,2048]{2,1,0:T(8,128)(2,1)S(1)}, bf16[1,8,2048]{2,1,0:T(8,128)(2,1)S(1)}, u32[]{:S(2)}, u32[]{:S(2)}) collective-permute-start(bf16[1,8,2048]{2,1,0:T(8,128)(2,1)S(1)} %slice_add_fusion), channel_id=1, source_target_pairs={{0,8},{4,12},{8,0},{12,4},{16,24},{20,28},{24,16},{28,20},{32,40},... | collective-permute-start | bytes 98312 | tf_op jit(solution)/shard_map/ppermute | solution.py:43
  16.4 51.8 %copy-start.1 = (bf16[1,8,2048]{2,1,0:T(8,128)(2,1)S(1)}, bf16[1,8,2048]{2,1,0:T(8,128)(2,1)}, u32[]{:S(2)}) copy-start(bf16[1,8,2048]{2,1,0:T(8,128)(2,1)} %param.3) | copy-start | bytes 98308
  21.3 10.2 %collective-permute-start.3 = (bf16[1,8,2048]{2,1,0:T(8,128)(2,1)S(1)}, bf16[1,8,2048]{2,1,0:T(8,128)(2,1)S(1)}, u32[]{:S(2)}, u32[]{:S(2)}) collective-permute-start(bf16[1,8,2048]{2,1,0:T(8,128)(2,1)S(1)} %add.168), channel_id=1, source_target_pairs={{0,16},{4,20},{8,24},{12,28},{16,0},{20,4},{24,8},{28,12},{32,48},... | collective-permute-start | bytes 98312 | tf_op jit(solution)/shard_map/ppermute | solution.py:43
  31.5 13.9 %collective-permute-start.4 = (bf16[1,8,2048]{2,1,0:T(8,128)(2,1)S(1)}, bf16[1,8,2048]{2,1,0:T(8,128)(2,1)S(1)}, u32[]{:S(2)}, u32[]{:S(2)}) collective-permute-start(bf16[1,8,2048]{2,1,0:T(8,128)(2,1)S(1)} %add.169), channel_id=1, source_target_pairs={{0,32},{4,36},{8,40},{12,44},{16,48},{20,52},{24,56},{28,60},{32,0... | collective-permute-start | bytes 98312 | tf_op jit(solution)/shard_map/ppermute | solution.py:43
  45.4 9.2 %collective-permute-start.5 = (bf16[1,8,2048]{2,1,0:T(8,128)(2,1)S(1)}, bf16[1,8,2048]{2,1,0:T(8,128)(2,1)S(1)}, u32[]{:S(2)}, u32[]{:S(2)}) collective-permute-start(bf16[1,8,2048]{2,1,0:T(8,128)(2,1)S(1)} %add.170), channel_id=1, source_target_pairs={{0,64},{4,68},{8,72},{12,76},{16,80},{20,84},{24,88},{28,92},{32,9... | collective-permute-start | bytes 98312 | tf_op jit(solution)/shard_map/ppermute | solution.py:43
  54.7 7.1 %collective-permute-start.6 = (bf16[1,8,2048]{2,1,0:T(8,128)(2,1)S(1)}, bf16[1,8,2048]{2,1,0:T(8,128)(2,1)S(1)}, u32[]{:S(2)}, u32[]{:S(2)}) collective-permute-start(bf16[1,8,2048]{2,1,0:T(8,128)(2,1)S(1)} %add.171), channel_id=1, source_target_pairs={{0,128},{4,132},{8,136},{12,140},{16,144},{20,148},{24,152},{28,15... | collective-permute-start | bytes 98312 | tf_op jit(solution)/shard_map/ppermute | solution.py:43
  61.8 6.3 %collective-permute-start.7 = (bf16[1,8,2048]{2,1,0:T(8,128)(2,1)S(1)}, bf16[1,8,2048]{2,1,0:T(8,128)(2,1)S(1)}, u32[]{:S(2)}, u32[]{:S(2)}) collective-permute-start(bf16[1,8,2048]{2,1,0:T(8,128)(2,1)S(1)} %add.172), channel_id=1, source_target_pairs={{0,256},{4,260},{8,264},{12,268},{16,272},{20,276},{24,280},{28,28... | collective-permute-start | bytes 98312 | tf_op jit(solution)/shard_map/ppermute | solution.py:43
  68.2 9.6 %collective-permute-start.8 = (bf16[1,23,2048]{2,1,0:T(8,128)(2,1)S(1)}, bf16[1,23,2048]{2,1,0:T(8,128)(2,1)S(1)}, u32[]{:S(2)}, u32[]{:S(2)}) collective-permute-start(bf16[1,23,2048]{2,1,0:T(8,128)(2,1)S(1)} %pad_maximum_fusion.3), channel_id=1, source_target_pairs={{0,1},{1,0},{2,3},{3,2},{4,5},{5,4},{6,7},{7,6},{8,9},{9,8},{10,11... | collective-permute-start | bytes 282632 | tf_op jit(solution)/shard_map/ppermute | solution.py:53
  77.9 8.0 %collective-permute-start.9 = (bf16[2,23,2048]{2,1,0:T(8,128)(2,1)S(1)}, bf16[2,23,2048]{2,1,0:T(8,128)(2,1)S(1)}, u32[]{:S(2)}, u32[]{:S(2)}) collective-permute-start(bf16[2,23,2048]{2,1,0:T(8,128)(2,1)S(1)} %pad_maximum_fusion.2), channel_id=1, source_target_pairs={{0,2},{1,3},{2,0},{3,1},{4,6},{5,7},{6,4},{7,5},{8,10},{9,11},{10,... | collective-permute-start | bytes 565256 | tf_op jit(solution)/shard_map/ppermute | solution.py:53
  86.1 3.5 %copy-start = (bf16[32,64,1024]{2,1,0:T(8,128)(2,1)S(1)}, bf16[32,64,1024]{2,1,0:T(8,128)(2,1)}, u32[]{:S(2)}) copy-start(bf16[32,64,1024]{2,1,0:T(8,128)(2,1)} %get-tuple-element.14) | copy-start | bytes 12582916

commit v8 on v7

--- a/solution.py
+++ b/solution.py
@@ -48,11 +48,11 @@
 
 def gather(block, axis):
     count = lax.axis_size(axis)
-    stride = 1
-    while stride < count:
+    stride = count // 2
+    while stride >= 1:
         partner = lax.ppermute(block, axis, [(i, i ^ stride) for i in range(count)])
         block = jnp.concatenate([block, partner], axis=0)
-        stride *= 2
+        stride //= 2
     return block
 
 
@@ -80,7 +80,7 @@
     return jnp.cos(angle), jnp.sin(angle)
 
 
-def make_forward(length):
+def make_forward(length, after):
     half = length // 2
     lo_count = 64
     hi_count = length // lo_count
@@ -89,11 +89,12 @@
     lo = jnp.arange(lo_count, dtype=jnp.int32)
     hi_c, hi_s = cos_sin(hi[:, None] * freqs[None, :] % hi_count, hi_count)
     lo_c, lo_s = cos_sin(lo[:, None] * freqs[None, :] % length, length)
+    hi_c, hi_s, lo_c, lo_s, after = lax.optimization_barrier((hi_c, hi_s, lo_c, lo_s, after))
     cos = hi_c[:, None, :] * lo_c[None, :, :] - hi_s[:, None, :] * lo_s[None, :, :]
     sin = hi_s[:, None, :] * lo_c[None, :, :] + hi_c[:, None, :] * lo_s[None, :, :]
     cos = cos.reshape(length, half).astype(jnp.bfloat16)
     sin = sin.reshape(length, half).astype(jnp.bfloat16)
-    return cos, sin
+    return cos, sin, after
 
 
 def inverse_transform(cross, lags):
@@ -160,12 +161,12 @@
     )
     rider, far, odd = edges(data, "fibre")
     received, near = broadcast(picked, "fibre", rider)
+    cos, sin, received = make_forward(length, received)
     window = halo(data, near, far, odd)
     rows = window.shape[1]
     block = jnp.concatenate([window, received], axis=1)
     block = gather(block, "seg")
     segs = block.shape[0]
-    cos, sin = make_forward(length)
     flat_rows = block.reshape(segs * block.shape[1], length)
     spectra = jnp.concatenate(
         [

time: 95.7 us -> 97.9 us (1.023)
  starting transfers between devices: 62.5 us -> 65.8 us
  waiting for transfers between devices: 12.6 us -> 10.1 us
  other arithmetic: 11 us -> 12.4 us
    ppermute x2, waiting for transfers between devices: 6.31 us -> 3.04 us  [gather(): partner = lax.ppermute(block, axis, [(i, i ^ stride) for i in range(count)])]
    ppermute x6, starting transfers between devices: 46.3 us -> 48 us  [broadcast(): total = total + lax.ppermute(block, axis, perm)]
    ppermute x2, starting transfers between devices: 11.2 us -> 12.7 us  [gather(): partner = lax.ppermute(block, axis, [(i, i ^ stride) for i in range(count)])]
  transfers between devices with their start and end apart: 10 -> 10, of which waited for: 7 -> 8; matrix products, arithmetic and copies ran while one was open for 7% -> 7% of each run, Pallas kernels for 0% -> 0%
where the time goes in v8:
time: 97.9 us; the launch traced here: 96.9 us
  starting transfers between devices  65.8 us (67%)
  other arithmetic  12.4 us (13%)
  waiting for transfers between devices  10.1 us (10%)
  matrix products  4.75 us (5%)
  local copies, waits for them, and re-layouts  3.44 us (4%)
    ppermute x6, starting transfers between devices, broadcast(): total = total + lax.ppermute(block, axis, perm)  48 us
    ppermute x2, starting transfers between devices, gather(): partner = lax.ppermute(block, axis, [(i, i ^ stride) for i in range(count)])  12.7 us
    ppermute x6, waiting for transfers between devices, broadcast(): total = total + lax.ppermute(block, axis, perm)  6.15 us
    convert_element_type x1, other arithmetic, make_forward(): cos = cos.reshape(length, half).astype(jnp.bfloat16)  4.79 us
    ppermute x1, starting transfers between devices, broadcast(): lax.ppermute(jnp.concatenate([block, rider], axis=1), axis, [(i, i ^ 1) f...  4.38 us
    dot_general x1, matrix products, shards(): jnp.dot(flat_rows, cos, preferred_element_type=jnp.float32)  3.13 us
    ppermute x2, waiting for transfers between devices, gather(): partner = lax.ppermute(block, axis, [(i, i ^ stride) for i in range(count)])  3.04 us
  transfers between devices with their start and end apart: 10, of which 8 were waited for; matrix products, arithmetic and copies ran while one was open for 7% of the time, Pallas kernels for 0%

profile of v8, /device:TPU:1, one launch (start us, length us, event | category | flops | bytes accessed | tf_op | source)
XLA Modules:
  0.0 96.9 jit_solution(3106283010587099509)
XLA Ops:
  0.0 0.7 broadcast_compare_fusion
  0.7 0.1 and.80
  0.8 0.8 eq.40
  1.7 0.9 broadcast_select_fusion.1
  2.6 0.9 select_reduce_fusion
  3.5 4.4 %collective-permute-start = (bf16[1,12,2048]{2,1,0:T(8,128)(2,1)S(1)}, bf16[1,12,2048]{2,1,0:T(8,128)(2,1)S(1)}, u32[]{:S(2)}, u32[]{:S(2)}) collective-permute-start(bf16[1,12,2048]{2,1,0:T(8,128)(2,1)S(1)} %pad_maximum_fusion.4), channel_id=1, source_target_pairs={{0,4},{4,0},{8,12},{12,8},{16,20},{20,16},{24,28},{28,24},{32,36},... | collective-permute-start | bytes 147464 | tf_op jit(solution)/shard_map/ppermute | solution.py:32
  7.9 0.7 collective-permute-start.1
  8.7 0.9 collective-permute-done
  9.6 5.3 %collective-permute-start.2 = (bf16[1,8,2048]{2,1,0:T(8,128)(2,1)S(1)}, bf16[1,8,2048]{2,1,0:T(8,128)(2,1)S(1)}, u32[]{:S(2)}, u32[]{:S(2)}) collective-permute-start(bf16[1,8,2048]{2,1,0:T(8,128)(2,1)S(1)} %slice_add_fusion), channel_id=1, source_target_pairs={{0,8},{4,12},{8,0},{12,4},{16,24},{20,28},{24,16},{28,20},{32,40},... | collective-permute-start | bytes 98312 | tf_op jit(solution)/shard_map/ppermute | solution.py:43
  14.9 1.0 %fusion.17 = (f32[64,1024]{1,0:T(8,128)S(1)}, f32[64,1024]{1,0:T(8,128)S(1)}) fusion(), kind=kLoop, calls=%fused_computation.41 | loop fusion | flops 917504 | bytes 524288 | tf_op jit(solution)/shard_map/sin | solution.py:80
  15.9 0.3 collective-permute-done.2
  16.3 8.8 %collective-permute-start.3 = (bf16[1,8,2048]{2,1,0:T(8,128)(2,1)S(1)}, bf16[1,8,2048]{2,1,0:T(8,128)(2,1)S(1)}, u32[]{:S(2)}, u32[]{:S(2)}) collective-permute-start(bf16[1,8,2048]{2,1,0:T(8,128)(2,1)S(1)} %add.156), channel_id=1, source_target_pairs={{0,16},{4,20},{8,24},{12,28},{16,0},{20,4},{24,8},{28,12},{32,48},... | collective-permute-start | bytes 98312 | tf_op jit(solution)/shard_map/ppermute | solution.py:43
  25.0 0.5 fusion.22
  25.6 0.8 collective-permute-done.3
  26.3 12.7 %collective-permute-start.4 = (bf16[1,8,2048]{2,1,0:T(8,128)(2,1)S(1)}, bf16[1,8,2048]{2,1,0:T(8,128)(2,1)S(1)}, u32[]{:S(2)}, u32[]{:S(2)}) collective-permute-start(bf16[1,8,2048]{2,1,0:T(8,128)(2,1)S(1)} %add.157), channel_id=1, source_target_pairs={{0,32},{4,36},{8,40},{12,44},{16,48},{20,52},{24,56},{28,60},{32,0... | collective-permute-start | bytes 98312 | tf_op jit(solution)/shard_map/ppermute | solution.py:43
  39.1 1.4 %collective-permute-done.4 = bf16[1,8,2048]{2,1,0:T(8,128)(2,1)S(1)} collective-permute-done((bf16[1,8,2048]{2,1,0:T(8,128)(2,1)S(1)}, bf16[1,8,2048]{2,1,0:T(8,128)(2,1)S(1)}, u32[]{:S(2)}, u32[]{:S(2)}) %collective-permute-start.4) | collective-permute-done | bytes 32800 | tf_op jit(solution)/shard_map/ppermute | solution.py:43
  40.4 10.5 %collective-permute-start.5 = (bf16[1,8,2048]{2,1,0:T(8,128)(2,1)S(1)}, bf16[1,8,2048]{2,1,0:T(8,128)(2,1)S(1)}, u32[]{:S(2)}, u32[]{:S(2)}) collective-permute-start(bf16[1,8,2048]{2,1,0:T(8,128)(2,1)S(1)} %add.158), channel_id=1, source_target_pairs={{0,64},{4,68},{8,72},{12,76},{16,80},{20,84},{24,88},{28,92},{32,9... | collective-permute-start | bytes 98312 | tf_op jit(solution)/shard_map/ppermute | solution.py:43
  51.0 1.2 %collective-permute-done.5 = bf16[1,8,2048]{2,1,0:T(8,128)(2,1)S(1)} collective-permute-done((bf16[1,8,2048]{2,1,0:T(8,128)(2,1)S(1)}, bf16[1,8,2048]{2,1,0:T(8,128)(2,1)S(1)}, u32[]{:S(2)}, u32[]{:S(2)}) %collective-permute-start.5) | collective-permute-done | bytes 32800 | tf_op jit(solution)/shard_map/ppermute | solution.py:43
  52.3 5.5 %collective-permute-start.6 = (bf16[1,8,2048]{2,1,0:T(8,128)(2,1)S(1)}, bf16[1,8,2048]{2,1,0:T(8,128)(2,1)S(1)}, u32[]{:S(2)}, u32[]{:S(2)}) collective-permute-start(bf16[1,8,2048]{2,1,0:T(8,128)(2,1)S(1)} %add.159), channel_id=1, source_target_pairs={{0,128},{4,132},{8,136},{12,140},{16,144},{20,148},{24,152},{28,15... | collective-permute-start | bytes 98312 | tf_op jit(solution)/shard_map/ppermute | solution.py:43
  57.8 1.3 %collective-permute-done.6 = bf16[1,8,2048]{2,1,0:T(8,128)(2,1)S(1)} collective-permute-done((bf16[1,8,2048]{2,1,0:T(8,128)(2,1)S(1)}, bf16[1,8,2048]{2,1,0:T(8,128)(2,1)S(1)}, u32[]{:S(2)}, u32[]{:S(2)}) %collective-permute-start.6) | collective-permute-done | bytes 32800 | tf_op jit(solution)/shard_map/ppermute | solution.py:43
  59.1 5.3 %collective-permute-start.7 = (bf16[1,8,2048]{2,1,0:T(8,128)(2,1)S(1)}, bf16[1,8,2048]{2,1,0:T(8,128)(2,1)S(1)}, u32[]{:S(2)}, u32[]{:S(2)}) collective-permute-start(bf16[1,8,2048]{2,1,0:T(8,128)(2,1)S(1)} %add.160), channel_id=1, source_target_pairs={{0,256},{4,260},{8,264},{12,268},{16,272},{20,276},{24,280},{28,28... | collective-permute-start | bytes 98312 | tf_op jit(solution)/shard_map/ppermute | solution.py:43
  64.4 1.3 %collective-permute-done.7 = bf16[1,8,2048]{2,1,0:T(8,128)(2,1)S(1)} collective-permute-done((bf16[1,8,2048]{2,1,0:T(8,128)(2,1)S(1)}, bf16[1,8,2048]{2,1,0:T(8,128)(2,1)S(1)}, u32[]{:S(2)}, u32[]{:S(2)}) %collective-permute-start.7) | collective-permute-done | bytes 32800 | tf_op jit(solution)/shard_map/ppermute | solution.py:43
  65.7 0.8 pad_maximum_fusion.3
  66.5 2.5 %collective-permute-start.8 = (bf16[1,23,2048]{2,1,0:T(8,128)(2,1)S(1)}, bf16[1,23,2048]{2,1,0:T(8,128)(2,1)S(1)}, u32[]{:S(2)}, u32[]{:S(2)}) collective-permute-start(bf16[1,23,2048]{2,1,0:T(8,128)(2,1)S(1)} %pad_maximum_fusion.3), channel_id=1, source_target_pairs={{0,2},{1,3},{2,0},{3,1},{4,6},{5,7},{6,4},{7,5},{8,10},{9,11},{10,... | collective-permute-start | bytes 282632 | tf_op jit(solution)/shard_map/ppermute | solution.py:53
  69.2 3.0 %collective-permute-done.8 = bf16[1,23,2048]{2,1,0:T(8,128)(2,1)S(1)} collective-permute-done((bf16[1,23,2048]{2,1,0:T(8,128)(2,1)S(1)}, bf16[1,23,2048]{2,1,0:T(8,128)(2,1)S(1)}, u32[]{:S(2)}, u32[]{:S(2)}) %collective-permute-start.8) | collective-permute-done | bytes 94240 | tf_op jit(solution)/shard_map/ppermute | solution.py:53
  72.2 0.8 pad_maximum_fusion.2
  73.0 10.1 %collective-permute-start.9 = (bf16[2,23,2048]{2,1,0:T(8,128)(2,1)S(1)}, bf16[2,23,2048]{2,1,0:T(8,128)(2,1)S(1)}, u32[]{:S(2)}, u32[]{:S(2)}) collective-permute-start(bf16[2,23,2048]{2,1,0:T(8,128)(2,1)S(1)} %pad_maximum_fusion.2), channel_id=1, source_target_pairs={{0,1},{1,0},{2,3},{3,2},{4,5},{5,4},{6,7},{7,6},{8,9},{9,8},{10,11... | collective-permute-start | bytes 565256 | tf_op jit(solution)/shard_map/ppermute | solution.py:53
  83.2 4.8 %subtract_convert_fusion = (bf16[32,64,1024]{2,1,0:T(8,128)(2,1)}, bf16[32,64,1024]{2,1,0:T(8,128)(2,1)}) fusion(f32[64,1024]{1,0:T(8,128)S(1)} %get-tuple-element.14, f32[32,1024]{1,0:T(8,128)S(1)} %get-tuple-element.13, f32[64,1024]{1,0:T(8,128)S(1)} %get-tuple-element.12, f32[32,1024]{1,0:T(8,128)S(1)} %get-tuple-element.11), kind=kLoop, calls=%fused_computation.1 | loop fusion | flops 16777216 | bytes 9175040 | tf_op jit(solution)/shard_map/convert_element_type | solution.py:95
  88.0 0.1 reshape.186
  88.2 3.1 %fusion.60 = f32[92,1024]{1,0:T(8,128)S(1)} fusion(bf16[92,2048]{1,0:T(8,128)(2,1)S(1)} %reshape.186, bf16[2048,1024]{1,0:T(8,128)(2,1)} %bitcast.35), kind=kOutput, calls=%fused_computation.112 | convolution fusion | flops 385875968 | bytes 4947968 | tf_op jit(solution)/shard_map/dot_general | solution.py:173
  91.3 0.3 copy-done
  91.6 0.8 convolution_negate_fusion
  92.4 0.2 fusion.59
  92.6 0.1 copy.14
  92.8 0.2 reduce_sum.61
  93.0 0.2 mul.405
  93.2 0.1 mul.406
  93.3 0.1 reshape_reshape.3
  93.6 0.4 bitcast_convert_fusion
  94.1 0.3 multiply_reduce_fusion.3
  94.4 0.2 add.174
  94.6 0.1 copy.12
  94.8 0.2 sub.24
  95.0 0.1 copy.13
  95.1 0.4 fusion.7
  95.6 0.1 multiply_subtract_fusion
  95.7 0.4 fusion
  96.1 0.7 mul.442
  (35 shorter events, 1.1 us)
Async XLA Ops:
  3.5 6.0 %collective-permute-start = (bf16[1,12,2048]{2,1,0:T(8,128)(2,1)S(1)}, bf16[1,12,2048]{2,1,0:T(8,128)(2,1)S(1)}, u32[]{:S(2)}, u32[]{:S(2)}) collective-permute-start(bf16[1,12,2048]{2,1,0:T(8,128)(2,1)S(1)} %pad_maximum_fusion.4), channel_id=1, source_target_pairs={{0,4},{4,0},{8,12},{12,8},{16,20},{20,16},{24,28},{28,24},{32,36},... | collective-permute-start | bytes 147464 | tf_op jit(solution)/shard_map/ppermute | solution.py:32
  7.9 49.9 %collective-permute-start.1 = (bf16[1,4,2048]{2,1,0:T(4,128)(2,1)S(1)}, bf16[1,4,2048]{2,1,0:T(4,128)(2,1)S(1)}, u32[]{:S(2)}, u32[]{:S(2)}) collective-permute-start(bf16[1,4,2048]{2,1,0:T(4,128)(2,1)S(1)} %get-tuple-element.33), channel_id=1, source_target_pairs={{4,8},{8,4},{12,16},{16,12},{20,24},{24,20},{28,32},{32,28},{36,40... | collective-permute-start | bytes 49160 | tf_op jit(solution)/shard_map/ppermute | solution.py:69
  9.6 6.7 %collective-permute-start.2 = (bf16[1,8,2048]{2,1,0:T(8,128)(2,1)S(1)}, bf16[1,8,2048]{2,1,0:T(8,128)(2,1)S(1)}, u32[]{:S(2)}, u32[]{:S(2)}) collective-permute-start(bf16[1,8,2048]{2,1,0:T(8,128)(2,1)S(1)} %slice_add_fusion), channel_id=1, source_target_pairs={{0,8},{4,12},{8,0},{12,4},{16,24},{20,28},{24,16},{28,20},{32,40},... | collective-permute-start | bytes 98312 | tf_op jit(solution)/shard_map/ppermute | solution.py:43
  16.3 10.0 %collective-permute-start.3 = (bf16[1,8,2048]{2,1,0:T(8,128)(2,1)S(1)}, bf16[1,8,2048]{2,1,0:T(8,128)(2,1)S(1)}, u32[]{:S(2)}, u32[]{:S(2)}) collective-permute-start(bf16[1,8,2048]{2,1,0:T(8,128)(2,1)S(1)} %add.156), channel_id=1, source_target_pairs={{0,16},{4,20},{8,24},{12,28},{16,0},{20,4},{24,8},{28,12},{32,48},... | collective-permute-start | bytes 98312 | tf_op jit(solution)/shard_map/ppermute | solution.py:43
  26.3 14.1 %collective-permute-start.4 = (bf16[1,8,2048]{2,1,0:T(8,128)(2,1)S(1)}, bf16[1,8,2048]{2,1,0:T(8,128)(2,1)S(1)}, u32[]{:S(2)}, u32[]{:S(2)}) collective-permute-start(bf16[1,8,2048]{2,1,0:T(8,128)(2,1)S(1)} %add.157), channel_id=1, source_target_pairs={{0,32},{4,36},{8,40},{12,44},{16,48},{20,52},{24,56},{28,60},{32,0... | collective-permute-start | bytes 98312 | tf_op jit(solution)/shard_map/ppermute | solution.py:43
  40.4 11.8 %collective-permute-start.5 = (bf16[1,8,2048]{2,1,0:T(8,128)(2,1)S(1)}, bf16[1,8,2048]{2,1,0:T(8,128)(2,1)S(1)}, u32[]{:S(2)}, u32[]{:S(2)}) collective-permute-start(bf16[1,8,2048]{2,1,0:T(8,128)(2,1)S(1)} %add.158), channel_id=1, source_target_pairs={{0,64},{4,68},{8,72},{12,76},{16,80},{20,84},{24,88},{28,92},{32,9... | collective-permute-start | bytes 98312 | tf_op jit(solution)/shard_map/ppermute | solution.py:43
  52.3 6.8 %collective-permute-start.6 = (bf16[1,8,2048]{2,1,0:T(8,128)(2,1)S(1)}, bf16[1,8,2048]{2,1,0:T(8,128)(2,1)S(1)}, u32[]{:S(2)}, u32[]{:S(2)}) collective-permute-start(bf16[1,8,2048]{2,1,0:T(8,128)(2,1)S(1)} %add.159), channel_id=1, source_target_pairs={{0,128},{4,132},{8,136},{12,140},{16,144},{20,148},{24,152},{28,15... | collective-permute-start | bytes 98312 | tf_op jit(solution)/shard_map/ppermute | solution.py:43
  59.1 6.6 %collective-permute-start.7 = (bf16[1,8,2048]{2,1,0:T(8,128)(2,1)S(1)}, bf16[1,8,2048]{2,1,0:T(8,128)(2,1)S(1)}, u32[]{:S(2)}, u32[]{:S(2)}) collective-permute-start(bf16[1,8,2048]{2,1,0:T(8,128)(2,1)S(1)} %add.160), channel_id=1, source_target_pairs={{0,256},{4,260},{8,264},{12,268},{16,272},{20,276},{24,280},{28,28... | collective-permute-start | bytes 98312 | tf_op jit(solution)/shard_map/ppermute | solution.py:43
  66.5 5.7 %collective-permute-start.8 = (bf16[1,23,2048]{2,1,0:T(8,128)(2,1)S(1)}, bf16[1,23,2048]{2,1,0:T(8,128)(2,1)S(1)}, u32[]{:S(2)}, u32[]{:S(2)}) collective-permute-start(bf16[1,23,2048]{2,1,0:T(8,128)(2,1)S(1)} %pad_maximum_fusion.3), channel_id=1, source_target_pairs={{0,2},{1,3},{2,0},{3,1},{4,6},{5,7},{6,4},{7,5},{8,10},{9,11},{10,... | collective-permute-start | bytes 282632 | tf_op jit(solution)/shard_map/ppermute | solution.py:53
  73.0 15.0 %copy-start.1 = (bf16[1,8,2048]{2,1,0:T(8,128)(2,1)S(1)}, bf16[1,8,2048]{2,1,0:T(8,128)(2,1)}, u32[]{:S(2)}) copy-start(bf16[1,8,2048]{2,1,0:T(8,128)(2,1)} %param.3) | copy-start | bytes 98308
  73.0 14.9 %collective-permute-start.9 = (bf16[2,23,2048]{2,1,0:T(8,128)(2,1)S(1)}, bf16[2,23,2048]{2,1,0:T(8,128)(2,1)S(1)}, u32[]{:S(2)}, u32[]{:S(2)}) collective-permute-start(bf16[2,23,2048]{2,1,0:T(8,128)(2,1)S(1)} %pad_maximum_fusion.2), channel_id=1, source_target_pairs={{0,1},{1,0},{2,3},{3,2},{4,5},{5,4},{6,7},{7,6},{8,9},{9,8},{10,11... | collective-permute-start | bytes 565256 | tf_op jit(solution)/shard_map/ppermute | solution.py:53
  88.2 3.5 %copy-start = (bf16[32,64,1024]{2,1,0:T(8,128)(2,1)S(1)}, bf16[32,64,1024]{2,1,0:T(8,128)(2,1)}, u32[]{:S(2)}) copy-start(bf16[32,64,1024]{2,1,0:T(8,128)(2,1)} %get-tuple-element.24) | copy-start | bytes 12582916

commit v9 on v7

--- a/solution.py
+++ b/solution.py
@@ -48,11 +48,11 @@
 
 def gather(block, axis):
     count = lax.axis_size(axis)
-    stride = 1
-    while stride < count:
+    stride = count // 2
+    while stride >= 1:
         partner = lax.ppermute(block, axis, [(i, i ^ stride) for i in range(count)])
         block = jnp.concatenate([block, partner], axis=0)
-        stride *= 2
+        stride //= 2
     return block
 
 

time: 95.7 us -> 93.9 us (0.981)
  waiting for transfers between devices: 12.6 us -> 10.8 us
    ppermute x2, waiting for transfers between devices: 6.31 us -> 4.44 us  [gather(): partner = lax.ppermute(block, axis, [(i, i ^ stride) for i in range(count)])]
where the time goes in v9:
time: 93.9 us; the launch traced here: 93.4 us
  starting transfers between devices  63 us (67%)
  other arithmetic  11 us (12%)
  waiting for transfers between devices  10.8 us (12%)
  matrix products  4.75 us (5%)
  local copies, waits for them, and re-layouts  3.43 us (4%)
    ppermute x6, starting transfers between devices, broadcast(): total = total + lax.ppermute(block, axis, perm)  46.3 us
    ppermute x2, starting transfers between devices, gather(): partner = lax.ppermute(block, axis, [(i, i ^ stride) for i in range(count)])  11.7 us
    ppermute x6, waiting for transfers between devices, broadcast(): total = total + lax.ppermute(block, axis, perm)  6.33 us
    convert_element_type x1, other arithmetic, make_forward(): cos = cos.reshape(length, half).astype(jnp.bfloat16)  4.88 us
    ppermute x2, waiting for transfers between devices, gather(): partner = lax.ppermute(block, axis, [(i, i ^ stride) for i in range(count)])  4.44 us
    ppermute x1, starting transfers between devices, broadcast(): lax.ppermute(jnp.concatenate([block, rider], axis=1), axis, [(i, i ^ 1) f...  4.38 us
    dot_general x1, matrix products, shards(): jnp.dot(flat_rows, cos, preferred_element_type=jnp.float32)  3.13 us
  transfers between devices with their start and end apart: 10, of which 7 were waited for; matrix products, arithmetic and copies ran while one was open for 7% of the time, Pallas kernels for 0%

profile of v9, /device:TPU:1, one launch (start us, length us, event | category | flops | bytes accessed | tf_op | source)
XLA Modules:
  0.0 93.4 jit_solution(15955589475513990594)
XLA Ops:
  0.0 0.7 broadcast_compare_fusion
  0.7 0.1 and.104
  0.8 0.8 eq.40
  1.7 0.9 broadcast_select_fusion.1
  2.6 0.9 %select_reduce_fusion = bf16[8,2048]{1,0:T(8,128)(2,1)S(1)} fusion(pred[8,8]{1,0:T(8,128)(4,1)S(1)} %fusion.56, bf16[8,2048]{1,0:T(8,128)(2,1)} %bitcast.39), kind=kLoop, calls=%fused_computation.29 | loop fusion | flops 245760 | bytes 65600 | tf_op jit(solution)/shard_map/reduce_sum | solution.py:157
  3.5 4.4 %collective-permute-start = (bf16[1,12,2048]{2,1,0:T(8,128)(2,1)S(1)}, bf16[1,12,2048]{2,1,0:T(8,128)(2,1)S(1)}, u32[]{:S(2)}, u32[]{:S(2)}) collective-permute-start(bf16[1,12,2048]{2,1,0:T(8,128)(2,1)S(1)} %pad_maximum_fusion.4), channel_id=1, source_target_pairs={{0,4},{4,0},{8,12},{12,8},{16,20},{20,16},{24,28},{28,24},{32,36},... | collective-permute-start | bytes 147464 | tf_op jit(solution)/shard_map/ppermute | solution.py:32
  7.9 0.7 collective-permute-start.1
  8.6 1.0 %fusion.17 = (f32[64,1024]{1,0:T(8,128)S(1)}, f32[64,1024]{1,0:T(8,128)S(1)}) fusion(), kind=kLoop, calls=%fused_computation.41 | loop fusion | flops 917504 | bytes 524288 | tf_op jit(solution)/shard_map/sin | solution.py:80
  9.6 0.5 fusion.22
  10.2 6.2 %collective-permute-start.2 = (bf16[1,8,2048]{2,1,0:T(8,128)(2,1)S(1)}, bf16[1,8,2048]{2,1,0:T(8,128)(2,1)S(1)}, u32[]{:S(2)}, u32[]{:S(2)}) collective-permute-start(bf16[1,8,2048]{2,1,0:T(8,128)(2,1)S(1)} %slice_add_fusion), channel_id=1, source_target_pairs={{0,8},{4,12},{8,0},{12,4},{16,24},{20,28},{24,16},{28,20},{32,40},... | collective-permute-start | bytes 98312 | tf_op jit(solution)/shard_map/ppermute | solution.py:43
  16.4 4.9 %subtract_convert_fusion = (bf16[32,64,1024]{2,1,0:T(8,128)(2,1)}, bf16[32,64,1024]{2,1,0:T(8,128)(2,1)}) fusion(f32[64,1024]{1,0:T(8,128)S(1)} %get-tuple-element.27, f32[32,1024]{1,0:T(8,128)S(1)} %get-tuple-element.29, f32[64,1024]{1,0:T(8,128)S(1)} %get-tuple-element.28, f32[32,1024]{1,0:T(8,128)S(1)} %get-tuple-element.30), kind=kLoop, calls=%fused_computation.1 | loop fusion | flops 16777216 | bytes 9175040 | tf_op jit(solution)/shard_map/convert_element_type | solution.py:94
  21.3 8.8 %collective-permute-start.3 = (bf16[1,8,2048]{2,1,0:T(8,128)(2,1)S(1)}, bf16[1,8,2048]{2,1,0:T(8,128)(2,1)S(1)}, u32[]{:S(2)}, u32[]{:S(2)}) collective-permute-start(bf16[1,8,2048]{2,1,0:T(8,128)(2,1)S(1)} %add.168), channel_id=1, source_target_pairs={{0,16},{4,20},{8,24},{12,28},{16,0},{20,4},{24,8},{28,12},{32,48},... | collective-permute-start | bytes 98312 | tf_op jit(solution)/shard_map/ppermute | solution.py:43
  30.1 0.1 fusion.47
  30.2 1.3 %collective-permute-done.3 = bf16[1,8,2048]{2,1,0:T(8,128)(2,1)S(1)} collective-permute-done((bf16[1,8,2048]{2,1,0:T(8,128)(2,1)S(1)}, bf16[1,8,2048]{2,1,0:T(8,128)(2,1)S(1)}, u32[]{:S(2)}, u32[]{:S(2)}) %collective-permute-start.3) | collective-permute-done | bytes 32800 | tf_op jit(solution)/shard_map/ppermute | solution.py:43
  31.5 12.5 %collective-permute-start.4 = (bf16[1,8,2048]{2,1,0:T(8,128)(2,1)S(1)}, bf16[1,8,2048]{2,1,0:T(8,128)(2,1)S(1)}, u32[]{:S(2)}, u32[]{:S(2)}) collective-permute-start(bf16[1,8,2048]{2,1,0:T(8,128)(2,1)S(1)} %add.169), channel_id=1, source_target_pairs={{0,32},{4,36},{8,40},{12,44},{16,48},{20,52},{24,56},{28,60},{32,0... | collective-permute-start | bytes 98312 | tf_op jit(solution)/shard_map/ppermute | solution.py:43
  44.0 0.1 fusion.54
  44.1 1.3 %collective-permute-done.4 = bf16[1,8,2048]{2,1,0:T(8,128)(2,1)S(1)} collective-permute-done((bf16[1,8,2048]{2,1,0:T(8,128)(2,1)S(1)}, bf16[1,8,2048]{2,1,0:T(8,128)(2,1)S(1)}, u32[]{:S(2)}, u32[]{:S(2)}) %collective-permute-start.4) | collective-permute-done | bytes 32800 | tf_op jit(solution)/shard_map/ppermute | solution.py:43
  45.4 7.9 %collective-permute-start.5 = (bf16[1,8,2048]{2,1,0:T(8,128)(2,1)S(1)}, bf16[1,8,2048]{2,1,0:T(8,128)(2,1)S(1)}, u32[]{:S(2)}, u32[]{:S(2)}) collective-permute-start(bf16[1,8,2048]{2,1,0:T(8,128)(2,1)S(1)} %add.170), channel_id=1, source_target_pairs={{0,64},{4,68},{8,72},{12,76},{16,80},{20,84},{24,88},{28,92},{32,9... | collective-permute-start | bytes 98312 | tf_op jit(solution)/shard_map/ppermute | solution.py:43
  53.4 1.2 %collective-permute-done.5 = bf16[1,8,2048]{2,1,0:T(8,128)(2,1)S(1)} collective-permute-done((bf16[1,8,2048]{2,1,0:T(8,128)(2,1)S(1)}, bf16[1,8,2048]{2,1,0:T(8,128)(2,1)S(1)}, u32[]{:S(2)}, u32[]{:S(2)}) %collective-permute-start.5) | collective-permute-done | bytes 32800 | tf_op jit(solution)/shard_map/ppermute | solution.py:43
  54.7 5.8 %collective-permute-start.6 = (bf16[1,8,2048]{2,1,0:T(8,128)(2,1)S(1)}, bf16[1,8,2048]{2,1,0:T(8,128)(2,1)S(1)}, u32[]{:S(2)}, u32[]{:S(2)}) collective-permute-start(bf16[1,8,2048]{2,1,0:T(8,128)(2,1)S(1)} %add.171), channel_id=1, source_target_pairs={{0,128},{4,132},{8,136},{12,140},{16,144},{20,148},{24,152},{28,15... | collective-permute-start | bytes 98312 | tf_op jit(solution)/shard_map/ppermute | solution.py:43
  60.5 1.3 %collective-permute-done.6 = bf16[1,8,2048]{2,1,0:T(8,128)(2,1)S(1)} collective-permute-done((bf16[1,8,2048]{2,1,0:T(8,128)(2,1)S(1)}, bf16[1,8,2048]{2,1,0:T(8,128)(2,1)S(1)}, u32[]{:S(2)}, u32[]{:S(2)}) %collective-permute-start.6) | collective-permute-done | bytes 32800 | tf_op jit(solution)/shard_map/ppermute | solution.py:43
  61.8 5.0 %collective-permute-start.7 = (bf16[1,8,2048]{2,1,0:T(8,128)(2,1)S(1)}, bf16[1,8,2048]{2,1,0:T(8,128)(2,1)S(1)}, u32[]{:S(2)}, u32[]{:S(2)}) collective-permute-start(bf16[1,8,2048]{2,1,0:T(8,128)(2,1)S(1)} %add.172), channel_id=1, source_target_pairs={{0,256},{4,260},{8,264},{12,268},{16,272},{20,276},{24,280},{28,28... | collective-permute-start | bytes 98312 | tf_op jit(solution)/shard_map/ppermute | solution.py:43
  66.8 1.3 %collective-permute-done.7 = bf16[1,8,2048]{2,1,0:T(8,128)(2,1)S(1)} collective-permute-done((bf16[1,8,2048]{2,1,0:T(8,128)(2,1)S(1)}, bf16[1,8,2048]{2,1,0:T(8,128)(2,1)S(1)}, u32[]{:S(2)}, u32[]{:S(2)}) %collective-permute-start.7) | collective-permute-done | bytes 32800 | tf_op jit(solution)/shard_map/ppermute | solution.py:43
  68.2 2.2 %collective-permute-start.8 = (bf16[1,23,2048]{2,1,0:T(8,128)(2,1)S(1)}, bf16[1,23,2048]{2,1,0:T(8,128)(2,1)S(1)}, u32[]{:S(2)}, u32[]{:S(2)}) collective-permute-start(bf16[1,23,2048]{2,1,0:T(8,128)(2,1)S(1)} %pad_maximum_fusion.3), channel_id=1, source_target_pairs={{0,2},{1,3},{2,0},{3,1},{4,6},{5,7},{6,4},{7,5},{8,10},{9,11},{10,... | collective-permute-start | bytes 282632 | tf_op jit(solution)/shard_map/ppermute | solution.py:53
  70.4 3.5 %collective-permute-done.8 = bf16[1,23,2048]{2,1,0:T(8,128)(2,1)S(1)} collective-permute-done((bf16[1,23,2048]{2,1,0:T(8,128)(2,1)S(1)}, bf16[1,23,2048]{2,1,0:T(8,128)(2,1)S(1)}, u32[]{:S(2)}, u32[]{:S(2)}) %collective-permute-start.8) | collective-permute-done | bytes 94240 | tf_op jit(solution)/shard_map/ppermute | solution.py:53
  73.9 9.5 %collective-permute-start.9 = (bf16[2,23,2048]{2,1,0:T(8,128)(2,1)S(1)}, bf16[2,23,2048]{2,1,0:T(8,128)(2,1)S(1)}, u32[]{:S(2)}, u32[]{:S(2)}) collective-permute-start(bf16[2,23,2048]{2,1,0:T(8,128)(2,1)S(1)} %pad_maximum_fusion.2), channel_id=1, source_target_pairs={{0,1},{1,0},{2,3},{3,2},{4,5},{5,4},{6,7},{7,6},{8,9},{9,8},{10,11... | collective-permute-start | bytes 565256 | tf_op jit(solution)/shard_map/ppermute | solution.py:53
  83.5 0.1 fusion.50
  83.6 1.0 %collective-permute-done.9 = bf16[2,23,2048]{2,1,0:T(8,128)(2,1)S(1)} collective-permute-done((bf16[2,23,2048]{2,1,0:T(8,128)(2,1)S(1)}, bf16[2,23,2048]{2,1,0:T(8,128)(2,1)S(1)}, u32[]{:S(2)}, u32[]{:S(2)}) %collective-permute-start.9) | collective-permute-done | bytes 188448 | tf_op jit(solution)/shard_map/ppermute | solution.py:53
  84.6 0.1 reshape.252
  84.7 3.1 %fusion.60 = f32[92,1024]{1,0:T(8,128)S(1)} fusion(bf16[92,2048]{1,0:T(8,128)(2,1)S(1)} %reshape.252, bf16[2048,1024]{1,0:T(8,128)(2,1)} %bitcast.35), kind=kOutput, calls=%fused_computation.112 | convolution fusion | flops 385875968 | bytes 4947968 | tf_op jit(solution)/shard_map/dot_general | solution.py:172
  87.9 0.3 copy-done
  88.2 0.8 convolution_negate_fusion
  89.0 0.2 fusion.59
  89.1 0.1 copy.14
  89.3 0.2 reduce_sum.61
  89.5 0.2 mul.441
  89.7 0.1 mul.442
  89.8 0.1 reshape_reshape.3
  90.2 0.4 bitcast_convert_fusion
  90.6 0.3 multiply_reduce_fusion.3
  91.0 0.2 add.188
  91.1 0.1 copy.12
  91.4 0.2 sub.24
  91.5 0.1 copy.13
  91.7 0.4 fusion.7
  92.1 0.1 multiply_subtract_fusion
  92.3 0.4 fusion
  92.7 0.7 mul.478
  (35 shorter events, 1.0 us)
Async XLA Ops:
  3.5 6.6 %collective-permute-start = (bf16[1,12,2048]{2,1,0:T(8,128)(2,1)S(1)}, bf16[1,12,2048]{2,1,0:T(8,128)(2,1)S(1)}, u32[]{:S(2)}, u32[]{:S(2)}) collective-permute-start(bf16[1,12,2048]{2,1,0:T(8,128)(2,1)S(1)} %pad_maximum_fusion.4), channel_id=1, source_target_pairs={{0,4},{4,0},{8,12},{12,8},{16,20},{20,16},{24,28},{28,24},{32,36},... | collective-permute-start | bytes 147464 | tf_op jit(solution)/shard_map/ppermute | solution.py:32
  7.9 52.5 %collective-permute-start.1 = (bf16[1,4,2048]{2,1,0:T(4,128)(2,1)S(1)}, bf16[1,4,2048]{2,1,0:T(4,128)(2,1)S(1)}, u32[]{:S(2)}, u32[]{:S(2)}) collective-permute-start(bf16[1,4,2048]{2,1,0:T(4,128)(2,1)S(1)} %get-tuple-element.23), channel_id=1, source_target_pairs={{4,8},{8,4},{12,16},{16,12},{20,24},{24,20},{28,32},{32,28},{36,40... | collective-permute-start | bytes 49160 | tf_op jit(solution)/shard_map/ppermute | solution.py:69
  10.2 11.1 %collective-permute-start.2 = (bf16[1,8,2048]{2,1,0:T(8,128)(2,1)S(1)}, bf16[1,8,2048]{2,1,0:T(8,128)(2,1)S(1)}, u32[]{:S(2)}, u32[]{:S(2)}) collective-permute-start(bf16[1,8,2048]{2,1,0:T(8,128)(2,1)S(1)} %slice_add_fusion), channel_id=1, source_target_pairs={{0,8},{4,12},{8,0},{12,4},{16,24},{20,28},{24,16},{28,20},{32,40},... | collective-permute-start | bytes 98312 | tf_op jit(solution)/shard_map/ppermute | solution.py:43
  16.4 51.8 %copy-start.1 = (bf16[1,8,2048]{2,1,0:T(8,128)(2,1)S(1)}, bf16[1,8,2048]{2,1,0:T(8,128)(2,1)}, u32[]{:S(2)}) copy-start(bf16[1,8,2048]{2,1,0:T(8,128)(2,1)} %param.3) | copy-start | bytes 98308
  21.3 10.2 %collective-permute-start.3 = (bf16[1,8,2048]{2,1,0:T(8,128)(2,1)S(1)}, bf16[1,8,2048]{2,1,0:T(8,128)(2,1)S(1)}, u32[]{:S(2)}, u32[]{:S(2)}) collective-permute-start(bf16[1,8,2048]{2,1,0:T(8,128)(2,1)S(1)} %add.168), channel_id=1, source_target_pairs={{0,16},{4,20},{8,24},{12,28},{16,0},{20,4},{24,8},{28,12},{32,48},... | collective-permute-start | bytes 98312 | tf_op jit(solution)/shard_map/ppermute | solution.py:43
  31.5 13.9 %collective-permute-start.4 = (bf16[1,8,2048]{2,1,0:T(8,128)(2,1)S(1)}, bf16[1,8,2048]{2,1,0:T(8,128)(2,1)S(1)}, u32[]{:S(2)}, u32[]{:S(2)}) collective-permute-start(bf16[1,8,2048]{2,1,0:T(8,128)(2,1)S(1)} %add.169), channel_id=1, source_target_pairs={{0,32},{4,36},{8,40},{12,44},{16,48},{20,52},{24,56},{28,60},{32,0... | collective-permute-start | bytes 98312 | tf_op jit(solution)/shard_map/ppermute | solution.py:43
  45.4 9.2 %collective-permute-start.5 = (bf16[1,8,2048]{2,1,0:T(8,128)(2,1)S(1)}, bf16[1,8,2048]{2,1,0:T(8,128)(2,1)S(1)}, u32[]{:S(2)}, u32[]{:S(2)}) collective-permute-start(bf16[1,8,2048]{2,1,0:T(8,128)(2,1)S(1)} %add.170), channel_id=1, source_target_pairs={{0,64},{4,68},{8,72},{12,76},{16,80},{20,84},{24,88},{28,92},{32,9... | collective-permute-start | bytes 98312 | tf_op jit(solution)/shard_map/ppermute | solution.py:43
  54.7 7.1 %collective-permute-start.6 = (bf16[1,8,2048]{2,1,0:T(8,128)(2,1)S(1)}, bf16[1,8,2048]{2,1,0:T(8,128)(2,1)S(1)}, u32[]{:S(2)}, u32[]{:S(2)}) collective-permute-start(bf16[1,8,2048]{2,1,0:T(8,128)(2,1)S(1)} %add.171), channel_id=1, source_target_pairs={{0,128},{4,132},{8,136},{12,140},{16,144},{20,148},{24,152},{28,15... | collective-permute-start | bytes 98312 | tf_op jit(solution)/shard_map/ppermute | solution.py:43
  61.8 6.3 %collective-permute-start.7 = (bf16[1,8,2048]{2,1,0:T(8,128)(2,1)S(1)}, bf16[1,8,2048]{2,1,0:T(8,128)(2,1)S(1)}, u32[]{:S(2)}, u32[]{:S(2)}) collective-permute-start(bf16[1,8,2048]{2,1,0:T(8,128)(2,1)S(1)} %add.172), channel_id=1, source_target_pairs={{0,256},{4,260},{8,264},{12,268},{16,272},{20,276},{24,280},{28,28... | collective-permute-start | bytes 98312 | tf_op jit(solution)/shard_map/ppermute | solution.py:43
  68.2 5.7 %collective-permute-start.8 = (bf16[1,23,2048]{2,1,0:T(8,128)(2,1)S(1)}, bf16[1,23,2048]{2,1,0:T(8,128)(2,1)S(1)}, u32[]{:S(2)}, u32[]{:S(2)}) collective-permute-start(bf16[1,23,2048]{2,1,0:T(8,128)(2,1)S(1)} %pad_maximum_fusion.3), channel_id=1, source_target_pairs={{0,2},{1,3},{2,0},{3,1},{4,6},{5,7},{6,4},{7,5},{8,10},{9,11},{10,... | collective-permute-start | bytes 282632 | tf_op jit(solution)/shard_map/ppermute | solution.py:53
  73.9 10.6 %collective-permute-start.9 = (bf16[2,23,2048]{2,1,0:T(8,128)(2,1)S(1)}, bf16[2,23,2048]{2,1,0:T(8,128)(2,1)S(1)}, u32[]{:S(2)}, u32[]{:S(2)}) collective-permute-start(bf16[2,23,2048]{2,1,0:T(8,128)(2,1)S(1)} %pad_maximum_fusion.2), channel_id=1, source_target_pairs={{0,1},{1,0},{2,3},{3,2},{4,5},{5,4},{6,7},{7,6},{8,9},{9,8},{10,11... | collective-permute-start | bytes 565256 | tf_op jit(solution)/shard_map/ppermute | solution.py:53
  84.7 3.5 %copy-start = (bf16[32,64,1024]{2,1,0:T(8,128)(2,1)S(1)}, bf16[32,64,1024]{2,1,0:T(8,128)(2,1)}, u32[]{:S(2)}) copy-start(bf16[32,64,1024]{2,1,0:T(8,128)(2,1)} %get-tuple-element.14) | copy-start | bytes 12582916

commit v10 on v9

--- a/solution.py
+++ b/solution.py
@@ -80,20 +80,34 @@
     return jnp.cos(angle), jnp.sin(angle)
 
 
-def make_forward(length):
+def forward_transform(rows):
+    count, length = rows.shape
     half = length // 2
-    lo_count = 64
-    hi_count = length // lo_count
-    freqs = jnp.arange(half, dtype=jnp.int32)
-    hi = jnp.arange(hi_count, dtype=jnp.int32)
-    lo = jnp.arange(lo_count, dtype=jnp.int32)
-    hi_c, hi_s = cos_sin(hi[:, None] * freqs[None, :] % hi_count, hi_count)
-    lo_c, lo_s = cos_sin(lo[:, None] * freqs[None, :] % length, length)
-    cos = hi_c[:, None, :] * lo_c[None, :, :] - hi_s[:, None, :] * lo_s[None, :, :]
-    sin = hi_s[:, None, :] * lo_c[None, :, :] + hi_c[:, None, :] * lo_s[None, :, :]
-    cos = cos.reshape(length, half).astype(jnp.bfloat16)
-    sin = sin.reshape(length, half).astype(jnp.bfloat16)
-    return cos, sin
+    inner = 64
+    outer = length // inner
+    laps = half // outer
+    fine = jnp.arange(inner, dtype=jnp.int32)
+    coarse = jnp.arange(outer, dtype=jnp.int32)
+    turns = jnp.arange(laps, dtype=jnp.int32)
+    w_c, w_s = cos_sin(coarse[:, None] * coarse[None, :] % outer, outer)
+    first = jnp.concatenate([w_c, -w_s], axis=1)
+    spun = jnp.einsum(
+        "rab,ak->rbk",
+        rows.reshape(count, outer, inner).astype(jnp.float32),
+        first,
+        precision=lax.Precision.HIGHEST,
+    )
+    y_re, y_im = spun[..., :outer], spun[..., outer:]
+    t_c, t_s = cos_sin(fine[:, None] * coarse[None, :] % length, length)
+    twisted = jnp.concatenate([y_re * t_c + y_im * t_s, y_im * t_c - y_re * t_s], axis=1)
+    g_c, g_s = cos_sin(fine[:, None] * turns[None, :] % inner, inner)
+    second = jnp.concatenate(
+        [jnp.concatenate([g_c, -g_s], axis=1), jnp.concatenate([g_s, g_c], axis=1)], axis=0
+    )
+    out = jnp.einsum("rnk,nq->rqk", twisted, second, precision=lax.Precision.HIGHEST)
+    return jnp.concatenate(
+        [out[:, :laps].reshape(count, half), out[:, laps:].reshape(count, half)], axis=-1
+    )
 
 
 def inverse_transform(cross, lags):
@@ -165,15 +179,7 @@
     block = jnp.concatenate([window, received], axis=1)
     block = gather(block, "seg")
     segs = block.shape[0]
-    cos, sin = make_forward(length)
-    flat_rows = block.reshape(segs * block.shape[1], length)
-    spectra = jnp.concatenate(
-        [
-            jnp.dot(flat_rows, cos, preferred_element_type=jnp.float32),
-            -jnp.dot(flat_rows, sin, preferred_element_type=jnp.float32),
-        ],
-        axis=-1,
-    )
+    spectra = forward_transform(block.reshape(segs * block.shape[1], length))
     white = whiten(spectra.reshape(block.shape), BAND).astype(jnp.bfloat16)
     chosen = white[:, rows:].reshape(segs, steps, nsrc, length)
     start = lax.axis_index("seg") * per

time: 93.9 us -> 114 us (1.21)
  local copies, waits for them, and re-layouts: 3.43 us -> 19.1 us
  starting transfers between devices: 63 us -> 66.7 us
  other arithmetic: 11 us -> 12.8 us
  waiting for transfers between devices: 10.8 us -> 9.61 us
    slice x0 -> x5, local copies, waits for them, and re-layouts: none -> 5.04 us  [the longest x3 2.55 us: forward_transform(): out[:, :laps].reshape(count, half)]
    convert_element_type x1 -> x0, other arithmetic: 4.88 us -> none  [make_forward(): cos = cos.reshape(length, half).astype(jnp.bfloat16)]
    reshape x1 -> x2, local copies, waits for them, and re-layouts: 0.11 us -> 3.27 us  [the longest x1 2 us: forward_transform(): out[:, laps:].reshape(count, half)]
    mul x2, local copies, waits for them, and re-layouts: 0.27 us -> 3.18 us  [whiten(): return (parts * scale[..., None, :, None]).reshape(spectra.shape)]
    ppermute x6, starting transfers between devices: 46.3 us -> 49 us  [broadcast(): total = total + lax.ppermute(block, axis, perm)]
    another operation x1 -> x2, local copies, waits for them, and re-layouts: 0.09 us -> 2.1 us  [forward_transform(): rows.reshape(count, outer, inner).astype(jnp.float32)]
    concatenate x2, other arithmetic: 0.13 us -> 1.65 us  [gather(): block = jnp.concatenate([block, partner], axis=0)]
    concatenate x0 -> x2, local copies, waits for them, and re-layouts: none -> 1.42 us  [forward_transform(): jnp.concatenate([out[:, :laps].reshape(count, half), out[:, laps:].reshap...]
  transfers between devices with their start and end apart: 10 -> 10, of which waited for: 7 -> 8; matrix products, arithmetic and copies ran while one was open for 7% -> 3% of each run, Pallas kernels for 0% -> 0%
where the time goes in v10:
time: 114 us; the launch traced here: 113 us
  starting transfers between devices  66.7 us (59%)
  local copies, waits for them, and re-layouts  19.1 us (17%)
  other arithmetic  12.8 us (11%)
  waiting for transfers between devices  9.61 us (8%)
  matrix products  4.34 us (4%)
    ppermute x6, starting transfers between devices, broadcast(): total = total + lax.ppermute(block, axis, perm)  49 us
    ppermute x2, starting transfers between devices, gather(): partner = lax.ppermute(block, axis, [(i, i ^ stride) for i in range(count)])  12.7 us
    ppermute x6, waiting for transfers between devices, broadcast(): total = total + lax.ppermute(block, axis, perm)  6.16 us
    ppermute x1, starting transfers between devices, broadcast(): lax.ppermute(jnp.concatenate([block, rider], axis=1), axis, [(i, i ^ 1) f...  4.38 us
    ppermute x2, waiting for transfers between devices, gather(): partner = lax.ppermute(block, axis, [(i, i ^ stride) for i in range(count)])  3.45 us
    mul x2, local copies, waits for them, and re-layouts, whiten(): return (parts * scale[..., None, :, None]).reshape(spectra.shape)  3.18 us
    slice x3, local copies, waits for them, and re-layouts, forward_transform(): out[:, :laps].reshape(count, half)  2.55 us
    slice x2, local copies, waits for them, and re-layouts, forward_transform(): out[:, laps:].reshape(count, half)  2.49 us
  transfers between devices with their start and end apart: 10, of which 8 were waited for; matrix products, arithmetic and copies ran while one was open for 3% of the time, Pallas kernels for 0%

profile of v10, /device:TPU:1, one launch (start us, length us, event | category | flops | bytes accessed | tf_op | source)
XLA Modules:
  0.0 113.1 jit_solution(5338116239355044214)
XLA Ops:
  0.0 0.7 broadcast_compare_fusion
  0.8 0.8 eq.41
  1.7 0.9 broadcast_select_fusion.1
  2.6 0.9 select_reduce_fusion
  3.5 4.4 %collective-permute-start = (bf16[1,12,2048]{2,1,0:T(8,128)(2,1)S(1)}, bf16[1,12,2048]{2,1,0:T(8,128)(2,1)S(1)}, u32[]{:S(2)}, u32[]{:S(2)}) collective-permute-start(bf16[1,12,2048]{2,1,0:T(8,128)(2,1)S(1)} %pad_maximum_fusion.4), channel_id=1, source_target_pairs={{0,4},{4,0},{8,12},{12,8},{16,20},{20,16},{24,28},{28,24},{32,36},... | collective-permute-start | bytes 147464 | tf_op jit(solution)/shard_map/ppermute | solution.py:32
  7.9 0.7 collective-permute-start.1
  8.8 0.7 fusion.63
  9.6 6.2 %collective-permute-start.2 = (bf16[1,8,2048]{2,1,0:T(8,128)(2,1)S(1)}, bf16[1,8,2048]{2,1,0:T(8,128)(2,1)S(1)}, u32[]{:S(2)}, u32[]{:S(2)}) collective-permute-start(bf16[1,8,2048]{2,1,0:T(8,128)(2,1)S(1)} %slice_add_fusion), channel_id=1, source_target_pairs={{0,8},{4,12},{8,0},{12,4},{16,24},{20,28},{24,16},{28,20},{32,40},... | collective-permute-start | bytes 98312 | tf_op jit(solution)/shard_map/ppermute | solution.py:43
  15.8 1.2 %collective-permute-done.2 = bf16[1,8,2048]{2,1,0:T(8,128)(2,1)S(1)} collective-permute-done((bf16[1,8,2048]{2,1,0:T(8,128)(2,1)S(1)}, bf16[1,8,2048]{2,1,0:T(8,128)(2,1)S(1)}, u32[]{:S(2)}, u32[]{:S(2)}) %collective-permute-start.2) | collective-permute-done | bytes 32800 | tf_op jit(solution)/shard_map/ppermute | solution.py:43
  17.1 8.8 %collective-permute-start.3 = (bf16[1,8,2048]{2,1,0:T(8,128)(2,1)S(1)}, bf16[1,8,2048]{2,1,0:T(8,128)(2,1)S(1)}, u32[]{:S(2)}, u32[]{:S(2)}) collective-permute-start(bf16[1,8,2048]{2,1,0:T(8,128)(2,1)S(1)} %add.168), channel_id=1, source_target_pairs={{0,16},{4,20},{8,24},{12,28},{16,0},{20,4},{24,8},{28,12},{32,48},... | collective-permute-start | bytes 98312 | tf_op jit(solution)/shard_map/ppermute | solution.py:43
  26.0 1.2 %collective-permute-done.3 = bf16[1,8,2048]{2,1,0:T(8,128)(2,1)S(1)} collective-permute-done((bf16[1,8,2048]{2,1,0:T(8,128)(2,1)S(1)}, bf16[1,8,2048]{2,1,0:T(8,128)(2,1)S(1)}, u32[]{:S(2)}, u32[]{:S(2)}) %collective-permute-start.3) | collective-permute-done | bytes 32800 | tf_op jit(solution)/shard_map/ppermute | solution.py:43
  27.2 12.4 %collective-permute-start.4 = (bf16[1,8,2048]{2,1,0:T(8,128)(2,1)S(1)}, bf16[1,8,2048]{2,1,0:T(8,128)(2,1)S(1)}, u32[]{:S(2)}, u32[]{:S(2)}) collective-permute-start(bf16[1,8,2048]{2,1,0:T(8,128)(2,1)S(1)} %add.169), channel_id=1, source_target_pairs={{0,32},{4,36},{8,40},{12,44},{16,48},{20,52},{24,56},{28,60},{32,0... | collective-permute-start | bytes 98312 | tf_op jit(solution)/shard_map/ppermute | solution.py:43
  39.5 0.7 fusion.76
  40.2 0.8 collective-permute-done.4
  41.0 10.8 %collective-permute-start.5 = (bf16[1,8,2048]{2,1,0:T(8,128)(2,1)S(1)}, bf16[1,8,2048]{2,1,0:T(8,128)(2,1)S(1)}, u32[]{:S(2)}, u32[]{:S(2)}) collective-permute-start(bf16[1,8,2048]{2,1,0:T(8,128)(2,1)S(1)} %add.170), channel_id=1, source_target_pairs={{0,64},{4,68},{8,72},{12,76},{16,80},{20,84},{24,88},{28,92},{32,9... | collective-permute-start | bytes 98312 | tf_op jit(solution)/shard_map/ppermute | solution.py:43
  51.8 0.7 sine_negate_fusion.1
  52.6 0.5 collective-permute-done.5
  53.1 5.5 %collective-permute-start.6 = (bf16[1,8,2048]{2,1,0:T(8,128)(2,1)S(1)}, bf16[1,8,2048]{2,1,0:T(8,128)(2,1)S(1)}, u32[]{:S(2)}, u32[]{:S(2)}) collective-permute-start(bf16[1,8,2048]{2,1,0:T(8,128)(2,1)S(1)} %add.171), channel_id=1, source_target_pairs={{0,128},{4,132},{8,136},{12,140},{16,144},{20,148},{24,152},{28,15... | collective-permute-start | bytes 98312 | tf_op jit(solution)/shard_map/ppermute | solution.py:43
  58.7 1.3 %collective-permute-done.6 = bf16[1,8,2048]{2,1,0:T(8,128)(2,1)S(1)} collective-permute-done((bf16[1,8,2048]{2,1,0:T(8,128)(2,1)S(1)}, bf16[1,8,2048]{2,1,0:T(8,128)(2,1)S(1)}, u32[]{:S(2)}, u32[]{:S(2)}) %collective-permute-start.6) | collective-permute-done | bytes 32800 | tf_op jit(solution)/shard_map/ppermute | solution.py:43
  60.0 5.3 %collective-permute-start.7 = (bf16[1,8,2048]{2,1,0:T(8,128)(2,1)S(1)}, bf16[1,8,2048]{2,1,0:T(8,128)(2,1)S(1)}, u32[]{:S(2)}, u32[]{:S(2)}) collective-permute-start(bf16[1,8,2048]{2,1,0:T(8,128)(2,1)S(1)} %add.172), channel_id=1, source_target_pairs={{0,256},{4,260},{8,264},{12,268},{16,272},{20,276},{24,280},{28,28... | collective-permute-start | bytes 98312 | tf_op jit(solution)/shard_map/ppermute | solution.py:43
  65.3 1.3 %collective-permute-done.7 = bf16[1,8,2048]{2,1,0:T(8,128)(2,1)S(1)} collective-permute-done((bf16[1,8,2048]{2,1,0:T(8,128)(2,1)S(1)}, bf16[1,8,2048]{2,1,0:T(8,128)(2,1)S(1)}, u32[]{:S(2)}, u32[]{:S(2)}) %collective-permute-start.7) | collective-permute-done | bytes 32800 | tf_op jit(solution)/shard_map/ppermute | solution.py:43
  66.6 0.8 pad_maximum_fusion.3
  67.4 2.5 %collective-permute-start.8 = (bf16[1,23,2048]{2,1,0:T(8,128)(2,1)S(1)}, bf16[1,23,2048]{2,1,0:T(8,128)(2,1)S(1)}, u32[]{:S(2)}, u32[]{:S(2)}) collective-permute-start(bf16[1,23,2048]{2,1,0:T(8,128)(2,1)S(1)} %pad_maximum_fusion.3), channel_id=1, source_target_pairs={{0,2},{1,3},{2,0},{3,1},{4,6},{5,7},{6,4},{7,5},{8,10},{9,11},{10,... | collective-permute-start | bytes 282632 | tf_op jit(solution)/shard_map/ppermute | solution.py:53
  70.0 3.1 %collective-permute-done.8 = bf16[1,23,2048]{2,1,0:T(8,128)(2,1)S(1)} collective-permute-done((bf16[1,23,2048]{2,1,0:T(8,128)(2,1)S(1)}, bf16[1,23,2048]{2,1,0:T(8,128)(2,1)S(1)}, u32[]{:S(2)}, u32[]{:S(2)}) %collective-permute-start.8) | collective-permute-done | bytes 94240 | tf_op jit(solution)/shard_map/ppermute | solution.py:53
  73.1 0.8 pad_maximum_fusion.2
  73.9 10.1 %collective-permute-start.9 = (bf16[2,23,2048]{2,1,0:T(8,128)(2,1)S(1)}, bf16[2,23,2048]{2,1,0:T(8,128)(2,1)S(1)}, u32[]{:S(2)}, u32[]{:S(2)}) collective-permute-start(bf16[2,23,2048]{2,1,0:T(8,128)(2,1)S(1)} %pad_maximum_fusion.2), channel_id=1, source_target_pairs={{0,1},{1,0},{2,3},{3,2},{4,5},{5,4},{6,7},{7,6},{8,9},{9,8},{10,11... | collective-permute-start | bytes 565256 | tf_op jit(solution)/shard_map/ppermute | solution.py:53
  84.0 0.7 fusion.66
  85.1 0.8 pad_maximum_fusion.1
  85.9 0.8 reshape_reshape.4
  86.7 1.3 %copy.41 = bf16[92,32,64]{0,1,2:T(8,128)(2,1)S(1)} copy(bf16[92,32,64]{2,1,0:T(8,128)(2,1)S(1)} %reshape_reshape.4) | data formatting | bytes 753664 | tf_op jit(solution)/shard_map/reshape;reshape | solution.py:96
  88.0 1.1 fusion.39
  89.1 0.9 multiply_add_fusion
  90.2 2.4 %fusion.2 = f32[92,64,32]{0,1,2:T(8,128)S(1)} fusion(f32[92,128,32]{0,2,1:T(8,128)S(1)} %pad_maximum_fusion, f32[64,32]{0,1:T(8,128)S(1)} %get-tuple-element.30, f32[64,32]{0,1:T(8,128)S(1)} %get-tuple-element.29, f32[64,32]{0,1:T(8,128)S(1)} %fusion.75), kind=kOutput, calls=%fused_computation.3 | convolution fusion | flops 289431552 | bytes 2285568 | tf_op jit(solution)/shard_map/rnk,nq->rqk/dot_general | solution.py:107
  92.8 1.1 copy.47
  93.9 1.4 %copy.45 = f32[92,32,32]{2,1,0:T(8,128)S(1)} copy(f32[92,32,32]{0,1,2:T(8,128)S(1)} %get-tuple-element.13) | data formatting | bytes 753664 | tf_op jit(solution)/shard_map/slice | solution.py:109
  95.2 1.1 copy.48
  96.4 1.4 %copy.46 = f32[92,32,32]{2,1,0:T(8,128)S(1)} copy(f32[92,32,32]{0,1,2:T(8,128)S(1)} %get-tuple-element.14) | data formatting | bytes 753664 | tf_op jit(solution)/shard_map/slice | solution.py:109
  97.7 1.3 %copy.49 = f32[92,1024]{1,0:T(8,128)S(1)} copy(f32[92,1024]{0,1:T(8,128)} %bitcast.42) | data formatting | bytes 753664 | tf_op jit(solution)/shard_map/reshape | solution.py:109
  99.0 2.0 %copy.50 = f32[92,1024]{1,0:T(8,128)} copy(f32[92,1024]{0,1:T(8,128)} %bitcast.43) | data formatting | bytes 753664 | tf_op jit(solution)/shard_map/reshape | solution.py:109
  101.0 1.1 maximum_multiply_fusion.1
  102.2 0.9 slice.119
  103.1 1.3 %reduce_sum.61 = f32[4,23,8]{2,1,0:T(8,128)S(1)} reduce(f32[4,23,2,8,128]{4,3,2,1,0:T(8,128)} %bitcast.41, f32[]{:T(128)} %constant.106.clone.1), dimensions={2,4}, to_apply=%region_1.2 | reduce | flops 187680 | bytes 756612 | tf_op jit(solution)/shard_map/reduce_sum | solution.py:147
  104.5 1.1 mul.434
  105.5 2.1 %mul.435 = f32[4,23,2048]{2,1,0:T(8,128)} reshape(f32[4,23,2,8,128]{4,3,2,1,0:T(8,128)} %mul.434) | data formatting | bytes 1507328 | tf_op jit(solution)/shard_map/mul | solution.py:149
  107.6 0.7 concatenate.68
  108.4 0.7 concatenate.69
  109.8 0.4 bitcast_convert_fusion
  112.4 0.7 mul.471
  (60 shorter events, 4.4 us)
Async XLA Ops:
  3.5 6.0 %collective-permute-start = (bf16[1,12,2048]{2,1,0:T(8,128)(2,1)S(1)}, bf16[1,12,2048]{2,1,0:T(8,128)(2,1)S(1)}, u32[]{:S(2)}, u32[]{:S(2)}) collective-permute-start(bf16[1,12,2048]{2,1,0:T(8,128)(2,1)S(1)} %pad_maximum_fusion.4), channel_id=1, source_target_pairs={{0,4},{4,0},{8,12},{12,8},{16,20},{20,16},{24,28},{28,24},{32,36},... | collective-permute-start | bytes 147464 | tf_op jit(solution)/shard_map/ppermute | solution.py:32
  7.9 50.7 %collective-permute-start.1 = (bf16[1,4,2048]{2,1,0:T(4,128)(2,1)S(1)}, bf16[1,4,2048]{2,1,0:T(4,128)(2,1)S(1)}, u32[]{:S(2)}, u32[]{:S(2)}) collective-permute-start(bf16[1,4,2048]{2,1,0:T(4,128)(2,1)S(1)} %get-tuple-element.23), channel_id=1, source_target_pairs={{4,8},{8,4},{12,16},{16,12},{20,24},{24,20},{28,32},{32,28},{36,40... | collective-permute-start | bytes 49160 | tf_op jit(solution)/shard_map/ppermute | solution.py:69
  9.6 7.5 %collective-permute-start.2 = (bf16[1,8,2048]{2,1,0:T(8,128)(2,1)S(1)}, bf16[1,8,2048]{2,1,0:T(8,128)(2,1)S(1)}, u32[]{:S(2)}, u32[]{:S(2)}) collective-permute-start(bf16[1,8,2048]{2,1,0:T(8,128)(2,1)S(1)} %slice_add_fusion), channel_id=1, source_target_pairs={{0,8},{4,12},{8,0},{12,4},{16,24},{20,28},{24,16},{28,20},{32,40},... | collective-permute-start | bytes 98312 | tf_op jit(solution)/shard_map/ppermute | solution.py:43
  17.1 10.1 %collective-permute-start.3 = (bf16[1,8,2048]{2,1,0:T(8,128)(2,1)S(1)}, bf16[1,8,2048]{2,1,0:T(8,128)(2,1)S(1)}, u32[]{:S(2)}, u32[]{:S(2)}) collective-permute-start(bf16[1,8,2048]{2,1,0:T(8,128)(2,1)S(1)} %add.168), channel_id=1, source_target_pairs={{0,16},{4,20},{8,24},{12,28},{16,0},{20,4},{24,8},{28,12},{32,48},... | collective-permute-start | bytes 98312 | tf_op jit(solution)/shard_map/ppermute | solution.py:43
  27.2 13.8 %collective-permute-start.4 = (bf16[1,8,2048]{2,1,0:T(8,128)(2,1)S(1)}, bf16[1,8,2048]{2,1,0:T(8,128)(2,1)S(1)}, u32[]{:S(2)}, u32[]{:S(2)}) collective-permute-start(bf16[1,8,2048]{2,1,0:T(8,128)(2,1)S(1)} %add.169), channel_id=1, source_target_pairs={{0,32},{4,36},{8,40},{12,44},{16,48},{20,52},{24,56},{28,60},{32,0... | collective-permute-start | bytes 98312 | tf_op jit(solution)/shard_map/ppermute | solution.py:43
  41.0 12.1 %collective-permute-start.5 = (bf16[1,8,2048]{2,1,0:T(8,128)(2,1)S(1)}, bf16[1,8,2048]{2,1,0:T(8,128)(2,1)S(1)}, u32[]{:S(2)}, u32[]{:S(2)}) collective-permute-start(bf16[1,8,2048]{2,1,0:T(8,128)(2,1)S(1)} %add.170), channel_id=1, source_target_pairs={{0,64},{4,68},{8,72},{12,76},{16,80},{20,84},{24,88},{28,92},{32,9... | collective-permute-start | bytes 98312 | tf_op jit(solution)/shard_map/ppermute | solution.py:43
  53.1 6.8 %collective-permute-start.6 = (bf16[1,8,2048]{2,1,0:T(8,128)(2,1)S(1)}, bf16[1,8,2048]{2,1,0:T(8,128)(2,1)S(1)}, u32[]{:S(2)}, u32[]{:S(2)}) collective-permute-start(bf16[1,8,2048]{2,1,0:T(8,128)(2,1)S(1)} %add.171), channel_id=1, source_target_pairs={{0,128},{4,132},{8,136},{12,140},{16,144},{20,148},{24,152},{28,15... | collective-permute-start | bytes 98312 | tf_op jit(solution)/shard_map/ppermute | solution.py:43
  60.0 6.6 %collective-permute-start.7 = (bf16[1,8,2048]{2,1,0:T(8,128)(2,1)S(1)}, bf16[1,8,2048]{2,1,0:T(8,128)(2,1)S(1)}, u32[]{:S(2)}, u32[]{:S(2)}) collective-permute-start(bf16[1,8,2048]{2,1,0:T(8,128)(2,1)S(1)} %add.172), channel_id=1, source_target_pairs={{0,256},{4,260},{8,264},{12,268},{16,272},{20,276},{24,280},{28,28... | collective-permute-start | bytes 98312 | tf_op jit(solution)/shard_map/ppermute | solution.py:43
  67.4 5.7 %collective-permute-start.8 = (bf16[1,23,2048]{2,1,0:T(8,128)(2,1)S(1)}, bf16[1,23,2048]{2,1,0:T(8,128)(2,1)S(1)}, u32[]{:S(2)}, u32[]{:S(2)}) collective-permute-start(bf16[1,23,2048]{2,1,0:T(8,128)(2,1)S(1)} %pad_maximum_fusion.3), channel_id=1, source_target_pairs={{0,2},{1,3},{2,0},{3,1},{4,6},{5,7},{6,4},{7,5},{8,10},{9,11},{10,... | collective-permute-start | bytes 282632 | tf_op jit(solution)/shard_map/ppermute | solution.py:53
  73.9 11.2 %collective-permute-start.9 = (bf16[2,23,2048]{2,1,0:T(8,128)(2,1)S(1)}, bf16[2,23,2048]{2,1,0:T(8,128)(2,1)S(1)}, u32[]{:S(2)}, u32[]{:S(2)}) collective-permute-start(bf16[2,23,2048]{2,1,0:T(8,128)(2,1)S(1)} %pad_maximum_fusion.2), channel_id=1, source_target_pairs={{0,1},{1,0},{2,3},{3,2},{4,5},{5,4},{6,7},{7,6},{8,9},{9,8},{10,11... | collective-permute-start | bytes 565256 | tf_op jit(solution)/shard_map/ppermute | solution.py:53
  108.3 1.1 %copy-start = (f32[4,23,2048]{2,1,0:T(8,128)S(1)}, f32[4,23,2048]{2,1,0:T(8,128)}, u32[]{:S(2)}) copy-start(f32[4,23,2048]{2,1,0:T(8,128)} %mul.435) | copy-start | bytes 2260996
  109.7 1.6 %copy-start.2 = (f32[32,64]{1,0:T(8,128)S(1)}, f32[32,64]{1,0:T(8,128)}, u32[]{:S(2)}) copy-start(f32[32,64]{1,0:T(8,128)} %get-tuple-element.31) | copy-start | bytes 24580
  109.7 1.6 %copy-start.3 = (f32[32,64]{1,0:T(8,128)S(1)}, f32[32,64]{1,0:T(8,128)}, u32[]{:S(2)}) copy-start(f32[32,64]{1,0:T(8,128)} %get-tuple-element.32) | copy-start | bytes 24580
  109.7 1.6 %copy-start.4 = (f32[32,64]{1,0:T(8,128)S(1)}, f32[32,64]{1,0:T(8,128)}, u32[]{:S(2)}) copy-start(f32[32,64]{1,0:T(8,128)} %fusion.76) | copy-start | bytes 24580
  109.8 2.0 %copy-start.1 = (f32[32,64]{1,0:T(8,128)S(1)}, f32[32,64]{1,0:T(8,128)}, u32[]{:S(2)}) copy-start(f32[32,64]{1,0:T(8,128)} %get-tuple-element.26) | copy-start | bytes 24580
  110.5 1.4 %copy-start.5 = (f32[32,16]{0,1:T(8,128)S(1)}, f32[32,16]{0,1:T(8,128)}, u32[]{:S(2)}) copy-start(f32[32,16]{0,1:T(8,128)} %get-tuple-element.33) | copy-start | bytes 6148
  110.5 1.4 %copy-start.6 = (f32[32,16]{0,1:T(8,128)S(1)}, f32[32,16]{0,1:T(8,128)}, u32[]{:S(2)}) copy-start(f32[32,16]{0,1:T(8,128)} %get-tuple-element.34) | copy-start | bytes 6148

commit v11 on v9

--- a/solution.py
+++ b/solution.py
@@ -60,10 +60,9 @@
     count = lax.axis_size(axis)
     odd = lax.axis_index(axis) % 2 == 1
     rows = cells.shape[1]
-    tail = lax.slice_in_dim(cells, rows - LOW, rows, axis=1)
-    head = jnp.pad(lax.slice_in_dim(cells, 0, HIGH, axis=1), ((0, 0), (0, LOW - HIGH), (0, 0)))
-    rider = jnp.where(odd, head, tail)
-    other = jnp.where(odd, tail, head)
+    first = jnp.where(odd, 0, rows - LOW)
+    rider = lax.dynamic_slice_in_dim(cells, first, LOW, axis=1)
+    other = lax.dynamic_slice_in_dim(cells, rows - LOW - first, LOW, axis=1)
     perm = [(i, i + 1) if i % 2 else (i, i - 1) for i in range(count)]
     perm = [(i, j) for i, j in perm if 0 <= j < count]
     return rider, lax.ppermute(other, axis, perm), odd
@@ -152,12 +151,13 @@
     seg_count = lax.axis_size("seg")
     per = ch_dev // seg_count
     here = lax.axis_index("fibre")
-    channels = jnp.arange(ch_dev, dtype=jnp.int32)
-    keep = (sources[:, :, None] == channels[None, None, :]) & (here == owners)[:, None, None]
-    picked = jnp.sum(
-        jnp.where(keep.reshape(1, steps * nsrc, ch_dev, 1), data[:, None], jnp.zeros_like(data[:, None])),
-        axis=2,
-    )
+    rows_of = [
+        lax.dynamic_slice_in_dim(data, sources[step, j], 1, axis=1)
+        for step in range(steps)
+        for j in range(nsrc)
+    ]
+    owned = jnp.repeat(here == owners, nsrc)
+    picked = jnp.where(owned[None, :, None], jnp.concatenate(rows_of, axis=1), jnp.zeros_like(data))
     rider, far, odd = edges(data, "fibre")
     received, near = broadcast(picked, "fibre", rider)
     window = halo(data, near, far, odd)

time: 93.9 us -> 110 us (1.17)
  between operations: 0.44 us -> 15.3 us
  local copies, waits for them, and re-layouts: 3.43 us -> 6.45 us
  other arithmetic: 11 us -> 9.22 us
    dynamic_slice x0 -> x2, local copies, waits for them, and re-layouts: none -> 2 us  [the longest x1 1.14 us: shards(): lax.dynamic_slice_in_dim(data, sources[step, j], 1, axis=1)]
    slice x0 -> x1, local copies, waits for them, and re-layouts: none -> 1.66 us  [shards(): sources[step, j]]
  transfers between devices with their start and end apart: 10 -> 10, of which waited for: 7 -> 7; matrix products, arithmetic and copies ran while one was open for 7% -> 6% of each run, Pallas kernels for 0% -> 0%
where the time goes in v11:
time: 110 us
  starting transfers between devices  63 us (57%)
  between operations  15.3 us (14%)
  waiting for transfers between devices  10.8 us (10%)
  other arithmetic  9.22 us (8%)
  local copies, waits for them, and re-layouts  6.45 us (6%)
  matrix products  4.75 us (4%)
    ppermute x6, starting transfers between devices, broadcast(): total = total + lax.ppermute(block, axis, perm)  46.3 us
    ppermute x2, starting transfers between devices, gather(): partner = lax.ppermute(block, axis, [(i, i ^ stride) for i in range(count)])  11.7 us
    ppermute x6, waiting for transfers between devices, broadcast(): total = total + lax.ppermute(block, axis, perm)  6.33 us
    convert_element_type x1, other arithmetic, make_forward(): cos = cos.reshape(length, half).astype(jnp.bfloat16)  4.88 us
    ppermute x2, waiting for transfers between devices, gather(): partner = lax.ppermute(block, axis, [(i, i ^ stride) for i in range(count)])  4.44 us
    ppermute x1, starting transfers between devices, broadcast(): lax.ppermute(jnp.concatenate([block, rider], axis=1), axis, [(i, i ^ 1) f...  4.38 us
    dot_general x1, matrix products, shards(): jnp.dot(flat_rows, cos, preferred_element_type=jnp.float32)  3.13 us
  transfers between devices with their start and end apart: 10, of which 7 were waited for; matrix products, arithmetic and copies ran while one was open for 6% of the time, Pallas kernels for 0%

profile of v11, /device:TPU:1, one launch (start us, length us, event | category | flops | bytes accessed | tf_op | source)
XLA Modules:
  0.0 109.5 jit_solution(11437833511270964367)
XLA Ops:
  0.0 1.7 %fusion.59 = (s32[1,1]{1,0:T(1,128)}, s32[1,1]{1,0:T(1,128)}, s32[1,1]{1,0:T(1,128)}, s32[1,1]{1,0:T(1,128)}, s32[1,1]{1,0:T(1,128)}, /*index=5*/s32[1,1]{1,0:T(1,128)}, s32[1,1]{1,0:T(1,128)}, s32[1,1]{1,0:T(1,128)}) fusion(s32[2,4]{1,0:T(2,128)} %param.4), kind=kLoop, calls=%fused_computation.117 | loop fusion | bytes 64 | tf_op jit(solution)/shard_map/slice | solution.py:155
  11.6 0.7 broadcast_compare_fusion
  12.3 0.1 broadcast_in_dim.20
  17.4 0.9 constant_dynamic-slice_fusion
  18.3 1.1 %constant_dynamic-slice_fusion.2 = (bf16[1,1,2048]{2,1,0:T(2,128)(2,1)S(1)}, bf16[1,1,2048]{2,1,0:T(2,128)(2,1)S(1)}, bf16[1,1,2048]{2,1,0:T(2,128)(2,1)S(1)}, b...) fusion(bf16[1,8,2048]{2,1,0:T(8,128)(2,1)} %param.3, ...), kind=kLoop, calls=%fused_computation.103 | loop fusion | bytes 65568 | tf_op jit(solution)/shard_map/dynamic_slice | solution.py:155
  19.4 0.1 concatenate.48
  19.6 4.4 %collective-permute-start = (bf16[1,12,2048]{2,1,0:T(8,128)(2,1)S(1)}, bf16[1,12,2048]{2,1,0:T(8,128)(2,1)S(1)}, u32[]{:S(2)}, u32[]{:S(2)}) collective-permute-start(bf16[1,12,2048]{2,1,0:T(8,128)(2,1)S(1)} %pad_maximum_fusion.4), channel_id=1, source_target_pairs={{0,4},{4,0},{8,12},{12,8},{16,20},{20,16},{24,28},{28,24},{32,36},... | collective-permute-start | bytes 147464 | tf_op jit(solution)/shard_map/ppermute | solution.py:32
  24.0 0.7 collective-permute-start.1
  24.7 1.0 fusion.17
  25.7 0.5 fusion.22
  26.3 6.1 %collective-permute-start.2 = (bf16[1,8,2048]{2,1,0:T(8,128)(2,1)S(1)}, bf16[1,8,2048]{2,1,0:T(8,128)(2,1)S(1)}, u32[]{:S(2)}, u32[]{:S(2)}) collective-permute-start(bf16[1,8,2048]{2,1,0:T(8,128)(2,1)S(1)} %slice_add_fusion), channel_id=1, source_target_pairs={{0,8},{4,12},{8,0},{12,4},{16,24},{20,28},{24,16},{28,20},{32,40},... | collective-permute-start | bytes 98312 | tf_op jit(solution)/shard_map/ppermute | solution.py:43
  32.5 4.9 %subtract_convert_fusion = (bf16[32,64,1024]{2,1,0:T(8,128)(2,1)}, bf16[32,64,1024]{2,1,0:T(8,128)(2,1)}) fusion(f32[64,1024]{1,0:T(8,128)S(1)} %get-tuple-element.45, f32[32,1024]{1,0:T(8,128)S(1)} %get-tuple-element.47, f32[64,1024]{1,0:T(8,128)S(1)} %get-tuple-element.46, f32[32,1024]{1,0:T(8,128)S(1)} %get-tuple-element.48), kind=kLoop, calls=%fused_computation.1 | loop fusion | flops 16777216 | bytes 9175040 | tf_op jit(solution)/shard_map/convert_element_type | solution.py:93
  37.4 8.8 %collective-permute-start.3 = (bf16[1,8,2048]{2,1,0:T(8,128)(2,1)S(1)}, bf16[1,8,2048]{2,1,0:T(8,128)(2,1)S(1)}, u32[]{:S(2)}, u32[]{:S(2)}) collective-permute-start(bf16[1,8,2048]{2,1,0:T(8,128)(2,1)S(1)} %add.206), channel_id=1, source_target_pairs={{0,16},{4,20},{8,24},{12,28},{16,0},{20,4},{24,8},{28,12},{32,48},... | collective-permute-start | bytes 98312 | tf_op jit(solution)/shard_map/ppermute | solution.py:43
  46.2 0.1 fusion.47
  46.3 1.3 %collective-permute-done.3 = bf16[1,8,2048]{2,1,0:T(8,128)(2,1)S(1)} collective-permute-done((bf16[1,8,2048]{2,1,0:T(8,128)(2,1)S(1)}, bf16[1,8,2048]{2,1,0:T(8,128)(2,1)S(1)}, u32[]{:S(2)}, u32[]{:S(2)}) %collective-permute-start.3) | collective-permute-done | bytes 32800 | tf_op jit(solution)/shard_map/ppermute | solution.py:43
  47.6 12.5 %collective-permute-start.4 = (bf16[1,8,2048]{2,1,0:T(8,128)(2,1)S(1)}, bf16[1,8,2048]{2,1,0:T(8,128)(2,1)S(1)}, u32[]{:S(2)}, u32[]{:S(2)}) collective-permute-start(bf16[1,8,2048]{2,1,0:T(8,128)(2,1)S(1)} %add.207), channel_id=1, source_target_pairs={{0,32},{4,36},{8,40},{12,44},{16,48},{20,52},{24,56},{28,60},{32,0... | collective-permute-start | bytes 98312 | tf_op jit(solution)/shard_map/ppermute | solution.py:43
  60.2 1.3 %collective-permute-done.4 = bf16[1,8,2048]{2,1,0:T(8,128)(2,1)S(1)} collective-permute-done((bf16[1,8,2048]{2,1,0:T(8,128)(2,1)S(1)}, bf16[1,8,2048]{2,1,0:T(8,128)(2,1)S(1)}, u32[]{:S(2)}, u32[]{:S(2)}) %collective-permute-start.4) | collective-permute-done | bytes 32800 | tf_op jit(solution)/shard_map/ppermute | solution.py:43
  61.5 7.9 %collective-permute-start.5 = (bf16[1,8,2048]{2,1,0:T(8,128)(2,1)S(1)}, bf16[1,8,2048]{2,1,0:T(8,128)(2,1)S(1)}, u32[]{:S(2)}, u32[]{:S(2)}) collective-permute-start(bf16[1,8,2048]{2,1,0:T(8,128)(2,1)S(1)} %add.208), channel_id=1, source_target_pairs={{0,64},{4,68},{8,72},{12,76},{16,80},{20,84},{24,88},{28,92},{32,9... | collective-permute-start | bytes 98312 | tf_op jit(solution)/shard_map/ppermute | solution.py:43
  69.5 1.2 %collective-permute-done.5 = bf16[1,8,2048]{2,1,0:T(8,128)(2,1)S(1)} collective-permute-done((bf16[1,8,2048]{2,1,0:T(8,128)(2,1)S(1)}, bf16[1,8,2048]{2,1,0:T(8,128)(2,1)S(1)}, u32[]{:S(2)}, u32[]{:S(2)}) %collective-permute-start.5) | collective-permute-done | bytes 32800 | tf_op jit(solution)/shard_map/ppermute | solution.py:43
  70.8 5.8 %collective-permute-start.6 = (bf16[1,8,2048]{2,1,0:T(8,128)(2,1)S(1)}, bf16[1,8,2048]{2,1,0:T(8,128)(2,1)S(1)}, u32[]{:S(2)}, u32[]{:S(2)}) collective-permute-start(bf16[1,8,2048]{2,1,0:T(8,128)(2,1)S(1)} %add.209), channel_id=1, source_target_pairs={{0,128},{4,132},{8,136},{12,140},{16,144},{20,148},{24,152},{28,15... | collective-permute-start | bytes 98312 | tf_op jit(solution)/shard_map/ppermute | solution.py:43
  76.6 1.3 %collective-permute-done.6 = bf16[1,8,2048]{2,1,0:T(8,128)(2,1)S(1)} collective-permute-done((bf16[1,8,2048]{2,1,0:T(8,128)(2,1)S(1)}, bf16[1,8,2048]{2,1,0:T(8,128)(2,1)S(1)}, u32[]{:S(2)}, u32[]{:S(2)}) %collective-permute-start.6) | collective-permute-done | bytes 32800 | tf_op jit(solution)/shard_map/ppermute | solution.py:43
  77.9 5.0 %collective-permute-start.7 = (bf16[1,8,2048]{2,1,0:T(8,128)(2,1)S(1)}, bf16[1,8,2048]{2,1,0:T(8,128)(2,1)S(1)}, u32[]{:S(2)}, u32[]{:S(2)}) collective-permute-start(bf16[1,8,2048]{2,1,0:T(8,128)(2,1)S(1)} %add.210), channel_id=1, source_target_pairs={{0,256},{4,260},{8,264},{12,268},{16,272},{20,276},{24,280},{28,28... | collective-permute-start | bytes 98312 | tf_op jit(solution)/shard_map/ppermute | solution.py:43
  82.9 1.3 %collective-permute-done.7 = bf16[1,8,2048]{2,1,0:T(8,128)(2,1)S(1)} collective-permute-done((bf16[1,8,2048]{2,1,0:T(8,128)(2,1)S(1)}, bf16[1,8,2048]{2,1,0:T(8,128)(2,1)S(1)}, u32[]{:S(2)}, u32[]{:S(2)}) %collective-permute-start.7) | collective-permute-done | bytes 32800 | tf_op jit(solution)/shard_map/ppermute | solution.py:43
  84.3 2.2 %collective-permute-start.8 = (bf16[1,23,2048]{2,1,0:T(8,128)(2,1)S(1)}, bf16[1,23,2048]{2,1,0:T(8,128)(2,1)S(1)}, u32[]{:S(2)}, u32[]{:S(2)}) collective-permute-start(bf16[1,23,2048]{2,1,0:T(8,128)(2,1)S(1)} %pad_maximum_fusion.3), channel_id=1, source_target_pairs={{0,2},{1,3},{2,0},{3,1},{4,6},{5,7},{6,4},{7,5},{8,10},{9,11},{10,... | collective-permute-start | bytes 282632 | tf_op jit(solution)/shard_map/ppermute | solution.py:53
  86.5 3.5 %collective-permute-done.8 = bf16[1,23,2048]{2,1,0:T(8,128)(2,1)S(1)} collective-permute-done((bf16[1,23,2048]{2,1,0:T(8,128)(2,1)S(1)}, bf16[1,23,2048]{2,1,0:T(8,128)(2,1)S(1)}, u32[]{:S(2)}, u32[]{:S(2)}) %collective-permute-start.8) | collective-permute-done | bytes 94240 | tf_op jit(solution)/shard_map/ppermute | solution.py:53
  90.0 9.5 %collective-permute-start.9 = (bf16[2,23,2048]{2,1,0:T(8,128)(2,1)S(1)}, bf16[2,23,2048]{2,1,0:T(8,128)(2,1)S(1)}, u32[]{:S(2)}, u32[]{:S(2)}) collective-permute-start(bf16[2,23,2048]{2,1,0:T(8,128)(2,1)S(1)} %pad_maximum_fusion.2), channel_id=1, source_target_pairs={{0,1},{1,0},{2,3},{3,2},{4,5},{5,4},{6,7},{7,6},{8,9},{9,8},{10,11... | collective-permute-start | bytes 565256 | tf_op jit(solution)/shard_map/ppermute | solution.py:53
  99.6 0.1 fusion.50
  99.7 1.0 collective-permute-done.9
  100.7 0.1 reshape.346
  100.8 3.1 %fusion.60 = f32[92,1024]{1,0:T(8,128)S(1)} fusion(bf16[92,2048]{1,0:T(8,128)(2,1)S(1)} %reshape.346, bf16[2048,1024]{1,0:T(8,128)(2,1)} %bitcast.40), kind=kOutput, calls=%fused_computation.118 | convolution fusion | flops 385875968 | bytes 4947968 | tf_op jit(solution)/shard_map/dot_general | solution.py:172
  104.0 0.3 copy-done
  104.3 0.8 convolution_negate_fusion
  105.1 0.2 fusion.58
  105.2 0.1 copy.10
  105.4 0.2 reduce_sum.45
  105.6 0.2 mul.441
  105.8 0.1 mul.442
  105.9 0.1 reshape_reshape.3
  106.3 0.4 bitcast_convert_fusion
  106.7 0.3 multiply_reduce_fusion.3
  107.1 0.2 add.226
  107.3 0.1 copy.8
  107.5 0.2 sub.28
  107.6 0.1 copy.9
  107.8 0.4 fusion.7
  108.2 0.1 multiply_subtract_fusion
  108.4 0.4 fusion
  108.8 0.7 mul.478
  (36 shorter events, 1.1 us)
Async XLA Ops:
  19.6 6.6 %collective-permute-start = (bf16[1,12,2048]{2,1,0:T(8,128)(2,1)S(1)}, bf16[1,12,2048]{2,1,0:T(8,128)(2,1)S(1)}, u32[]{:S(2)}, u32[]{:S(2)}) collective-permute-start(bf16[1,12,2048]{2,1,0:T(8,128)(2,1)S(1)} %pad_maximum_fusion.4), channel_id=1, source_target_pairs={{0,4},{4,0},{8,12},{12,8},{16,20},{20,16},{24,28},{28,24},{32,36},... | collective-permute-start | bytes 147464 | tf_op jit(solution)/shard_map/ppermute | solution.py:32
  24.0 52.6 %collective-permute-start.1 = (bf16[1,4,2048]{2,1,0:T(4,128)(2,1)S(1)}, bf16[1,4,2048]{2,1,0:T(4,128)(2,1)S(1)}, u32[]{:S(2)}, u32[]{:S(2)}) collective-permute-start(bf16[1,4,2048]{2,1,0:T(4,128)(2,1)S(1)} %get-tuple-element.23), channel_id=1, source_target_pairs={{4,8},{8,4},{12,16},{16,12},{20,24},{24,20},{28,32},{32,28},{36,40... | collective-permute-start | bytes 49160 | tf_op jit(solution)/shard_map/ppermute | solution.py:68
  26.3 11.1 %collective-permute-start.2 = (bf16[1,8,2048]{2,1,0:T(8,128)(2,1)S(1)}, bf16[1,8,2048]{2,1,0:T(8,128)(2,1)S(1)}, u32[]{:S(2)}, u32[]{:S(2)}) collective-permute-start(bf16[1,8,2048]{2,1,0:T(8,128)(2,1)S(1)} %slice_add_fusion), channel_id=1, source_target_pairs={{0,8},{4,12},{8,0},{12,4},{16,24},{20,28},{24,16},{28,20},{32,40},... | collective-permute-start | bytes 98312 | tf_op jit(solution)/shard_map/ppermute | solution.py:43
  32.5 51.8 %copy-start.1 = (bf16[1,8,2048]{2,1,0:T(8,128)(2,1)S(1)}, bf16[1,8,2048]{2,1,0:T(8,128)(2,1)}, u32[]{:S(2)}) copy-start(bf16[1,8,2048]{2,1,0:T(8,128)(2,1)} %param.3) | copy-start | bytes 98308
  37.4 10.2 %collective-permute-start.3 = (bf16[1,8,2048]{2,1,0:T(8,128)(2,1)S(1)}, bf16[1,8,2048]{2,1,0:T(8,128)(2,1)S(1)}, u32[]{:S(2)}, u32[]{:S(2)}) collective-permute-start(bf16[1,8,2048]{2,1,0:T(8,128)(2,1)S(1)} %add.206), channel_id=1, source_target_pairs={{0,16},{4,20},{8,24},{12,28},{16,0},{20,4},{24,8},{28,12},{32,48},... | collective-permute-start | bytes 98312 | tf_op jit(solution)/shard_map/ppermute | solution.py:43
  47.6 13.9 %collective-permute-start.4 = (bf16[1,8,2048]{2,1,0:T(8,128)(2,1)S(1)}, bf16[1,8,2048]{2,1,0:T(8,128)(2,1)S(1)}, u32[]{:S(2)}, u32[]{:S(2)}) collective-permute-start(bf16[1,8,2048]{2,1,0:T(8,128)(2,1)S(1)} %add.207), channel_id=1, source_target_pairs={{0,32},{4,36},{8,40},{12,44},{16,48},{20,52},{24,56},{28,60},{32,0... | collective-permute-start | bytes 98312 | tf_op jit(solution)/shard_map/ppermute | solution.py:43
  61.5 9.2 %collective-permute-start.5 = (bf16[1,8,2048]{2,1,0:T(8,128)(2,1)S(1)}, bf16[1,8,2048]{2,1,0:T(8,128)(2,1)S(1)}, u32[]{:S(2)}, u32[]{:S(2)}) collective-permute-start(bf16[1,8,2048]{2,1,0:T(8,128)(2,1)S(1)} %add.208), channel_id=1, source_target_pairs={{0,64},{4,68},{8,72},{12,76},{16,80},{20,84},{24,88},{28,92},{32,9... | collective-permute-start | bytes 98312 | tf_op jit(solution)/shard_map/ppermute | solution.py:43
  70.8 7.1 %collective-permute-start.6 = (bf16[1,8,2048]{2,1,0:T(8,128)(2,1)S(1)}, bf16[1,8,2048]{2,1,0:T(8,128)(2,1)S(1)}, u32[]{:S(2)}, u32[]{:S(2)}) collective-permute-start(bf16[1,8,2048]{2,1,0:T(8,128)(2,1)S(1)} %add.209), channel_id=1, source_target_pairs={{0,128},{4,132},{8,136},{12,140},{16,144},{20,148},{24,152},{28,15... | collective-permute-start | bytes 98312 | tf_op jit(solution)/shard_map/ppermute | solution.py:43
  77.9 6.3 %collective-permute-start.7 = (bf16[1,8,2048]{2,1,0:T(8,128)(2,1)S(1)}, bf16[1,8,2048]{2,1,0:T(8,128)(2,1)S(1)}, u32[]{:S(2)}, u32[]{:S(2)}) collective-permute-start(bf16[1,8,2048]{2,1,0:T(8,128)(2,1)S(1)} %add.210), channel_id=1, source_target_pairs={{0,256},{4,260},{8,264},{12,268},{16,272},{20,276},{24,280},{28,28... | collective-permute-start | bytes 98312 | tf_op jit(solution)/shard_map/ppermute | solution.py:43
  84.3 5.7 %collective-permute-start.8 = (bf16[1,23,2048]{2,1,0:T(8,128)(2,1)S(1)}, bf16[1,23,2048]{2,1,0:T(8,128)(2,1)S(1)}, u32[]{:S(2)}, u32[]{:S(2)}) collective-permute-start(bf16[1,23,2048]{2,1,0:T(8,128)(2,1)S(1)} %pad_maximum_fusion.3), channel_id=1, source_target_pairs={{0,2},{1,3},{2,0},{3,1},{4,6},{5,7},{6,4},{7,5},{8,10},{9,11},{10,... | collective-permute-start | bytes 282632 | tf_op jit(solution)/shard_map/ppermute | solution.py:53
  90.0 10.6 %collective-permute-start.9 = (bf16[2,23,2048]{2,1,0:T(8,128)(2,1)S(1)}, bf16[2,23,2048]{2,1,0:T(8,128)(2,1)S(1)}, u32[]{:S(2)}, u32[]{:S(2)}) collective-permute-start(bf16[2,23,2048]{2,1,0:T(8,128)(2,1)S(1)} %pad_maximum_fusion.2), channel_id=1, source_target_pairs={{0,1},{1,0},{2,3},{3,2},{4,5},{5,4},{6,7},{7,6},{8,9},{9,8},{10,11... | collective-permute-start | bytes 565256 | tf_op jit(solution)/shard_map/ppermute | solution.py:53
  100.8 3.5 %copy-start = (bf16[32,64,1024]{2,1,0:T(8,128)(2,1)S(1)}, bf16[32,64,1024]{2,1,0:T(8,128)(2,1)}, u32[]{:S(2)}) copy-start(bf16[32,64,1024]{2,1,0:T(8,128)(2,1)} %get-tuple-element.14) | copy-start | bytes 12582916

commit v12 on v9

--- a/solution.py
+++ b/solution.py
@@ -11,38 +11,17 @@
 HIGH = 3
 
 
-def radices(count):
-    if count == 64:
-        return [2] * 6
-    out = []
-    while count % 4 == 0:
-        out.append(4)
-        count //= 4
-    while count % 2 == 0:
-        out.append(2)
-        count //= 2
-    if count > 1:
-        out.append(count)
-    return out
-
-
 def broadcast(block, axis, rider):
     count = lax.axis_size(axis)
     width = block.shape[1]
     both = lax.ppermute(jnp.concatenate([block, rider], axis=1), axis, [(i, i ^ 1) for i in range(count)])
     block = block + both[:, :width]
     carried = both[:, width:]
-    stride = 2
-    for radix in radices(count // 2):
-        total = block
-        for shift in range(1, radix):
-            perm = []
-            for i in range(count):
-                digit = (i // stride) % radix
-                perm.append((i, i + ((digit + shift) % radix - digit) * stride))
-            total = total + lax.ppermute(block, axis, perm)
-        block = total
-        stride *= radix
+    strides = [1 << bit for bit in range(1, count.bit_length() - 1)]
+    if count == 128:
+        strides = [8, 4, 2, 16, 32, 64]
+    for stride in strides:
+        block = block + lax.ppermute(block, axis, [(i, i ^ stride) for i in range(count)])
     return block, carried
 
 

time: 93.9 us -> 94 us (level)
  starting transfers between devices: 63 us -> 61 us
  waiting for transfers between devices: 10.8 us -> 12.5 us
    ppermute x6, starting transfers between devices: 46.3 us -> 44 us  [broadcast(): lax.ppermute(block, axis, [(i, i ^ stride) for i in range(count)])]
    ppermute x6, waiting for transfers between devices: 6.33 us -> 7.91 us  [broadcast(): lax.ppermute(block, axis, [(i, i ^ stride) for i in range(count)])]
where the time goes in v12:
time: 94 us; the launch traced here: 93.1 us
  starting transfers between devices  61 us (65%)
  waiting for transfers between devices  12.5 us (13%)
  other arithmetic  11 us (12%)
  matrix products  4.75 us (5%)
  local copies, waits for them, and re-layouts  3.44 us (4%)
    ppermute x6, starting transfers between devices, broadcast(): lax.ppermute(block, axis, [(i, i ^ stride) for i in range(count)])  44 us
    ppermute x2, starting transfers between devices, gather(): partner = lax.ppermute(block, axis, [(i, i ^ stride) for i in range(count)])  12 us
    ppermute x6, waiting for transfers between devices, broadcast(): lax.ppermute(block, axis, [(i, i ^ stride) for i in range(count)])  7.91 us
    convert_element_type x1, other arithmetic, make_forward(): cos = cos.reshape(length, half).astype(jnp.bfloat16)  4.88 us
    ppermute x2, waiting for transfers between devices, gather(): partner = lax.ppermute(block, axis, [(i, i ^ stride) for i in range(count)])  4.56 us
    ppermute x1, starting transfers between devices, broadcast(): lax.ppermute(jnp.concatenate([block, rider], axis=1), axis, [(i, i ^ 1) f...  4.38 us
    dot_general x1, matrix products, shards(): jnp.dot(flat_rows, cos, preferred_element_type=jnp.float32)  3.13 us
  transfers between devices with their start and end apart: 10, of which 7 were waited for; matrix products, arithmetic and copies ran while one was open for 7% of the time, Pallas kernels for 0%

profile of v12, /device:TPU:1, one launch (start us, length us, event | category | flops | bytes accessed | tf_op | source)
XLA Modules:
  0.0 93.1 jit_solution(11971126122185786263)
XLA Ops:
  0.0 0.7 broadcast_compare_fusion
  0.7 0.1 and.104
  0.8 0.8 eq.40
  1.7 0.9 broadcast_select_fusion.1
  2.6 0.9 %select_reduce_fusion = bf16[8,2048]{1,0:T(8,128)(2,1)S(1)} fusion(pred[8,8]{1,0:T(8,128)(4,1)S(1)} %fusion.56, bf16[8,2048]{1,0:T(8,128)(2,1)} %bitcast.39), kind=kLoop, calls=%fused_computation.29 | loop fusion | flops 245760 | bytes 65600 | tf_op jit(solution)/shard_map/reduce_sum | solution.py:136
  3.5 4.4 %collective-permute-start = (bf16[1,12,2048]{2,1,0:T(8,128)(2,1)S(1)}, bf16[1,12,2048]{2,1,0:T(8,128)(2,1)S(1)}, u32[]{:S(2)}, u32[]{:S(2)}) collective-permute-start(bf16[1,12,2048]{2,1,0:T(8,128)(2,1)S(1)} %pad_maximum_fusion.4), channel_id=1, source_target_pairs={{0,4},{4,0},{8,12},{12,8},{16,20},{20,16},{24,28},{28,24},{32,36},... | collective-permute-start | bytes 147464 | tf_op jit(solution)/shard_map/ppermute | solution.py:17
  7.9 0.7 collective-permute-start.1
  8.6 1.0 %fusion.17 = (f32[64,1024]{1,0:T(8,128)S(1)}, f32[64,1024]{1,0:T(8,128)S(1)}) fusion(), kind=kLoop, calls=%fused_computation.41 | loop fusion | flops 917504 | bytes 524288 | tf_op jit(solution)/shard_map/sin | solution.py:59
  9.6 0.5 fusion.22
  10.2 15.8 %collective-permute-start.2 = (bf16[1,8,2048]{2,1,0:T(8,128)(2,1)S(1)}, bf16[1,8,2048]{2,1,0:T(8,128)(2,1)S(1)}, u32[]{:S(2)}, u32[]{:S(2)}) collective-permute-start(bf16[1,8,2048]{2,1,0:T(8,128)(2,1)S(1)} %slice_add_fusion), channel_id=1, source_target_pairs={{0,32},{4,36},{8,40},{12,44},{16,48},{20,52},{24,56},{28,60},{32,0... | collective-permute-start | bytes 98312 | tf_op jit(solution)/shard_map/ppermute | solution.py:24
  26.0 4.9 %subtract_convert_fusion = (bf16[32,64,1024]{2,1,0:T(8,128)(2,1)}, bf16[32,64,1024]{2,1,0:T(8,128)(2,1)}) fusion(f32[64,1024]{1,0:T(8,128)S(1)} %get-tuple-element.27, f32[32,1024]{1,0:T(8,128)S(1)} %get-tuple-element.29, f32[64,1024]{1,0:T(8,128)S(1)} %get-tuple-element.28, f32[32,1024]{1,0:T(8,128)S(1)} %get-tuple-element.30), kind=kLoop, calls=%fused_computation.1 | loop fusion | flops 16777216 | bytes 9175040 | tf_op jit(solution)/shard_map/convert_element_type | solution.py:73
  30.9 5.9 %collective-permute-start.3 = (bf16[1,8,2048]{2,1,0:T(8,128)(2,1)S(1)}, bf16[1,8,2048]{2,1,0:T(8,128)(2,1)S(1)}, u32[]{:S(2)}, u32[]{:S(2)}) collective-permute-start(bf16[1,8,2048]{2,1,0:T(8,128)(2,1)S(1)} %add.168), channel_id=1, source_target_pairs={{0,16},{4,20},{8,24},{12,28},{16,0},{20,4},{24,8},{28,12},{32,48},... | collective-permute-start | bytes 98312 | tf_op jit(solution)/shard_map/ppermute | solution.py:24
  36.8 0.1 fusion.47
  36.9 2.5 %collective-permute-done.3 = bf16[1,8,2048]{2,1,0:T(8,128)(2,1)S(1)} collective-permute-done((bf16[1,8,2048]{2,1,0:T(8,128)(2,1)S(1)}, bf16[1,8,2048]{2,1,0:T(8,128)(2,1)S(1)}, u32[]{:S(2)}, u32[]{:S(2)}) %collective-permute-start.3) | collective-permute-done | bytes 32800 | tf_op jit(solution)/shard_map/ppermute | solution.py:24
  39.5 3.8 %collective-permute-start.4 = (bf16[1,8,2048]{2,1,0:T(8,128)(2,1)S(1)}, bf16[1,8,2048]{2,1,0:T(8,128)(2,1)S(1)}, u32[]{:S(2)}, u32[]{:S(2)}) collective-permute-start(bf16[1,8,2048]{2,1,0:T(8,128)(2,1)S(1)} %add.169), channel_id=1, source_target_pairs={{0,8},{4,12},{8,0},{12,4},{16,24},{20,28},{24,16},{28,20},{32,40},... | collective-permute-start | bytes 98312 | tf_op jit(solution)/shard_map/ppermute | solution.py:24
  43.3 0.1 fusion.54
  43.4 1.6 %collective-permute-done.4 = bf16[1,8,2048]{2,1,0:T(8,128)(2,1)S(1)} collective-permute-done((bf16[1,8,2048]{2,1,0:T(8,128)(2,1)S(1)}, bf16[1,8,2048]{2,1,0:T(8,128)(2,1)S(1)}, u32[]{:S(2)}, u32[]{:S(2)}) %collective-permute-start.4) | collective-permute-done | bytes 32800 | tf_op jit(solution)/shard_map/ppermute | solution.py:24
  45.1 7.2 %collective-permute-start.5 = (bf16[1,8,2048]{2,1,0:T(8,128)(2,1)S(1)}, bf16[1,8,2048]{2,1,0:T(8,128)(2,1)S(1)}, u32[]{:S(2)}, u32[]{:S(2)}) collective-permute-start(bf16[1,8,2048]{2,1,0:T(8,128)(2,1)S(1)} %add.170), channel_id=1, source_target_pairs={{0,64},{4,68},{8,72},{12,76},{16,80},{20,84},{24,88},{28,92},{32,9... | collective-permute-start | bytes 98312 | tf_op jit(solution)/shard_map/ppermute | solution.py:24
  52.3 1.2 %collective-permute-done.5 = bf16[1,8,2048]{2,1,0:T(8,128)(2,1)S(1)} collective-permute-done((bf16[1,8,2048]{2,1,0:T(8,128)(2,1)S(1)}, bf16[1,8,2048]{2,1,0:T(8,128)(2,1)S(1)}, u32[]{:S(2)}, u32[]{:S(2)}) %collective-permute-start.5) | collective-permute-done | bytes 32800 | tf_op jit(solution)/shard_map/ppermute | solution.py:24
  53.5 6.3 %collective-permute-start.6 = (bf16[1,8,2048]{2,1,0:T(8,128)(2,1)S(1)}, bf16[1,8,2048]{2,1,0:T(8,128)(2,1)S(1)}, u32[]{:S(2)}, u32[]{:S(2)}) collective-permute-start(bf16[1,8,2048]{2,1,0:T(8,128)(2,1)S(1)} %add.171), channel_id=1, source_target_pairs={{0,128},{4,132},{8,136},{12,140},{16,144},{20,148},{24,152},{28,15... | collective-permute-start | bytes 98312 | tf_op jit(solution)/shard_map/ppermute | solution.py:24
  59.9 1.3 %collective-permute-done.6 = bf16[1,8,2048]{2,1,0:T(8,128)(2,1)S(1)} collective-permute-done((bf16[1,8,2048]{2,1,0:T(8,128)(2,1)S(1)}, bf16[1,8,2048]{2,1,0:T(8,128)(2,1)S(1)}, u32[]{:S(2)}, u32[]{:S(2)}) %collective-permute-start.6) | collective-permute-done | bytes 32800 | tf_op jit(solution)/shard_map/ppermute | solution.py:24
  61.2 5.0 %collective-permute-start.7 = (bf16[1,8,2048]{2,1,0:T(8,128)(2,1)S(1)}, bf16[1,8,2048]{2,1,0:T(8,128)(2,1)S(1)}, u32[]{:S(2)}, u32[]{:S(2)}) collective-permute-start(bf16[1,8,2048]{2,1,0:T(8,128)(2,1)S(1)} %add.172), channel_id=1, source_target_pairs={{0,256},{4,260},{8,264},{12,268},{16,272},{20,276},{24,280},{28,28... | collective-permute-start | bytes 98312 | tf_op jit(solution)/shard_map/ppermute | solution.py:24
  66.2 1.3 %collective-permute-done.7 = bf16[1,8,2048]{2,1,0:T(8,128)(2,1)S(1)} collective-permute-done((bf16[1,8,2048]{2,1,0:T(8,128)(2,1)S(1)}, bf16[1,8,2048]{2,1,0:T(8,128)(2,1)S(1)}, u32[]{:S(2)}, u32[]{:S(2)}) %collective-permute-start.7) | collective-permute-done | bytes 32800 | tf_op jit(solution)/shard_map/ppermute | solution.py:24
  67.5 2.0 %collective-permute-start.8 = (bf16[1,23,2048]{2,1,0:T(8,128)(2,1)S(1)}, bf16[1,23,2048]{2,1,0:T(8,128)(2,1)S(1)}, u32[]{:S(2)}, u32[]{:S(2)}) collective-permute-start(bf16[1,23,2048]{2,1,0:T(8,128)(2,1)S(1)} %pad_maximum_fusion.3), channel_id=1, source_target_pairs={{0,2},{1,3},{2,0},{3,1},{4,6},{5,7},{6,4},{7,5},{8,10},{9,11},{10,... | collective-permute-start | bytes 282632 | tf_op jit(solution)/shard_map/ppermute | solution.py:32
  69.6 3.6 %collective-permute-done.8 = bf16[1,23,2048]{2,1,0:T(8,128)(2,1)S(1)} collective-permute-done((bf16[1,23,2048]{2,1,0:T(8,128)(2,1)S(1)}, bf16[1,23,2048]{2,1,0:T(8,128)(2,1)S(1)}, u32[]{:S(2)}, u32[]{:S(2)}) %collective-permute-start.8) | collective-permute-done | bytes 94240 | tf_op jit(solution)/shard_map/ppermute | solution.py:32
  73.3 9.9 %collective-permute-start.9 = (bf16[2,23,2048]{2,1,0:T(8,128)(2,1)S(1)}, bf16[2,23,2048]{2,1,0:T(8,128)(2,1)S(1)}, u32[]{:S(2)}, u32[]{:S(2)}) collective-permute-start(bf16[2,23,2048]{2,1,0:T(8,128)(2,1)S(1)} %pad_maximum_fusion.2), channel_id=1, source_target_pairs={{0,1},{1,0},{2,3},{3,2},{4,5},{5,4},{6,7},{7,6},{8,9},{9,8},{10,11... | collective-permute-start | bytes 565256 | tf_op jit(solution)/shard_map/ppermute | solution.py:32
  83.2 0.1 fusion.50
  83.3 1.0 %collective-permute-done.9 = bf16[2,23,2048]{2,1,0:T(8,128)(2,1)S(1)} collective-permute-done((bf16[2,23,2048]{2,1,0:T(8,128)(2,1)S(1)}, bf16[2,23,2048]{2,1,0:T(8,128)(2,1)S(1)}, u32[]{:S(2)}, u32[]{:S(2)}) %collective-permute-start.9) | collective-permute-done | bytes 188448 | tf_op jit(solution)/shard_map/ppermute | solution.py:32
  84.3 0.1 reshape.252
  84.4 3.1 %fusion.60 = f32[92,1024]{1,0:T(8,128)S(1)} fusion(bf16[92,2048]{1,0:T(8,128)(2,1)S(1)} %reshape.252, bf16[2048,1024]{1,0:T(8,128)(2,1)} %bitcast.35), kind=kOutput, calls=%fused_computation.112 | convolution fusion | flops 385875968 | bytes 4947968 | tf_op jit(solution)/shard_map/dot_general | solution.py:151
  87.6 0.3 copy-done
  87.9 0.8 convolution_negate_fusion
  88.7 0.2 fusion.59
  88.8 0.1 copy.14
  89.1 0.2 reduce_sum.61
  89.3 0.2 mul.441
  89.4 0.1 mul.442
  89.5 0.1 reshape_reshape.3
  89.9 0.4 bitcast_convert_fusion
  90.4 0.3 multiply_reduce_fusion.3
  90.7 0.2 add.188
  90.9 0.1 copy.12
  91.1 0.2 sub.24
  91.3 0.1 copy.13
  91.4 0.4 fusion.7
  91.8 0.1 multiply_subtract_fusion
  92.0 0.4 fusion
  92.4 0.7 mul.478
  (35 shorter events, 1.0 us)
Async XLA Ops:
  3.5 6.6 %collective-permute-start = (bf16[1,12,2048]{2,1,0:T(8,128)(2,1)S(1)}, bf16[1,12,2048]{2,1,0:T(8,128)(2,1)S(1)}, u32[]{:S(2)}, u32[]{:S(2)}) collective-permute-start(bf16[1,12,2048]{2,1,0:T(8,128)(2,1)S(1)} %pad_maximum_fusion.4), channel_id=1, source_target_pairs={{0,4},{4,0},{8,12},{12,8},{16,20},{20,16},{24,28},{28,24},{32,36},... | collective-permute-start | bytes 147464 | tf_op jit(solution)/shard_map/ppermute | solution.py:17
  7.9 51.9 %collective-permute-start.1 = (bf16[1,4,2048]{2,1,0:T(4,128)(2,1)S(1)}, bf16[1,4,2048]{2,1,0:T(4,128)(2,1)S(1)}, u32[]{:S(2)}, u32[]{:S(2)}) collective-permute-start(bf16[1,4,2048]{2,1,0:T(4,128)(2,1)S(1)} %get-tuple-element.23), channel_id=1, source_target_pairs={{4,8},{8,4},{12,16},{16,12},{20,24},{24,20},{28,32},{32,28},{36,40... | collective-permute-start | bytes 49160 | tf_op jit(solution)/shard_map/ppermute | solution.py:48
  10.2 20.7 %collective-permute-start.2 = (bf16[1,8,2048]{2,1,0:T(8,128)(2,1)S(1)}, bf16[1,8,2048]{2,1,0:T(8,128)(2,1)S(1)}, u32[]{:S(2)}, u32[]{:S(2)}) collective-permute-start(bf16[1,8,2048]{2,1,0:T(8,128)(2,1)S(1)} %slice_add_fusion), channel_id=1, source_target_pairs={{0,32},{4,36},{8,40},{12,44},{16,48},{20,52},{24,56},{28,60},{32,0... | collective-permute-start | bytes 98312 | tf_op jit(solution)/shard_map/ppermute | solution.py:24
  26.0 41.5 %copy-start.1 = (bf16[1,8,2048]{2,1,0:T(8,128)(2,1)S(1)}, bf16[1,8,2048]{2,1,0:T(8,128)(2,1)}, u32[]{:S(2)}) copy-start(bf16[1,8,2048]{2,1,0:T(8,128)(2,1)} %param.3) | copy-start | bytes 98308
  30.9 8.6 %collective-permute-start.3 = (bf16[1,8,2048]{2,1,0:T(8,128)(2,1)S(1)}, bf16[1,8,2048]{2,1,0:T(8,128)(2,1)S(1)}, u32[]{:S(2)}, u32[]{:S(2)}) collective-permute-start(bf16[1,8,2048]{2,1,0:T(8,128)(2,1)S(1)} %add.168), channel_id=1, source_target_pairs={{0,16},{4,20},{8,24},{12,28},{16,0},{20,4},{24,8},{28,12},{32,48},... | collective-permute-start | bytes 98312 | tf_op jit(solution)/shard_map/ppermute | solution.py:24
  39.5 5.6 %collective-permute-start.4 = (bf16[1,8,2048]{2,1,0:T(8,128)(2,1)S(1)}, bf16[1,8,2048]{2,1,0:T(8,128)(2,1)S(1)}, u32[]{:S(2)}, u32[]{:S(2)}) collective-permute-start(bf16[1,8,2048]{2,1,0:T(8,128)(2,1)S(1)} %add.169), channel_id=1, source_target_pairs={{0,8},{4,12},{8,0},{12,4},{16,24},{20,28},{24,16},{28,20},{32,40},... | collective-permute-start | bytes 98312 | tf_op jit(solution)/shard_map/ppermute | solution.py:24
  45.1 8.5 %collective-permute-start.5 = (bf16[1,8,2048]{2,1,0:T(8,128)(2,1)S(1)}, bf16[1,8,2048]{2,1,0:T(8,128)(2,1)S(1)}, u32[]{:S(2)}, u32[]{:S(2)}) collective-permute-start(bf16[1,8,2048]{2,1,0:T(8,128)(2,1)S(1)} %add.170), channel_id=1, source_target_pairs={{0,64},{4,68},{8,72},{12,76},{16,80},{20,84},{24,88},{28,92},{32,9... | collective-permute-start | bytes 98312 | tf_op jit(solution)/shard_map/ppermute | solution.py:24
  53.5 7.6 %collective-permute-start.6 = (bf16[1,8,2048]{2,1,0:T(8,128)(2,1)S(1)}, bf16[1,8,2048]{2,1,0:T(8,128)(2,1)S(1)}, u32[]{:S(2)}, u32[]{:S(2)}) collective-permute-start(bf16[1,8,2048]{2,1,0:T(8,128)(2,1)S(1)} %add.171), channel_id=1, source_target_pairs={{0,128},{4,132},{8,136},{12,140},{16,144},{20,148},{24,152},{28,15... | collective-permute-start | bytes 98312 | tf_op jit(solution)/shard_map/ppermute | solution.py:24
  61.2 6.3 %collective-permute-start.7 = (bf16[1,8,2048]{2,1,0:T(8,128)(2,1)S(1)}, bf16[1,8,2048]{2,1,0:T(8,128)(2,1)S(1)}, u32[]{:S(2)}, u32[]{:S(2)}) collective-permute-start(bf16[1,8,2048]{2,1,0:T(8,128)(2,1)S(1)} %add.172), channel_id=1, source_target_pairs={{0,256},{4,260},{8,264},{12,268},{16,272},{20,276},{24,280},{28,28... | collective-permute-start | bytes 98312 | tf_op jit(solution)/shard_map/ppermute | solution.py:24
  67.5 5.7 %collective-permute-start.8 = (bf16[1,23,2048]{2,1,0:T(8,128)(2,1)S(1)}, bf16[1,23,2048]{2,1,0:T(8,128)(2,1)S(1)}, u32[]{:S(2)}, u32[]{:S(2)}) collective-permute-start(bf16[1,23,2048]{2,1,0:T(8,128)(2,1)S(1)} %pad_maximum_fusion.3), channel_id=1, source_target_pairs={{0,2},{1,3},{2,0},{3,1},{4,6},{5,7},{6,4},{7,5},{8,10},{9,11},{10,... | collective-permute-start | bytes 282632 | tf_op jit(solution)/shard_map/ppermute | solution.py:32
  73.3 11.0 %collective-permute-start.9 = (bf16[2,23,2048]{2,1,0:T(8,128)(2,1)S(1)}, bf16[2,23,2048]{2,1,0:T(8,128)(2,1)S(1)}, u32[]{:S(2)}, u32[]{:S(2)}) collective-permute-start(bf16[2,23,2048]{2,1,0:T(8,128)(2,1)S(1)} %pad_maximum_fusion.2), channel_id=1, source_target_pairs={{0,1},{1,0},{2,3},{3,2},{4,5},{5,4},{6,7},{7,6},{8,9},{9,8},{10,11... | collective-permute-start | bytes 565256 | tf_op jit(solution)/shard_map/ppermute | solution.py:32
  84.4 3.5 %copy-start = (bf16[32,64,1024]{2,1,0:T(8,128)(2,1)S(1)}, bf16[32,64,1024]{2,1,0:T(8,128)(2,1)}, u32[]{:S(2)}) copy-start(bf16[32,64,1024]{2,1,0:T(8,128)(2,1)} %get-tuple-element.14) | copy-start | bytes 12582916

commit v13 on v12

--- a/solution.py
+++ b/solution.py
@@ -62,17 +62,40 @@
 def make_forward(length):
     half = length // 2
     lo_count = 64
-    hi_count = length // lo_count
+    period = length // lo_count
     freqs = jnp.arange(half, dtype=jnp.int32)
-    hi = jnp.arange(hi_count, dtype=jnp.int32)
+    hi = jnp.arange(half // lo_count, dtype=jnp.int32)
     lo = jnp.arange(lo_count, dtype=jnp.int32)
-    hi_c, hi_s = cos_sin(hi[:, None] * freqs[None, :] % hi_count, hi_count)
+    hi_c, hi_s = cos_sin(hi[:, None] * freqs[None, :] % period, period)
     lo_c, lo_s = cos_sin(lo[:, None] * freqs[None, :] % length, length)
     cos = hi_c[:, None, :] * lo_c[None, :, :] - hi_s[:, None, :] * lo_s[None, :, :]
     sin = hi_s[:, None, :] * lo_c[None, :, :] + hi_c[:, None, :] * lo_s[None, :, :]
-    cos = cos.reshape(length, half).astype(jnp.bfloat16)
-    sin = sin.reshape(length, half).astype(jnp.bfloat16)
+    cos = cos.reshape(half, half).astype(jnp.bfloat16)
+    sin = sin.reshape(half, half).astype(jnp.bfloat16)
     return cos, sin
+
+
+def split(values):
+    high = values.astype(jnp.bfloat16)
+    low = (values - high.astype(jnp.float32)).astype(jnp.bfloat16)
+    return jnp.concatenate([high, low], axis=0)
+
+
+def forward_transform(rows, cos, sin):
+    count, length = rows.shape
+    half = length // 2
+    wide = rows.astype(jnp.float32)
+    front = wide[:, :half]
+    mirror = jnp.concatenate([wide[:, :1], wide[:, : half : -1]], axis=1)
+    first = (jnp.arange(half) == 0)[None, :]
+    even = front + jnp.where(first, 0.0, mirror)
+    odd = front - jnp.where(first, front, mirror)
+    sign = 1.0 - 2.0 * (jnp.arange(half) % 2).astype(jnp.float32)
+    real = jnp.dot(split(even), cos, preferred_element_type=jnp.float32)
+    imag = jnp.dot(split(odd), sin, preferred_element_type=jnp.float32)
+    real = real[:count] + real[count:] + wide[:, half : half + 1] * sign[None, :]
+    imag = -(imag[:count] + imag[count:])
+    return jnp.concatenate([real, imag], axis=-1)
 
 
 def inverse_transform(cross, lags):
@@ -145,14 +168,7 @@
     block = gather(block, "seg")
     segs = block.shape[0]
     cos, sin = make_forward(length)
-    flat_rows = block.reshape(segs * block.shape[1], length)
-    spectra = jnp.concatenate(
-        [
-            jnp.dot(flat_rows, cos, preferred_element_type=jnp.float32),
-            -jnp.dot(flat_rows, sin, preferred_element_type=jnp.float32),
-        ],
-        axis=-1,
-    )
+    spectra = forward_transform(block.reshape(segs * block.shape[1], length), cos, sin)
     white = whiten(spectra.reshape(block.shape), BAND).astype(jnp.bfloat16)
     chosen = white[:, rows:].reshape(segs, steps, nsrc, length)
     start = lax.axis_index("seg") * per

time: 94 us -> 101 us (1.074)
  local copies, waits for them, and re-layouts: 3.44 us -> 8.96 us
  starting transfers between devices: 61 us -> 65.2 us
  matrix products: 4.75 us -> 1.93 us
  other arithmetic: 11 us -> 9.85 us
    ppermute x6, starting transfers between devices: 44 us -> 48.2 us  [broadcast(): lax.ppermute(block, axis, [(i, i ^ stride) for i in range(count)])]
    unnamed x6 -> x8, local copies, waits for them, and re-layouts: 0.51 us -> 4.64 us
    dot_general x2, matrix products: 3.93 us -> 1.11 us  [the longest x1 0.56 us: forward_transform(): real = jnp.dot(split(even), cos, preferred_element_type=jnp.float32)]
    convert_element_type x0 -> x1, local copies, waits for them, and re-layouts: none -> 1.23 us  [forward_transform(): wide = rows.astype(jnp.float32)]
    convert_element_type x1 -> x3, other arithmetic: 4.88 us -> 3.88 us  [the longest x1 2.69 us: make_forward(): cos = cos.reshape(half, half).astype(jnp.bfloat16)]
  transfers between devices with their start and end apart: 10 -> 10, of which waited for: 7 -> 8; matrix products, arithmetic and copies ran while one was open for 7% -> 4% of each run, Pallas kernels for 0% -> 0%
where the time goes in v13:
time: 101 us; the launch traced here: 99.7 us
  starting transfers between devices  65.2 us (65%)
  waiting for transfers between devices  13.3 us (13%)
  other arithmetic  9.85 us (10%)
  local copies, waits for them, and re-layouts  8.96 us (9%)
  matrix products  1.93 us (2%)
    ppermute x6, starting transfers between devices, broadcast(): lax.ppermute(block, axis, [(i, i ^ stride) for i in range(count)])  48.2 us
    ppermute x2, starting transfers between devices, gather(): partner = lax.ppermute(block, axis, [(i, i ^ stride) for i in range(count)])  11.9 us
    ppermute x6, waiting for transfers between devices, broadcast(): lax.ppermute(block, axis, [(i, i ^ stride) for i in range(count)])  8.65 us
    ppermute x2, waiting for transfers between devices, gather(): partner = lax.ppermute(block, axis, [(i, i ^ stride) for i in range(count)])  4.65 us
    unnamed x8, local copies, waits for them, and re-layouts  4.64 us
    ppermute x1, starting transfers between devices, broadcast(): lax.ppermute(jnp.concatenate([block, rider], axis=1), axis, [(i, i ^ 1) f...  4.38 us
    convert_element_type x1, other arithmetic, make_forward(): cos = cos.reshape(half, half).astype(jnp.bfloat16)  2.69 us
  transfers between devices with their start and end apart: 10, of which 8 were waited for; matrix products, arithmetic and copies ran while one was open for 4% of the time, Pallas kernels for 0%

profile of v13, /device:TPU:1, one launch (start us, length us, event | category | flops | bytes accessed | tf_op | source)
XLA Modules:
  0.0 99.7 jit_solution(5737662600592714298)
XLA Ops:
  0.0 0.7 broadcast_compare_fusion
  0.8 0.8 eq.54
  1.7 0.9 broadcast_select_fusion.1
  2.6 0.9 select_reduce_fusion
  3.5 4.4 %collective-permute-start = (bf16[1,12,2048]{2,1,0:T(8,128)(2,1)S(1)}, bf16[1,12,2048]{2,1,0:T(8,128)(2,1)S(1)}, u32[]{:S(2)}, u32[]{:S(2)}) collective-permute-start(bf16[1,12,2048]{2,1,0:T(8,128)(2,1)S(1)} %pad_maximum_fusion.4), channel_id=1, source_target_pairs={{0,4},{4,0},{8,12},{12,8},{16,20},{20,16},{24,28},{28,24},{32,36},... | collective-permute-start | bytes 147464 | tf_op jit(solution)/shard_map/ppermute | solution.py:17
  7.9 0.7 collective-permute-start.1
  8.6 1.0 %fusion.24 = (f32[64,1024]{1,0:T(8,128)S(1)}, f32[64,1024]{1,0:T(8,128)S(1)}) fusion(), kind=kLoop, calls=%fused_computation.51 | loop fusion | flops 917504 | bytes 524288 | tf_op jit(solution)/shard_map/sin | solution.py:59
  9.6 0.3 fusion.38
  9.9 2.7 %subtract_convert_fusion = (bf16[16,64,1024]{2,1,0:T(8,128)(2,1)S(1)}, bf16[16,64,1024]{2,1,0:T(8,128)(2,1)}) fusion(f32[64,1024]{1,0:T(8,128)S(1)} %get-tuple-element.35, f32[16,1024]{1,0:T(8,128)S(1)} %get-tuple-element.37, f32[64,1024]{1,0:T(8,128)S(1)} %get-tuple-element.36, f32[16,1024]{1,0:T(8,128)S(1)} %get-tuple-element.38), kind=kLoop, calls=%fused_computation.1 | loop fusion | flops 8388608 | bytes 4849664 | tf_op jit(solution)/shard_map/convert_element_type | solution.py:73
  12.7 15.8 %collective-permute-start.2 = (bf16[1,8,2048]{2,1,0:T(8,128)(2,1)S(1)}, bf16[1,8,2048]{2,1,0:T(8,128)(2,1)S(1)}, u32[]{:S(2)}, u32[]{:S(2)}) collective-permute-start(bf16[1,8,2048]{2,1,0:T(8,128)(2,1)S(1)} %slice_add_fusion.2), channel_id=1, source_target_pairs={{0,32},{4,36},{8,40},{12,44},{16,48},{20,52},{24,56},{28,60},{32,0... | collective-permute-start | bytes 98312 | tf_op jit(solution)/shard_map/ppermute | solution.py:24
  28.6 1.3 %collective-permute-done.2 = bf16[1,8,2048]{2,1,0:T(8,128)(2,1)S(1)} collective-permute-done((bf16[1,8,2048]{2,1,0:T(8,128)(2,1)S(1)}, bf16[1,8,2048]{2,1,0:T(8,128)(2,1)S(1)}, u32[]{:S(2)}, u32[]{:S(2)}) %collective-permute-start.2) | collective-permute-done | bytes 32800 | tf_op jit(solution)/shard_map/ppermute | solution.py:24
  30.0 6.2 %collective-permute-start.3 = (bf16[1,8,2048]{2,1,0:T(8,128)(2,1)S(1)}, bf16[1,8,2048]{2,1,0:T(8,128)(2,1)S(1)}, u32[]{:S(2)}, u32[]{:S(2)}) collective-permute-start(bf16[1,8,2048]{2,1,0:T(8,128)(2,1)S(1)} %add.184), channel_id=1, source_target_pairs={{0,16},{4,20},{8,24},{12,28},{16,0},{20,4},{24,8},{28,12},{32,48},... | collective-permute-start | bytes 98312 | tf_op jit(solution)/shard_map/ppermute | solution.py:24
  36.3 2.3 %collective-permute-done.3 = bf16[1,8,2048]{2,1,0:T(8,128)(2,1)S(1)} collective-permute-done((bf16[1,8,2048]{2,1,0:T(8,128)(2,1)S(1)}, bf16[1,8,2048]{2,1,0:T(8,128)(2,1)S(1)}, u32[]{:S(2)}, u32[]{:S(2)}) %collective-permute-start.3) | collective-permute-done | bytes 32800 | tf_op jit(solution)/shard_map/ppermute | solution.py:24
  38.5 4.8 %collective-permute-start.4 = (bf16[1,8,2048]{2,1,0:T(8,128)(2,1)S(1)}, bf16[1,8,2048]{2,1,0:T(8,128)(2,1)S(1)}, u32[]{:S(2)}, u32[]{:S(2)}) collective-permute-start(bf16[1,8,2048]{2,1,0:T(8,128)(2,1)S(1)} %add.185), channel_id=1, source_target_pairs={{0,8},{4,12},{8,0},{12,4},{16,24},{20,28},{24,16},{28,20},{32,40},... | collective-permute-start | bytes 98312 | tf_op jit(solution)/shard_map/ppermute | solution.py:24
  43.4 1.3 %collective-permute-done.4 = bf16[1,8,2048]{2,1,0:T(8,128)(2,1)S(1)} collective-permute-done((bf16[1,8,2048]{2,1,0:T(8,128)(2,1)S(1)}, bf16[1,8,2048]{2,1,0:T(8,128)(2,1)S(1)}, u32[]{:S(2)}, u32[]{:S(2)}) %collective-permute-start.4) | collective-permute-done | bytes 32800 | tf_op jit(solution)/shard_map/ppermute | solution.py:24
  44.7 9.7 %collective-permute-start.5 = (bf16[1,8,2048]{2,1,0:T(8,128)(2,1)S(1)}, bf16[1,8,2048]{2,1,0:T(8,128)(2,1)S(1)}, u32[]{:S(2)}, u32[]{:S(2)}) collective-permute-start(bf16[1,8,2048]{2,1,0:T(8,128)(2,1)S(1)} %add.186), channel_id=1, source_target_pairs={{0,64},{4,68},{8,72},{12,76},{16,80},{20,84},{24,88},{28,92},{32,9... | collective-permute-start | bytes 98312 | tf_op jit(solution)/shard_map/ppermute | solution.py:24
  54.4 1.3 %collective-permute-done.5 = bf16[1,8,2048]{2,1,0:T(8,128)(2,1)S(1)} collective-permute-done((bf16[1,8,2048]{2,1,0:T(8,128)(2,1)S(1)}, bf16[1,8,2048]{2,1,0:T(8,128)(2,1)S(1)}, u32[]{:S(2)}, u32[]{:S(2)}) %collective-permute-start.5) | collective-permute-done | bytes 32800 | tf_op jit(solution)/shard_map/ppermute | solution.py:24
  55.7 6.7 %collective-permute-start.6 = (bf16[1,8,2048]{2,1,0:T(8,128)(2,1)S(1)}, bf16[1,8,2048]{2,1,0:T(8,128)(2,1)S(1)}, u32[]{:S(2)}, u32[]{:S(2)}) collective-permute-start(bf16[1,8,2048]{2,1,0:T(8,128)(2,1)S(1)} %add.187), channel_id=1, source_target_pairs={{0,128},{4,132},{8,136},{12,140},{16,144},{20,148},{24,152},{28,15... | collective-permute-start | bytes 98312 | tf_op jit(solution)/shard_map/ppermute | solution.py:24
  62.4 1.3 %collective-permute-done.6 = bf16[1,8,2048]{2,1,0:T(8,128)(2,1)S(1)} collective-permute-done((bf16[1,8,2048]{2,1,0:T(8,128)(2,1)S(1)}, bf16[1,8,2048]{2,1,0:T(8,128)(2,1)S(1)}, u32[]{:S(2)}, u32[]{:S(2)}) %collective-permute-start.6) | collective-permute-done | bytes 32800 | tf_op jit(solution)/shard_map/ppermute | solution.py:24
  63.7 5.0 %collective-permute-start.7 = (bf16[1,8,2048]{2,1,0:T(8,128)(2,1)S(1)}, bf16[1,8,2048]{2,1,0:T(8,128)(2,1)S(1)}, u32[]{:S(2)}, u32[]{:S(2)}) collective-permute-start(bf16[1,8,2048]{2,1,0:T(8,128)(2,1)S(1)} %add.188), channel_id=1, source_target_pairs={{0,256},{4,260},{8,264},{12,268},{16,272},{20,276},{24,280},{28,28... | collective-permute-start | bytes 98312 | tf_op jit(solution)/shard_map/ppermute | solution.py:24
  68.7 1.3 %collective-permute-done.7 = bf16[1,8,2048]{2,1,0:T(8,128)(2,1)S(1)} collective-permute-done((bf16[1,8,2048]{2,1,0:T(8,128)(2,1)S(1)}, bf16[1,8,2048]{2,1,0:T(8,128)(2,1)S(1)}, u32[]{:S(2)}, u32[]{:S(2)}) %collective-permute-start.7) | collective-permute-done | bytes 32800 | tf_op jit(solution)/shard_map/ppermute | solution.py:24
  70.1 1.9 %collective-permute-start.8 = (bf16[1,23,2048]{2,1,0:T(8,128)(2,1)S(1)}, bf16[1,23,2048]{2,1,0:T(8,128)(2,1)S(1)}, u32[]{:S(2)}, u32[]{:S(2)}) collective-permute-start(bf16[1,23,2048]{2,1,0:T(8,128)(2,1)S(1)} %pad_maximum_fusion.3), channel_id=1, source_target_pairs={{0,2},{1,3},{2,0},{3,1},{4,6},{5,7},{6,4},{7,5},{8,10},{9,11},{10,... | collective-permute-start | bytes 282632 | tf_op jit(solution)/shard_map/ppermute | solution.py:32
  72.0 3.7 %collective-permute-done.8 = bf16[1,23,2048]{2,1,0:T(8,128)(2,1)S(1)} collective-permute-done((bf16[1,23,2048]{2,1,0:T(8,128)(2,1)S(1)}, bf16[1,23,2048]{2,1,0:T(8,128)(2,1)S(1)}, u32[]{:S(2)}, u32[]{:S(2)}) %collective-permute-start.8) | collective-permute-done | bytes 94240 | tf_op jit(solution)/shard_map/ppermute | solution.py:32
  75.8 9.9 %collective-permute-start.9 = (bf16[2,23,2048]{2,1,0:T(8,128)(2,1)S(1)}, bf16[2,23,2048]{2,1,0:T(8,128)(2,1)S(1)}, u32[]{:S(2)}, u32[]{:S(2)}) collective-permute-start(bf16[2,23,2048]{2,1,0:T(8,128)(2,1)S(1)} %pad_maximum_fusion.2), channel_id=1, source_target_pairs={{0,1},{1,0},{2,3},{3,2},{4,5},{5,4},{6,7},{7,6},{8,9},{9,8},{10,11... | collective-permute-start | bytes 565256 | tf_op jit(solution)/shard_map/ppermute | solution.py:32
  85.8 1.0 collective-permute-done.9
  86.8 1.0 maximum_convert_fusion
  87.8 1.2 %reshape.244 = f32[92,2048]{1,0:T(8,128)S(1)} reshape(f32[4,23,2048]{2,1,0:T(8,128)} %maximum_convert_fusion) | data formatting | bytes 1507328 | tf_op jit(solution)/shard_map/convert_element_type | solution.py:87
  89.0 0.2 slice.125
  89.3 3.0 %reverse = f32[92,1024]{1,0:T(8,128)} reverse(f32[92,1024]{1,0:T(8,128)S(1)} %bitcast.38), dimensions={1} | reverse | bytes 753664
  92.2 1.3 %slice.179 = f32[92,1023]{1,0:T(8,128)S(1)} slice(f32[92,1024]{1,0:T(8,128)} %reverse), slice={[0:92], [1:1024]} | slice | bytes 752928
  93.5 0.2 subtract_convert_fusion.2
  93.8 0.2 copy-done
  93.9 0.6 fusion.10
  94.6 0.6 fusion.6
  95.2 0.2 fusion.79
  95.4 0.1 copy.21
  95.6 0.2 reduce_sum.61
  95.8 0.2 mul.448
  96.5 0.4 bitcast_convert_fusion
  96.9 0.3 multiply_reduce_fusion.3
  97.3 0.2 add.209
  97.4 0.1 copy.19
  97.7 0.2 sub.42
  97.8 0.1 copy.20
  98.0 0.4 fusion.17
  98.4 0.1 multiply_subtract_fusion
  98.5 0.4 fusion
  98.9 0.7 mul.485
  (44 shorter events, 1.7 us)
Async XLA Ops:
  3.5 9.2 %collective-permute-start = (bf16[1,12,2048]{2,1,0:T(8,128)(2,1)S(1)}, bf16[1,12,2048]{2,1,0:T(8,128)(2,1)S(1)}, u32[]{:S(2)}, u32[]{:S(2)}) collective-permute-start(bf16[1,12,2048]{2,1,0:T(8,128)(2,1)S(1)} %pad_maximum_fusion.4), channel_id=1, source_target_pairs={{0,4},{4,0},{8,12},{12,8},{16,20},{20,16},{24,28},{28,24},{32,36},... | collective-permute-start | bytes 147464 | tf_op jit(solution)/shard_map/ppermute | solution.py:17
  7.9 54.5 %collective-permute-start.1 = (bf16[1,4,2048]{2,1,0:T(4,128)(2,1)S(1)}, bf16[1,4,2048]{2,1,0:T(4,128)(2,1)S(1)}, u32[]{:S(2)}, u32[]{:S(2)}) collective-permute-start(bf16[1,4,2048]{2,1,0:T(4,128)(2,1)S(1)} %get-tuple-element.31), channel_id=1, source_target_pairs={{4,8},{8,4},{12,16},{16,12},{20,24},{24,20},{28,32},{32,28},{36,40... | collective-permute-start | bytes 49160 | tf_op jit(solution)/shard_map/ppermute | solution.py:48
  9.9 60.1 %copy-start.1 = (bf16[1,8,2048]{2,1,0:T(8,128)(2,1)S(1)}, bf16[1,8,2048]{2,1,0:T(8,128)(2,1)}, u32[]{:S(2)}) copy-start(bf16[1,8,2048]{2,1,0:T(8,128)(2,1)} %param.3) | copy-start | bytes 98308
  12.7 17.2 %collective-permute-start.2 = (bf16[1,8,2048]{2,1,0:T(8,128)(2,1)S(1)}, bf16[1,8,2048]{2,1,0:T(8,128)(2,1)S(1)}, u32[]{:S(2)}, u32[]{:S(2)}) collective-permute-start(bf16[1,8,2048]{2,1,0:T(8,128)(2,1)S(1)} %slice_add_fusion.2), channel_id=1, source_target_pairs={{0,32},{4,36},{8,40},{12,44},{16,48},{20,52},{24,56},{28,60},{32,0... | collective-permute-start | bytes 98312 | tf_op jit(solution)/shard_map/ppermute | solution.py:24
  30.0 8.6 %collective-permute-start.3 = (bf16[1,8,2048]{2,1,0:T(8,128)(2,1)S(1)}, bf16[1,8,2048]{2,1,0:T(8,128)(2,1)S(1)}, u32[]{:S(2)}, u32[]{:S(2)}) collective-permute-start(bf16[1,8,2048]{2,1,0:T(8,128)(2,1)S(1)} %add.184), channel_id=1, source_target_pairs={{0,16},{4,20},{8,24},{12,28},{16,0},{20,4},{24,8},{28,12},{32,48},... | collective-permute-start | bytes 98312 | tf_op jit(solution)/shard_map/ppermute | solution.py:24
  38.5 6.1 %collective-permute-start.4 = (bf16[1,8,2048]{2,1,0:T(8,128)(2,1)S(1)}, bf16[1,8,2048]{2,1,0:T(8,128)(2,1)S(1)}, u32[]{:S(2)}, u32[]{:S(2)}) collective-permute-start(bf16[1,8,2048]{2,1,0:T(8,128)(2,1)S(1)} %add.185), channel_id=1, source_target_pairs={{0,8},{4,12},{8,0},{12,4},{16,24},{20,28},{24,16},{28,20},{32,40},... | collective-permute-start | bytes 98312 | tf_op jit(solution)/shard_map/ppermute | solution.py:24
  44.7 11.0 %collective-permute-start.5 = (bf16[1,8,2048]{2,1,0:T(8,128)(2,1)S(1)}, bf16[1,8,2048]{2,1,0:T(8,128)(2,1)S(1)}, u32[]{:S(2)}, u32[]{:S(2)}) collective-permute-start(bf16[1,8,2048]{2,1,0:T(8,128)(2,1)S(1)} %add.186), channel_id=1, source_target_pairs={{0,64},{4,68},{8,72},{12,76},{16,80},{20,84},{24,88},{28,92},{32,9... | collective-permute-start | bytes 98312 | tf_op jit(solution)/shard_map/ppermute | solution.py:24
  55.7 8.0 %collective-permute-start.6 = (bf16[1,8,2048]{2,1,0:T(8,128)(2,1)S(1)}, bf16[1,8,2048]{2,1,0:T(8,128)(2,1)S(1)}, u32[]{:S(2)}, u32[]{:S(2)}) collective-permute-start(bf16[1,8,2048]{2,1,0:T(8,128)(2,1)S(1)} %add.187), channel_id=1, source_target_pairs={{0,128},{4,132},{8,136},{12,140},{16,144},{20,148},{24,152},{28,15... | collective-permute-start | bytes 98312 | tf_op jit(solution)/shard_map/ppermute | solution.py:24
  63.7 6.3 %collective-permute-start.7 = (bf16[1,8,2048]{2,1,0:T(8,128)(2,1)S(1)}, bf16[1,8,2048]{2,1,0:T(8,128)(2,1)S(1)}, u32[]{:S(2)}, u32[]{:S(2)}) collective-permute-start(bf16[1,8,2048]{2,1,0:T(8,128)(2,1)S(1)} %add.188), channel_id=1, source_target_pairs={{0,256},{4,260},{8,264},{12,268},{16,272},{20,276},{24,280},{28,28... | collective-permute-start | bytes 98312 | tf_op jit(solution)/shard_map/ppermute | solution.py:24
  70.1 5.7 %collective-permute-start.8 = (bf16[1,23,2048]{2,1,0:T(8,128)(2,1)S(1)}, bf16[1,23,2048]{2,1,0:T(8,128)(2,1)S(1)}, u32[]{:S(2)}, u32[]{:S(2)}) collective-permute-start(bf16[1,23,2048]{2,1,0:T(8,128)(2,1)S(1)} %pad_maximum_fusion.3), channel_id=1, source_target_pairs={{0,2},{1,3},{2,0},{3,1},{4,6},{5,7},{6,4},{7,5},{8,10},{9,11},{10,... | collective-permute-start | bytes 282632 | tf_op jit(solution)/shard_map/ppermute | solution.py:32
  75.8 11.0 %collective-permute-start.9 = (bf16[2,23,2048]{2,1,0:T(8,128)(2,1)S(1)}, bf16[2,23,2048]{2,1,0:T(8,128)(2,1)S(1)}, u32[]{:S(2)}, u32[]{:S(2)}) collective-permute-start(bf16[2,23,2048]{2,1,0:T(8,128)(2,1)S(1)} %pad_maximum_fusion.2), channel_id=1, source_target_pairs={{0,1},{1,0},{2,3},{3,2},{4,5},{5,4},{6,7},{7,6},{8,9},{9,8},{10,11... | collective-permute-start | bytes 565256 | tf_op jit(solution)/shard_map/ppermute | solution.py:32
  92.2 1.7 %copy-start = (bf16[16,64,1024]{2,1,0:T(8,128)(2,1)S(1)}, bf16[16,64,1024]{2,1,0:T(8,128)(2,1)}, u32[]{:S(2)}) copy-start(bf16[16,64,1024]{2,1,0:T(8,128)(2,1)} %get-tuple-element.22) | copy-start | bytes 6291460

commit v14 on v12

--- a/solution.py
+++ b/solution.py
@@ -75,6 +75,31 @@
     return cos, sin
 
 
+def chunked_forward(rows, length, pieces):
+    half = length // 2
+    lo_count = 64
+    hi_count = length // lo_count
+    step = hi_count // pieces
+    freqs = jnp.arange(half, dtype=jnp.int32)
+    lo = jnp.arange(lo_count, dtype=jnp.int32)
+    lo_c, lo_s = cos_sin(lo[:, None] * freqs[None, :] % length, length)
+    real = None
+    imag = None
+    for piece in range(pieces):
+        hi = jnp.arange(piece * step, (piece + 1) * step, dtype=jnp.int32)
+        hi_c, hi_s = cos_sin(hi[:, None] * freqs[None, :] % hi_count, hi_count)
+        cos = hi_c[:, None, :] * lo_c[None, :, :] - hi_s[:, None, :] * lo_s[None, :, :]
+        sin = hi_s[:, None, :] * lo_c[None, :, :] + hi_c[:, None, :] * lo_s[None, :, :]
+        cos = cos.reshape(step * lo_count, half).astype(jnp.bfloat16)
+        sin = sin.reshape(step * lo_count, half).astype(jnp.bfloat16)
+        part = rows[:, piece * step * lo_count : (piece + 1) * step * lo_count]
+        re = jnp.dot(part, cos, preferred_element_type=jnp.float32)
+        im = jnp.dot(part, sin, preferred_element_type=jnp.float32)
+        real = re if real is None else real + re
+        imag = im if imag is None else imag + im
+    return jnp.concatenate([real, -imag], axis=-1)
+
+
 def inverse_transform(cross, lags):
     count, length = cross.shape
     half = length // 2
@@ -144,15 +169,7 @@
     block = jnp.concatenate([window, received], axis=1)
     block = gather(block, "seg")
     segs = block.shape[0]
-    cos, sin = make_forward(length)
-    flat_rows = block.reshape(segs * block.shape[1], length)
-    spectra = jnp.concatenate(
-        [
-            jnp.dot(flat_rows, cos, preferred_element_type=jnp.float32),
-            -jnp.dot(flat_rows, sin, preferred_element_type=jnp.float32),
-        ],
-        axis=-1,
-    )
+    spectra = chunked_forward(block.reshape(segs * block.shape[1], length), length, 4)
     white = whiten(spectra.reshape(block.shape), BAND).astype(jnp.bfloat16)
     chosen = white[:, rows:].reshape(segs, steps, nsrc, length)
     start = lax.axis_index("seg") * per

time: 94 us -> 97.3 us (1.035)
  local copies, waits for them, and re-layouts: 3.44 us -> 6.98 us
  other arithmetic: 11 us -> 13.4 us
  waiting for transfers between devices: 12.5 us -> 10.2 us
  matrix products: 4.75 us -> 3.29 us
    unnamed x6 -> x26, local copies, waits for them, and re-layouts: 0.51 us -> 3.06 us
    ppermute x6, waiting for transfers between devices: 7.91 us -> 6.11 us  [broadcast(): lax.ppermute(block, axis, [(i, i ^ stride) for i in range(count)])]
    dot_general x2 -> x8, matrix products: 3.93 us -> 2.47 us  [the longest x4 1.24 us: chunked_forward(): re = jnp.dot(part, cos, preferred_element_type=jnp.float32)]
    cos x1 -> x3, other arithmetic: 0.09 us -> 1.24 us  [cos_sin(): return (jnp.cos(angle), jnp.sin(angle))]
    reshape x1, local copies, waits for them, and re-layouts: 0.11 us -> 1.1 us  [shards(): block.reshape(segs * block.shape[1], length)]
  transfers between devices with their start and end apart: 10 -> 10, of which waited for: 7 -> 7; matrix products, arithmetic and copies ran while one was open for 7% -> 9% of each run, Pallas kernels for 0% -> 0%
where the time goes in v14:
time: 97.3 us; the launch traced here: 96.3 us
  starting transfers between devices  61.9 us (64%)
  other arithmetic  13.4 us (14%)
  waiting for transfers between devices  10.2 us (10%)
  local copies, waits for them, and re-layouts  6.98 us (7%)
  matrix products  3.29 us (3%)
    ppermute x6, starting transfers between devices, broadcast(): lax.ppermute(block, axis, [(i, i ^ stride) for i in range(count)])  45 us
    ppermute x2, starting transfers between devices, gather(): partner = lax.ppermute(block, axis, [(i, i ^ stride) for i in range(count)])  11.9 us
    ppermute x6, waiting for transfers between devices, broadcast(): lax.ppermute(block, axis, [(i, i ^ stride) for i in range(count)])  6.11 us
    ppermute x1, starting transfers between devices, broadcast(): lax.ppermute(jnp.concatenate([block, rider], axis=1), axis, [(i, i ^ 1) f...  4.38 us
    ppermute x2, waiting for transfers between devices, gather(): partner = lax.ppermute(block, axis, [(i, i ^ stride) for i in range(count)])  4.05 us
    convert_element_type x1, other arithmetic, chunked_forward(): cos = cos.reshape(step * lo_count, half).astype(jnp.bfloat16)  3.91 us
    unnamed x26, local copies, waits for them, and re-layouts  3.06 us
  transfers between devices with their start and end apart: 10, of which 7 were waited for; matrix products, arithmetic and copies ran while one was open for 9% of the time, Pallas kernels for 0%

profile of v14, /device:TPU:1, one launch (start us, length us, event | category | flops | bytes accessed | tf_op | source)
XLA Modules:
  0.0 96.3 jit_solution(11746698199426336105)
XLA Ops:
  0.0 0.8 eq.43
  0.8 0.7 broadcast_compare_fusion
  1.7 0.9 broadcast_select_fusion.1
  2.6 0.9 select_reduce_fusion
  3.5 4.4 %collective-permute-start = (bf16[1,12,2048]{2,1,0:T(8,128)(2,1)S(1)}, bf16[1,12,2048]{2,1,0:T(8,128)(2,1)S(1)}, u32[]{:S(2)}, u32[]{:S(2)}) collective-permute-start(bf16[1,12,2048]{2,1,0:T(8,128)(2,1)S(1)} %pad_maximum_fusion.4), channel_id=1, source_target_pairs={{0,4},{4,0},{8,12},{12,8},{16,20},{20,16},{24,28},{28,24},{32,36},... | collective-permute-start | bytes 147464 | tf_op jit(solution)/shard_map/ppermute | solution.py:17
  7.9 0.7 collective-permute-start.1
  8.6 1.0 %fusion.15 = (f32[64,1024]{1,0:T(8,128)S(1)}, f32[64,1024]{1,0:T(8,128)S(1)}) fusion(), kind=kLoop, calls=%fused_computation.47 | loop fusion | flops 917504 | bytes 524288 | tf_op jit(solution)/shard_map/sin | solution.py:59
  9.7 0.2 fusion.74
  9.9 0.3 fusion.70
  10.4 15.8 %collective-permute-start.2 = (bf16[1,8,2048]{2,1,0:T(8,128)(2,1)S(1)}, bf16[1,8,2048]{2,1,0:T(8,128)(2,1)S(1)}, u32[]{:S(2)}, u32[]{:S(2)}) collective-permute-start(bf16[1,8,2048]{2,1,0:T(8,128)(2,1)S(1)} %slice_add_fusion), channel_id=1, source_target_pairs={{0,32},{4,36},{8,40},{12,44},{16,48},{20,52},{24,56},{28,60},{32,0... | collective-permute-start | bytes 98312 | tf_op jit(solution)/shard_map/ppermute | solution.py:24
  26.2 3.9 %subtract_convert_fusion = (bf16[8,64,1024]{2,1,0:T(8,128)(2,1)S(1)}, bf16[8,64,1024]{2,1,0:T(8,128)(2,1)}, bf16[8,64,1024]{2,1,0:T(8,128)(2,1)S(1)}, bf16[8,64,...) fusion(f32[8,1024]{1,0:T(8,128)S(1)} %get-tuple-element.40, ...), kind=kLoop, calls=%fused_computation.4 | loop fusion | flops 16777216 | bytes 9175040 | tf_op jit(solution)/shard_map/convert_element_type | solution.py:93
  30.2 5.9 %collective-permute-start.3 = (bf16[1,8,2048]{2,1,0:T(8,128)(2,1)S(1)}, bf16[1,8,2048]{2,1,0:T(8,128)(2,1)S(1)}, u32[]{:S(2)}, u32[]{:S(2)}) collective-permute-start(bf16[1,8,2048]{2,1,0:T(8,128)(2,1)S(1)} %add.273), channel_id=1, source_target_pairs={{0,16},{4,20},{8,24},{12,28},{16,0},{20,4},{24,8},{28,12},{32,48},... | collective-permute-start | bytes 98312 | tf_op jit(solution)/shard_map/ppermute | solution.py:24
  36.1 0.7 fusion.82
  36.8 1.9 %collective-permute-done.3 = bf16[1,8,2048]{2,1,0:T(8,128)(2,1)S(1)} collective-permute-done((bf16[1,8,2048]{2,1,0:T(8,128)(2,1)S(1)}, bf16[1,8,2048]{2,1,0:T(8,128)(2,1)S(1)}, u32[]{:S(2)}, u32[]{:S(2)}) %collective-permute-start.3) | collective-permute-done | bytes 32800 | tf_op jit(solution)/shard_map/ppermute | solution.py:24
  38.7 3.8 %collective-permute-start.4 = (bf16[1,8,2048]{2,1,0:T(8,128)(2,1)S(1)}, bf16[1,8,2048]{2,1,0:T(8,128)(2,1)S(1)}, u32[]{:S(2)}, u32[]{:S(2)}) collective-permute-start(bf16[1,8,2048]{2,1,0:T(8,128)(2,1)S(1)} %add.274), channel_id=1, source_target_pairs={{0,8},{4,12},{8,0},{12,4},{16,24},{20,28},{24,16},{28,20},{32,40},... | collective-permute-start | bytes 98312 | tf_op jit(solution)/shard_map/ppermute | solution.py:24
  42.6 0.7 fusion.89
  43.3 1.0 %collective-permute-done.4 = bf16[1,8,2048]{2,1,0:T(8,128)(2,1)S(1)} collective-permute-done((bf16[1,8,2048]{2,1,0:T(8,128)(2,1)S(1)}, bf16[1,8,2048]{2,1,0:T(8,128)(2,1)S(1)}, u32[]{:S(2)}, u32[]{:S(2)}) %collective-permute-start.4) | collective-permute-done | bytes 32800 | tf_op jit(solution)/shard_map/ppermute | solution.py:24
  44.3 8.5 %collective-permute-start.5 = (bf16[1,8,2048]{2,1,0:T(8,128)(2,1)S(1)}, bf16[1,8,2048]{2,1,0:T(8,128)(2,1)S(1)}, u32[]{:S(2)}, u32[]{:S(2)}) collective-permute-start(bf16[1,8,2048]{2,1,0:T(8,128)(2,1)S(1)} %add.275), channel_id=1, source_target_pairs={{0,64},{4,68},{8,72},{12,76},{16,80},{20,84},{24,88},{28,92},{32,9... | collective-permute-start | bytes 98312 | tf_op jit(solution)/shard_map/ppermute | solution.py:24
  52.8 0.7 sine_negate_fusion
  53.5 0.6 collective-permute-done.5
  54.1 6.0 %collective-permute-start.6 = (bf16[1,8,2048]{2,1,0:T(8,128)(2,1)S(1)}, bf16[1,8,2048]{2,1,0:T(8,128)(2,1)S(1)}, u32[]{:S(2)}, u32[]{:S(2)}) collective-permute-start(bf16[1,8,2048]{2,1,0:T(8,128)(2,1)S(1)} %add.276), channel_id=1, source_target_pairs={{0,128},{4,132},{8,136},{12,140},{16,144},{20,148},{24,152},{28,15... | collective-permute-start | bytes 98312 | tf_op jit(solution)/shard_map/ppermute | solution.py:24
  60.1 1.3 %collective-permute-done.6 = bf16[1,8,2048]{2,1,0:T(8,128)(2,1)S(1)} collective-permute-done((bf16[1,8,2048]{2,1,0:T(8,128)(2,1)S(1)}, bf16[1,8,2048]{2,1,0:T(8,128)(2,1)S(1)}, u32[]{:S(2)}, u32[]{:S(2)}) %collective-permute-start.6) | collective-permute-done | bytes 32800 | tf_op jit(solution)/shard_map/ppermute | solution.py:24
  61.4 5.0 %collective-permute-start.7 = (bf16[1,8,2048]{2,1,0:T(8,128)(2,1)S(1)}, bf16[1,8,2048]{2,1,0:T(8,128)(2,1)S(1)}, u32[]{:S(2)}, u32[]{:S(2)}) collective-permute-start(bf16[1,8,2048]{2,1,0:T(8,128)(2,1)S(1)} %add.277), channel_id=1, source_target_pairs={{0,256},{4,260},{8,264},{12,268},{16,272},{20,276},{24,280},{28,28... | collective-permute-start | bytes 98312 | tf_op jit(solution)/shard_map/ppermute | solution.py:24
  66.4 1.3 %collective-permute-done.7 = bf16[1,8,2048]{2,1,0:T(8,128)(2,1)S(1)} collective-permute-done((bf16[1,8,2048]{2,1,0:T(8,128)(2,1)S(1)}, bf16[1,8,2048]{2,1,0:T(8,128)(2,1)S(1)}, u32[]{:S(2)}, u32[]{:S(2)}) %collective-permute-start.7) | collective-permute-done | bytes 32800 | tf_op jit(solution)/shard_map/ppermute | solution.py:24
  67.8 1.9 %collective-permute-start.8 = (bf16[1,23,2048]{2,1,0:T(8,128)(2,1)S(1)}, bf16[1,23,2048]{2,1,0:T(8,128)(2,1)S(1)}, u32[]{:S(2)}, u32[]{:S(2)}) collective-permute-start(bf16[1,23,2048]{2,1,0:T(8,128)(2,1)S(1)} %pad_maximum_fusion.3), channel_id=1, source_target_pairs={{0,2},{1,3},{2,0},{3,1},{4,6},{5,7},{6,4},{7,5},{8,10},{9,11},{10,... | collective-permute-start | bytes 282632 | tf_op jit(solution)/shard_map/ppermute | solution.py:32
  69.7 3.7 %collective-permute-done.8 = bf16[1,23,2048]{2,1,0:T(8,128)(2,1)S(1)} collective-permute-done((bf16[1,23,2048]{2,1,0:T(8,128)(2,1)S(1)}, bf16[1,23,2048]{2,1,0:T(8,128)(2,1)S(1)}, u32[]{:S(2)}, u32[]{:S(2)}) %collective-permute-start.8) | collective-permute-done | bytes 94240 | tf_op jit(solution)/shard_map/ppermute | solution.py:32
  73.5 9.9 %collective-permute-start.9 = (bf16[2,23,2048]{2,1,0:T(8,128)(2,1)S(1)}, bf16[2,23,2048]{2,1,0:T(8,128)(2,1)S(1)}, u32[]{:S(2)}, u32[]{:S(2)}) collective-permute-start(bf16[2,23,2048]{2,1,0:T(8,128)(2,1)S(1)} %pad_maximum_fusion.2), channel_id=1, source_target_pairs={{0,1},{1,0},{2,3},{3,2},{4,5},{5,4},{6,7},{7,6},{8,9},{9,8},{10,11... | collective-permute-start | bytes 565256 | tf_op jit(solution)/shard_map/ppermute | solution.py:32
  83.4 0.7 fusion.85
  84.1 0.4 collective-permute-done.9
  84.5 0.8 pad_maximum_fusion.1
  85.3 1.1 %reshape.435 = bf16[92,2048]{1,0:T(8,128)(2,1)S(1)} reshape(bf16[4,23,2048]{2,1,0:T(8,128)(2,1)} %pad_maximum_fusion.1) | data formatting | bytes 753664 | tf_op jit(solution)/shard_map/reshape | solution.py:172
  86.4 0.3 fusion.21
  86.7 0.3 fusion.23
  87.0 0.9 copy-done.4
  87.9 0.3 convolution_add_fusion.2
  88.3 0.3 convolution_add_fusion.1
  88.6 0.8 copy-done.2
  89.5 0.3 fusion
  89.9 0.3 convolution_add_fusion.5
  90.3 0.8 copy-done
  91.1 0.3 convolution_add_fusion.4
  91.4 0.3 convolution_add_fusion.3
  92.2 0.2 reduce_sum.61
  92.9 0.4 bitcast_convert_fusion
  93.4 0.3 multiply_reduce_fusion.3
  94.5 0.4 fusion.8
  95.2 0.4 fusion.1
  95.6 0.7 mul.822
  (66 shorter events, 2.8 us)
Async XLA Ops:
  3.5 6.8 %collective-permute-start = (bf16[1,12,2048]{2,1,0:T(8,128)(2,1)S(1)}, bf16[1,12,2048]{2,1,0:T(8,128)(2,1)S(1)}, u32[]{:S(2)}, u32[]{:S(2)}) collective-permute-start(bf16[1,12,2048]{2,1,0:T(8,128)(2,1)S(1)} %pad_maximum_fusion.4), channel_id=1, source_target_pairs={{0,4},{4,0},{8,12},{12,8},{16,20},{20,16},{24,28},{28,24},{32,36},... | collective-permute-start | bytes 147464 | tf_op jit(solution)/shard_map/ppermute | solution.py:17
  7.9 52.2 %collective-permute-start.1 = (bf16[1,4,2048]{2,1,0:T(4,128)(2,1)S(1)}, bf16[1,4,2048]{2,1,0:T(4,128)(2,1)S(1)}, u32[]{:S(2)}, u32[]{:S(2)}) collective-permute-start(bf16[1,4,2048]{2,1,0:T(4,128)(2,1)S(1)} %get-tuple-element.35), channel_id=1, source_target_pairs={{4,8},{8,4},{12,16},{16,12},{20,24},{24,20},{28,32},{32,28},{36,40... | collective-permute-start | bytes 49160 | tf_op jit(solution)/shard_map/ppermute | solution.py:48
  10.4 19.7 %collective-permute-start.2 = (bf16[1,8,2048]{2,1,0:T(8,128)(2,1)S(1)}, bf16[1,8,2048]{2,1,0:T(8,128)(2,1)S(1)}, u32[]{:S(2)}, u32[]{:S(2)}) collective-permute-start(bf16[1,8,2048]{2,1,0:T(8,128)(2,1)S(1)} %slice_add_fusion), channel_id=1, source_target_pairs={{0,32},{4,36},{8,40},{12,44},{16,48},{20,52},{24,56},{28,60},{32,0... | collective-permute-start | bytes 98312 | tf_op jit(solution)/shard_map/ppermute | solution.py:24
  26.2 41.5 %copy-start.5 = (bf16[1,8,2048]{2,1,0:T(8,128)(2,1)S(1)}, bf16[1,8,2048]{2,1,0:T(8,128)(2,1)}, u32[]{:S(2)}) copy-start(bf16[1,8,2048]{2,1,0:T(8,128)(2,1)} %param.3) | copy-start | bytes 98308
  30.2 8.6 %collective-permute-start.3 = (bf16[1,8,2048]{2,1,0:T(8,128)(2,1)S(1)}, bf16[1,8,2048]{2,1,0:T(8,128)(2,1)S(1)}, u32[]{:S(2)}, u32[]{:S(2)}) collective-permute-start(bf16[1,8,2048]{2,1,0:T(8,128)(2,1)S(1)} %add.273), channel_id=1, source_target_pairs={{0,16},{4,20},{8,24},{12,28},{16,0},{20,4},{24,8},{28,12},{32,48},... | collective-permute-start | bytes 98312 | tf_op jit(solution)/shard_map/ppermute | solution.py:24
  38.7 5.6 %collective-permute-start.4 = (bf16[1,8,2048]{2,1,0:T(8,128)(2,1)S(1)}, bf16[1,8,2048]{2,1,0:T(8,128)(2,1)S(1)}, u32[]{:S(2)}, u32[]{:S(2)}) collective-permute-start(bf16[1,8,2048]{2,1,0:T(8,128)(2,1)S(1)} %add.274), channel_id=1, source_target_pairs={{0,8},{4,12},{8,0},{12,4},{16,24},{20,28},{24,16},{28,20},{32,40},... | collective-permute-start | bytes 98312 | tf_op jit(solution)/shard_map/ppermute | solution.py:24
  44.3 9.8 %collective-permute-start.5 = (bf16[1,8,2048]{2,1,0:T(8,128)(2,1)S(1)}, bf16[1,8,2048]{2,1,0:T(8,128)(2,1)S(1)}, u32[]{:S(2)}, u32[]{:S(2)}) collective-permute-start(bf16[1,8,2048]{2,1,0:T(8,128)(2,1)S(1)} %add.275), channel_id=1, source_target_pairs={{0,64},{4,68},{8,72},{12,76},{16,80},{20,84},{24,88},{28,92},{32,9... | collective-permute-start | bytes 98312 | tf_op jit(solution)/shard_map/ppermute | solution.py:24
  54.1 7.3 %collective-permute-start.6 = (bf16[1,8,2048]{2,1,0:T(8,128)(2,1)S(1)}, bf16[1,8,2048]{2,1,0:T(8,128)(2,1)S(1)}, u32[]{:S(2)}, u32[]{:S(2)}) collective-permute-start(bf16[1,8,2048]{2,1,0:T(8,128)(2,1)S(1)} %add.276), channel_id=1, source_target_pairs={{0,128},{4,132},{8,136},{12,140},{16,144},{20,148},{24,152},{28,15... | collective-permute-start | bytes 98312 | tf_op jit(solution)/shard_map/ppermute | solution.py:24
  61.4 6.3 %collective-permute-start.7 = (bf16[1,8,2048]{2,1,0:T(8,128)(2,1)S(1)}, bf16[1,8,2048]{2,1,0:T(8,128)(2,1)S(1)}, u32[]{:S(2)}, u32[]{:S(2)}) collective-permute-start(bf16[1,8,2048]{2,1,0:T(8,128)(2,1)S(1)} %add.277), channel_id=1, source_target_pairs={{0,256},{4,260},{8,264},{12,268},{16,272},{20,276},{24,280},{28,28... | collective-permute-start | bytes 98312 | tf_op jit(solution)/shard_map/ppermute | solution.py:24
  67.8 5.7 %collective-permute-start.8 = (bf16[1,23,2048]{2,1,0:T(8,128)(2,1)S(1)}, bf16[1,23,2048]{2,1,0:T(8,128)(2,1)S(1)}, u32[]{:S(2)}, u32[]{:S(2)}) collective-permute-start(bf16[1,23,2048]{2,1,0:T(8,128)(2,1)S(1)} %pad_maximum_fusion.3), channel_id=1, source_target_pairs={{0,2},{1,3},{2,0},{3,1},{4,6},{5,7},{6,4},{7,5},{8,10},{9,11},{10,... | collective-permute-start | bytes 282632 | tf_op jit(solution)/shard_map/ppermute | solution.py:32
  73.5 11.0 %collective-permute-start.9 = (bf16[2,23,2048]{2,1,0:T(8,128)(2,1)S(1)}, bf16[2,23,2048]{2,1,0:T(8,128)(2,1)S(1)}, u32[]{:S(2)}, u32[]{:S(2)}) collective-permute-start(bf16[2,23,2048]{2,1,0:T(8,128)(2,1)S(1)} %pad_maximum_fusion.2), channel_id=1, source_target_pairs={{0,1},{1,0},{2,3},{3,2},{4,5},{5,4},{6,7},{7,6},{8,9},{9,8},{10,11... | collective-permute-start | bytes 565256 | tf_op jit(solution)/shard_map/ppermute | solution.py:32
  86.7 1.2 %copy-start.4 = (bf16[8,64,1024]{2,1,0:T(8,128)(2,1)S(1)}, bf16[8,64,1024]{2,1,0:T(8,128)(2,1)}, u32[]{:S(2)}) copy-start(bf16[8,64,1024]{2,1,0:T(8,128)(2,1)} %get-tuple-element.25) | copy-start | bytes 3145732
  87.0 1.3 %copy-start.3 = (bf16[8,64,1024]{2,1,0:T(8,128)(2,1)S(1)}, bf16[8,64,1024]{2,1,0:T(8,128)(2,1)}, u32[]{:S(2)}) copy-start(bf16[8,64,1024]{2,1,0:T(8,128)(2,1)} %get-tuple-element.23) | copy-start | bytes 3145732
  88.2 1.2 %copy-start.2 = (bf16[8,64,1024]{2,1,0:T(8,128)(2,1)S(1)}, bf16[8,64,1024]{2,1,0:T(8,128)(2,1)}, u32[]{:S(2)}) copy-start(bf16[8,64,1024]{2,1,0:T(8,128)(2,1)} %get-tuple-element.14) | copy-start | bytes 3145732
  88.6 1.3 %copy-start.1 = (bf16[8,64,1024]{2,1,0:T(8,128)(2,1)S(1)}, bf16[8,64,1024]{2,1,0:T(8,128)(2,1)}, u32[]{:S(2)}) copy-start(bf16[8,64,1024]{2,1,0:T(8,128)(2,1)} %get-tuple-element.26) | copy-start | bytes 3145732
  89.8 1.3 %copy-start = (bf16[8,64,1024]{2,1,0:T(8,128)(2,1)S(1)}, bf16[8,64,1024]{2,1,0:T(8,128)(2,1)}, u32[]{:S(2)}) copy-start(bf16[8,64,1024]{2,1,0:T(8,128)(2,1)} %get-tuple-element.24) | copy-start | bytes 3145732
  93.7 0.8 copy-start.7
  93.7 0.8 copy-start.8
  93.7 0.8 copy-start.9
  94.0 0.9 copy-start.6
  94.4 0.7 copy-start.10
  94.5 0.7 copy-start.11

commit v15 on v12

--- a/solution.py
+++ b/solution.py
@@ -140,9 +140,44 @@
     rider, far, odd = edges(data, "fibre")
     received, near = broadcast(picked, "fibre", rider)
     window = halo(data, near, far, odd)
-    rows = window.shape[1]
-    block = jnp.concatenate([window, received], axis=1)
-    block = gather(block, "seg")
+    rows = per + LOW + HIGH
+    mine_at = lax.axis_index("seg")
+    if seg_count == 4:
+        span = rows + per
+        lead = lax.dynamic_slice_in_dim(window, 2 * per * (1 - mine_at // 2), span, axis=1)
+        first = lax.ppermute(
+            jnp.concatenate([lead, received], axis=1), "seg", [(i, i ^ 2) for i in range(4)]
+        )
+        far_win, far_src = first[:, :span], first[:, span:]
+        pair = jnp.bitwise_xor(mine_at, 1)
+        base = 2 * per * (mine_at // 2)
+        sent = jnp.concatenate(
+            [
+                jnp.concatenate(
+                    [lax.dynamic_slice_in_dim(window, per * pair, rows, axis=1), received], axis=1
+                ),
+                jnp.concatenate(
+                    [lax.dynamic_slice_in_dim(far_win, per * pair - base, rows, axis=1), far_src],
+                    axis=1,
+                ),
+            ],
+            axis=0,
+        )
+        second = lax.ppermute(sent, "seg", [(i, i ^ 1) for i in range(4)])
+        own = jnp.concatenate(
+            [lax.dynamic_slice_in_dim(window, per * mine_at, rows, axis=1), received], axis=1
+        )
+        beside = jnp.concatenate(
+            [lax.dynamic_slice_in_dim(far_win, per * mine_at - base, rows, axis=1), far_src], axis=1
+        )
+        block = jnp.concatenate([own, beside, second], axis=0)
+    else:
+        block = gather(jnp.concatenate([window, received], axis=1), "seg")
+        block = jnp.concatenate(
+            [lax.dynamic_slice_in_dim(block[:, : window.shape[1]], per * mine_at, rows, axis=1),
+             block[:, window.shape[1] :]],
+            axis=1,
+        )
     segs = block.shape[0]
     cos, sin = make_forward(length)
     flat_rows = block.reshape(segs * block.shape[1], length)
@@ -155,8 +190,7 @@
     )
     white = whiten(spectra.reshape(block.shape), BAND).astype(jnp.bfloat16)
     chosen = white[:, rows:].reshape(segs, steps, nsrc, length)
-    start = lax.axis_index("seg") * per
-    part = lax.dynamic_slice_in_dim(white[:, :rows], start, per + LOW + HIGH, axis=1)
+    part = white[:, :rows]
     total = part[:, 0:per].astype(jnp.float32)
     for offset in range(1, LOW + HIGH + 1):
         total = total + part[:, offset : offset + per].astype(jnp.float32)

time: 94 us -> 99 us (1.053)
  starting transfers between devices: 61 us -> 65.4 us
    ppermute x6, starting transfers between devices: 44 us -> 48.2 us  [broadcast(): lax.ppermute(block, axis, [(i, i ^ stride) for i in range(count)])]
  transfers between devices with their start and end apart: 10 -> 10, of which waited for: 7 -> 8; matrix products, arithmetic and copies ran while one was open for 7% -> 7% of each run, Pallas kernels for 0% -> 0%
where the time goes in v15:
time: 99 us; the launch traced here: 98.2 us
  starting transfers between devices  65.4 us (66%)
  waiting for transfers between devices  12.8 us (13%)
  other arithmetic  10.9 us (11%)
  matrix products  4.87 us (5%)
  local copies, waits for them, and re-layouts  3.67 us (4%)
    ppermute x6, starting transfers between devices, broadcast(): lax.ppermute(block, axis, [(i, i ^ stride) for i in range(count)])  48.2 us
    ppermute x1, starting transfers between devices, shards(): second = lax.ppermute(sent, 'seg', [(i, i ^ 1) for i in range(4)])  10.2 us
    ppermute x6, waiting for transfers between devices, broadcast(): lax.ppermute(block, axis, [(i, i ^ stride) for i in range(count)])  8.53 us
    convert_element_type x1, other arithmetic, make_forward(): cos = cos.reshape(length, half).astype(jnp.bfloat16)  4.88 us
    ppermute x1, starting transfers between devices, broadcast(): lax.ppermute(jnp.concatenate([block, rider], axis=1), axis, [(i, i ^ 1) f...  4.38 us
    ppermute x1, waiting for transfers between devices, shards(): lax.ppermute(jnp.concatenate([lead, received], axis=1), 'seg', [(i, i ^ 2...  3.36 us
    dot_general x1, matrix products, shards(): jnp.dot(flat_rows, cos, preferred_element_type=jnp.float32)  3.19 us
  transfers between devices with their start and end apart: 10, of which 8 were waited for; matrix products, arithmetic and copies ran while one was open for 7% of the time, Pallas kernels for 0%

profile of v15, /device:TPU:1, one launch (start us, length us, event | category | flops | bytes accessed | tf_op | source)
XLA Modules:
  0.0 98.2 jit_solution(6536517397451219650)
XLA Ops:
  0.0 0.7 broadcast_compare_fusion
  0.7 0.1 and.110
  0.8 0.8 eq.40
  1.7 0.9 broadcast_select_fusion.1
  2.6 0.9 select_reduce_fusion
  3.5 4.4 %collective-permute-start = (bf16[1,12,2048]{2,1,0:T(8,128)(2,1)S(1)}, bf16[1,12,2048]{2,1,0:T(8,128)(2,1)S(1)}, u32[]{:S(2)}, u32[]{:S(2)}) collective-permute-start(bf16[1,12,2048]{2,1,0:T(8,128)(2,1)S(1)} %pad_maximum_fusion.3), channel_id=1, source_target_pairs={{0,4},{4,0},{8,12},{12,8},{16,20},{20,16},{24,28},{28,24},{32,36},... | collective-permute-start | bytes 147464 | tf_op jit(solution)/shard_map/ppermute | solution.py:17
  7.9 0.7 collective-permute-start.1
  8.6 1.0 %fusion.18 = (f32[64,1024]{1,0:T(8,128)S(1)}, f32[64,1024]{1,0:T(8,128)S(1)}) fusion(), kind=kLoop, calls=%fused_computation.42 | loop fusion | flops 917504 | bytes 524288 | tf_op jit(solution)/shard_map/sin | solution.py:59
  9.6 0.5 fusion.23
  10.2 4.9 %subtract_convert_fusion = (bf16[32,64,1024]{2,1,0:T(8,128)(2,1)}, bf16[32,64,1024]{2,1,0:T(8,128)(2,1)}) fusion(f32[64,1024]{1,0:T(8,128)S(1)} %get-tuple-element.31, f32[32,1024]{1,0:T(8,128)S(1)} %get-tuple-element.33, f32[64,1024]{1,0:T(8,128)S(1)} %get-tuple-element.32, f32[32,1024]{1,0:T(8,128)S(1)} %get-tuple-element.34), kind=kLoop, calls=%fused_computation.1 | loop fusion | flops 16777216 | bytes 9175040 | tf_op jit(solution)/shard_map/convert_element_type | solution.py:73
  15.1 15.8 %collective-permute-start.2 = (bf16[1,8,2048]{2,1,0:T(8,128)(2,1)S(1)}, bf16[1,8,2048]{2,1,0:T(8,128)(2,1)S(1)}, u32[]{:S(2)}, u32[]{:S(2)}) collective-permute-start(bf16[1,8,2048]{2,1,0:T(8,128)(2,1)S(1)} %slice_add_fusion), channel_id=1, source_target_pairs={{0,32},{4,36},{8,40},{12,44},{16,48},{20,52},{24,56},{28,60},{32,0... | collective-permute-start | bytes 98312 | tf_op jit(solution)/shard_map/ppermute | solution.py:24
  31.0 1.3 %collective-permute-done.2 = bf16[1,8,2048]{2,1,0:T(8,128)(2,1)S(1)} collective-permute-done((bf16[1,8,2048]{2,1,0:T(8,128)(2,1)S(1)}, bf16[1,8,2048]{2,1,0:T(8,128)(2,1)S(1)}, u32[]{:S(2)}, u32[]{:S(2)}) %collective-permute-start.2) | collective-permute-done | bytes 32800 | tf_op jit(solution)/shard_map/ppermute | solution.py:24
  32.3 6.2 %collective-permute-start.3 = (bf16[1,8,2048]{2,1,0:T(8,128)(2,1)S(1)}, bf16[1,8,2048]{2,1,0:T(8,128)(2,1)S(1)}, u32[]{:S(2)}, u32[]{:S(2)}) collective-permute-start(bf16[1,8,2048]{2,1,0:T(8,128)(2,1)S(1)} %add.182), channel_id=1, source_target_pairs={{0,16},{4,20},{8,24},{12,28},{16,0},{20,4},{24,8},{28,12},{32,48},... | collective-permute-start | bytes 98312 | tf_op jit(solution)/shard_map/ppermute | solution.py:24
  38.7 2.2 %collective-permute-done.3 = bf16[1,8,2048]{2,1,0:T(8,128)(2,1)S(1)} collective-permute-done((bf16[1,8,2048]{2,1,0:T(8,128)(2,1)S(1)}, bf16[1,8,2048]{2,1,0:T(8,128)(2,1)S(1)}, u32[]{:S(2)}, u32[]{:S(2)}) %collective-permute-start.3) | collective-permute-done | bytes 32800 | tf_op jit(solution)/shard_map/ppermute | solution.py:24
  40.9 4.8 %collective-permute-start.4 = (bf16[1,8,2048]{2,1,0:T(8,128)(2,1)S(1)}, bf16[1,8,2048]{2,1,0:T(8,128)(2,1)S(1)}, u32[]{:S(2)}, u32[]{:S(2)}) collective-permute-start(bf16[1,8,2048]{2,1,0:T(8,128)(2,1)S(1)} %add.183), channel_id=1, source_target_pairs={{0,8},{4,12},{8,0},{12,4},{16,24},{20,28},{24,16},{28,20},{32,40},... | collective-permute-start | bytes 98312 | tf_op jit(solution)/shard_map/ppermute | solution.py:24
  45.8 1.3 %collective-permute-done.4 = bf16[1,8,2048]{2,1,0:T(8,128)(2,1)S(1)} collective-permute-done((bf16[1,8,2048]{2,1,0:T(8,128)(2,1)S(1)}, bf16[1,8,2048]{2,1,0:T(8,128)(2,1)S(1)}, u32[]{:S(2)}, u32[]{:S(2)}) %collective-permute-start.4) | collective-permute-done | bytes 32800 | tf_op jit(solution)/shard_map/ppermute | solution.py:24
  47.0 9.7 %collective-permute-start.5 = (bf16[1,8,2048]{2,1,0:T(8,128)(2,1)S(1)}, bf16[1,8,2048]{2,1,0:T(8,128)(2,1)S(1)}, u32[]{:S(2)}, u32[]{:S(2)}) collective-permute-start(bf16[1,8,2048]{2,1,0:T(8,128)(2,1)S(1)} %add.184), channel_id=1, source_target_pairs={{0,64},{4,68},{8,72},{12,76},{16,80},{20,84},{24,88},{28,92},{32,9... | collective-permute-start | bytes 98312 | tf_op jit(solution)/shard_map/ppermute | solution.py:24
  56.8 1.3 %collective-permute-done.5 = bf16[1,8,2048]{2,1,0:T(8,128)(2,1)S(1)} collective-permute-done((bf16[1,8,2048]{2,1,0:T(8,128)(2,1)S(1)}, bf16[1,8,2048]{2,1,0:T(8,128)(2,1)S(1)}, u32[]{:S(2)}, u32[]{:S(2)}) %collective-permute-start.5) | collective-permute-done | bytes 32800 | tf_op jit(solution)/shard_map/ppermute | solution.py:24
  58.1 6.7 %collective-permute-start.6 = (bf16[1,8,2048]{2,1,0:T(8,128)(2,1)S(1)}, bf16[1,8,2048]{2,1,0:T(8,128)(2,1)S(1)}, u32[]{:S(2)}, u32[]{:S(2)}) collective-permute-start(bf16[1,8,2048]{2,1,0:T(8,128)(2,1)S(1)} %add.185), channel_id=1, source_target_pairs={{0,128},{4,132},{8,136},{12,140},{16,144},{20,148},{24,152},{28,15... | collective-permute-start | bytes 98312 | tf_op jit(solution)/shard_map/ppermute | solution.py:24
  64.8 1.2 %collective-permute-done.6 = bf16[1,8,2048]{2,1,0:T(8,128)(2,1)S(1)} collective-permute-done((bf16[1,8,2048]{2,1,0:T(8,128)(2,1)S(1)}, bf16[1,8,2048]{2,1,0:T(8,128)(2,1)S(1)}, u32[]{:S(2)}, u32[]{:S(2)}) %collective-permute-start.6) | collective-permute-done | bytes 32800 | tf_op jit(solution)/shard_map/ppermute | solution.py:24
  66.1 5.0 %collective-permute-start.7 = (bf16[1,8,2048]{2,1,0:T(8,128)(2,1)S(1)}, bf16[1,8,2048]{2,1,0:T(8,128)(2,1)S(1)}, u32[]{:S(2)}, u32[]{:S(2)}) collective-permute-start(bf16[1,8,2048]{2,1,0:T(8,128)(2,1)S(1)} %add.186), channel_id=1, source_target_pairs={{0,256},{4,260},{8,264},{12,268},{16,272},{20,276},{24,280},{28,28... | collective-permute-start | bytes 98312 | tf_op jit(solution)/shard_map/ppermute | solution.py:24
  71.1 1.3 %collective-permute-done.7 = bf16[1,8,2048]{2,1,0:T(8,128)(2,1)S(1)} collective-permute-done((bf16[1,8,2048]{2,1,0:T(8,128)(2,1)S(1)}, bf16[1,8,2048]{2,1,0:T(8,128)(2,1)S(1)}, u32[]{:S(2)}, u32[]{:S(2)}) %collective-permute-start.7) | collective-permute-done | bytes 32800 | tf_op jit(solution)/shard_map/ppermute | solution.py:24
  72.4 1.9 %collective-permute-start.8 = (bf16[1,19,2048]{2,1,0:T(8,128)(2,1)S(1)}, bf16[1,19,2048]{2,1,0:T(8,128)(2,1)S(1)}, u32[]{:S(2)}, u32[]{:S(2)}) collective-permute-start(bf16[1,19,2048]{2,1,0:T(8,128)(2,1)S(1)} %pad_maximum_fusion.2), channel_id=1, source_target_pairs={{0,2},{1,3},{2,0},{3,1},{4,6},{5,7},{6,4},{7,5},{8,10},{9,11},{10,... | collective-permute-start | bytes 233480 | tf_op jit(solution)/shard_map/ppermute | solution.py:148
  74.4 3.4 %collective-permute-done.8 = bf16[1,19,2048]{2,1,0:T(8,128)(2,1)S(1)} collective-permute-done((bf16[1,19,2048]{2,1,0:T(8,128)(2,1)S(1)}, bf16[1,19,2048]{2,1,0:T(8,128)(2,1)S(1)}, u32[]{:S(2)}, u32[]{:S(2)}) %collective-permute-start.8) | collective-permute-done | bytes 77856 | tf_op jit(solution)/shard_map/ppermute | solution.py:148
  77.9 10.2 %collective-permute-start.9 = (bf16[2,17,2048]{2,1,0:T(8,128)(2,1)S(1)}, bf16[2,17,2048]{2,1,0:T(8,128)(2,1)S(1)}, u32[]{:S(2)}, u32[]{:S(2)}) collective-permute-start(bf16[2,17,2048]{2,1,0:T(8,128)(2,1)S(1)} %maximum_maximum_fusion), channel_id=1, source_target_pairs={{0,1},{1,0},{2,3},{3,2},{4,5},{5,4},{6,7},{7,6},{8,9},{9,8},{10,11... | collective-permute-start | bytes 417800 | tf_op jit(solution)/shard_map/ppermute | solution.py:166
  88.2 0.9 collective-permute-done.9
  89.2 0.1 reshape.252
  89.3 3.2 %fusion.61 = f32[68,1024]{1,0:T(8,128)S(1)} fusion(bf16[68,2048]{1,0:T(8,128)(2,1)S(1)} %reshape.252, bf16[2048,1024]{1,0:T(8,128)(2,1)} %bitcast.37), kind=kOutput, calls=%fused_computation.119 | convolution fusion | flops 285212672 | bytes 4751360 | tf_op jit(solution)/shard_map/dot_general | solution.py:186
  92.5 0.2 copy-done
  92.7 0.9 convolution_negate_fusion
  93.6 0.1 fusion.60
  93.7 0.1 copy.24
  93.9 0.1 reduce_sum.61
  94.0 0.1 copy.17
  94.1 0.1 copy.18
  94.2 0.1 mul.456
  94.4 0.2 mul.457
  94.7 0.4 fusion.1
  95.1 0.2 bitcast_convert_fusion
  95.4 0.3 multiply_reduce_fusion.3
  95.8 0.2 add.205
  95.9 0.1 copy.22
  96.1 0.2 sub.42
  96.3 0.1 copy.23
  96.4 0.4 fusion.8
  96.9 0.1 multiply_subtract_fusion
  97.0 0.4 fusion
  97.4 0.7 mul.492
  (42 shorter events, 1.3 us)
Async XLA Ops:
  3.5 11.5 %collective-permute-start = (bf16[1,12,2048]{2,1,0:T(8,128)(2,1)S(1)}, bf16[1,12,2048]{2,1,0:T(8,128)(2,1)S(1)}, u32[]{:S(2)}, u32[]{:S(2)}) collective-permute-start(bf16[1,12,2048]{2,1,0:T(8,128)(2,1)S(1)} %pad_maximum_fusion.3), channel_id=1, source_target_pairs={{0,4},{4,0},{8,12},{12,8},{16,20},{20,16},{24,28},{28,24},{32,36},... | collective-permute-start | bytes 147464 | tf_op jit(solution)/shard_map/ppermute | solution.py:17
  7.9 37.8 %collective-permute-start.1 = (bf16[1,4,2048]{2,1,0:T(4,128)(2,1)S(1)}, bf16[1,4,2048]{2,1,0:T(4,128)(2,1)S(1)}, u32[]{:S(2)}, u32[]{:S(2)}) collective-permute-start(bf16[1,4,2048]{2,1,0:T(4,128)(2,1)S(1)} %get-tuple-element.27), channel_id=1, source_target_pairs={{4,8},{8,4},{12,16},{16,12},{20,24},{24,20},{28,32},{32,28},{36,40... | collective-permute-start | bytes 49160 | tf_op jit(solution)/shard_map/ppermute | solution.py:48
  10.2 54.6 %copy-start.1 = (bf16[1,8,2048]{2,1,0:T(8,128)(2,1)S(1)}, bf16[1,8,2048]{2,1,0:T(8,128)(2,1)}, u32[]{:S(2)}) copy-start(bf16[1,8,2048]{2,1,0:T(8,128)(2,1)} %param.3) | copy-start | bytes 98308
  15.1 17.2 %collective-permute-start.2 = (bf16[1,8,2048]{2,1,0:T(8,128)(2,1)S(1)}, bf16[1,8,2048]{2,1,0:T(8,128)(2,1)S(1)}, u32[]{:S(2)}, u32[]{:S(2)}) collective-permute-start(bf16[1,8,2048]{2,1,0:T(8,128)(2,1)S(1)} %slice_add_fusion), channel_id=1, source_target_pairs={{0,32},{4,36},{8,40},{12,44},{16,48},{20,52},{24,56},{28,60},{32,0... | collective-permute-start | bytes 98312 | tf_op jit(solution)/shard_map/ppermute | solution.py:24
  32.3 8.6 %collective-permute-start.3 = (bf16[1,8,2048]{2,1,0:T(8,128)(2,1)S(1)}, bf16[1,8,2048]{2,1,0:T(8,128)(2,1)S(1)}, u32[]{:S(2)}, u32[]{:S(2)}) collective-permute-start(bf16[1,8,2048]{2,1,0:T(8,128)(2,1)S(1)} %add.182), channel_id=1, source_target_pairs={{0,16},{4,20},{8,24},{12,28},{16,0},{20,4},{24,8},{28,12},{32,48},... | collective-permute-start | bytes 98312 | tf_op jit(solution)/shard_map/ppermute | solution.py:24
  40.9 6.1 %collective-permute-start.4 = (bf16[1,8,2048]{2,1,0:T(8,128)(2,1)S(1)}, bf16[1,8,2048]{2,1,0:T(8,128)(2,1)S(1)}, u32[]{:S(2)}, u32[]{:S(2)}) collective-permute-start(bf16[1,8,2048]{2,1,0:T(8,128)(2,1)S(1)} %add.183), channel_id=1, source_target_pairs={{0,8},{4,12},{8,0},{12,4},{16,24},{20,28},{24,16},{28,20},{32,40},... | collective-permute-start | bytes 98312 | tf_op jit(solution)/shard_map/ppermute | solution.py:24
  47.0 11.0 %collective-permute-start.5 = (bf16[1,8,2048]{2,1,0:T(8,128)(2,1)S(1)}, bf16[1,8,2048]{2,1,0:T(8,128)(2,1)S(1)}, u32[]{:S(2)}, u32[]{:S(2)}) collective-permute-start(bf16[1,8,2048]{2,1,0:T(8,128)(2,1)S(1)} %add.184), channel_id=1, source_target_pairs={{0,64},{4,68},{8,72},{12,76},{16,80},{20,84},{24,88},{28,92},{32,9... | collective-permute-start | bytes 98312 | tf_op jit(solution)/shard_map/ppermute | solution.py:24
  58.1 8.0 %collective-permute-start.6 = (bf16[1,8,2048]{2,1,0:T(8,128)(2,1)S(1)}, bf16[1,8,2048]{2,1,0:T(8,128)(2,1)S(1)}, u32[]{:S(2)}, u32[]{:S(2)}) collective-permute-start(bf16[1,8,2048]{2,1,0:T(8,128)(2,1)S(1)} %add.185), channel_id=1, source_target_pairs={{0,128},{4,132},{8,136},{12,140},{16,144},{20,148},{24,152},{28,15... | collective-permute-start | bytes 98312 | tf_op jit(solution)/shard_map/ppermute | solution.py:24
  66.1 6.3 %collective-permute-start.7 = (bf16[1,8,2048]{2,1,0:T(8,128)(2,1)S(1)}, bf16[1,8,2048]{2,1,0:T(8,128)(2,1)S(1)}, u32[]{:S(2)}, u32[]{:S(2)}) collective-permute-start(bf16[1,8,2048]{2,1,0:T(8,128)(2,1)S(1)} %add.186), channel_id=1, source_target_pairs={{0,256},{4,260},{8,264},{12,268},{16,272},{20,276},{24,280},{28,28... | collective-permute-start | bytes 98312 | tf_op jit(solution)/shard_map/ppermute | solution.py:24
  72.4 5.4 %collective-permute-start.8 = (bf16[1,19,2048]{2,1,0:T(8,128)(2,1)S(1)}, bf16[1,19,2048]{2,1,0:T(8,128)(2,1)S(1)}, u32[]{:S(2)}, u32[]{:S(2)}) collective-permute-start(bf16[1,19,2048]{2,1,0:T(8,128)(2,1)S(1)} %pad_maximum_fusion.2), channel_id=1, source_target_pairs={{0,2},{1,3},{2,0},{3,1},{4,6},{5,7},{6,4},{7,5},{8,10},{9,11},{10,... | collective-permute-start | bytes 233480 | tf_op jit(solution)/shard_map/ppermute | solution.py:148
  77.9 11.3 %collective-permute-start.9 = (bf16[2,17,2048]{2,1,0:T(8,128)(2,1)S(1)}, bf16[2,17,2048]{2,1,0:T(8,128)(2,1)S(1)}, u32[]{:S(2)}, u32[]{:S(2)}) collective-permute-start(bf16[2,17,2048]{2,1,0:T(8,128)(2,1)S(1)} %maximum_maximum_fusion), channel_id=1, source_target_pairs={{0,1},{1,0},{2,3},{3,2},{4,5},{5,4},{6,7},{7,6},{8,9},{9,8},{10,11... | collective-permute-start | bytes 417800 | tf_op jit(solution)/shard_map/ppermute | solution.py:166
  89.3 3.5 %copy-start = (bf16[32,64,1024]{2,1,0:T(8,128)(2,1)S(1)}, bf16[32,64,1024]{2,1,0:T(8,128)(2,1)}, u32[]{:S(2)}) copy-start(bf16[32,64,1024]{2,1,0:T(8,128)(2,1)} %get-tuple-element.12) | copy-start | bytes 12582916

commit v16 on v12

--- a/solution.py
+++ b/solution.py
@@ -38,19 +38,15 @@
 def edges(cells, axis):
     count = lax.axis_size(axis)
     odd = lax.axis_index(axis) % 2 == 1
-    rows = cells.shape[1]
-    tail = lax.slice_in_dim(cells, rows - LOW, rows, axis=1)
-    head = jnp.pad(lax.slice_in_dim(cells, 0, HIGH, axis=1), ((0, 0), (0, LOW - HIGH), (0, 0)))
-    rider = jnp.where(odd, head, tail)
-    other = jnp.where(odd, tail, head)
     perm = [(i, i + 1) if i % 2 else (i, i - 1) for i in range(count)]
     perm = [(i, j) for i, j in perm if 0 <= j < count]
-    return rider, lax.ppermute(other, axis, perm), odd
+    return cells, lax.ppermute(cells, axis, perm), odd
 
 
 def halo(cells, near, far, odd):
-    lower = jnp.where(odd, near, far)
-    upper = jnp.where(odd, far, near)[:, :HIGH]
+    rows = cells.shape[1]
+    lower = jnp.where(odd, near[:, rows - LOW :], far[:, rows - LOW :])
+    upper = jnp.where(odd, far[:, :HIGH], near[:, :HIGH])
     return jnp.concatenate([lower, cells, upper], axis=1)
 
 

time: 94 us -> 95.3 us (1.014)
  starting transfers between devices: 61 us -> 62.7 us
    ppermute x1, starting transfers between devices: 4.38 us -> 7.25 us  [broadcast(): lax.ppermute(jnp.concatenate([block, rider], axis=1), axis, [(i, i ^ 1) f...]
    ppermute x6, starting transfers between devices: 44 us -> 42.1 us  [broadcast(): lax.ppermute(block, axis, [(i, i ^ stride) for i in range(count)])]
  transfers between devices with their start and end apart: 10 -> 10, of which waited for: 7 -> 8; matrix products, arithmetic and copies ran while one was open for 7% -> 11% of each run, Pallas kernels for 0% -> 0%
where the time goes in v16:
time: 95.3 us; the launch traced here: 94.5 us
  starting transfers between devices  62.7 us (66%)
  waiting for transfers between devices  12.4 us (13%)
  other arithmetic  10.9 us (11%)
  matrix products  4.75 us (5%)
  local copies, waits for them, and re-layouts  3.43 us (4%)
    ppermute x6, starting transfers between devices, broadcast(): lax.ppermute(block, axis, [(i, i ^ stride) for i in range(count)])  42.1 us
    ppermute x2, starting transfers between devices, gather(): partner = lax.ppermute(block, axis, [(i, i ^ stride) for i in range(count)])  12.6 us
    ppermute x6, waiting for transfers between devices, broadcast(): lax.ppermute(block, axis, [(i, i ^ stride) for i in range(count)])  7.92 us
    ppermute x1, starting transfers between devices, broadcast(): lax.ppermute(jnp.concatenate([block, rider], axis=1), axis, [(i, i ^ 1) f...  7.25 us
    convert_element_type x1, other arithmetic, make_forward(): cos = cos.reshape(length, half).astype(jnp.bfloat16)  4.89 us
    ppermute x2, waiting for transfers between devices, gather(): partner = lax.ppermute(block, axis, [(i, i ^ stride) for i in range(count)])  4.38 us
    dot_general x1, matrix products, shards(): jnp.dot(flat_rows, cos, preferred_element_type=jnp.float32)  3.13 us
  transfers between devices with their start and end apart: 10, of which 8 were waited for; matrix products, arithmetic and copies ran while one was open for 11% of the time, Pallas kernels for 0%

profile of v16, /device:TPU:1, one launch (start us, length us, event | category | flops | bytes accessed | tf_op | source)
XLA Modules:
  0.0 94.5 jit_solution(15934175982789192476)
XLA Ops:
  0.0 0.7 collective-permute-start.1
  0.7 0.7 broadcast_compare_fusion
  1.4 0.1 and.104
  1.5 0.8 eq.40
  2.3 0.9 select_reduce_fusion
  3.3 0.8 pad_maximum_fusion.4
  4.0 7.2 %collective-permute-start = (bf16[1,16,2048]{2,1,0:T(8,128)(2,1)S(1)}, bf16[1,16,2048]{2,1,0:T(8,128)(2,1)S(1)}, u32[]{:S(2)}, u32[]{:S(2)}) collective-permute-start(bf16[1,16,2048]{2,1,0:T(8,128)(2,1)S(1)} %pad_maximum_fusion.4), channel_id=1, source_target_pairs={{0,4},{4,0},{8,12},{12,8},{16,20},{20,16},{24,28},{28,24},{32,36},... | collective-permute-start | bytes 196616 | tf_op jit(solution)/shard_map/ppermute | solution.py:17
  11.3 1.0 %fusion.17 = (f32[64,1024]{1,0:T(8,128)S(1)}, f32[64,1024]{1,0:T(8,128)S(1)}) fusion(), kind=kLoop, calls=%fused_computation.41 | loop fusion | flops 917504 | bytes 524288 | tf_op jit(solution)/shard_map/sin | solution.py:55
  12.3 0.5 fusion.22
  12.9 13.6 %collective-permute-start.2 = (bf16[1,8,2048]{2,1,0:T(8,128)(2,1)S(1)}, bf16[1,8,2048]{2,1,0:T(8,128)(2,1)S(1)}, u32[]{:S(2)}, u32[]{:S(2)}) collective-permute-start(bf16[1,8,2048]{2,1,0:T(8,128)(2,1)S(1)} %slice_add_fusion), channel_id=1, source_target_pairs={{0,32},{4,36},{8,40},{12,44},{16,48},{20,52},{24,56},{28,60},{32,0... | collective-permute-start | bytes 98312 | tf_op jit(solution)/shard_map/ppermute | solution.py:24
  26.6 4.9 %subtract_convert_fusion = (bf16[32,64,1024]{2,1,0:T(8,128)(2,1)}, bf16[32,64,1024]{2,1,0:T(8,128)(2,1)}) fusion(f32[64,1024]{1,0:T(8,128)S(1)} %get-tuple-element.23, f32[32,1024]{1,0:T(8,128)S(1)} %get-tuple-element.25, f32[64,1024]{1,0:T(8,128)S(1)} %get-tuple-element.24, f32[32,1024]{1,0:T(8,128)S(1)} %get-tuple-element.26), kind=kLoop, calls=%fused_computation.1 | loop fusion | flops 16777216 | bytes 9175040 | tf_op jit(solution)/shard_map/convert_element_type | solution.py:69
  31.5 5.9 %collective-permute-start.3 = (bf16[1,8,2048]{2,1,0:T(8,128)(2,1)S(1)}, bf16[1,8,2048]{2,1,0:T(8,128)(2,1)S(1)}, u32[]{:S(2)}, u32[]{:S(2)}) collective-permute-start(bf16[1,8,2048]{2,1,0:T(8,128)(2,1)S(1)} %add.168), channel_id=1, source_target_pairs={{0,16},{4,20},{8,24},{12,28},{16,0},{20,4},{24,8},{28,12},{32,48},... | collective-permute-start | bytes 98312 | tf_op jit(solution)/shard_map/ppermute | solution.py:24
  37.4 0.1 fusion.47
  37.5 2.5 %collective-permute-done.3 = bf16[1,8,2048]{2,1,0:T(8,128)(2,1)S(1)} collective-permute-done((bf16[1,8,2048]{2,1,0:T(8,128)(2,1)S(1)}, bf16[1,8,2048]{2,1,0:T(8,128)(2,1)S(1)}, u32[]{:S(2)}, u32[]{:S(2)}) %collective-permute-start.3) | collective-permute-done | bytes 32800 | tf_op jit(solution)/shard_map/ppermute | solution.py:24
  40.1 3.8 %collective-permute-start.4 = (bf16[1,8,2048]{2,1,0:T(8,128)(2,1)S(1)}, bf16[1,8,2048]{2,1,0:T(8,128)(2,1)S(1)}, u32[]{:S(2)}, u32[]{:S(2)}) collective-permute-start(bf16[1,8,2048]{2,1,0:T(8,128)(2,1)S(1)} %add.169), channel_id=1, source_target_pairs={{0,8},{4,12},{8,0},{12,4},{16,24},{20,28},{24,16},{28,20},{32,40},... | collective-permute-start | bytes 98312 | tf_op jit(solution)/shard_map/ppermute | solution.py:24
  43.9 0.1 fusion.54
  44.0 1.7 %collective-permute-done.4 = bf16[1,8,2048]{2,1,0:T(8,128)(2,1)S(1)} collective-permute-done((bf16[1,8,2048]{2,1,0:T(8,128)(2,1)S(1)}, bf16[1,8,2048]{2,1,0:T(8,128)(2,1)S(1)}, u32[]{:S(2)}, u32[]{:S(2)}) %collective-permute-start.4) | collective-permute-done | bytes 32800 | tf_op jit(solution)/shard_map/ppermute | solution.py:24
  45.7 7.6 %collective-permute-start.5 = (bf16[1,8,2048]{2,1,0:T(8,128)(2,1)S(1)}, bf16[1,8,2048]{2,1,0:T(8,128)(2,1)S(1)}, u32[]{:S(2)}, u32[]{:S(2)}) collective-permute-start(bf16[1,8,2048]{2,1,0:T(8,128)(2,1)S(1)} %add.170), channel_id=1, source_target_pairs={{0,64},{4,68},{8,72},{12,76},{16,80},{20,84},{24,88},{28,92},{32,9... | collective-permute-start | bytes 98312 | tf_op jit(solution)/shard_map/ppermute | solution.py:24
  53.3 1.2 %collective-permute-done.5 = bf16[1,8,2048]{2,1,0:T(8,128)(2,1)S(1)} collective-permute-done((bf16[1,8,2048]{2,1,0:T(8,128)(2,1)S(1)}, bf16[1,8,2048]{2,1,0:T(8,128)(2,1)S(1)}, u32[]{:S(2)}, u32[]{:S(2)}) %collective-permute-start.5) | collective-permute-done | bytes 32800 | tf_op jit(solution)/shard_map/ppermute | solution.py:24
  54.5 6.0 %collective-permute-start.6 = (bf16[1,8,2048]{2,1,0:T(8,128)(2,1)S(1)}, bf16[1,8,2048]{2,1,0:T(8,128)(2,1)S(1)}, u32[]{:S(2)}, u32[]{:S(2)}) collective-permute-start(bf16[1,8,2048]{2,1,0:T(8,128)(2,1)S(1)} %add.171), channel_id=1, source_target_pairs={{0,128},{4,132},{8,136},{12,140},{16,144},{20,148},{24,152},{28,15... | collective-permute-start | bytes 98312 | tf_op jit(solution)/shard_map/ppermute | solution.py:24
  60.6 1.3 %collective-permute-done.6 = bf16[1,8,2048]{2,1,0:T(8,128)(2,1)S(1)} collective-permute-done((bf16[1,8,2048]{2,1,0:T(8,128)(2,1)S(1)}, bf16[1,8,2048]{2,1,0:T(8,128)(2,1)S(1)}, u32[]{:S(2)}, u32[]{:S(2)}) %collective-permute-start.6) | collective-permute-done | bytes 32800 | tf_op jit(solution)/shard_map/ppermute | solution.py:24
  61.9 5.2 %collective-permute-start.7 = (bf16[1,8,2048]{2,1,0:T(8,128)(2,1)S(1)}, bf16[1,8,2048]{2,1,0:T(8,128)(2,1)S(1)}, u32[]{:S(2)}, u32[]{:S(2)}) collective-permute-start(bf16[1,8,2048]{2,1,0:T(8,128)(2,1)S(1)} %add.172), channel_id=1, source_target_pairs={{0,256},{4,260},{8,264},{12,268},{16,272},{20,276},{24,280},{28,28... | collective-permute-start | bytes 98312 | tf_op jit(solution)/shard_map/ppermute | solution.py:24
  67.1 1.3 %collective-permute-done.7 = bf16[1,8,2048]{2,1,0:T(8,128)(2,1)S(1)} collective-permute-done((bf16[1,8,2048]{2,1,0:T(8,128)(2,1)S(1)}, bf16[1,8,2048]{2,1,0:T(8,128)(2,1)S(1)}, u32[]{:S(2)}, u32[]{:S(2)}) %collective-permute-start.7) | collective-permute-done | bytes 32800 | tf_op jit(solution)/shard_map/ppermute | solution.py:24
  68.4 1.9 %collective-permute-start.8 = (bf16[1,23,2048]{2,1,0:T(8,128)(2,1)S(1)}, bf16[1,23,2048]{2,1,0:T(8,128)(2,1)S(1)}, u32[]{:S(2)}, u32[]{:S(2)}) collective-permute-start(bf16[1,23,2048]{2,1,0:T(8,128)(2,1)S(1)} %pad_maximum_fusion.3), channel_id=1, source_target_pairs={{0,2},{1,3},{2,0},{3,1},{4,6},{5,7},{6,4},{7,5},{8,10},{9,11},{10,... | collective-permute-start | bytes 282632 | tf_op jit(solution)/shard_map/ppermute | solution.py:32
  70.4 3.4 %collective-permute-done.8 = bf16[1,23,2048]{2,1,0:T(8,128)(2,1)S(1)} collective-permute-done((bf16[1,23,2048]{2,1,0:T(8,128)(2,1)S(1)}, bf16[1,23,2048]{2,1,0:T(8,128)(2,1)S(1)}, u32[]{:S(2)}, u32[]{:S(2)}) %collective-permute-start.8) | collective-permute-done | bytes 94240 | tf_op jit(solution)/shard_map/ppermute | solution.py:32
  73.8 10.7 %collective-permute-start.9 = (bf16[2,23,2048]{2,1,0:T(8,128)(2,1)S(1)}, bf16[2,23,2048]{2,1,0:T(8,128)(2,1)S(1)}, u32[]{:S(2)}, u32[]{:S(2)}) collective-permute-start(bf16[2,23,2048]{2,1,0:T(8,128)(2,1)S(1)} %pad_maximum_fusion.2), channel_id=1, source_target_pairs={{0,1},{1,0},{2,3},{3,2},{4,5},{5,4},{6,7},{7,6},{8,9},{9,8},{10,11... | collective-permute-start | bytes 565256 | tf_op jit(solution)/shard_map/ppermute | solution.py:32
  84.6 0.1 fusion.50
  84.7 1.0 %collective-permute-done.9 = bf16[2,23,2048]{2,1,0:T(8,128)(2,1)S(1)} collective-permute-done((bf16[2,23,2048]{2,1,0:T(8,128)(2,1)S(1)}, bf16[2,23,2048]{2,1,0:T(8,128)(2,1)S(1)}, u32[]{:S(2)}, u32[]{:S(2)}) %collective-permute-start.9) | collective-permute-done | bytes 188448 | tf_op jit(solution)/shard_map/ppermute | solution.py:32
  85.7 0.1 reshape.252
  85.8 3.1 %fusion.60 = f32[92,1024]{1,0:T(8,128)S(1)} fusion(bf16[92,2048]{1,0:T(8,128)(2,1)S(1)} %reshape.252, bf16[2048,1024]{1,0:T(8,128)(2,1)} %bitcast.35), kind=kOutput, calls=%fused_computation.109 | convolution fusion | flops 385875968 | bytes 4947968 | tf_op jit(solution)/shard_map/dot_general | solution.py:147
  88.9 0.3 copy-done
  89.3 0.8 convolution_negate_fusion
  90.1 0.2 fusion.59
  90.2 0.1 copy.14
  90.4 0.2 reduce_sum.61
  90.6 0.2 mul.441
  90.8 0.1 mul.442
  90.9 0.1 reshape_reshape.3
  91.3 0.4 bitcast_convert_fusion
  91.7 0.3 multiply_reduce_fusion.3
  92.1 0.2 add.188
  92.2 0.1 copy.12
  92.5 0.2 sub.24
  92.6 0.1 copy.13
  92.8 0.4 fusion.7
  93.2 0.1 multiply_subtract_fusion
  93.4 0.4 fusion
  93.8 0.7 mul.478
  (34 shorter events, 1.1 us)
Async XLA Ops:
  0.0 60.5 %collective-permute-start.1 = (bf16[1,8,2048]{2,1,0:T(8,128)(2,1)}, bf16[1,8,2048]{2,1,0:T(8,128)(2,1)S(1)}, u32[]{:S(2)}, u32[]{:S(2)}) collective-permute-start(bf16[1,8,2048]{2,1,0:T(8,128)(2,1)} %param.3), channel_id=1, source_target_pairs={{4,8},{8,4},{12,16},{16,12},{20,24},{24,20},{28,32},{32,28},{36,40... | collective-permute-start | bytes 98312 | tf_op jit(solution)/shard_map/ppermute | solution.py:43
  4.0 8.9 %collective-permute-start = (bf16[1,16,2048]{2,1,0:T(8,128)(2,1)S(1)}, bf16[1,16,2048]{2,1,0:T(8,128)(2,1)S(1)}, u32[]{:S(2)}, u32[]{:S(2)}) collective-permute-start(bf16[1,16,2048]{2,1,0:T(8,128)(2,1)S(1)} %pad_maximum_fusion.4), channel_id=1, source_target_pairs={{0,4},{4,0},{8,12},{12,8},{16,20},{20,16},{24,28},{28,24},{32,36},... | collective-permute-start | bytes 196616 | tf_op jit(solution)/shard_map/ppermute | solution.py:17
  12.9 18.5 %collective-permute-start.2 = (bf16[1,8,2048]{2,1,0:T(8,128)(2,1)S(1)}, bf16[1,8,2048]{2,1,0:T(8,128)(2,1)S(1)}, u32[]{:S(2)}, u32[]{:S(2)}) collective-permute-start(bf16[1,8,2048]{2,1,0:T(8,128)(2,1)S(1)} %slice_add_fusion), channel_id=1, source_target_pairs={{0,32},{4,36},{8,40},{12,44},{16,48},{20,52},{24,56},{28,60},{32,0... | collective-permute-start | bytes 98312 | tf_op jit(solution)/shard_map/ppermute | solution.py:24
  26.6 41.8 %copy-start.1 = (bf16[1,8,2048]{2,1,0:T(8,128)(2,1)S(1)}, bf16[1,8,2048]{2,1,0:T(8,128)(2,1)}, u32[]{:S(2)}) copy-start(bf16[1,8,2048]{2,1,0:T(8,128)(2,1)} %param.3) | copy-start | bytes 98308
  31.5 8.6 %collective-permute-start.3 = (bf16[1,8,2048]{2,1,0:T(8,128)(2,1)S(1)}, bf16[1,8,2048]{2,1,0:T(8,128)(2,1)S(1)}, u32[]{:S(2)}, u32[]{:S(2)}) collective-permute-start(bf16[1,8,2048]{2,1,0:T(8,128)(2,1)S(1)} %add.168), channel_id=1, source_target_pairs={{0,16},{4,20},{8,24},{12,28},{16,0},{20,4},{24,8},{28,12},{32,48},... | collective-permute-start | bytes 98312 | tf_op jit(solution)/shard_map/ppermute | solution.py:24
  40.1 5.6 %collective-permute-start.4 = (bf16[1,8,2048]{2,1,0:T(8,128)(2,1)S(1)}, bf16[1,8,2048]{2,1,0:T(8,128)(2,1)S(1)}, u32[]{:S(2)}, u32[]{:S(2)}) collective-permute-start(bf16[1,8,2048]{2,1,0:T(8,128)(2,1)S(1)} %add.169), channel_id=1, source_target_pairs={{0,8},{4,12},{8,0},{12,4},{16,24},{20,28},{24,16},{28,20},{32,40},... | collective-permute-start | bytes 98312 | tf_op jit(solution)/shard_map/ppermute | solution.py:24
  45.7 8.9 %collective-permute-start.5 = (bf16[1,8,2048]{2,1,0:T(8,128)(2,1)S(1)}, bf16[1,8,2048]{2,1,0:T(8,128)(2,1)S(1)}, u32[]{:S(2)}, u32[]{:S(2)}) collective-permute-start(bf16[1,8,2048]{2,1,0:T(8,128)(2,1)S(1)} %add.170), channel_id=1, source_target_pairs={{0,64},{4,68},{8,72},{12,76},{16,80},{20,84},{24,88},{28,92},{32,9... | collective-permute-start | bytes 98312 | tf_op jit(solution)/shard_map/ppermute | solution.py:24
  54.5 7.3 %collective-permute-start.6 = (bf16[1,8,2048]{2,1,0:T(8,128)(2,1)S(1)}, bf16[1,8,2048]{2,1,0:T(8,128)(2,1)S(1)}, u32[]{:S(2)}, u32[]{:S(2)}) collective-permute-start(bf16[1,8,2048]{2,1,0:T(8,128)(2,1)S(1)} %add.171), channel_id=1, source_target_pairs={{0,128},{4,132},{8,136},{12,140},{16,144},{20,148},{24,152},{28,15... | collective-permute-start | bytes 98312 | tf_op jit(solution)/shard_map/ppermute | solution.py:24
  61.9 6.5 %collective-permute-start.7 = (bf16[1,8,2048]{2,1,0:T(8,128)(2,1)S(1)}, bf16[1,8,2048]{2,1,0:T(8,128)(2,1)S(1)}, u32[]{:S(2)}, u32[]{:S(2)}) collective-permute-start(bf16[1,8,2048]{2,1,0:T(8,128)(2,1)S(1)} %add.172), channel_id=1, source_target_pairs={{0,256},{4,260},{8,264},{12,268},{16,272},{20,276},{24,280},{28,28... | collective-permute-start | bytes 98312 | tf_op jit(solution)/shard_map/ppermute | solution.py:24
  68.4 5.4 %collective-permute-start.8 = (bf16[1,23,2048]{2,1,0:T(8,128)(2,1)S(1)}, bf16[1,23,2048]{2,1,0:T(8,128)(2,1)S(1)}, u32[]{:S(2)}, u32[]{:S(2)}) collective-permute-start(bf16[1,23,2048]{2,1,0:T(8,128)(2,1)S(1)} %pad_maximum_fusion.3), channel_id=1, source_target_pairs={{0,2},{1,3},{2,0},{3,1},{4,6},{5,7},{6,4},{7,5},{8,10},{9,11},{10,... | collective-permute-start | bytes 282632 | tf_op jit(solution)/shard_map/ppermute | solution.py:32
  73.8 11.8 %collective-permute-start.9 = (bf16[2,23,2048]{2,1,0:T(8,128)(2,1)S(1)}, bf16[2,23,2048]{2,1,0:T(8,128)(2,1)S(1)}, u32[]{:S(2)}, u32[]{:S(2)}) collective-permute-start(bf16[2,23,2048]{2,1,0:T(8,128)(2,1)S(1)} %pad_maximum_fusion.2), channel_id=1, source_target_pairs={{0,1},{1,0},{2,3},{3,2},{4,5},{5,4},{6,7},{7,6},{8,9},{9,8},{10,11... | collective-permute-start | bytes 565256 | tf_op jit(solution)/shard_map/ppermute | solution.py:32
  85.8 3.5 %copy-start = (bf16[32,64,1024]{2,1,0:T(8,128)(2,1)S(1)}, bf16[32,64,1024]{2,1,0:T(8,128)(2,1)}, u32[]{:S(2)}) copy-start(bf16[32,64,1024]{2,1,0:T(8,128)(2,1)} %get-tuple-element.14) | copy-start | bytes 12582916
